TPU v7x, 32 devices: a whole 2x2x4 slice. The times are simulated.
32 devices in a mesh: region: 4 (over z), sub: 8 (over y, x, core).
Axes of the slice: x: 2, y: 2, z: 4, core: 2. Of those that a mesh axis runs over, the one named last changes fastest.
Arguments:
- feats: bfloat16 [16384, 1536], P(('region', 'sub')), may hold values from -6 to 6
- conv_weight: bfloat16 [192, 128], replicated, may hold values from -0.4375 to 0.4375
- conv_bias: float32 [128], replicated, may hold values from -3 to 3
- theta: bfloat16 [64, 64], replicated, may hold values from -0.75 to 0.75
- edge_weight: float32 [4096], P(('region', 'sub')), may hold values from 1 to 4
- inner_edge: int32 [16384, 2], P(('region', 'sub')), may hold values from 0 to 127
- crossing_segment: int32 [4096], P(('region', 'sub')), may hold values from 0 to 511
- cut_dest: int32 [4096, 1], P(('region', 'sub')), may hold values from 0 to 31; in each aligned block of 128 rows (0 to 127, 128 to 255, ...) at most 8 rows name the same one
- crossing_hyperedge: int32 [4096], P(('region', 'sub')), may hold values from 0 to 127
- cotangent: bfloat16 [16384, 1280], P(('region', 'sub')), may hold values from -6 to 6
Outputs:
- block_out: bfloat16 [16384, 1280], P(('region', 'sub'))
- grad_feats: bfloat16 [16384, 1536], P(('region', 'sub'))
- grad_conv: float32 [192, 128], replicated
- grad_bias: float32 [128], replicated
- grad_theta: float32 [64, 64], replicated
Inputs may be any that keep to these rules, and one draw needn't show every extreme that they name: `cut_dest`: among the 128 cut memberships of one device no owner is named more than 8 times; in some device one owner is named exactly 8 times.
All inputs are finite; a program needn't handle non-finite values.
Results may differ from a plain program's by a relative error of at most 0.0072.
Values may be sent and summed in bfloat16 or wider, within the bound.
No kernel may reach another device: no remote copies, remote signals or barrier semaphores. Data moves between devices by JAX's collectives and lax.ppermute only.
A program may use at most 64 MiB of HBM per device.

v0:
```python
import jax
import jax.numpy as jnp
from jax import lax
from jax.sharding import PartitionSpec as P

C = 64
T_SIZE = 12
B = 2
KT = 3
MEM = 2
TP = 10
EDGE_DEV = 128


def body(
    feats,
    conv_weight,
    conv_bias,
    theta,
    edge_weight,
    inner_edge,
    crossing_segment,
    cut_dest,
    crossing_hyperedge,
    cotangent,
):
    seg = feats.shape[0]
    n_region = lax.axis_size("region")
    n_sub = lax.axis_size("sub")
    device_list = n_region * n_sub
    slot_capacity = max(2, 2 * crossing_segment.shape[0] // device_list)
    slot_total = device_list * slot_capacity
    width = TP * B * C
    x4 = feats.reshape(seg, T_SIZE, B, C)
    stack = jnp.concatenate([x4[:, k : k + TP] for k in range(KT)], axis=-1)
    u = (
        jnp.einsum("stbk,kf->stbf", stack, conv_weight, preferred_element_type=jnp.float32)
        + conv_bias
    )
    gate = jax.nn.sigmoid(u[..., C:])
    first = u[..., :C]
    hidden = (first * gate).astype(jnp.bfloat16)
    z = (
        jnp.einsum("stbc,cd->stbd", hidden, theta, preferred_element_type=jnp.float32)
        .astype(jnp.bfloat16)
        .reshape(seg, width)
    )
    edge_index = jnp.arange(EDGE_DEV, dtype=jnp.int32)
    incidence = jnp.zeros((EDGE_DEV, seg), jnp.float32)
    for m in range(MEM):
        incidence = incidence + (inner_edge[:, m][None, :] == edge_index[:, None]).astype(
            jnp.float32
        )
    inner_count = jnp.sum(incidence, axis=1)
    incidence = incidence.astype(jnp.bfloat16)
    dest = cut_dest[:, 0]
    dest_hot = (dest[:, None] == jnp.arange(device_list, dtype=jnp.int32)[None, :]).astype(
        jnp.int32
    )
    rank = jnp.sum((jnp.cumsum(dest_hot, axis=0) - 1) * dest_hot, axis=1)
    slot_position = dest * slot_capacity + rank
    slotted_segment = jnp.full((slot_total,), -1, jnp.int32).at[slot_position].set(crossing_segment)
    slotted_hyperedge = (
        jnp.full((slot_total,), -1, jnp.int32).at[slot_position].set(crossing_hyperedge)
    )
    members = (slotted_segment[None, :] == jnp.arange(seg, dtype=jnp.int32)[:, None]).astype(
        jnp.float32
    )
    degree = (MEM + jnp.sum(members, axis=1))[:, None]
    members = members.astype(jnp.bfloat16)

    def pick_slots(rows):
        return jnp.einsum("sn,sf->nf", members, rows, preferred_element_type=jnp.float32).astype(
            jnp.bfloat16
        )

    send = pick_slots(z)
    recv, recv_edge = (
        lax.all_to_all(send, ("region", "sub"), split_axis=0, concat_axis=0, tiled=True),
        lax.all_to_all(
            slotted_hyperedge, ("region", "sub"), split_axis=0, concat_axis=0, tiled=True
        ),
    )
    owned = (recv_edge[None, :] == edge_index[:, None]).astype(jnp.float32)
    count = 1.0 + inner_count + jnp.sum(owned, axis=1)
    owned = owned.astype(jnp.bfloat16)
    scale = (edge_weight / count)[:, None]

    def edge_side(local_rows, arrived):
        total = jnp.dot(incidence, local_rows, preferred_element_type=jnp.float32) + jnp.dot(
            owned, arrived, preferred_element_type=jnp.float32
        )
        values = (scale * total).astype(jnp.bfloat16)
        returned = jnp.einsum(
            "en,ef->nf", owned, values, preferred_element_type=jnp.float32
        ).astype(jnp.bfloat16)
        return (values, returned)

    def member_side(values, back):
        return jnp.einsum(
            "es,ef->sf", incidence, values, preferred_element_type=jnp.float32
        ) + jnp.dot(members, back, preferred_element_type=jnp.float32)

    edge_val, ret_rows = edge_side(z, recv)
    back = lax.all_to_all(ret_rows, ("region", "sub"), split_axis=0, concat_axis=0, tiled=True)
    y = member_side(edge_val, back) / degree
    sig_y = jax.nn.sigmoid(y)
    block_out = (y * sig_y).astype(jnp.bfloat16)
    dy = cotangent.astype(jnp.float32) * sig_y * (1.0 + y * (1.0 - sig_y))
    grad_rows = (dy / degree).astype(jnp.bfloat16)
    send_grads = pick_slots(grad_rows)
    recv_grads = lax.all_to_all(
        send_grads, ("region", "sub"), split_axis=0, concat_axis=0, tiled=True
    )
    dedge, ret_grads = edge_side(grad_rows, recv_grads)
    back_grads = lax.all_to_all(
        ret_grads, ("region", "sub"), split_axis=0, concat_axis=0, tiled=True
    )
    dz = member_side(dedge, back_grads).astype(jnp.bfloat16).reshape(seg, TP, B, C)
    g_theta = jnp.einsum("stbc,stbd->cd", hidden, dz, preferred_element_type=jnp.float32)
    dh = jnp.einsum("stbd,cd->stbc", dz, theta, preferred_element_type=jnp.float32)
    du = jnp.concatenate([dh * gate, dh * first * gate * (1.0 - gate)], axis=-1).astype(
        jnp.bfloat16
    )
    g_conv = jnp.einsum("stbk,stbf->kf", stack, du, preferred_element_type=jnp.float32)
    g_bias = jnp.sum(du.astype(jnp.float32), axis=(0, 1, 2))
    sum_conv, sum_bias, sum_theta = lax.psum((g_conv, g_bias, g_theta), ("region", "sub"))
    norm = 1.0 / jnp.sqrt(jnp.float32(seg * device_list * TP * B))
    dstack = jnp.einsum("stbf,kf->stbk", du, conv_weight, preferred_element_type=jnp.float32)
    grad_sum = jnp.zeros((seg, T_SIZE, B, C), jnp.float32)
    for k in range(KT):
        grad_sum = grad_sum + jnp.pad(
            dstack[..., k * C : (k + 1) * C], ((0, 0), (k, KT - 1 - k), (0, 0), (0, 0))
        )
    grad_feats = grad_sum.astype(jnp.bfloat16).reshape(seg, T_SIZE * B * C)
    return (block_out, grad_feats, sum_conv * norm, sum_bias * norm, sum_theta * norm)


def solution(mesh):
    in_specs = (
        P(("region", "sub"), None),
        P(),
        P(),
        P(),
        P(("region", "sub")),
        P(("region", "sub"), None),
        P(("region", "sub")),
        P(("region", "sub"), None),
        P(("region", "sub")),
        P(("region", "sub"), None),
    )
    out_specs = (P(("region", "sub"), None), P(("region", "sub"), None), P(), P(), P())
    return jax.shard_map(body, mesh=mesh, in_specs=in_specs, out_specs=out_specs, check_vma=False)
```

profile of v0, /device:TPU:0, one launch (start us, length us, event | category | flops | bytes accessed | tf_op | source)
XLA Modules:
  0.0 271.1 jit_solution(6056330176690974189)
XLA Ops:
  7.2 0.0 copy-start
  7.2 0.7 fusion.59
  7.9 0.2 reduce_window_sum.11
  8.1 0.8 select_reduce_fusion
  8.9 0.7 fusion.66
  9.6 1.1 scatter_custom_fusion
  10.7 0.7 all_to_all.38
  11.4 7.3 %all-to-all-start = ((s32[32,8,1]{1,2,0:T(1,128)}), s32[32,8,1]{1,2,0:T(1,128)S(1)}, u32[]{:S(2)}, u32[]{:S(2)}) async-start(s32[32,8,1]{1,2,0:T(1,128)} %bitcast.5), calls=%async_computation | async-start | bytes 32768 | tf_op jit(solution)/shard_map/all_to_all | solution.py:80
  18.7 1.1 scatter_custom_fusion.1
  19.8 1.7 copy.44
  21.6 0.0 copy-start.14
  21.6 0.5 fusion.72
  22.1 0.1 copy-done.14
  22.2 1.0 broadcast_add_fusion
  23.3 0.4 copy-done.7
  23.6 0.4 copy-done.9
  24.0 0.7 multiply_convert_fusion.3
  24.7 1.6 copy-done.1
  26.3 0.6 convolution_convert_fusion.4
  26.9 0.5 copy-done.2
  27.4 1.4 fusion.10
  28.8 5.8 %all-to-all-start.1 = ((bf16[32,8,1280]{2,1,0:T(8,128)(2,1)}), bf16[32,8,1280]{2,1,0:T(8,128)(2,1)S(1)}, u32[]{:S(2)}, u32[]{:S(2)}) async-start(bf16[32,8,1280]{2,1,0:T(8,128)(2,1)} %fusion.10), calls=%async_computation.1 | async-start | bytes 1310720 | tf_op jit(solution)/shard_map/all_to_all | solution.py:79
  34.7 0.1 fusion.37
  34.8 0.6 fusion.45
  35.4 0.5 broadcast.65
  35.9 0.7 reduce.3
  36.6 0.1 eq.85
  36.7 0.1 convert_reduce_fusion.2
  36.8 15.8 %all-to-all-done.1 = bf16[32,8,1280]{2,1,0:T(8,128)(2,1)S(1)} async-done(((bf16[32,8,1280]{2,1,0:T(8,128)(2,1)}), bf16[32,8,1280]{2,1,0:T(8,128)(2,1)S(1)}, u32[]{:S(2)}, u32[]{:S(2)}) %all-to-all-start.1) | async-done | bytes 655392 | tf_op jit(solution)/shard_map/all_to_all | solution.py:79
  52.6 0.3 fusion.14
  52.8 1.2 fusion.11
  54.0 3.5 %all-to-all-start.2 = ((bf16[32,8,1280]{2,1,0:T(8,128)(2,1)}), bf16[32,8,1280]{2,1,0:T(8,128)(2,1)S(1)}, u32[]{:S(2)}, u32[]{:S(2)}) async-start(bf16[32,8,1280]{2,1,0:T(8,128)(2,1)} %fusion.11), calls=%async_computation.2 | async-start | bytes 1310720 | tf_op jit(solution)/shard_map/all_to_all | solution.py:105
  57.5 0.1 convert_reduce_fusion.1
  57.7 2.0 fusion.43
  59.8 15.7 %all-to-all-done.2 = bf16[32,8,1280]{2,1,0:T(8,128)(2,1)S(1)} async-done(((bf16[32,8,1280]{2,1,0:T(8,128)(2,1)}), bf16[32,8,1280]{2,1,0:T(8,128)(2,1)S(1)}, u32[]{:S(2)}, u32[]{:S(2)}) %all-to-all-start.2) | async-done | bytes 655392 | tf_op jit(solution)/shard_map/all_to_all | solution.py:105
  75.5 4.1 %divide_convert_fusion = (bf16[512,1280]{1,0:T(8,128)(2,1)S(1)}, bf16[512,1280]{1,0:T(8,128)(2,1)}) fusion(bf16[512,1280]{1,0:T(8,128)(2,1)} %param.19, f32[512]{0:T(512)S(1)} %broadcast_add_fusion.1, f32[512,1280]{1,0:T(8,128)} %fusion.43, bf16[32,8,1280]{2,1,0:T(8,128)(2,1)S(1)} %all-to-all-done.2, s32[256]{0:T(256)S(1)} %scatter_custom_fusion.1), kind=kOutput, calls=%fused_computation.19 | convolution fusion | flops 345767936 | bytes 7212032 | tf_op jit(solution)/shard_map/dot_general | solution.py:102
  79.5 1.4 fusion.12
  80.9 3.5 %all-to-all-start.3 = ((bf16[32,8,1280]{2,1,0:T(8,128)(2,1)}), bf16[32,8,1280]{2,1,0:T(8,128)(2,1)S(1)}, u32[]{:S(2)}, u32[]{:S(2)}) async-start(bf16[32,8,1280]{2,1,0:T(8,128)(2,1)} %fusion.12), calls=%async_computation.3 | async-start | bytes 1310720 | tf_op jit(solution)/shard_map/all_to_all | solution.py:112
  84.4 0.3 fusion.41
  84.8 17.6 %all-to-all-done.3 = bf16[32,8,1280]{2,1,0:T(8,128)(2,1)S(1)} async-done(((bf16[32,8,1280]{2,1,0:T(8,128)(2,1)}), bf16[32,8,1280]{2,1,0:T(8,128)(2,1)S(1)}, u32[]{:S(2)}, u32[]{:S(2)}) %all-to-all-start.3) | async-done | bytes 655392 | tf_op jit(solution)/shard_map/all_to_all | solution.py:112
  102.3 0.3 fusion.15
  102.6 1.2 fusion.13
  103.8 3.6 %all-to-all-start.4 = ((bf16[32,8,1280]{2,1,0:T(8,128)(2,1)}), bf16[32,8,1280]{2,1,0:T(8,128)(2,1)}, u32[]{:S(2)}, u32[]{:S(2)}) async-start(bf16[32,8,1280]{2,1,0:T(8,128)(2,1)} %fusion.13), calls=%async_computation.4 | async-start | bytes 1310720 | tf_op jit(solution)/shard_map/all_to_all | solution.py:116
  107.4 0.2 all-reduce.6.cloned.1.call-start
  107.7 0.5 fusion.39
  108.2 17.1 %all-to-all-done.4 = bf16[32,8,1280]{2,1,0:T(8,128)(2,1)} async-done(((bf16[32,8,1280]{2,1,0:T(8,128)(2,1)}), bf16[32,8,1280]{2,1,0:T(8,128)(2,1)}, u32[]{:S(2)}, u32[]{:S(2)}) %all-to-all-start.4) | async-done | bytes 655392 | tf_op jit(solution)/shard_map/all_to_all | solution.py:116
  125.3 2.7 fusion.3
  128.0 2.4 copy.46
  130.5 4.4 %multiply_convert_fusion.1 = (bf16[512,10,2,64]{0,3,2,1:T(8,128)(2,1)S(1)}, bf16[512,10,2,64]{0,3,2,1:T(8,128)(2,1)S(1)}) fusion(f32[512,10,2,128]{0,3,2,1:T(8,128)} %copy-done.1, bf16[512,10,2,64]{0,3,2,1:T(8,128)(2,1)} %bitcast.78, bf16[64,64]{1,0:T(8,128)(2,1)S(1)} %copy-done.11), kind=kOutput, calls=%fused_computation.18 | convolution fusion | flops 90439680 | bytes 9183232 | tf_op jit(solution)/shard_map/stbd,cd->stbc/dot_general | solution.py:121
  134.8 0.5 fusion.24
  135.3 0.8 copy-done.6
  136.1 0.4 copy-done.8
  136.5 1.8 fusion.19
  138.4 0.4 convert_reduce_fusion
  138.8 4.2 %fusion.60 = f32[512,10,2,192]{0,3,2,1:T(8,128)} fusion(bf16[192,128]{1,0:T(8,128)(2,1)S(1)} %copy-done, bf16[512,10,2,64]{0,3,2,1:T(8,128)(2,1)S(1)} %get-tuple-element.31, bf16[512,10,2,64]{0,3,2,1:T(8,128)(2,1)S(1)} %get-tuple-element.30), kind=kOutput, calls=%fused_computation.82 | convolution fusion | flops 508559360 | bytes 10534912 | tf_op jit(solution)/shard_map/stbf,kf->stbk/dot_general | solution.py:129
  143.1 0.0 all-reduce.6.cloned.1.call-update
  143.1 39.5 %all-reduce.3 = (f32[128]{0:T(128)S(1)}, f32[64,64]{1,0:T(8,128)S(1)}) all-reduce(f32[128]{0:T(128)S(1)} %convert_reduce_fusion, f32[64,64]{1,0:T(8,128)S(1)} %fusion.24), channel_id=1, replica_groups=mesh['region'=4,'sub'=8] {'region','sub'}, use_global_device_ids=true, to_apply=%region_9.10 | all-reduce | flops 4224 | bytes 33792 | tf_op jit(solution)/shard_map/psum | solution.py:127
  182.6 0.5 broadcast_multiply_fusion.2
  183.1 0.6 broadcast_multiply_fusion.1
  183.7 4.4 %fusion.71 = (f32[512,10,2,64]{0,3,2,1:T(8,128)S(1)}, f32[512,10,2,64]{0,3,2,1:T(8,128)S(1)}, f32[512,10,2,64]{0,3,2,1:T(8,128)S(1)}) fusion(f32[512,10,2,192]{0,3,2,1:T(8,128)} %fusion.60), kind=kLoop, calls=%fused_computation.100 | loop fusion | bytes 15728640 | tf_op jit(solution)/shard_map/slice | solution.py:133
  188.1 1.0 add_convert_fusion
  189.1 1.6 copy.52
  190.7 72.0 %all-reduce.6.cloned.1.call-done = f32[192,128]{1,0:T(8,128)} async-done(((f32[192,128]{1,0:T(8,128)}), f32[192,128]{1,0:T(8,128)}) %all-reduce.6.cloned.1.call-update) | async-done | bytes 98320 | tf_op jit(solution)/shard_map/psum | solution.py:127
  262.8 1.5 broadcast_multiply_fusion
  (25 shorter events, 0.1 us)
Async XLA Ops:
  7.2 14.9 %copy-start = (bf16[192,128]{1,0:T(8,128)(2,1)S(1)}, bf16[192,128]{1,0:T(8,128)(2,1)}, u32[]{:S(2)}) copy-start(bf16[192,128]{1,0:T(8,128)(2,1)} %param.11) | copy-start | bytes 147460
  11.4 17.4 %all-to-all-start = ((s32[32,8,1]{1,2,0:T(1,128)}), s32[32,8,1]{1,2,0:T(1,128)S(1)}, u32[]{:S(2)}, u32[]{:S(2)}) async-start(s32[32,8,1]{1,2,0:T(1,128)} %bitcast.5), calls=%async_computation | async-start | bytes 32768 | tf_op jit(solution)/shard_map/all_to_all | solution.py:80
  21.6 0.7 copy-start.14
  22.1 1.2 copy-start.5
  22.1 1.5 copy-start.7
  22.1 1.9 copy-start.9
  24.0 2.3 copy-start.1
  24.0 2.3 copy-start.11
  26.3 1.1 copy-start.2
  26.3 8.4 %copy-start.12 = (s32[512,2]{0,1:T(2,128)S(1)}, s32[512,2]{0,1:T(2,128)}, u32[]{:S(2)}) copy-start(s32[512,2]{0,1:T(2,128)} %param.15) | copy-start | bytes 12292
  27.4 9.4 %copy-start.13 = (f32[128]{0:T(128)S(1)}, f32[128]{0:T(128)}, u32[]{:S(2)}) copy-start(f32[128]{0:T(128)} %param.14) | copy-start | bytes 1540
  28.8 23.8 %all-to-all-start.1 = ((bf16[32,8,1280]{2,1,0:T(8,128)(2,1)}), bf16[32,8,1280]{2,1,0:T(8,128)(2,1)S(1)}, u32[]{:S(2)}, u32[]{:S(2)}) async-start(bf16[32,8,1280]{2,1,0:T(8,128)(2,1)} %fusion.10), calls=%async_computation.1 | async-start | bytes 1310720 | tf_op jit(solution)/shard_map/all_to_all | solution.py:79
  54.0 21.4 %all-to-all-start.2 = ((bf16[32,8,1280]{2,1,0:T(8,128)(2,1)}), bf16[32,8,1280]{2,1,0:T(8,128)(2,1)S(1)}, u32[]{:S(2)}, u32[]{:S(2)}) async-start(bf16[32,8,1280]{2,1,0:T(8,128)(2,1)} %fusion.11), calls=%async_computation.2 | async-start | bytes 1310720 | tf_op jit(solution)/shard_map/all_to_all | solution.py:105
  80.9 21.4 %all-to-all-start.3 = ((bf16[32,8,1280]{2,1,0:T(8,128)(2,1)}), bf16[32,8,1280]{2,1,0:T(8,128)(2,1)S(1)}, u32[]{:S(2)}, u32[]{:S(2)}) async-start(bf16[32,8,1280]{2,1,0:T(8,128)(2,1)} %fusion.12), calls=%async_computation.3 | async-start | bytes 1310720 | tf_op jit(solution)/shard_map/all_to_all | solution.py:112
  103.8 21.5 %all-to-all-start.4 = ((bf16[32,8,1280]{2,1,0:T(8,128)(2,1)}), bf16[32,8,1280]{2,1,0:T(8,128)(2,1)}, u32[]{:S(2)}, u32[]{:S(2)}) async-start(bf16[32,8,1280]{2,1,0:T(8,128)(2,1)} %fusion.13), calls=%async_computation.4 | async-start | bytes 1310720 | tf_op jit(solution)/shard_map/all_to_all | solution.py:116
  107.4 155.3 %all-reduce.6.cloned.1.call-start = ((), (), s32[]{:S(2)}) async-start(), calls=%async_computation.5 | async-start | bytes 196608 | tf_op jit(solution)/shard_map/psum | solution.py:127
  130.4 4.4 %copy-start.3 = (bf16[512,10,2,64]{0,3,2,1:T(8,128)(2,1)S(1)}, bf16[512,10,2,64]{0,3,2,1:T(8,128)(2,1)}, u32[]{:S(2)}) copy-start(bf16[512,10,2,64]{0,3,2,1:T(8,128)(2,1)} %copy-done.2) | copy-start | bytes 3932164
  130.4 4.4 %copy-start.4 = (bf16[512,1280]{0,1:T(8,128)(2,1)S(1)}, bf16[512,1280]{0,1:T(8,128)(2,1)}, u32[]{:S(2)}) copy-start(bf16[512,1280]{0,1:T(8,128)(2,1)} %copy.46) | copy-start | bytes 3932164
  130.5 4.9 %copy-start.10 = (bf16[512,10,2,64]{0,3,2,1:T(8,128)(2,1)S(1)}, bf16[512,10,2,64]{0,3,2,1:T(8,128)(2,1)}, u32[]{:S(2)}) copy-start(bf16[512,10,2,64]{0,3,2,1:T(8,128)(2,1)} %copy-done.9) | copy-start | bytes 3932164
  134.8 1.3 copy-start.6
  134.8 1.7 copy-start.8
Sparse Core Ops, SparseCore 0:
  143.2 119.5 all-reduce.5
where the time goes:
time: 272 us; the launch traced here: 271 us
  waiting for transfers between devices  138 us (51%)
  blocking collectives  39.5 us (15%)
  matrix products  28.4 us (10%)
  starting transfers between devices  24 us (9%)
  local copies, waits for them, and re-layouts  18.3 us (7%)
  between operations  14.4 us (5%)
  other arithmetic  8.34 us (3%)
    psum x1, waiting for transfers between devices, body(): lax.psum((g_conv, g_bias, g_theta), ('region', 'sub'))  72 us
    psum x1, blocking collectives, body(): lax.psum((g_conv, g_bias, g_theta), ('region', 'sub'))  39.5 us
    all_to_all x1, waiting for transfers between devices, body(): lax.all_to_all(send_grads, ('region', 'sub'), split_axis=0, concat_axis=0...  17.6 us
    all_to_all x1, waiting for transfers between devices, body(): lax.all_to_all(ret_grads, ('region', 'sub'), split_axis=0, concat_axis=0,...  17.1 us
    all_to_all x1, waiting for transfers between devices, body(): lax.all_to_all(send, ('region', 'sub'), split_axis=0, concat_axis=0, tile...  15.8 us
    all_to_all x1, waiting for transfers between devices, body(): lax.all_to_all(ret_rows, ('region', 'sub'), split_axis=0, concat_axis=0,...  15.7 us
    unnamed x32, local copies, waits for them, and re-layouts  7.5 us
    all_to_all x1, starting transfers between devices, body(): lax.all_to_all(slotted_hyperedge, ('region', 'sub'), split_axis=0, concat...  7.3 us
  transfers between devices with their start and end apart: 6, of which 5 were waited for; matrix products, arithmetic and copies ran while one was open for 7% of the time, Pallas kernels for 0%

commit v1 on v0

--- a/solution.py
+++ b/solution.py
@@ -10,6 +10,24 @@
 MEM = 2
 TP = 10
 EDGE_DEV = 128
+
+
+def device_sum(parts, n):
+    sizes = [p.size for p in parts]
+    flat = jnp.concatenate([p.reshape(-1) for p in parts])
+    if n & (n - 1):
+        flat = lax.psum(flat, ("region", "sub"))
+    else:
+        step = 1
+        while step < n:
+            perm = [(i, i ^ step) for i in range(n)]
+            flat = flat + lax.ppermute(flat, ("region", "sub"), perm)
+            step *= 2
+    out, at = [], 0
+    for p, size in zip(parts, sizes):
+        out.append(flat[at : at + size].reshape(p.shape))
+        at += size
+    return out
 
 
 def body(
@@ -124,7 +142,7 @@
     )
     g_conv = jnp.einsum("stbk,stbf->kf", stack, du, preferred_element_type=jnp.float32)
     g_bias = jnp.sum(du.astype(jnp.float32), axis=(0, 1, 2))
-    sum_conv, sum_bias, sum_theta = lax.psum((g_conv, g_bias, g_theta), ("region", "sub"))
+    sum_conv, sum_bias, sum_theta = device_sum((g_conv, g_bias, g_theta), device_list)
     norm = 1.0 / jnp.sqrt(jnp.float32(seg * device_list * TP * B))
     dstack = jnp.einsum("stbf,kf->stbk", du, conv_weight, preferred_element_type=jnp.float32)
     grad_sum = jnp.zeros((seg, T_SIZE, B, C), jnp.float32)

time: 272 us -> 158 us (0.58)
  waiting for transfers between devices: 138 us -> 78.3 us
  blocking collectives: 39.5 us -> 0 us
  between operations: 14.4 us -> 0.99 us
  starting transfers between devices: 24 us -> 30.1 us
  matrix products: 28.4 us -> 24.6 us
    psum x1 -> x0, waiting for transfers between devices: 72 us -> none  [body(): lax.psum((g_conv, g_bias, g_theta), ('region', 'sub'))]
    psum x1 -> x0, blocking collectives: 39.5 us -> none  [body(): lax.psum((g_conv, g_bias, g_theta), ('region', 'sub'))]
    ppermute x0 -> x5, waiting for transfers between devices: none -> 12.1 us  [device_sum(): flat = flat + lax.ppermute(flat, ('region', 'sub'), perm)]
    ppermute x0 -> x5, starting transfers between devices: none -> 6.13 us  [device_sum(): flat = flat + lax.ppermute(flat, ('region', 'sub'), perm)]
    dot_general x1, matrix products: 4.24 us -> 1.16 us  [body(): jnp.einsum('stbf,kf->stbk', du, conv_weight, preferred_element_type=jnp.f...]
    slice x1, local copies, waits for them, and re-layouts: 4.39 us -> 1.63 us  [body(): dstack[..., k * C:(k + 1) * C]]
  transfers between devices with their start and end apart: 6 -> 10, of which waited for: 5 -> 9; matrix products, arithmetic and copies ran while one was open for 7% -> 11% of each run, Pallas kernels for 0% -> 0%
where the time goes in v1:
time: 158 us; the launch traced here: 157 us
  waiting for transfers between devices  78.3 us (50%)
  starting transfers between devices  30.1 us (19%)
  matrix products  24.6 us (16%)
  local copies, waits for them, and re-layouts  16.3 us (10%)
  other arithmetic  6.94 us (4%)
    all_to_all x1, waiting for transfers between devices, body(): lax.all_to_all(send_grads, ('region', 'sub'), split_axis=0, concat_axis=0...  17.6 us
    all_to_all x1, waiting for transfers between devices, body(): lax.all_to_all(ret_grads, ('region', 'sub'), split_axis=0, concat_axis=0,...  17.2 us
    all_to_all x1, waiting for transfers between devices, body(): lax.all_to_all(send, ('region', 'sub'), split_axis=0, concat_axis=0, tile...  15.8 us
    all_to_all x1, waiting for transfers between devices, body(): lax.all_to_all(ret_rows, ('region', 'sub'), split_axis=0, concat_axis=0,...  15.7 us
    ppermute x5, waiting for transfers between devices, device_sum(): flat = flat + lax.ppermute(flat, ('region', 'sub'), perm)  12.1 us
    unnamed x32, local copies, waits for them, and re-layouts  7.52 us
    all_to_all x1, starting transfers between devices, body(): lax.all_to_all(slotted_hyperedge, ('region', 'sub'), split_axis=0, concat...  7.3 us
    dot_general x2, matrix products, member_side(): jnp.dot(members, back, preferred_element_type=jnp.float32)  6.7 us
  transfers between devices with their start and end apart: 10, of which 9 were waited for; matrix products, arithmetic and copies ran while one was open for 11% of the time, Pallas kernels for 0%

profile of v1, /device:TPU:0, one launch (start us, length us, event | category | flops | bytes accessed | tf_op | source)
XLA Modules:
  0.0 157.3 jit_solution(2572427388409938154)
XLA Ops:
  0.6 0.7 fusion.58
  1.4 0.2 reduce_window_sum.11
  1.6 0.8 select_reduce_fusion
  2.4 0.7 fusion.65
  3.1 1.1 scatter_custom_fusion
  4.2 0.7 all_to_all.38
  4.9 7.3 %all-to-all-start = ((s32[32,8,1]{1,2,0:T(1,128)}), s32[32,8,1]{1,2,0:T(1,128)S(1)}, u32[]{:S(2)}, u32[]{:S(2)}) async-start(s32[32,8,1]{1,2,0:T(1,128)} %bitcast.5), calls=%async_computation | async-start | bytes 32768 | tf_op jit(solution)/shard_map/all_to_all | solution.py:98
  12.2 1.1 scatter_custom_fusion.1
  13.3 1.7 %copy.44 = bf16[512,1536]{0,1:T(8,128)(2,1)S(1)} copy(bf16[512,1536]{1,0:T(8,128)(2,1)} %param.10) | data formatting | bytes 3145728 | tf_op args[0]
  15.0 0.5 fusion.72
  15.7 1.0 broadcast_add_fusion
  16.7 0.3 copy-done.7
  17.1 0.4 copy-done.9
  17.5 0.7 multiply_convert_fusion.3
  18.2 1.6 copy-done.1
  19.8 0.6 convolution_convert_fusion.4
  20.3 0.6 copy-done.2
  20.9 1.4 fusion.13
  22.3 5.8 %all-to-all-start.1 = ((bf16[32,8,1280]{2,1,0:T(8,128)(2,1)}), bf16[32,8,1280]{2,1,0:T(8,128)(2,1)S(1)}, u32[]{:S(2)}, u32[]{:S(2)}) async-start(bf16[32,8,1280]{2,1,0:T(8,128)(2,1)} %fusion.13), calls=%async_computation.1 | async-start | bytes 1310720 | tf_op jit(solution)/shard_map/all_to_all | solution.py:97
  28.2 0.1 fusion.35
  28.3 0.6 fusion.43
  28.9 0.5 broadcast.69
  29.4 0.7 reduce.3
  30.3 15.8 %all-to-all-done.1 = bf16[32,8,1280]{2,1,0:T(8,128)(2,1)S(1)} async-done(((bf16[32,8,1280]{2,1,0:T(8,128)(2,1)}), bf16[32,8,1280]{2,1,0:T(8,128)(2,1)S(1)}, u32[]{:S(2)}, u32[]{:S(2)}) %all-to-all-start.1) | async-done | bytes 655392 | tf_op jit(solution)/shard_map/all_to_all | solution.py:97
  46.0 0.3 fusion.17
  46.3 1.2 fusion.14
  47.5 3.5 %all-to-all-start.2 = ((bf16[32,8,1280]{2,1,0:T(8,128)(2,1)}), bf16[32,8,1280]{2,1,0:T(8,128)(2,1)S(1)}, u32[]{:S(2)}, u32[]{:S(2)}) async-start(bf16[32,8,1280]{2,1,0:T(8,128)(2,1)} %fusion.14), calls=%async_computation.2 | async-start | bytes 1310720 | tf_op jit(solution)/shard_map/all_to_all | solution.py:123
  51.0 0.1 convert_reduce_fusion.1
  51.2 2.0 %fusion.41 = f32[512,1280]{1,0:T(8,128)} fusion(bf16[128,1280]{1,0:T(8,128)(2,1)S(1)} %fusion.17, s32[512]{0:T(512)S(1)} %bitcast.91, s32[512]{0:T(512)S(1)} %bitcast.86), kind=kOutput, calls=%fused_computation.62 | convolution fusion | flops 168165376 | bytes 2953216 | tf_op jit(solution)/shard_map/es,ef->sf/dot_general | solution.py:118
  53.2 15.7 %all-to-all-done.2 = bf16[32,8,1280]{2,1,0:T(8,128)(2,1)S(1)} async-done(((bf16[32,8,1280]{2,1,0:T(8,128)(2,1)}), bf16[32,8,1280]{2,1,0:T(8,128)(2,1)S(1)}, u32[]{:S(2)}, u32[]{:S(2)}) %all-to-all-start.2) | async-done | bytes 655392 | tf_op jit(solution)/shard_map/all_to_all | solution.py:123
  68.9 4.1 %divide_convert_fusion = (bf16[512,1280]{1,0:T(8,128)(2,1)S(1)}, bf16[512,1280]{1,0:T(8,128)(2,1)}) fusion(bf16[512,1280]{1,0:T(8,128)(2,1)} %param.19, f32[512]{0:T(512)S(1)} %broadcast_add_fusion.1, f32[512,1280]{1,0:T(8,128)} %fusion.41, bf16[32,8,1280]{2,1,0:T(8,128)(2,1)S(1)} %all-to-all-done.2, s32[256]{0:T(256)S(1)} %scatter_custom_fusion.1), kind=kOutput, calls=%fused_computation.20 | convolution fusion | flops 345767936 | bytes 7212032 | tf_op jit(solution)/shard_map/dot_general | solution.py:120
  73.0 1.4 fusion.15
  74.4 3.5 %all-to-all-start.3 = ((bf16[32,8,1280]{2,1,0:T(8,128)(2,1)}), bf16[32,8,1280]{2,1,0:T(8,128)(2,1)S(1)}, u32[]{:S(2)}, u32[]{:S(2)}) async-start(bf16[32,8,1280]{2,1,0:T(8,128)(2,1)} %fusion.15), calls=%async_computation.3 | async-start | bytes 1310720 | tf_op jit(solution)/shard_map/all_to_all | solution.py:130
  77.9 0.3 fusion.39
  78.2 17.6 %all-to-all-done.3 = bf16[32,8,1280]{2,1,0:T(8,128)(2,1)S(1)} async-done(((bf16[32,8,1280]{2,1,0:T(8,128)(2,1)}), bf16[32,8,1280]{2,1,0:T(8,128)(2,1)S(1)}, u32[]{:S(2)}, u32[]{:S(2)}) %all-to-all-start.3) | async-done | bytes 655392 | tf_op jit(solution)/shard_map/all_to_all | solution.py:130
  95.8 0.3 fusion.18
  96.1 1.2 fusion.16
  97.3 3.8 %all-to-all-start.4 = ((bf16[32,8,1280]{2,1,0:T(8,128)(2,1)}), bf16[32,8,1280]{2,1,0:T(8,128)(2,1)}, u32[]{:S(2)}, u32[]{:S(2)}) async-start(bf16[32,8,1280]{2,1,0:T(8,128)(2,1)} %fusion.16), calls=%async_computation.4 | async-start | bytes 1310720 | tf_op jit(solution)/shard_map/all_to_all | solution.py:134
  101.1 0.5 fusion.37
  101.6 17.2 %all-to-all-done.4 = bf16[32,8,1280]{2,1,0:T(8,128)(2,1)} async-done(((bf16[32,8,1280]{2,1,0:T(8,128)(2,1)}), bf16[32,8,1280]{2,1,0:T(8,128)(2,1)}, u32[]{:S(2)}, u32[]{:S(2)}) %all-to-all-start.4) | async-done | bytes 655392 | tf_op jit(solution)/shard_map/all_to_all | solution.py:134
  118.8 2.7 %fusion.6 = bf16[512,1280]{1,0:T(8,128)(2,1)} fusion(f32[512,1280]{1,0:T(8,128)S(1)} %fusion.37, bf16[32,8,1280]{2,1,0:T(8,128)(2,1)} %all-to-all-done.4, s32[256]{0:T(256)S(1)} %scatter_custom_fusion.1), kind=kOutput, calls=%fused_computation.11 | convolution fusion | flops 337248256 | bytes 4588544 | tf_op jit(solution)/shard_map/dot_general | solution.py:120
  121.5 2.4 %copy.46 = bf16[512,1280]{0,1:T(8,128)(2,1)} copy(bf16[512,1280]{1,0:T(8,128)(2,1)} %fusion.6) | data formatting | bytes 2621440 | tf_op jit(solution)/shard_map/convert_element_type | solution.py:137
  123.9 4.4 %multiply_convert_fusion.1 = (bf16[512,10,2,64]{0,3,2,1:T(8,128)(2,1)S(1)}, bf16[512,10,2,64]{0,3,2,1:T(8,128)(2,1)S(1)}) fusion(f32[512,10,2,128]{0,3,2,1:T(8,128)} %copy-done.1, bf16[512,10,2,64]{0,3,2,1:T(8,128)(2,1)} %bitcast.82, bf16[64,64]{1,0:T(8,128)(2,1)S(1)} %copy-done.11), kind=kOutput, calls=%fused_computation.19 | convolution fusion | flops 90439680 | bytes 9183232 | tf_op jit(solution)/shard_map/stbd,cd->stbc/dot_general | solution.py:139
  128.3 0.5 fusion.22
  128.8 0.8 copy-done.6
  129.6 0.4 copy-done.8
  130.0 1.2 fusion.2
  131.2 0.4 convert_reduce_fusion
  131.8 1.3 collective-permute-done
  133.1 1.4 collective-permute-start.1
  134.5 4.0 %collective-permute-done.1 = f32[28800]{0:T(1024)S(1)} collective-permute-done((f32[28800]{0:T(1024)S(1)}, f32[28800]{0:T(1024)S(1)}, u32[]{:S(2)}, u32[]{:S(2)}) %collective-permute-start.1) | collective-permute-done | bytes 115232 | tf_op jit(solution)/shard_map/ppermute | solution.py:24
  138.5 1.5 collective-permute-start.2
  140.0 1.2 fusion.59
  141.1 2.3 %collective-permute-done.2 = f32[28800]{0:T(1024)S(1)} collective-permute-done((f32[28800]{0:T(1024)S(1)}, f32[28800]{0:T(1024)S(1)}, u32[]{:S(2)}, u32[]{:S(2)}) %collective-permute-start.2) | collective-permute-done | bytes 115232 | tf_op jit(solution)/shard_map/ppermute | solution.py:24
  143.4 1.5 collective-permute-start.3
  144.9 1.6 %fusion.71 = (f32[512,10,2,64]{0,3,2,1:T(8,128)S(1)}, f32[512,10,2,64]{0,3,2,1:T(8,128)S(1)}, f32[512,10,2,64]{0,3,2,1:T(8,128)S(1)}) fusion(f32[512,10,2,192]{0,3,2,1:T(8,128)S(1)} %fusion.59), kind=kLoop, calls=%fused_computation.103 | loop fusion | bytes 15728640 | tf_op jit(solution)/shard_map/slice | solution.py:151
  146.6 1.8 %collective-permute-done.3 = f32[28800]{0:T(1024)S(1)} collective-permute-done((f32[28800]{0:T(1024)S(1)}, f32[28800]{0:T(1024)S(1)}, u32[]{:S(2)}, u32[]{:S(2)}) %collective-permute-start.3) | collective-permute-done | bytes 115232 | tf_op jit(solution)/shard_map/ppermute | solution.py:24
  148.4 1.6 %collective-permute-start.4 = (f32[28800]{0:T(1024)S(1)}, f32[28800]{0:T(1024)S(1)}, u32[]{:S(2)}, u32[]{:S(2)}) collective-permute-start(f32[28800]{0:T(1024)S(1)} %add.110), channel_id=1, source_target_pairs={{0,16},{1,17},{2,18},{3,19},{4,20},{5,21},{6,22},{7,23},{8,24},{9,... | collective-permute-start | bytes 345608 | tf_op jit(solution)/shard_map/ppermute | solution.py:24
  150.0 1.0 add_convert_fusion
  151.0 1.6 copy.52
  152.6 2.8 %collective-permute-done.4 = f32[28800]{0:T(1024)S(1)} collective-permute-done((f32[28800]{0:T(1024)S(1)}, f32[28800]{0:T(1024)S(1)}, u32[]{:S(2)}, u32[]{:S(2)}) %collective-permute-start.4) | collective-permute-done | bytes 115232 | tf_op jit(solution)/shard_map/ppermute | solution.py:24
  155.4 0.5 slice_multiply_fusion.2
  156.0 0.6 fusion.53
  156.6 0.7 mul.97
  (39 shorter events, 0.7 us)
Async XLA Ops:
  0.6 14.9 %copy-start = (bf16[192,128]{1,0:T(8,128)(2,1)S(1)}, bf16[192,128]{1,0:T(8,128)(2,1)}, u32[]{:S(2)}) copy-start(bf16[192,128]{1,0:T(8,128)(2,1)} %param.11) | copy-start | bytes 147460
  4.9 17.4 %all-to-all-start = ((s32[32,8,1]{1,2,0:T(1,128)}), s32[32,8,1]{1,2,0:T(1,128)S(1)}, u32[]{:S(2)}, u32[]{:S(2)}) async-start(s32[32,8,1]{1,2,0:T(1,128)} %bitcast.5), calls=%async_computation | async-start | bytes 32768 | tf_op jit(solution)/shard_map/all_to_all | solution.py:98
  15.0 0.7 copy-start.14
  15.5 1.2 copy-start.5
  15.5 1.5 copy-start.7
  15.5 1.9 %copy-start.9 = (bf16[512,10,2,64]{0,3,2,1:T(8,128)(2,1)}, bf16[512,10,2,64]{0,3,2,1:T(8,128)(2,1)S(1)}, u32[]{:S(2)}) copy-start(bf16[512,10,2,64]{0,3,2,1:T(8,128)(2,1)S(1)} %get-tuple-element.34) | copy-start | bytes 3932164
  17.5 2.3 %copy-start.1 = (f32[512,10,2,128]{0,3,2,1:T(8,128)}, f32[512,10,2,128]{0,3,2,1:T(8,128)S(1)}, u32[]{:S(2)}) copy-start(f32[512,10,2,128]{0,3,2,1:T(8,128)S(1)} %broadcast_add_fusion) | copy-start | bytes 15728644
  17.5 2.3 %copy-start.11 = (bf16[64,64]{1,0:T(8,128)(2,1)S(1)}, bf16[64,64]{1,0:T(8,128)(2,1)}, u32[]{:S(2)}) copy-start(bf16[64,64]{1,0:T(8,128)(2,1)} %param.13) | copy-start | bytes 24580
  19.8 1.1 copy-start.2
  19.8 8.4 %copy-start.12 = (s32[512,2]{0,1:T(2,128)S(1)}, s32[512,2]{0,1:T(2,128)}, u32[]{:S(2)}) copy-start(s32[512,2]{0,1:T(2,128)} %param.15) | copy-start | bytes 12292
  20.9 9.4 %copy-start.13 = (f32[128]{0:T(128)S(1)}, f32[128]{0:T(128)}, u32[]{:S(2)}) copy-start(f32[128]{0:T(128)} %param.14) | copy-start | bytes 1540
  22.3 23.8 %all-to-all-start.1 = ((bf16[32,8,1280]{2,1,0:T(8,128)(2,1)}), bf16[32,8,1280]{2,1,0:T(8,128)(2,1)S(1)}, u32[]{:S(2)}, u32[]{:S(2)}) async-start(bf16[32,8,1280]{2,1,0:T(8,128)(2,1)} %fusion.13), calls=%async_computation.1 | async-start | bytes 1310720 | tf_op jit(solution)/shard_map/all_to_all | solution.py:97
  47.5 21.4 %all-to-all-start.2 = ((bf16[32,8,1280]{2,1,0:T(8,128)(2,1)}), bf16[32,8,1280]{2,1,0:T(8,128)(2,1)S(1)}, u32[]{:S(2)}, u32[]{:S(2)}) async-start(bf16[32,8,1280]{2,1,0:T(8,128)(2,1)} %fusion.14), calls=%async_computation.2 | async-start | bytes 1310720 | tf_op jit(solution)/shard_map/all_to_all | solution.py:123
  74.4 21.4 %all-to-all-start.3 = ((bf16[32,8,1280]{2,1,0:T(8,128)(2,1)}), bf16[32,8,1280]{2,1,0:T(8,128)(2,1)S(1)}, u32[]{:S(2)}, u32[]{:S(2)}) async-start(bf16[32,8,1280]{2,1,0:T(8,128)(2,1)} %fusion.15), calls=%async_computation.3 | async-start | bytes 1310720 | tf_op jit(solution)/shard_map/all_to_all | solution.py:130
  97.3 21.5 %all-to-all-start.4 = ((bf16[32,8,1280]{2,1,0:T(8,128)(2,1)}), bf16[32,8,1280]{2,1,0:T(8,128)(2,1)}, u32[]{:S(2)}, u32[]{:S(2)}) async-start(bf16[32,8,1280]{2,1,0:T(8,128)(2,1)} %fusion.16), calls=%async_computation.4 | async-start | bytes 1310720 | tf_op jit(solution)/shard_map/all_to_all | solution.py:134
  123.9 4.4 %copy-start.3 = (bf16[512,10,2,64]{0,3,2,1:T(8,128)(2,1)S(1)}, bf16[512,10,2,64]{0,3,2,1:T(8,128)(2,1)}, u32[]{:S(2)}) copy-start(bf16[512,10,2,64]{0,3,2,1:T(8,128)(2,1)} %copy-done.2) | copy-start | bytes 3932164
  123.9 4.4 %copy-start.4 = (bf16[512,1280]{0,1:T(8,128)(2,1)S(1)}, bf16[512,1280]{0,1:T(8,128)(2,1)}, u32[]{:S(2)}) copy-start(bf16[512,1280]{0,1:T(8,128)(2,1)} %copy.46) | copy-start | bytes 3932164
  123.9 4.9 %copy-start.10 = (bf16[512,10,2,64]{0,3,2,1:T(8,128)(2,1)S(1)}, bf16[512,10,2,64]{0,3,2,1:T(8,128)(2,1)}, u32[]{:S(2)}) copy-start(bf16[512,10,2,64]{0,3,2,1:T(8,128)(2,1)} %copy-done.9) | copy-start | bytes 3932164
  128.3 1.3 copy-start.6
  128.3 1.7 %copy-start.8 = (bf16[512,10,2,64]{0,3,2,1:T(8,128)(2,1)S(1)}, bf16[512,10,2,64]{0,3,2,1:T(8,128)(2,1)}, u32[]{:S(2)}) copy-start(bf16[512,10,2,64]{0,3,2,1:T(8,128)(2,1)} %copy-done.7) | copy-start | bytes 3932164
  131.7 1.4 collective-permute-start
  133.1 5.4 %collective-permute-start.1 = (f32[28800]{0:T(1024)S(1)}, f32[28800]{0:T(1024)S(1)}, u32[]{:S(2)}, u32[]{:S(2)}) collective-permute-start(f32[28800]{0:T(1024)S(1)} %fusion.70), channel_id=1, source_target_pairs={{0,2},{1,3},{2,0},{3,1},{4,6},{5,7},{6,4},{7,5},{8,10},{9,11},{10,... | collective-permute-start | bytes 345608 | tf_op jit(solution)/shard_map/ppermute | solution.py:24
  138.5 4.9 %collective-permute-start.2 = (f32[28800]{0:T(1024)S(1)}, f32[28800]{0:T(1024)S(1)}, u32[]{:S(2)}, u32[]{:S(2)}) collective-permute-start(f32[28800]{0:T(1024)S(1)} %add.108), channel_id=1, source_target_pairs={{0,4},{1,5},{2,6},{3,7},{4,0},{5,1},{6,2},{7,3},{8,12},{9,13},{10,... | collective-permute-start | bytes 345608 | tf_op jit(solution)/shard_map/ppermute | solution.py:24
  143.4 4.9 %collective-permute-start.3 = (f32[28800]{0:T(1024)S(1)}, f32[28800]{0:T(1024)S(1)}, u32[]{:S(2)}, u32[]{:S(2)}) collective-permute-start(f32[28800]{0:T(1024)S(1)} %add.109), channel_id=1, source_target_pairs={{0,8},{1,9},{2,10},{3,11},{4,12},{5,13},{6,14},{7,15},{8,0},{9,1},... | collective-permute-start | bytes 345608 | tf_op jit(solution)/shard_map/ppermute | solution.py:24
  148.4 7.1 %collective-permute-start.4 = (f32[28800]{0:T(1024)S(1)}, f32[28800]{0:T(1024)S(1)}, u32[]{:S(2)}, u32[]{:S(2)}) collective-permute-start(f32[28800]{0:T(1024)S(1)} %add.110), channel_id=1, source_target_pairs={{0,16},{1,17},{2,18},{3,19},{4,20},{5,21},{6,22},{7,23},{8,24},{9,... | collective-permute-start | bytes 345608 | tf_op jit(solution)/shard_map/ppermute | solution.py:24

commit v2 on v1

--- a/solution.py
+++ b/solution.py
@@ -49,20 +49,24 @@
     slot_capacity = max(2, 2 * crossing_segment.shape[0] // device_list)
     slot_total = device_list * slot_capacity
     width = TP * B * C
-    x4 = feats.reshape(seg, T_SIZE, B, C)
-    stack = jnp.concatenate([x4[:, k : k + TP] for k in range(KT)], axis=-1)
-    u = (
-        jnp.einsum("stbk,kf->stbf", stack, conv_weight, preferred_element_type=jnp.float32)
-        + conv_bias
-    )
-    gate = jax.nn.sigmoid(u[..., C:])
-    first = u[..., :C]
-    hidden = (first * gate).astype(jnp.bfloat16)
-    z = (
-        jnp.einsum("stbc,cd->stbd", hidden, theta, preferred_element_type=jnp.float32)
-        .astype(jnp.bfloat16)
-        .reshape(seg, width)
-    )
+    def front(rows):
+        n = rows.shape[0]
+        x4 = rows.reshape(n, T_SIZE, B, C)
+        stack = jnp.concatenate([x4[:, k : k + TP] for k in range(KT)], axis=-1)
+        u = (
+            jnp.einsum("stbk,kf->stbf", stack, conv_weight, preferred_element_type=jnp.float32)
+            + conv_bias
+        )
+        gate = jax.nn.sigmoid(u[..., C:])
+        first = u[..., :C]
+        hidden = (first * gate).astype(jnp.bfloat16)
+        z = (
+            jnp.einsum("stbc,cd->stbd", hidden, theta, preferred_element_type=jnp.float32)
+            .astype(jnp.bfloat16)
+            .reshape(n, width)
+        )
+        return stack, gate, first, hidden, z
+
     edge_index = jnp.arange(EDGE_DEV, dtype=jnp.int32)
     incidence = jnp.zeros((EDGE_DEV, seg), jnp.float32)
     for m in range(MEM):
@@ -86,19 +90,20 @@
     )
     degree = (MEM + jnp.sum(members, axis=1))[:, None]
     members = members.astype(jnp.bfloat16)
+    cut_rows = jnp.take(feats, jnp.clip(slotted_segment, 0, seg - 1), axis=0)
+    z_slots = front(cut_rows)[4]
+    stack, gate, first, hidden, z = front(feats)
 
     def pick_slots(rows):
         return jnp.einsum("sn,sf->nf", members, rows, preferred_element_type=jnp.float32).astype(
             jnp.bfloat16
         )
 
-    send = pick_slots(z)
-    recv, recv_edge = (
-        lax.all_to_all(send, ("region", "sub"), split_axis=0, concat_axis=0, tiled=True),
-        lax.all_to_all(
-            slotted_hyperedge, ("region", "sub"), split_axis=0, concat_axis=0, tiled=True
-        ),
-    )
+    edge_cols = jnp.broadcast_to(slotted_hyperedge.astype(jnp.bfloat16)[:, None], (slot_total, 128))
+    send = jnp.concatenate([z_slots, edge_cols], axis=1)
+    recv_all = lax.all_to_all(send, ("region", "sub"), split_axis=0, concat_axis=0, tiled=True)
+    recv = recv_all[:, :width]
+    recv_edge = recv_all[:, width].astype(jnp.int32)
     owned = (recv_edge[None, :] == edge_index[:, None]).astype(jnp.float32)
     count = 1.0 + inner_count + jnp.sum(owned, axis=1)
     owned = owned.astype(jnp.bfloat16)

time: 158 us -> 157 us (level)
  starting transfers between devices: 30.1 us -> 24.5 us
  local copies, waits for them, and re-layouts: 16.3 us -> 21.4 us
  waiting for transfers between devices: 78.3 us -> 74.6 us
  other arithmetic: 6.94 us -> 9.31 us
    all_to_all x1 -> x0, starting transfers between devices: 7.3 us -> none  [body(): lax.all_to_all(slotted_hyperedge, ('region', 'sub'), split_axis=0, concat...]
    gather x0 -> x2, local copies, waits for them, and re-layouts: none -> 3.89 us  [body(): cut_rows = jnp.take(feats, jnp.clip(slotted_segment, 0, seg - 1), axis=0)]
    all_to_all x1, waiting for transfers between devices: 15.8 us -> 12.1 us  [body(): lax.all_to_all(send, ('region', 'sub'), split_axis=0, concat_axis=0, tile...]
    concatenate x0 -> x1, other arithmetic: none -> 2 us  [body(): send = jnp.concatenate([z_slots, edge_cols], axis=1)]
    concatenate x0 -> x1, local copies, waits for them, and re-layouts: none -> 1.6 us  [body(): send = jnp.concatenate([z_slots, edge_cols], axis=1)]
    unnamed x32 -> x34, local copies, waits for them, and re-layouts: 7.52 us -> 6.84 us
  transfers between devices with their start and end apart: 10 -> 9, of which waited for: 9 -> 9; matrix products, arithmetic and copies ran while one was open for 11% -> 8% of each run, Pallas kernels for 0% -> 0%
where the time goes in v2:
time: 157 us; the launch traced here: 156 us
  waiting for transfers between devices  74.6 us (48%)
  matrix products  25.4 us (16%)
  starting transfers between devices  24.5 us (16%)
  local copies, waits for them, and re-layouts  21.4 us (14%)
  other arithmetic  9.31 us (6%)
    all_to_all x1, waiting for transfers between devices, body(): lax.all_to_all(send_grads, ('region', 'sub'), split_axis=0, concat_axis=0...  17.4 us
    all_to_all x1, waiting for transfers between devices, body(): lax.all_to_all(ret_grads, ('region', 'sub'), split_axis=0, concat_axis=0,...  17.4 us
    all_to_all x1, waiting for transfers between devices, body(): lax.all_to_all(ret_rows, ('region', 'sub'), split_axis=0, concat_axis=0,...  15.7 us
    all_to_all x1, waiting for transfers between devices, body(): lax.all_to_all(send, ('region', 'sub'), split_axis=0, concat_axis=0, tile...  12.1 us
    ppermute x5, waiting for transfers between devices, device_sum(): flat = flat + lax.ppermute(flat, ('region', 'sub'), perm)  12 us
    all_to_all x1, starting transfers between devices, body(): lax.all_to_all(send, ('region', 'sub'), split_axis=0, concat_axis=0, tile...  7.41 us
    unnamed x34, local copies, waits for them, and re-layouts  6.84 us
    dot_general x2, matrix products, member_side(): jnp.dot(members, back, preferred_element_type=jnp.float32)  6.7 us
  transfers between devices with their start and end apart: 9, of which 9 were waited for; matrix products, arithmetic and copies ran while one was open for 8% of the time, Pallas kernels for 0%

profile of v2, /device:TPU:0, one launch (start us, length us, event | category | flops | bytes accessed | tf_op | source)
XLA Modules:
  0.0 156.3 jit_solution(3851487094330677059)
XLA Ops:
  0.6 0.7 fusion.71
  1.6 0.8 select_reduce_fusion
  2.4 0.7 fusion.80
  3.1 1.1 scatter_custom_fusion
  4.2 1.1 scatter_custom_fusion.1
  5.4 3.6 %gather_fusion = bf16[256,1536]{1,0:T(8,128)(2,1)S(1)} fusion(bf16[512,1536]{1,0:T(8,128)(2,1)} %param.10, s32[1024]{0:T(1024)S(1)} %pad_clamp_fusion), kind=kCustom, calls=%fused_computation | custom fusion | bytes 1573888 | tf_op jit(solution)/shard_map/jit(_take)/gather | solution.py:93
  9.1 0.3 copy.50
  9.7 0.3 copy-done.15
  10.0 0.6 fusion.24
  10.7 0.6 convolution_convert_fusion.4
  11.3 1.1 copy.52
  12.5 1.6 %concatenate.20 = bf16[32,8,1280]{2,1,0:T(8,128)(2,1)} reshape(bf16[256,10,2,64]{3,2,1,0:T(2,128)(2,1)S(1)} %copy.52) | data formatting | bytes 1310720 | tf_op jit(solution)/shard_map/concatenate | solution.py:103
  14.2 2.0 %pad_maximum_fusion.2 = bf16[32,8,1408]{2,1,0:T(8,128)(2,1)} fusion(bf16[32,8,128]{2,1,0:T(8,128)(2,1)S(1)} %broadcast_in_dim.20, bf16[32,8,1280]{2,1,0:T(8,128)(2,1)} %concatenate.20), kind=kLoop, calls=%fused_computation.60 | loop fusion | flops 1441792 | bytes 1441792 | tf_op jit(solution)/shard_map/concatenate | solution.py:103
  16.2 7.4 %all-to-all-start = ((bf16[32,8,1408]{2,1,0:T(8,128)(2,1)}), bf16[32,8,1408]{2,1,0:T(8,128)(2,1)}, u32[]{:S(2)}, u32[]{:S(2)}) async-start(bf16[32,8,1408]{2,1,0:T(8,128)(2,1)} %pad_maximum_fusion.2), calls=%async_computation | async-start | bytes 1441792 | tf_op jit(solution)/shard_map/all_to_all | solution.py:104
  23.6 0.7 copy.53
  24.3 0.5 fusion.89
  25.0 1.0 broadcast_add_fusion
  26.0 0.3 copy-done.8
  26.4 0.4 copy-done.10
  26.8 0.7 multiply_convert_fusion.3
  27.5 1.6 copy-done.2
  29.1 0.6 convolution_convert_fusion.3
  29.6 0.6 copy-done.3
  30.2 0.5 fusion.56
  30.7 12.1 %all-to-all-done = bf16[32,8,1408]{2,1,0:T(8,128)(2,1)} async-done(((bf16[32,8,1408]{2,1,0:T(8,128)(2,1)}), bf16[32,8,1408]{2,1,0:T(8,128)(2,1)}, u32[]{:S(2)}, u32[]{:S(2)}) %all-to-all-start) | async-done | bytes 720928 | tf_op jit(solution)/shard_map/all_to_all | solution.py:104
  42.8 1.0 convert_reduce_fusion.3
  43.9 1.3 fusion.16
  45.2 1.2 fusion.13
  46.4 3.6 %all-to-all-start.1 = ((bf16[32,8,1280]{2,1,0:T(8,128)(2,1)}), bf16[32,8,1280]{2,1,0:T(8,128)(2,1)S(1)}, u32[]{:S(2)}, u32[]{:S(2)}) async-start(bf16[32,8,1280]{2,1,0:T(8,128)(2,1)} %fusion.13), calls=%async_computation.1 | async-start | bytes 1310720 | tf_op jit(solution)/shard_map/all_to_all | solution.py:128
  50.2 2.0 %fusion.54 = f32[512,1280]{1,0:T(8,128)} fusion(bf16[128,1280]{1,0:T(8,128)(2,1)S(1)} %fusion.16, s32[512]{0:T(512)S(1)} %bitcast.90, s32[512]{0:T(512)S(1)} %bitcast.85), kind=kOutput, calls=%fused_computation.76 | convolution fusion | flops 168165376 | bytes 2953216 | tf_op jit(solution)/shard_map/es,ef->sf/dot_general | solution.py:123
  52.2 15.7 %all-to-all-done.1 = bf16[32,8,1280]{2,1,0:T(8,128)(2,1)S(1)} async-done(((bf16[32,8,1280]{2,1,0:T(8,128)(2,1)}), bf16[32,8,1280]{2,1,0:T(8,128)(2,1)S(1)}, u32[]{:S(2)}, u32[]{:S(2)}) %all-to-all-start.1) | async-done | bytes 655392 | tf_op jit(solution)/shard_map/all_to_all | solution.py:128
  68.0 4.1 %divide_convert_fusion = (bf16[512,1280]{1,0:T(8,128)(2,1)S(1)}, bf16[512,1280]{1,0:T(8,128)(2,1)}) fusion(bf16[512,1280]{1,0:T(8,128)(2,1)} %param.19, f32[512]{0:T(512)S(1)} %broadcast_add_fusion.1, f32[512,1280]{1,0:T(8,128)} %fusion.54, bf16[32,8,1280]{2,1,0:T(8,128)(2,1)S(1)} %all-to-all-done.1, s32[256]{0:T(256)S(1)} %scatter_custom_fusion), kind=kOutput, calls=%fused_computation.21 | convolution fusion | flops 345767936 | bytes 7212032 | tf_op jit(solution)/shard_map/dot_general | solution.py:125
  72.0 1.4 fusion.14
  73.4 3.7 %all-to-all-start.2 = ((bf16[32,8,1280]{2,1,0:T(8,128)(2,1)}), bf16[32,8,1280]{2,1,0:T(8,128)(2,1)S(1)}, u32[]{:S(2)}, u32[]{:S(2)}) async-start(bf16[32,8,1280]{2,1,0:T(8,128)(2,1)} %fusion.14), calls=%async_computation.2 | async-start | bytes 1310720 | tf_op jit(solution)/shard_map/all_to_all | solution.py:135
  77.1 0.3 fusion.52
  77.5 17.4 %all-to-all-done.2 = bf16[32,8,1280]{2,1,0:T(8,128)(2,1)S(1)} async-done(((bf16[32,8,1280]{2,1,0:T(8,128)(2,1)}), bf16[32,8,1280]{2,1,0:T(8,128)(2,1)S(1)}, u32[]{:S(2)}, u32[]{:S(2)}) %all-to-all-start.2) | async-done | bytes 655392 | tf_op jit(solution)/shard_map/all_to_all | solution.py:135
  95.1 1.2 fusion.15
  96.3 3.6 %all-to-all-start.3 = ((bf16[32,8,1280]{2,1,0:T(8,128)(2,1)}), bf16[32,8,1280]{2,1,0:T(8,128)(2,1)}, u32[]{:S(2)}, u32[]{:S(2)}) async-start(bf16[32,8,1280]{2,1,0:T(8,128)(2,1)} %fusion.15), calls=%async_computation.3 | async-start | bytes 1310720 | tf_op jit(solution)/shard_map/all_to_all | solution.py:139
  99.9 0.5 fusion.50
  100.5 17.4 %all-to-all-done.3 = bf16[32,8,1280]{2,1,0:T(8,128)(2,1)} async-done(((bf16[32,8,1280]{2,1,0:T(8,128)(2,1)}), bf16[32,8,1280]{2,1,0:T(8,128)(2,1)}, u32[]{:S(2)}, u32[]{:S(2)}) %all-to-all-start.3) | async-done | bytes 655392 | tf_op jit(solution)/shard_map/all_to_all | solution.py:139
  117.9 2.7 %fusion.6 = bf16[512,1280]{1,0:T(8,128)(2,1)} fusion(f32[512,1280]{1,0:T(8,128)S(1)} %fusion.50, bf16[32,8,1280]{2,1,0:T(8,128)(2,1)} %all-to-all-done.3, s32[256]{0:T(256)S(1)} %scatter_custom_fusion), kind=kOutput, calls=%fused_computation.12 | convolution fusion | flops 337248256 | bytes 4588544 | tf_op jit(solution)/shard_map/dot_general | solution.py:125
  120.5 2.4 %copy.55 = bf16[512,1280]{0,1:T(8,128)(2,1)} copy(bf16[512,1280]{1,0:T(8,128)(2,1)} %fusion.6) | data formatting | bytes 2621440 | tf_op jit(solution)/shard_map/convert_element_type | solution.py:142
  123.0 4.4 %multiply_convert_fusion.1 = (bf16[512,10,2,64]{0,3,2,1:T(8,128)(2,1)S(1)}, bf16[512,10,2,64]{0,3,2,1:T(8,128)(2,1)S(1)}) fusion(f32[512,10,2,128]{0,3,2,1:T(8,128)} %copy-done.2, bf16[512,10,2,64]{0,3,2,1:T(8,128)(2,1)} %bitcast.81, bf16[64,64]{1,0:T(8,128)(2,1)S(1)} %copy-done.12), kind=kOutput, calls=%fused_computation.20 | convolution fusion | flops 90439680 | bytes 9183232 | tf_op jit(solution)/shard_map/stbd,cd->stbc/dot_general | solution.py:144
  127.4 0.5 fusion.35
  127.9 0.8 copy-done.7
  128.7 0.4 copy-done.9
  129.0 1.2 fusion.2
  130.2 0.4 convert_reduce_fusion
  130.9 1.2 collective-permute-done
  132.2 1.4 collective-permute-start.1
  133.6 3.9 %collective-permute-done.1 = f32[28800]{0:T(1024)S(1)} collective-permute-done((f32[28800]{0:T(1024)S(1)}, f32[28800]{0:T(1024)S(1)}, u32[]{:S(2)}, u32[]{:S(2)}) %collective-permute-start.1) | collective-permute-done | bytes 115232 | tf_op jit(solution)/shard_map/ppermute | solution.py:24
  137.5 1.5 collective-permute-start.2
  139.0 1.2 fusion.72
  140.2 2.3 %collective-permute-done.2 = f32[28800]{0:T(1024)S(1)} collective-permute-done((f32[28800]{0:T(1024)S(1)}, f32[28800]{0:T(1024)S(1)}, u32[]{:S(2)}, u32[]{:S(2)}) %collective-permute-start.2) | collective-permute-done | bytes 115232 | tf_op jit(solution)/shard_map/ppermute | solution.py:24
  142.5 1.5 collective-permute-start.3
  144.0 1.6 %fusion.88 = (f32[512,10,2,64]{0,3,2,1:T(8,128)S(1)}, f32[512,10,2,64]{0,3,2,1:T(8,128)S(1)}, f32[512,10,2,64]{0,3,2,1:T(8,128)S(1)}) fusion(f32[512,10,2,192]{0,3,2,1:T(8,128)S(1)} %fusion.72), kind=kLoop, calls=%fused_computation.125 | loop fusion | bytes 15728640 | tf_op jit(solution)/shard_map/slice | solution.py:156
  145.6 1.7 %collective-permute-done.3 = f32[28800]{0:T(1024)S(1)} collective-permute-done((f32[28800]{0:T(1024)S(1)}, f32[28800]{0:T(1024)S(1)}, u32[]{:S(2)}, u32[]{:S(2)}) %collective-permute-start.3) | collective-permute-done | bytes 115232 | tf_op jit(solution)/shard_map/ppermute | solution.py:24
  147.4 1.6 %collective-permute-start.4 = (f32[28800]{0:T(1024)S(1)}, f32[28800]{0:T(1024)S(1)}, u32[]{:S(2)}, u32[]{:S(2)}) collective-permute-start(f32[28800]{0:T(1024)S(1)} %add.134), channel_id=1, source_target_pairs={{0,16},{1,17},{2,18},{3,19},{4,20},{5,21},{6,22},{7,23},{8,24},{9,... | collective-permute-start | bytes 345608 | tf_op jit(solution)/shard_map/ppermute | solution.py:24
  149.0 1.0 add_convert_fusion
  150.0 1.6 %copy.61 = bf16[512,1536]{1,0:T(8,128)(2,1)} copy(bf16[512,1536]{0,1:T(8,128)(2,1)S(1)} %bitcast.78) | data formatting | bytes 3145728
  151.6 2.8 %collective-permute-done.4 = f32[28800]{0:T(1024)S(1)} collective-permute-done((f32[28800]{0:T(1024)S(1)}, f32[28800]{0:T(1024)S(1)}, u32[]{:S(2)}, u32[]{:S(2)}) %collective-permute-start.4) | collective-permute-done | bytes 115232 | tf_op jit(solution)/shard_map/ppermute | solution.py:24
  154.5 0.5 slice_multiply_fusion.2
  155.0 0.6 fusion.66
  155.6 0.7 mul.101
  (50 shorter events, 1.9 us)
Async XLA Ops:
  0.6 9.1 %copy-start = (bf16[192,128]{1,0:T(8,128)(2,1)S(1)}, bf16[192,128]{1,0:T(8,128)(2,1)}, u32[]{:S(2)}) copy-start(bf16[192,128]{1,0:T(8,128)(2,1)} %param.11) | copy-start | bytes 147460
  9.3 0.7 copy-start.15
  10.0 0.7 copy-start.12
  12.4 11.1 %copy-start.1 = (bf16[512,1536]{1,0:T(8,128)(2,1)S(1)}, bf16[512,1536]{1,0:T(8,128)(2,1)}, u32[]{:S(2)}) copy-start(bf16[512,1536]{1,0:T(8,128)(2,1)} %param.10) | copy-start | bytes 4718596
  16.2 8.1 %copy-start.13 = (s32[512,2]{0,1:T(2,128)S(1)}, s32[512,2]{0,1:T(2,128)}, u32[]{:S(2)}) copy-start(s32[512,2]{0,1:T(2,128)} %param.15) | copy-start | bytes 12292
  16.2 26.6 %all-to-all-start = ((bf16[32,8,1408]{2,1,0:T(8,128)(2,1)}), bf16[32,8,1408]{2,1,0:T(8,128)(2,1)}, u32[]{:S(2)}, u32[]{:S(2)}) async-start(bf16[32,8,1408]{2,1,0:T(8,128)(2,1)} %pad_maximum_fusion.2), calls=%async_computation | async-start | bytes 1441792 | tf_op jit(solution)/shard_map/all_to_all | solution.py:104
  24.8 1.2 copy-start.6
  24.8 1.5 copy-start.8
  24.8 1.9 %copy-start.10 = (bf16[512,10,2,64]{0,3,2,1:T(8,128)(2,1)}, bf16[512,10,2,64]{0,3,2,1:T(8,128)(2,1)S(1)}, u32[]{:S(2)}) copy-start(bf16[512,10,2,64]{0,3,2,1:T(8,128)(2,1)S(1)} %get-tuple-element.34) | copy-start | bytes 3932164
  26.8 2.3 %copy-start.2 = (f32[512,10,2,128]{0,3,2,1:T(8,128)}, f32[512,10,2,128]{0,3,2,1:T(8,128)S(1)}, u32[]{:S(2)}) copy-start(f32[512,10,2,128]{0,3,2,1:T(8,128)S(1)} %broadcast_add_fusion) | copy-start | bytes 15728644
  29.1 1.1 copy-start.3
  29.1 14.8 %copy-start.14 = (f32[128]{0:T(128)S(1)}, f32[128]{0:T(128)}, u32[]{:S(2)}) copy-start(f32[128]{0:T(128)} %param.14) | copy-start | bytes 1540
  46.4 21.5 %all-to-all-start.1 = ((bf16[32,8,1280]{2,1,0:T(8,128)(2,1)}), bf16[32,8,1280]{2,1,0:T(8,128)(2,1)S(1)}, u32[]{:S(2)}, u32[]{:S(2)}) async-start(bf16[32,8,1280]{2,1,0:T(8,128)(2,1)} %fusion.13), calls=%async_computation.1 | async-start | bytes 1310720 | tf_op jit(solution)/shard_map/all_to_all | solution.py:128
  73.4 21.4 %all-to-all-start.2 = ((bf16[32,8,1280]{2,1,0:T(8,128)(2,1)}), bf16[32,8,1280]{2,1,0:T(8,128)(2,1)S(1)}, u32[]{:S(2)}, u32[]{:S(2)}) async-start(bf16[32,8,1280]{2,1,0:T(8,128)(2,1)} %fusion.14), calls=%async_computation.2 | async-start | bytes 1310720 | tf_op jit(solution)/shard_map/all_to_all | solution.py:135
  96.3 21.5 %all-to-all-start.3 = ((bf16[32,8,1280]{2,1,0:T(8,128)(2,1)}), bf16[32,8,1280]{2,1,0:T(8,128)(2,1)}, u32[]{:S(2)}, u32[]{:S(2)}) async-start(bf16[32,8,1280]{2,1,0:T(8,128)(2,1)} %fusion.15), calls=%async_computation.3 | async-start | bytes 1310720 | tf_op jit(solution)/shard_map/all_to_all | solution.py:139
  122.9 4.4 %copy-start.4 = (bf16[512,10,2,64]{0,3,2,1:T(8,128)(2,1)S(1)}, bf16[512,10,2,64]{0,3,2,1:T(8,128)(2,1)}, u32[]{:S(2)}) copy-start(bf16[512,10,2,64]{0,3,2,1:T(8,128)(2,1)} %copy-done.3) | copy-start | bytes 3932164
  122.9 4.4 %copy-start.5 = (bf16[512,1280]{0,1:T(8,128)(2,1)S(1)}, bf16[512,1280]{0,1:T(8,128)(2,1)}, u32[]{:S(2)}) copy-start(bf16[512,1280]{0,1:T(8,128)(2,1)} %copy.55) | copy-start | bytes 3932164
  123.0 4.9 %copy-start.11 = (bf16[512,10,2,64]{0,3,2,1:T(8,128)(2,1)S(1)}, bf16[512,10,2,64]{0,3,2,1:T(8,128)(2,1)}, u32[]{:S(2)}) copy-start(bf16[512,10,2,64]{0,3,2,1:T(8,128)(2,1)} %copy-done.10) | copy-start | bytes 3932164
  127.3 1.3 copy-start.7
  127.3 1.7 %copy-start.9 = (bf16[512,10,2,64]{0,3,2,1:T(8,128)(2,1)S(1)}, bf16[512,10,2,64]{0,3,2,1:T(8,128)(2,1)}, u32[]{:S(2)}) copy-start(bf16[512,10,2,64]{0,3,2,1:T(8,128)(2,1)} %copy-done.8) | copy-start | bytes 3932164
  130.8 1.4 collective-permute-start
  132.2 5.4 %collective-permute-start.1 = (f32[28800]{0:T(1024)S(1)}, f32[28800]{0:T(1024)S(1)}, u32[]{:S(2)}, u32[]{:S(2)}) collective-permute-start(f32[28800]{0:T(1024)S(1)} %fusion.87), channel_id=1, source_target_pairs={{0,2},{1,3},{2,0},{3,1},{4,6},{5,7},{6,4},{7,5},{8,10},{9,11},{10,... | collective-permute-start | bytes 345608 | tf_op jit(solution)/shard_map/ppermute | solution.py:24
  137.5 4.9 %collective-permute-start.2 = (f32[28800]{0:T(1024)S(1)}, f32[28800]{0:T(1024)S(1)}, u32[]{:S(2)}, u32[]{:S(2)}) collective-permute-start(f32[28800]{0:T(1024)S(1)} %add.132), channel_id=1, source_target_pairs={{0,4},{1,5},{2,6},{3,7},{4,0},{5,1},{6,2},{7,3},{8,12},{9,13},{10,... | collective-permute-start | bytes 345608 | tf_op jit(solution)/shard_map/ppermute | solution.py:24
  142.5 4.9 %collective-permute-start.3 = (f32[28800]{0:T(1024)S(1)}, f32[28800]{0:T(1024)S(1)}, u32[]{:S(2)}, u32[]{:S(2)}) collective-permute-start(f32[28800]{0:T(1024)S(1)} %add.133), channel_id=1, source_target_pairs={{0,8},{1,9},{2,10},{3,11},{4,12},{5,13},{6,14},{7,15},{8,0},{9,1},... | collective-permute-start | bytes 345608 | tf_op jit(solution)/shard_map/ppermute | solution.py:24
  147.4 7.1 %collective-permute-start.4 = (f32[28800]{0:T(1024)S(1)}, f32[28800]{0:T(1024)S(1)}, u32[]{:S(2)}, u32[]{:S(2)}) collective-permute-start(f32[28800]{0:T(1024)S(1)} %add.134), channel_id=1, source_target_pairs={{0,16},{1,17},{2,18},{3,19},{4,20},{5,21},{6,22},{7,23},{8,24},{9,... | collective-permute-start | bytes 345608 | tf_op jit(solution)/shard_map/ppermute | solution.py:24

commit v3 on v2

--- a/solution.py
+++ b/solution.py
@@ -91,7 +91,6 @@
     degree = (MEM + jnp.sum(members, axis=1))[:, None]
     members = members.astype(jnp.bfloat16)
     cut_rows = jnp.take(feats, jnp.clip(slotted_segment, 0, seg - 1), axis=0)
-    z_slots = front(cut_rows)[4]
     stack, gate, first, hidden, z = front(feats)
 
     def pick_slots(rows):
@@ -100,10 +99,11 @@
         )
 
     edge_cols = jnp.broadcast_to(slotted_hyperedge.astype(jnp.bfloat16)[:, None], (slot_total, 128))
-    send = jnp.concatenate([z_slots, edge_cols], axis=1)
+    in_width = feats.shape[1]
+    send = jnp.concatenate([cut_rows, edge_cols], axis=1)
     recv_all = lax.all_to_all(send, ("region", "sub"), split_axis=0, concat_axis=0, tiled=True)
-    recv = recv_all[:, :width]
-    recv_edge = recv_all[:, width].astype(jnp.int32)
+    r_stack, r_gate, r_first, r_hidden, recv = front(recv_all[:, :in_width])
+    recv_edge = recv_all[:, in_width].astype(jnp.int32)
     owned = (recv_edge[None, :] == edge_index[:, None]).astype(jnp.float32)
     count = 1.0 + inner_count + jnp.sum(owned, axis=1)
     owned = owned.astype(jnp.bfloat16)
@@ -140,14 +140,30 @@
         ret_grads, ("region", "sub"), split_axis=0, concat_axis=0, tiled=True
     )
     dz = member_side(dedge, back_grads).astype(jnp.bfloat16).reshape(seg, TP, B, C)
-    g_theta = jnp.einsum("stbc,stbd->cd", hidden, dz, preferred_element_type=jnp.float32)
+
+    def weight_grads(st, gt, fi, hi, dzr):
+        g_theta = jnp.einsum("stbc,stbd->cd", hi, dzr, preferred_element_type=jnp.float32)
+        dh = jnp.einsum("stbd,cd->stbc", dzr, theta, preferred_element_type=jnp.float32)
+        du = jnp.concatenate([dh * gt, dh * fi * gt * (1.0 - gt)], axis=-1).astype(jnp.bfloat16)
+        g_conv = jnp.einsum("stbk,stbf->kf", st, du, preferred_element_type=jnp.float32)
+        g_bias = jnp.sum(du.astype(jnp.float32), axis=(0, 1, 2))
+        return du, g_conv, g_bias, g_theta
+
+    dz_inner = (
+        jnp.einsum("es,ef->sf", incidence, dedge, preferred_element_type=jnp.float32)
+        .astype(jnp.bfloat16)
+        .reshape(seg, TP, B, C)
+    )
+    _, ga_conv, ga_bias, ga_theta = weight_grads(stack, gate, first, hidden, dz_inner)
+    dz_slots = ret_grads.reshape(slot_total, TP, B, C)
+    _, gb_conv, gb_bias, gb_theta = weight_grads(r_stack, r_gate, r_first, r_hidden, dz_slots)
+    sum_conv, sum_bias, sum_theta = device_sum(
+        (ga_conv + gb_conv, ga_bias + gb_bias, ga_theta + gb_theta), device_list
+    )
     dh = jnp.einsum("stbd,cd->stbc", dz, theta, preferred_element_type=jnp.float32)
     du = jnp.concatenate([dh * gate, dh * first * gate * (1.0 - gate)], axis=-1).astype(
         jnp.bfloat16
     )
-    g_conv = jnp.einsum("stbk,stbf->kf", stack, du, preferred_element_type=jnp.float32)
-    g_bias = jnp.sum(du.astype(jnp.float32), axis=(0, 1, 2))
-    sum_conv, sum_bias, sum_theta = device_sum((g_conv, g_bias, g_theta), device_list)
     norm = 1.0 / jnp.sqrt(jnp.float32(seg * device_list * TP * B))
     dstack = jnp.einsum("stbf,kf->stbk", du, conv_weight, preferred_element_type=jnp.float32)
     grad_sum = jnp.zeros((seg, T_SIZE, B, C), jnp.float32)

time: 157 us -> 157 us (level)
  waiting for transfers between devices: 74.6 us -> 64 us
  matrix products: 25.4 us -> 31.5 us
  local copies, waits for them, and re-layouts: 21.4 us -> 25.6 us
    all_to_all x1, waiting for transfers between devices: 17.4 us -> 4.32 us  [body(): lax.all_to_all(ret_grads, ('region', 'sub'), split_axis=0, concat_axis=0,...]
    dot_general x2 -> x6, matrix products: 1.66 us -> 11.6 us  [the longest x2 6.1 us: weight_grads(): jnp.einsum('stbd,cd->stbc', dzr, theta, preferred_element_type=jnp.float32)]
    dot_general x1, matrix products: 4.36 us -> 0.48 us  [body(): jnp.einsum('stbd,cd->stbc', dz, theta, preferred_element_type=jnp.float32)]
    convert_element_type x1 -> x2, local copies, waits for them, and re-layouts: 1.13 us -> 4.74 us  [the longest x1 2.52 us: body(): dz_inner = jnp.einsum('es,ef->sf', incidence, dedge, preferred_element_ty...]
    all_to_all x1, waiting for transfers between devices: 12.1 us -> 14.7 us  [body(): lax.all_to_all(send, ('region', 'sub'), split_axis=0, concat_axis=0, tile...]
    unnamed x34 -> x52, local copies, waits for them, and re-layouts: 6.84 us -> 8.69 us
    concatenate x1 -> x0, local copies, waits for them, and re-layouts: 1.6 us -> none  [body(): send = jnp.concatenate([z_slots, edge_cols], axis=1)]
    gather x2 -> x1, local copies, waits for them, and re-layouts: 3.89 us -> 3.62 us  [body(): cut_rows = jnp.take(feats, jnp.clip(slotted_segment, 0, seg - 1), axis=0)]
  transfers between devices with their start and end apart: 9 -> 9, of which waited for: 9 -> 9; matrix products, arithmetic and copies ran while one was open for 8% -> 16% of each run, Pallas kernels for 0% -> 0%
where the time goes in v3:
time: 157 us; the launch traced here: 156 us
  waiting for transfers between devices  64 us (41%)
  matrix products  31.5 us (20%)
  local copies, waits for them, and re-layouts  25.6 us (16%)
  starting transfers between devices  24.6 us (16%)
  other arithmetic  8.98 us (6%)
    all_to_all x1, waiting for transfers between devices, body(): lax.all_to_all(send_grads, ('region', 'sub'), split_axis=0, concat_axis=0...  17.4 us
    all_to_all x1, waiting for transfers between devices, body(): lax.all_to_all(ret_rows, ('region', 'sub'), split_axis=0, concat_axis=0,...  15.6 us
    all_to_all x1, waiting for transfers between devices, body(): lax.all_to_all(send, ('region', 'sub'), split_axis=0, concat_axis=0, tile...  14.7 us
    ppermute x5, waiting for transfers between devices, device_sum(): flat = flat + lax.ppermute(flat, ('region', 'sub'), perm)  12 us
    unnamed x52, local copies, waits for them, and re-layouts  8.69 us
    all_to_all x1, starting transfers between devices, body(): lax.all_to_all(send, ('region', 'sub'), split_axis=0, concat_axis=0, tile...  7.41 us
    dot_general x2, matrix products, member_side(): jnp.dot(members, back, preferred_element_type=jnp.float32)  6.7 us
    ppermute x5, starting transfers between devices, device_sum(): flat = flat + lax.ppermute(flat, ('region', 'sub'), perm)  6.23 us
  transfers between devices with their start and end apart: 9, of which 9 were waited for; matrix products, arithmetic and copies ran while one was open for 16% of the time, Pallas kernels for 0%

profile of v3, /device:TPU:0, one launch (start us, length us, event | category | flops | bytes accessed | tf_op | source)
XLA Modules:
  0.0 155.9 jit_solution(13556070235260745839)
XLA Ops:
  0.6 0.7 fusion.88
  1.6 0.8 select_reduce_fusion
  2.4 0.7 fusion.100
  3.1 1.1 scatter_custom_fusion
  4.2 1.1 scatter_custom_fusion.1
  5.5 3.6 %gather_fusion = bf16[256,1536]{1,0:T(8,128)(2,1)S(1)} fusion(bf16[512,1536]{1,0:T(8,128)(2,1)} %param.10, s32[1024]{0:T(1024)S(1)} %pad_clamp_fusion), kind=kCustom, calls=%fused_computation | custom fusion | bytes 1573888 | tf_op jit(solution)/shard_map/jit(_take)/gather | solution.py:93
  9.4 1.0 pad_maximum_fusion.4
  10.4 7.4 %all-to-all-start = ((bf16[32,8,1664]{2,1,0:T(8,128)(2,1)}), bf16[32,8,1664]{2,1,0:T(8,128)(2,1)}, u32[]{:S(2)}, u32[]{:S(2)}) async-start(bf16[32,8,1664]{2,1,0:T(8,128)(2,1)} %pad_maximum_fusion.4), calls=%async_computation | async-start | bytes 1703936 | tf_op jit(solution)/shard_map/all_to_all | solution.py:104
  17.8 0.7 copy.66
  18.6 0.5 fusion.108
  19.4 1.0 broadcast_add_fusion
  20.8 0.4 copy-done.12
  21.2 0.7 multiply_convert_fusion.5
  21.9 1.6 %copy-done.2 = f32[512,10,2,128]{0,3,2,1:T(8,128)} copy-done((f32[512,10,2,128]{0,3,2,1:T(8,128)}, f32[512,10,2,128]{0,3,2,1:T(8,128)S(1)}, u32[]{:S(2)}) %copy-start.2) | copy-done | bytes 5242904
  23.5 0.6 convolution_convert_fusion.3
  24.1 0.5 copy-done.3
  24.6 0.6 fusion.73
  25.1 14.7 %all-to-all-done = bf16[32,8,1664]{2,1,0:T(8,128)(2,1)} async-done(((bf16[32,8,1664]{2,1,0:T(8,128)(2,1)}), bf16[32,8,1664]{2,1,0:T(8,128)(2,1)}, u32[]{:S(2)}, u32[]{:S(2)}) %all-to-all-start) | async-done | bytes 852000 | tf_op jit(solution)/shard_map/all_to_all | solution.py:104
  39.8 1.0 convert_reduce_fusion.4
  40.8 1.2 slice.104
  42.6 0.5 convolution_add_fusion.4
  45.5 1.2 fusion.14
  46.7 3.6 %all-to-all-start.1 = ((bf16[32,8,1280]{2,1,0:T(8,128)(2,1)}), bf16[32,8,1280]{2,1,0:T(8,128)(2,1)S(1)}, u32[]{:S(2)}, u32[]{:S(2)}) async-start(bf16[32,8,1280]{2,1,0:T(8,128)(2,1)} %fusion.14), calls=%async_computation.1 | async-start | bytes 1310720 | tf_op jit(solution)/shard_map/all_to_all | solution.py:128
  50.5 2.1 %fusion.71 = f32[512,1280]{1,0:T(8,128)} fusion(bf16[128,1280]{1,0:T(8,128)(2,1)S(1)} %fusion.16, s32[512]{0:T(512)S(1)} %bitcast.122, s32[512]{0:T(512)S(1)} %bitcast.117), kind=kOutput, calls=%fused_computation.88 | convolution fusion | flops 168165376 | bytes 2953216 | tf_op jit(solution)/shard_map/es,ef->sf/dot_general | solution.py:123
  52.7 15.6 %all-to-all-done.1 = bf16[32,8,1280]{2,1,0:T(8,128)(2,1)S(1)} async-done(((bf16[32,8,1280]{2,1,0:T(8,128)(2,1)}), bf16[32,8,1280]{2,1,0:T(8,128)(2,1)S(1)}, u32[]{:S(2)}, u32[]{:S(2)}) %all-to-all-start.1) | async-done | bytes 655392 | tf_op jit(solution)/shard_map/all_to_all | solution.py:128
  68.3 4.1 %divide_convert_fusion = (bf16[512,1280]{1,0:T(8,128)(2,1)S(1)}, bf16[512,1280]{1,0:T(8,128)(2,1)}) fusion(bf16[512,1280]{1,0:T(8,128)(2,1)} %param.19, f32[512]{0:T(512)S(1)} %broadcast_add_fusion.1, f32[512,1280]{1,0:T(8,128)} %fusion.71, bf16[32,8,1280]{2,1,0:T(8,128)(2,1)S(1)} %all-to-all-done.1, s32[256]{0:T(256)S(1)} %scatter_custom_fusion), kind=kOutput, calls=%fused_computation.27 | convolution fusion | flops 345767936 | bytes 7212032 | tf_op jit(solution)/shard_map/dot_general | solution.py:125
  72.3 1.4 fusion.15
  73.7 3.7 %all-to-all-start.2 = ((bf16[32,8,1280]{2,1,0:T(8,128)(2,1)}), bf16[32,8,1280]{2,1,0:T(8,128)(2,1)S(1)}, u32[]{:S(2)}, u32[]{:S(2)}) async-start(bf16[32,8,1280]{2,1,0:T(8,128)(2,1)} %fusion.15), calls=%async_computation.2 | async-start | bytes 1310720 | tf_op jit(solution)/shard_map/all_to_all | solution.py:135
  77.8 17.4 %all-to-all-done.2 = bf16[32,8,1280]{2,1,0:T(8,128)(2,1)S(1)} async-done(((bf16[32,8,1280]{2,1,0:T(8,128)(2,1)}), bf16[32,8,1280]{2,1,0:T(8,128)(2,1)S(1)}, u32[]{:S(2)}, u32[]{:S(2)}) %all-to-all-start.2) | async-done | bytes 655392 | tf_op jit(solution)/shard_map/all_to_all | solution.py:135
  95.4 1.2 convolution_convert_fusion
  96.6 3.6 %all-to-all-start.3 = ((bf16[32,8,1280]{2,1,0:T(8,128)(2,1)}), bf16[32,8,1280]{2,1,0:T(8,128)(2,1)}, u32[]{:S(2)}, u32[]{:S(2)}) async-start(bf16[32,8,1280]{2,1,0:T(8,128)(2,1)} %bitcast.20), calls=%async_computation.3 | async-start | bytes 1310720 | tf_op jit(solution)/shard_map/all_to_all | solution.py:139
  100.3 1.6 %fusion.111 = (bf16[512,1280]{1,0:T(8,128)(2,1)}, f32[512,1280]{1,0:T(8,128)S(1)}) fusion(bf16[128,1280]{1,0:T(8,128)(2,1)S(1)} %fusion.17, s32[512]{0:T(512)S(1)} %bitcast.124, s32[512]{0:T(512)S(1)} %bitcast.119), kind=kOutput, calls=%fused_computation.143 | convolution fusion | flops 168820736 | bytes 4263936 | tf_op jit(solution)/shard_map/es,ef->sf/dot_general | solution.py:123
  101.9 2.2 %copy.75 = bf16[256,1280]{0,1:T(8,128)(2,1)} copy(bf16[256,1280]{1,0:T(8,128)(2,1)} %convolution_convert_fusion) | data formatting | bytes 1310720 | tf_op jit(solution)/shard_map/convert_element_type | solution.py:119
  104.1 2.5 %copy.72 = bf16[512,1280]{0,1:T(8,128)(2,1)} copy(bf16[512,1280]{1,0:T(8,128)(2,1)} %get-tuple-element.46) | data formatting | bytes 2621440 | tf_op jit(solution)/shard_map/convert_element_type | solution.py:154
  106.6 1.4 convolution_bitcast_fusion
  108.0 2.3 %fusion.52 = f32[64,64]{1,0:T(8,128)S(1)} fusion(f32[64,64]{1,0:T(8,128)S(1)} %convolution_bitcast_fusion, bf16[512,10,2,64]{0,3,2,1:T(8,128)(2,1)} %bitcast.111, bf16[512,10,2,64]{0,3,2,1:T(8,128)(2,1)} %copy-done.3), kind=kOutput, calls=%fused_computation.67 | convolution fusion | flops 83890176 | bytes 2654208 | tf_op jit(solution)/shard_map/stbc,stbd->cd/dot_general | solution.py:145
  110.4 2.5 %multiply_convert_fusion.7 = (bf16[256,10,2,64]{0,3,2,1:T(8,128)(2,1)S(1)}, bf16[256,10,2,64]{0,3,2,1:T(8,128)(2,1)S(1)}) fusion(f32[256,10,2,128]{0,3,2,1:T(8,128)} %copy-done.4, bf16[256,10,2,64]{0,3,2,1:T(8,128)(2,1)S(1)} %bitcast.114, bf16[64,64]{1,0:T(8,128)(2,1)S(1)} %copy-done.21), kind=kOutput, calls=%fused_computation.59 | convolution fusion | flops 45219840 | bytes 4595712 | tf_op jit(solution)/shard_map/stbd,cd->stbc/dot_general | solution.py:146
  113.2 0.7 fusion.27
  113.9 4.3 %all-to-all-done.3 = bf16[32,8,1280]{2,1,0:T(8,128)(2,1)} async-done(((bf16[32,8,1280]{2,1,0:T(8,128)(2,1)}), bf16[32,8,1280]{2,1,0:T(8,128)(2,1)}, u32[]{:S(2)}, u32[]{:S(2)}) %all-to-all-start.3) | async-done | bytes 655392 | tf_op jit(solution)/shard_map/all_to_all | solution.py:139
  118.2 2.7 %fusion.3 = bf16[512,1280]{1,0:T(8,128)(2,1)} fusion(f32[512,1280]{1,0:T(8,128)S(1)} %get-tuple-element.47, bf16[32,8,1280]{2,1,0:T(8,128)(2,1)} %all-to-all-done.3, s32[256]{0:T(256)S(1)} %scatter_custom_fusion), kind=kOutput, calls=%fused_computation.11 | convolution fusion | flops 337248256 | bytes 4588544 | tf_op jit(solution)/shard_map/dot_general | solution.py:125
  120.8 1.6 %copy.70 = bf16[512,1280]{0,1:T(8,128)(2,1)S(1)} copy(bf16[512,1280]{1,0:T(8,128)(2,1)} %fusion.3) | data formatting | bytes 2621440 | tf_op jit(solution)/shard_map/convert_element_type | solution.py:142
  122.5 0.5 fusion.92
  122.9 0.8 copy-done.7
  123.8 3.6 %multiply_convert_fusion.1 = (bf16[512,10,2,64]{0,3,2,1:T(8,128)(2,1)S(1)}, bf16[512,10,2,64]{0,3,2,1:T(8,128)(2,1)S(1)}, bf16[512,10,2,64]{0,3,2,1:T(8,128)(2,1)S(1)}, bf16[512,10,2,64]{0,3,2,1:T(8,128)(2,1)S(1)}) fusion(f32[512,10,2,128]{0,3,2,1:T(8,128)} %copy-done.2, f32[512,10,2,64]{0,3,2,1:T(8,128)S(1)} %fusion.92, ...), kind=kOutput, calls=%fused_computation.24 | convolution fusion | flops 94371840 | bytes 14426112 | tf_op jit(solution)/shard_map/stbd,cd->stbc/dot_general | solution.py:146
  127.4 0.4 convert_reduce_fusion
  127.8 0.9 copy-done.9
  128.7 0.4 copy-done.11
  129.1 1.2 fusion.42
  130.5 1.2 collective-permute-done
  131.7 1.4 collective-permute-start.1
  133.2 3.9 %collective-permute-done.1 = f32[28800]{0:T(1024)S(1)} collective-permute-done((f32[28800]{0:T(1024)S(1)}, f32[28800]{0:T(1024)S(1)}, u32[]{:S(2)}, u32[]{:S(2)}) %collective-permute-start.1) | collective-permute-done | bytes 115232 | tf_op jit(solution)/shard_map/ppermute | solution.py:24
  137.1 1.5 collective-permute-start.2
  138.6 1.2 fusion.7
  139.8 2.2 %collective-permute-done.2 = f32[28800]{0:T(1024)S(1)} collective-permute-done((f32[28800]{0:T(1024)S(1)}, f32[28800]{0:T(1024)S(1)}, u32[]{:S(2)}, u32[]{:S(2)}) %collective-permute-start.2) | collective-permute-done | bytes 115232 | tf_op jit(solution)/shard_map/ppermute | solution.py:24
  142.0 1.5 collective-permute-start.3
  143.6 1.6 %fusion.107 = (f32[512,10,2,64]{0,3,2,1:T(8,128)S(1)}, f32[512,10,2,64]{0,3,2,1:T(8,128)S(1)}, f32[512,10,2,64]{0,3,2,1:T(8,128)S(1)}) fusion(f32[512,10,2,192]{0,3,2,1:T(8,128)S(1)} %fusion.7), kind=kLoop, calls=%fused_computation.139 | loop fusion | bytes 15728640 | tf_op jit(solution)/shard_map/slice | solution.py:172
  145.2 1.8 %collective-permute-done.3 = f32[28800]{0:T(1024)S(1)} collective-permute-done((f32[28800]{0:T(1024)S(1)}, f32[28800]{0:T(1024)S(1)}, u32[]{:S(2)}, u32[]{:S(2)}) %collective-permute-start.3) | collective-permute-done | bytes 115232 | tf_op jit(solution)/shard_map/ppermute | solution.py:24
  147.0 1.7 %collective-permute-start.4 = (f32[28800]{0:T(1024)S(1)}, f32[28800]{0:T(1024)S(1)}, u32[]{:S(2)}, u32[]{:S(2)}) collective-permute-start(f32[28800]{0:T(1024)S(1)} %add.146), channel_id=1, source_target_pairs={{0,16},{1,17},{2,18},{3,19},{4,20},{5,21},{6,22},{7,23},{8,24},{9,... | collective-permute-start | bytes 345608 | tf_op jit(solution)/shard_map/ppermute | solution.py:24
  148.6 1.0 add_convert_fusion
  149.6 1.6 %copy.82 = bf16[512,1536]{1,0:T(8,128)(2,1)} copy(bf16[512,1536]{0,1:T(8,128)(2,1)S(1)} %bitcast.107) | data formatting | bytes 3145728
  151.2 2.8 %collective-permute-done.4 = f32[28800]{0:T(1024)S(1)} collective-permute-done((f32[28800]{0:T(1024)S(1)}, f32[28800]{0:T(1024)S(1)}, u32[]{:S(2)}, u32[]{:S(2)}) %collective-permute-start.4) | collective-permute-done | bytes 115232 | tf_op jit(solution)/shard_map/ppermute | solution.py:24
  154.1 0.5 slice_multiply_fusion.2
  154.6 0.6 fusion.83
  155.2 0.7 mul.133
  (77 shorter events, 5.7 us)
Async XLA Ops:
  0.6 18.8 %copy-start = (bf16[192,128]{1,0:T(8,128)(2,1)S(1)}, bf16[192,128]{1,0:T(8,128)(2,1)}, u32[]{:S(2)}) copy-start(bf16[192,128]{1,0:T(8,128)(2,1)} %param.11) | copy-start | bytes 147460
  9.2 8.6 %copy-start.1 = (bf16[512,1536]{1,0:T(8,128)(2,1)S(1)}, bf16[512,1536]{1,0:T(8,128)(2,1)}, u32[]{:S(2)}) copy-start(bf16[512,1536]{1,0:T(8,128)(2,1)} %param.10) | copy-start | bytes 4718596
  10.4 29.4 %all-to-all-start = ((bf16[32,8,1664]{2,1,0:T(8,128)(2,1)}), bf16[32,8,1664]{2,1,0:T(8,128)(2,1)}, u32[]{:S(2)}, u32[]{:S(2)}) async-start(bf16[32,8,1664]{2,1,0:T(8,128)(2,1)} %pad_maximum_fusion.4), calls=%async_computation | async-start | bytes 1703936 | tf_op jit(solution)/shard_map/all_to_all | solution.py:104
  18.5 0.7 copy-start.22
  18.6 0.8 copy-start.24
  19.2 1.2 copy-start.8
  19.2 1.6 copy-start.10
  19.2 2.0 %copy-start.12 = (bf16[512,10,2,64]{0,3,2,1:T(8,128)(2,1)}, bf16[512,10,2,64]{0,3,2,1:T(8,128)(2,1)S(1)}, u32[]{:S(2)}) copy-start(bf16[512,10,2,64]{0,3,2,1:T(8,128)(2,1)S(1)} %get-tuple-element.40) | copy-start | bytes 3932164
  21.2 2.3 %copy-start.2 = (f32[512,10,2,128]{0,3,2,1:T(8,128)}, f32[512,10,2,128]{0,3,2,1:T(8,128)S(1)}, u32[]{:S(2)}) copy-start(f32[512,10,2,128]{0,3,2,1:T(8,128)S(1)} %broadcast_add_fusion) | copy-start | bytes 15728644
  21.2 2.3 %copy-start.21 = (bf16[64,64]{1,0:T(8,128)(2,1)S(1)}, bf16[64,64]{1,0:T(8,128)(2,1)}, u32[]{:S(2)}) copy-start(bf16[64,64]{1,0:T(8,128)(2,1)} %param.13) | copy-start | bytes 24580
  23.5 1.1 copy-start.3
  42.6 0.8 copy-start.15
  42.6 1.1 copy-start.17
  42.6 1.2 copy-start.19
  43.8 1.5 copy-start.4
  43.8 0.8 copy-start.23
  44.2 1.3 copy-start.5
  46.7 21.5 %all-to-all-start.1 = ((bf16[32,8,1280]{2,1,0:T(8,128)(2,1)}), bf16[32,8,1280]{2,1,0:T(8,128)(2,1)S(1)}, u32[]{:S(2)}, u32[]{:S(2)}) async-start(bf16[32,8,1280]{2,1,0:T(8,128)(2,1)} %fusion.14), calls=%async_computation.1 | async-start | bytes 1310720 | tf_op jit(solution)/shard_map/all_to_all | solution.py:128
  73.7 21.4 %all-to-all-start.2 = ((bf16[32,8,1280]{2,1,0:T(8,128)(2,1)}), bf16[32,8,1280]{2,1,0:T(8,128)(2,1)S(1)}, u32[]{:S(2)}, u32[]{:S(2)}) async-start(bf16[32,8,1280]{2,1,0:T(8,128)(2,1)} %fusion.15), calls=%async_computation.2 | async-start | bytes 1310720 | tf_op jit(solution)/shard_map/all_to_all | solution.py:135
  96.6 21.5 %all-to-all-start.3 = ((bf16[32,8,1280]{2,1,0:T(8,128)(2,1)}), bf16[32,8,1280]{2,1,0:T(8,128)(2,1)}, u32[]{:S(2)}, u32[]{:S(2)}) async-start(bf16[32,8,1280]{2,1,0:T(8,128)(2,1)} %bitcast.20), calls=%async_computation.3 | async-start | bytes 1310720 | tf_op jit(solution)/shard_map/all_to_all | solution.py:139
  101.9 4.7 %copy-start.6 = (bf16[256,10,2,64]{0,3,2,1:T(8,128)(2,1)S(1)}, bf16[256,10,2,64]{0,3,2,1:T(8,128)(2,1)}, u32[]{:S(2)}) copy-start(bf16[256,10,2,64]{0,3,2,1:T(8,128)(2,1)} %copy-done.5) | copy-start | bytes 1966084
  108.0 2.4 %copy-start.14 = (bf16[256,1280]{0,1:T(8,128)(2,1)S(1)}, bf16[256,1280]{0,1:T(8,128)(2,1)}, u32[]{:S(2)}) copy-start(bf16[256,1280]{0,1:T(8,128)(2,1)} %copy.75) | copy-start | bytes 1966084
  110.4 2.8 %copy-start.16 = (bf16[256,10,2,64]{0,3,2,1:T(8,128)(2,1)S(1)}, bf16[256,10,2,64]{0,3,2,1:T(8,128)(2,1)}, u32[]{:S(2)}) copy-start(bf16[256,10,2,64]{0,3,2,1:T(8,128)(2,1)} %copy-done.15) | copy-start | bytes 1966084
  110.4 2.8 %copy-start.18 = (bf16[256,10,2,64]{0,3,2,1:T(8,128)(2,1)S(1)}, bf16[256,10,2,64]{0,3,2,1:T(8,128)(2,1)}, u32[]{:S(2)}) copy-start(bf16[256,10,2,64]{0,3,2,1:T(8,128)(2,1)} %copy-done.17) | copy-start | bytes 1966084
  110.4 2.8 %copy-start.20 = (bf16[256,10,2,64]{0,3,2,1:T(8,128)(2,1)S(1)}, bf16[256,10,2,64]{0,3,2,1:T(8,128)(2,1)}, u32[]{:S(2)}) copy-start(bf16[256,10,2,64]{0,3,2,1:T(8,128)(2,1)} %copy-done.19) | copy-start | bytes 1966084
  122.4 1.3 copy-start.7
  123.8 4.1 %copy-start.13 = (bf16[512,10,2,64]{0,3,2,1:T(8,128)(2,1)S(1)}, bf16[512,10,2,64]{0,3,2,1:T(8,128)(2,1)}, u32[]{:S(2)}) copy-start(bf16[512,10,2,64]{0,3,2,1:T(8,128)(2,1)} %copy-done.12) | copy-start | bytes 3932164
  127.4 1.3 copy-start.9
  127.4 1.7 %copy-start.11 = (bf16[512,10,2,64]{0,3,2,1:T(8,128)(2,1)S(1)}, bf16[512,10,2,64]{0,3,2,1:T(8,128)(2,1)}, u32[]{:S(2)}) copy-start(bf16[512,10,2,64]{0,3,2,1:T(8,128)(2,1)} %copy-done.10) | copy-start | bytes 3932164
  130.3 1.4 collective-permute-start
  131.7 5.4 %collective-permute-start.1 = (f32[28800]{0:T(1024)S(1)}, f32[28800]{0:T(1024)S(1)}, u32[]{:S(2)}, u32[]{:S(2)}) collective-permute-start(f32[28800]{0:T(1024)S(1)} %fusion.106), channel_id=1, source_target_pairs={{0,2},{1,3},{2,0},{3,1},{4,6},{5,7},{6,4},{7,5},{8,10},{9,11},{10,... | collective-permute-start | bytes 345608 | tf_op jit(solution)/shard_map/ppermute | solution.py:24
  137.1 4.9 %collective-permute-start.2 = (f32[28800]{0:T(1024)S(1)}, f32[28800]{0:T(1024)S(1)}, u32[]{:S(2)}, u32[]{:S(2)}) collective-permute-start(f32[28800]{0:T(1024)S(1)} %add.144), channel_id=1, source_target_pairs={{0,4},{1,5},{2,6},{3,7},{4,0},{5,1},{6,2},{7,3},{8,12},{9,13},{10,... | collective-permute-start | bytes 345608 | tf_op jit(solution)/shard_map/ppermute | solution.py:24
  142.0 4.9 %collective-permute-start.3 = (f32[28800]{0:T(1024)S(1)}, f32[28800]{0:T(1024)S(1)}, u32[]{:S(2)}, u32[]{:S(2)}) collective-permute-start(f32[28800]{0:T(1024)S(1)} %add.145), channel_id=1, source_target_pairs={{0,8},{1,9},{2,10},{3,11},{4,12},{5,13},{6,14},{7,15},{8,0},{9,1},... | collective-permute-start | bytes 345608 | tf_op jit(solution)/shard_map/ppermute | solution.py:24
  147.0 7.1 %collective-permute-start.4 = (f32[28800]{0:T(1024)S(1)}, f32[28800]{0:T(1024)S(1)}, u32[]{:S(2)}, u32[]{:S(2)}) collective-permute-start(f32[28800]{0:T(1024)S(1)} %add.146), channel_id=1, source_target_pairs={{0,16},{1,17},{2,18},{3,19},{4,20},{5,21},{6,22},{7,23},{8,24},{9,... | collective-permute-start | bytes 345608 | tf_op jit(solution)/shard_map/ppermute | solution.py:24

commit v4 on v3

--- a/solution.py
+++ b/solution.py
@@ -136,10 +136,11 @@
         send_grads, ("region", "sub"), split_axis=0, concat_axis=0, tiled=True
     )
     dedge, ret_grads = edge_side(grad_rows, recv_grads)
+    inner_sum = jnp.einsum("es,ef->sf", incidence, dedge, preferred_element_type=jnp.float32)
+    inner_sum, ret_grads = lax.optimization_barrier((inner_sum, ret_grads))
     back_grads = lax.all_to_all(
         ret_grads, ("region", "sub"), split_axis=0, concat_axis=0, tiled=True
     )
-    dz = member_side(dedge, back_grads).astype(jnp.bfloat16).reshape(seg, TP, B, C)
 
     def weight_grads(st, gt, fi, hi, dzr):
         g_theta = jnp.einsum("stbc,stbd->cd", hi, dzr, preferred_element_type=jnp.float32)
@@ -149,16 +150,17 @@
         g_bias = jnp.sum(du.astype(jnp.float32), axis=(0, 1, 2))
         return du, g_conv, g_bias, g_theta
 
-    dz_inner = (
-        jnp.einsum("es,ef->sf", incidence, dedge, preferred_element_type=jnp.float32)
-        .astype(jnp.bfloat16)
-        .reshape(seg, TP, B, C)
-    )
+    dz_inner = inner_sum.astype(jnp.bfloat16).reshape(seg, TP, B, C)
     _, ga_conv, ga_bias, ga_theta = weight_grads(stack, gate, first, hidden, dz_inner)
     dz_slots = ret_grads.reshape(slot_total, TP, B, C)
     _, gb_conv, gb_bias, gb_theta = weight_grads(r_stack, r_gate, r_first, r_hidden, dz_slots)
-    sum_conv, sum_bias, sum_theta = device_sum(
-        (ga_conv + gb_conv, ga_bias + gb_bias, ga_theta + gb_theta), device_list
+    partial = (ga_conv + gb_conv, ga_bias + gb_bias, ga_theta + gb_theta)
+    sum_conv, sum_bias, sum_theta = device_sum(partial, device_list)
+    _, back_grads = lax.optimization_barrier((partial, back_grads))
+    dz = (
+        (inner_sum + jnp.dot(members, back_grads, preferred_element_type=jnp.float32))
+        .astype(jnp.bfloat16)
+        .reshape(seg, TP, B, C)
     )
     dh = jnp.einsum("stbd,cd->stbc", dz, theta, preferred_element_type=jnp.float32)
     du = jnp.concatenate([dh * gate, dh * first * gate * (1.0 - gate)], axis=-1).astype(

time: 157 us -> 166 us (1.057)
  other arithmetic: 8.98 us -> 13.6 us
  waiting for transfers between devices: 64 us -> 68.6 us
  matrix products: 31.5 us -> 34.1 us
  local copies, waits for them, and re-layouts: 25.6 us -> 23.4 us
    ppermute x5, waiting for transfers between devices: 12 us -> 20.9 us  [device_sum(): flat = flat + lax.ppermute(flat, ('region', 'sub'), perm)]
    all_to_all x1, waiting for transfers between devices: 4.32 us -> 0.01 us  [body(): lax.all_to_all(ret_grads, ('region', 'sub'), split_axis=0, concat_axis=0,...]
    dot_general x1, matrix products: 0.48 us -> 3.83 us  [body(): jnp.einsum('stbd,cd->stbc', dz, theta, preferred_element_type=jnp.float32)]
    dot_general x2, matrix products: 3.67 us -> 0.81 us  [weight_grads(): jnp.einsum('stbc,stbd->cd', hi, dzr, preferred_element_type=jnp.float32)]
    dot_general x2 -> x1, matrix products: 6.7 us -> 4.05 us  [member_side(): jnp.dot(members, back, preferred_element_type=jnp.float32)]
    dot_general x2, matrix products: 6.1 us -> 8.57 us  [weight_grads(): jnp.einsum('stbd,cd->stbc', dzr, theta, preferred_element_type=jnp.float32)]
    convert_element_type x3 -> x2, local copies, waits for them, and re-layouts: 6.35 us -> 4.05 us  [the longest x1 2.44 us: body(): dz_inner = inner_sum.astype(jnp.bfloat16).reshape(seg, TP, B, C)]
    optimization_barrier x0 -> x1, local copies, waits for them, and re-layouts: none -> 2.16 us  [body(): inner_sum, ret_grads = lax.optimization_barrier((inner_sum, ret_grads))]
  transfers between devices with their start and end apart: 9 -> 9, of which waited for: 9 -> 7; matrix products, arithmetic and copies ran while one was open for 16% -> 6% of each run, Pallas kernels for 0% -> 0%
where the time goes in v4:
time: 166 us
  waiting for transfers between devices  68.6 us (41%)
  matrix products  34.1 us (21%)
  starting transfers between devices  24.8 us (15%)
  local copies, waits for them, and re-layouts  23.4 us (14%)
  other arithmetic  13.6 us (8%)
    ppermute x5, waiting for transfers between devices, device_sum(): flat = flat + lax.ppermute(flat, ('region', 'sub'), perm)  20.9 us
    all_to_all x1, waiting for transfers between devices, body(): lax.all_to_all(send_grads, ('region', 'sub'), split_axis=0, concat_axis=0...  17.4 us
    all_to_all x1, waiting for transfers between devices, body(): lax.all_to_all(ret_rows, ('region', 'sub'), split_axis=0, concat_axis=0,...  15.7 us
    all_to_all x1, waiting for transfers between devices, body(): lax.all_to_all(send, ('region', 'sub'), split_axis=0, concat_axis=0, tile...  14.7 us
    dot_general x2, matrix products, weight_grads(): jnp.einsum('stbd,cd->stbc', dzr, theta, preferred_element_type=jnp.float32)  8.57 us
    all_to_all x1, starting transfers between devices, body(): lax.all_to_all(send, ('region', 'sub'), split_axis=0, concat_axis=0, tile...  7.41 us
    unnamed x48, local copies, waits for them, and re-layouts  6.53 us
    ppermute x5, starting transfers between devices, device_sum(): flat = flat + lax.ppermute(flat, ('region', 'sub'), perm)  6.33 us
  transfers between devices with their start and end apart: 9, of which 7 were waited for; matrix products, arithmetic and copies ran while one was open for 6% of the time, Pallas kernels for 0%

profile of v4, /device:TPU:0, one launch (start us, length us, event | category | flops | bytes accessed | tf_op | source)
XLA Modules:
  0.0 165.7 jit_solution(12831700245986107811)
XLA Ops:
  0.6 0.7 fusion.82
  1.6 0.8 select_reduce_fusion
  2.4 0.7 fusion.94
  3.1 1.1 scatter_custom_fusion
  4.2 1.1 scatter_custom_fusion.1
  5.5 3.6 %gather_fusion = bf16[256,1536]{1,0:T(8,128)(2,1)S(1)} fusion(bf16[512,1536]{1,0:T(8,128)(2,1)} %param.10, s32[1024]{0:T(1024)S(1)} %pad_clamp_fusion), kind=kCustom, calls=%fused_computation | custom fusion | bytes 1573888 | tf_op jit(solution)/shard_map/jit(_take)/gather | solution.py:93
  9.4 1.0 pad_maximum_fusion.4
  10.4 7.4 %all-to-all-start = ((bf16[32,8,1664]{2,1,0:T(8,128)(2,1)}), bf16[32,8,1664]{2,1,0:T(8,128)(2,1)}, u32[]{:S(2)}, u32[]{:S(2)}) async-start(bf16[32,8,1664]{2,1,0:T(8,128)(2,1)} %pad_maximum_fusion.4), calls=%async_computation | async-start | bytes 1703936 | tf_op jit(solution)/shard_map/all_to_all | solution.py:104
  17.8 0.7 copy.66
  18.6 0.5 fusion.102
  19.4 1.0 broadcast_add_fusion
  20.7 0.5 copy-done.11
  21.2 0.7 multiply_convert_fusion.5
  21.9 1.6 copy-done.2
  23.5 0.5 convolution_convert_fusion.3
  24.1 0.5 copy-done.3
  24.6 0.6 fusion.67
  25.1 14.7 %all-to-all-done = bf16[32,8,1664]{2,1,0:T(8,128)(2,1)} async-done(((bf16[32,8,1664]{2,1,0:T(8,128)(2,1)}), bf16[32,8,1664]{2,1,0:T(8,128)(2,1)}, u32[]{:S(2)}, u32[]{:S(2)}) %all-to-all-start) | async-done | bytes 852000 | tf_op jit(solution)/shard_map/all_to_all | solution.py:104
  39.8 1.0 convert_reduce_fusion.4
  40.8 1.2 slice.104
  42.6 0.6 convolution_add_fusion.4
  43.8 0.4 multiply_convert_fusion.8
  44.2 0.4 convolution_convert_fusion.4
  44.6 0.4 fusion.16
  45.3 1.2 fusion.14
  46.5 3.6 %all-to-all-start.1 = ((bf16[32,8,1280]{2,1,0:T(8,128)(2,1)}), bf16[32,8,1280]{2,1,0:T(8,128)(2,1)S(1)}, u32[]{:S(2)}, u32[]{:S(2)}) async-start(bf16[32,8,1280]{2,1,0:T(8,128)(2,1)} %fusion.14), calls=%async_computation.1 | async-start | bytes 1310720 | tf_op jit(solution)/shard_map/all_to_all | solution.py:128
  50.3 2.1 %fusion.65 = f32[512,1280]{1,0:T(8,128)} fusion(bf16[128,1280]{1,0:T(8,128)(2,1)S(1)} %fusion.16, s32[512]{0:T(512)S(1)} %bitcast.123, s32[512]{0:T(512)S(1)} %bitcast.118), kind=kOutput, calls=%fused_computation.86 | convolution fusion | flops 168165376 | bytes 2953216 | tf_op jit(solution)/shard_map/es,ef->sf/dot_general | solution.py:123
  52.4 15.7 %all-to-all-done.1 = bf16[32,8,1280]{2,1,0:T(8,128)(2,1)S(1)} async-done(((bf16[32,8,1280]{2,1,0:T(8,128)(2,1)}), bf16[32,8,1280]{2,1,0:T(8,128)(2,1)S(1)}, u32[]{:S(2)}, u32[]{:S(2)}) %all-to-all-start.1) | async-done | bytes 655392 | tf_op jit(solution)/shard_map/all_to_all | solution.py:128
  68.0 4.1 %divide_convert_fusion = (bf16[512,1280]{1,0:T(8,128)(2,1)S(1)}, bf16[512,1280]{1,0:T(8,128)(2,1)}) fusion(bf16[512,1280]{1,0:T(8,128)(2,1)} %param.19, f32[512]{0:T(512)S(1)} %broadcast_add_fusion.1, f32[512,1280]{1,0:T(8,128)} %fusion.65, bf16[32,8,1280]{2,1,0:T(8,128)(2,1)S(1)} %all-to-all-done.1, s32[256]{0:T(256)S(1)} %scatter_custom_fusion), kind=kOutput, calls=%fused_computation.27 | convolution fusion | flops 345767936 | bytes 7212032 | tf_op jit(solution)/shard_map/dot_general | solution.py:125
  72.1 1.4 fusion.15
  73.5 3.7 %all-to-all-start.2 = ((bf16[32,8,1280]{2,1,0:T(8,128)(2,1)}), bf16[32,8,1280]{2,1,0:T(8,128)(2,1)S(1)}, u32[]{:S(2)}, u32[]{:S(2)}) async-start(bf16[32,8,1280]{2,1,0:T(8,128)(2,1)} %fusion.15), calls=%async_computation.2 | async-start | bytes 1310720 | tf_op jit(solution)/shard_map/all_to_all | solution.py:135
  77.5 17.4 %all-to-all-done.2 = bf16[32,8,1280]{2,1,0:T(8,128)(2,1)S(1)} async-done(((bf16[32,8,1280]{2,1,0:T(8,128)(2,1)}), bf16[32,8,1280]{2,1,0:T(8,128)(2,1)S(1)}, u32[]{:S(2)}, u32[]{:S(2)}) %all-to-all-start.2) | async-done | bytes 655392 | tf_op jit(solution)/shard_map/all_to_all | solution.py:135
  95.2 1.3 convolution_convert_fusion
  96.4 0.5 fusion.61
  97.0 2.2 %copy.73 = bf16[256,1280]{0,1:T(8,128)(2,1)} copy(bf16[256,1280]{1,0:T(8,128)(2,1)} %convolution_convert_fusion) | data formatting | bytes 1310720 | tf_op jit(solution)/shard_map/optimization_barrier | solution.py:140
  99.1 2.7 %multiply_convert_fusion.7 = (bf16[256,10,2,64]{0,3,2,1:T(8,128)(2,1)S(1)}, bf16[256,10,2,64]{0,3,2,1:T(8,128)(2,1)S(1)}) fusion(f32[256,10,2,128]{0,3,2,1:T(8,128)} %copy-done.5, bf16[256,10,2,64]{0,3,2,1:T(8,128)(2,1)} %bitcast.112, bf16[64,64]{1,0:T(8,128)(2,1)S(1)} %copy-done.19), kind=kOutput, calls=%fused_computation.59 | convolution fusion | flops 45219840 | bytes 4595712 | tf_op jit(solution)/shard_map/stbd,cd->stbc/dot_general | solution.py:147
  102.2 0.7 fusion.27
  103.1 1.2 convert_element_type.120
  104.3 2.4 %copy.70 = bf16[512,1280]{0,1:T(8,128)(2,1)} copy(bf16[512,1280]{1,0:T(8,128)(2,1)} %convert_element_type.120) | data formatting | bytes 2621440 | tf_op jit(solution)/shard_map/convert_element_type | solution.py:153
  106.8 5.9 %multiply_convert_fusion.3 = (bf16[512,10,2,64]{0,3,2,1:T(8,128)(2,1)}, bf16[512,10,2,64]{0,3,2,1:T(8,128)(2,1)}) fusion(f32[512,10,2,128]{0,3,2,1:T(8,128)} %copy-done.2, bf16[512,10,2,64]{0,3,2,1:T(8,128)(2,1)} %bitcast.109, bf16[64,64]{1,0:T(8,128)(2,1)S(1)} %copy-done.19), kind=kOutput, calls=%fused_computation.26 | convolution fusion | flops 90439680 | bytes 9183232 | tf_op jit(solution)/shard_map/stbd,cd->stbc/dot_general | solution.py:147
  112.6 0.5 fusion.47
  113.2 2.3 %convert_reduce_fusion = f32[128]{0:T(128)S(1)} fusion(bf16[512,10,2,64]{0,3,2,1:T(8,128)(2,1)} %get-tuple-element.37, bf16[512,10,2,64]{0,3,2,1:T(8,128)(2,1)} %get-tuple-element.36), kind=kLoop, calls=%fused_computation.3 | loop fusion | flops 6553472 | bytes 2621952 | tf_op jit(solution)/shard_map/reduce_sum | solution.py:150
  115.7 2.9 %fusion.37 = f32[192,128]{1,0:T(8,128)S(1)} fusion(f32[192,128]{1,0:T(8,128)S(1)} %fusion.27, bf16[512,10,2,64]{0,3,2,1:T(8,128)(2,1)} %copy-done.10, bf16[512,10,2,64]{0,3,2,1:T(8,128)(2,1)} %copy-done.11, bf16[512,10,2,64]{0,3,2,1:T(8,128)(2,1)} %copy-done.9, bf16[512,10,2,64]{0,3,2,1:T(8,128)(2,1)S(1)} %copy-done.8, ...), kind=kOutput, calls=%fused_computation.63 | convolution fusion | flops 520380416 | bytes 6750208 | tf_op jit(solution)/shard_map/stbk,stbf->kf/dot_general | solution.py:149
  118.7 0.7 pad_maximum_fusion.5
  119.4 3.8 %all-to-all-start.3 = ((bf16[32,8,1280]{2,1,0:T(8,128)(2,1)}), bf16[32,8,1280]{2,1,0:T(8,128)(2,1)S(1)}, u32[]{:S(2)}, u32[]{:S(2)}) async-start(bf16[32,8,1280]{2,1,0:T(8,128)(2,1)} %bitcast.33), calls=%async_computation.3 | async-start | bytes 1310720 | tf_op jit(solution)/shard_map/all_to_all | solution.py:141
  123.2 0.9 fusion.100
  124.1 1.6 collective-permute-start.1
  125.7 7.9 %collective-permute-done.1 = f32[28800]{0:T(1024)S(1)} collective-permute-done((f32[28800]{0:T(1024)S(1)}, f32[28800]{0:T(1024)S(1)}, u32[]{:S(2)}, u32[]{:S(2)}) %collective-permute-start.1) | collective-permute-done | bytes 115232 | tf_op jit(solution)/shard_map/ppermute | solution.py:24
  133.7 1.3 collective-permute-start.2
  135.0 4.3 %collective-permute-done.2 = f32[28800]{0:T(1024)S(1)} collective-permute-done((f32[28800]{0:T(1024)S(1)}, f32[28800]{0:T(1024)S(1)}, u32[]{:S(2)}, u32[]{:S(2)}) %collective-permute-start.2) | collective-permute-done | bytes 115232 | tf_op jit(solution)/shard_map/ppermute | solution.py:24
  139.3 1.0 collective-permute-start.3
  140.4 3.9 %collective-permute-done.3 = f32[28800]{0:T(1024)S(1)} collective-permute-done((f32[28800]{0:T(1024)S(1)}, f32[28800]{0:T(1024)S(1)}, u32[]{:S(2)}, u32[]{:S(2)}) %collective-permute-start.3) | collective-permute-done | bytes 115232 | tf_op jit(solution)/shard_map/ppermute | solution.py:24
  144.3 2.3 %collective-permute-start.4 = (f32[28800]{0:T(1024)S(1)}, f32[28800]{0:T(1024)S(1)}, u32[]{:S(2)}, u32[]{:S(2)}) collective-permute-start(f32[28800]{0:T(1024)S(1)} %add.146), channel_id=1, source_target_pairs={{0,16},{1,17},{2,18},{3,19},{4,20},{5,21},{6,22},{7,23},{8,24},{9,... | collective-permute-start | bytes 345608 | tf_op jit(solution)/shard_map/ppermute | solution.py:24
  146.5 4.8 %collective-permute-done.4 = f32[28800]{0:T(1024)S(1)} collective-permute-done((f32[28800]{0:T(1024)S(1)}, f32[28800]{0:T(1024)S(1)}, u32[]{:S(2)}, u32[]{:S(2)}) %collective-permute-start.4) | collective-permute-done | bytes 115232 | tf_op jit(solution)/shard_map/ppermute | solution.py:24
  151.4 0.7 mul.133
  152.1 0.5 slice_multiply_fusion.2
  152.6 0.6 fusion.77
  153.2 1.6 fusion.3
  154.8 1.6 copy.80
  156.4 3.8 %multiply_convert_fusion.1 = (bf16[512,10,2,64]{0,3,2,1:T(8,128)(2,1)S(1)}, bf16[512,10,2,64]{0,3,2,1:T(8,128)(2,1)S(1)}) fusion(f32[512,10,2,128]{0,3,2,1:T(8,128)} %copy-done.2, bf16[512,10,2,64]{0,3,2,1:T(8,128)(2,1)S(1)} %bitcast.111, bf16[64,64]{1,0:T(8,128)(2,1)S(1)} %copy-done.19), kind=kOutput, calls=%fused_computation.23 | convolution fusion | flops 90439680 | bytes 9183232 | tf_op jit(solution)/shard_map/stbd,cd->stbc/dot_general | solution.py:165
  160.3 1.2 fusion.7
  161.4 1.6 fusion.101
  163.1 1.0 add_convert_fusion
  164.1 1.6 copy.82
  (74 shorter events, 4.6 us)
Async XLA Ops:
  0.6 18.8 %copy-start = (bf16[192,128]{1,0:T(8,128)(2,1)S(1)}, bf16[192,128]{1,0:T(8,128)(2,1)}, u32[]{:S(2)}) copy-start(bf16[192,128]{1,0:T(8,128)(2,1)} %param.11) | copy-start | bytes 147460
  9.2 8.6 %copy-start.1 = (bf16[512,1536]{1,0:T(8,128)(2,1)S(1)}, bf16[512,1536]{1,0:T(8,128)(2,1)}, u32[]{:S(2)}) copy-start(bf16[512,1536]{1,0:T(8,128)(2,1)} %param.10) | copy-start | bytes 4718596
  10.4 29.4 %all-to-all-start = ((bf16[32,8,1664]{2,1,0:T(8,128)(2,1)}), bf16[32,8,1664]{2,1,0:T(8,128)(2,1)}, u32[]{:S(2)}, u32[]{:S(2)}) async-start(bf16[32,8,1664]{2,1,0:T(8,128)(2,1)} %pad_maximum_fusion.4), calls=%async_computation | async-start | bytes 1703936 | tf_op jit(solution)/shard_map/all_to_all | solution.py:104
  18.5 0.7 copy-start.20
  18.6 0.8 copy-start.22
  19.2 1.2 copy-start.9
  19.2 1.5 copy-start.10
  19.2 2.0 %copy-start.11 = (bf16[512,10,2,64]{0,3,2,1:T(8,128)(2,1)}, bf16[512,10,2,64]{0,3,2,1:T(8,128)(2,1)S(1)}, u32[]{:S(2)}) copy-start(bf16[512,10,2,64]{0,3,2,1:T(8,128)(2,1)S(1)} %get-tuple-element.44) | copy-start | bytes 3932164
  21.2 2.3 %copy-start.2 = (f32[512,10,2,128]{0,3,2,1:T(8,128)}, f32[512,10,2,128]{0,3,2,1:T(8,128)S(1)}, u32[]{:S(2)}) copy-start(f32[512,10,2,128]{0,3,2,1:T(8,128)S(1)} %broadcast_add_fusion) | copy-start | bytes 15728644
  21.2 2.3 %copy-start.19 = (bf16[64,64]{1,0:T(8,128)(2,1)S(1)}, bf16[64,64]{1,0:T(8,128)(2,1)}, u32[]{:S(2)}) copy-start(bf16[64,64]{1,0:T(8,128)(2,1)} %param.13) | copy-start | bytes 24580
  23.5 1.1 copy-start.3
  42.6 0.8 copy-start.13
  42.6 1.1 copy-start.15
  42.6 1.2 copy-start.17
  43.8 1.5 copy-start.5
  43.8 0.8 copy-start.21
  46.5 21.5 %all-to-all-start.1 = ((bf16[32,8,1280]{2,1,0:T(8,128)(2,1)}), bf16[32,8,1280]{2,1,0:T(8,128)(2,1)S(1)}, u32[]{:S(2)}, u32[]{:S(2)}) async-start(bf16[32,8,1280]{2,1,0:T(8,128)(2,1)} %fusion.14), calls=%async_computation.1 | async-start | bytes 1310720 | tf_op jit(solution)/shard_map/all_to_all | solution.py:128
  73.5 21.4 %all-to-all-start.2 = ((bf16[32,8,1280]{2,1,0:T(8,128)(2,1)}), bf16[32,8,1280]{2,1,0:T(8,128)(2,1)S(1)}, u32[]{:S(2)}, u32[]{:S(2)}) async-start(bf16[32,8,1280]{2,1,0:T(8,128)(2,1)} %fusion.15), calls=%async_computation.2 | async-start | bytes 1310720 | tf_op jit(solution)/shard_map/all_to_all | solution.py:135
  99.1 2.7 %copy-start.12 = (bf16[256,1280]{0,1:T(8,128)(2,1)S(1)}, bf16[256,1280]{0,1:T(8,128)(2,1)}, u32[]{:S(2)}) copy-start(bf16[256,1280]{0,1:T(8,128)(2,1)} %copy.73) | copy-start | bytes 1966084
  99.1 3.0 %copy-start.14 = (bf16[256,10,2,64]{0,3,2,1:T(8,128)(2,1)S(1)}, bf16[256,10,2,64]{0,3,2,1:T(8,128)(2,1)}, u32[]{:S(2)}) copy-start(bf16[256,10,2,64]{0,3,2,1:T(8,128)(2,1)} %copy-done.13) | copy-start | bytes 1966084
  99.1 3.0 %copy-start.16 = (bf16[256,10,2,64]{0,3,2,1:T(8,128)(2,1)S(1)}, bf16[256,10,2,64]{0,3,2,1:T(8,128)(2,1)}, u32[]{:S(2)}) copy-start(bf16[256,10,2,64]{0,3,2,1:T(8,128)(2,1)} %copy-done.15) | copy-start | bytes 1966084
  99.1 3.1 %copy-start.18 = (bf16[256,10,2,64]{0,3,2,1:T(8,128)(2,1)S(1)}, bf16[256,10,2,64]{0,3,2,1:T(8,128)(2,1)}, u32[]{:S(2)}) copy-start(bf16[256,10,2,64]{0,3,2,1:T(8,128)(2,1)} %copy-done.17) | copy-start | bytes 1966084
  106.8 5.9 %copy-start.4 = (bf16[512,10,2,64]{0,3,2,1:T(8,128)(2,1)S(1)}, bf16[512,10,2,64]{0,3,2,1:T(8,128)(2,1)}, u32[]{:S(2)}) copy-start(bf16[512,10,2,64]{0,3,2,1:T(8,128)(2,1)} %copy-done.3) | copy-start | bytes 3932164
  106.8 5.9 %copy-start.6 = (bf16[512,1280]{0,1:T(8,128)(2,1)S(1)}, bf16[512,1280]{0,1:T(8,128)(2,1)}, u32[]{:S(2)}) copy-start(bf16[512,1280]{0,1:T(8,128)(2,1)} %copy.70) | copy-start | bytes 3932164
  113.2 2.3 %copy-start.7 = (bf16[512,10,2,64]{0,3,2,1:T(8,128)(2,1)S(1)}, bf16[512,10,2,64]{0,3,2,1:T(8,128)(2,1)}, u32[]{:S(2)}) copy-start(bf16[512,10,2,64]{0,3,2,1:T(8,128)(2,1)} %get-tuple-element.36) | copy-start | bytes 3932164
  113.2 2.5 %copy-start.8 = (bf16[512,10,2,64]{0,3,2,1:T(8,128)(2,1)S(1)}, bf16[512,10,2,64]{0,3,2,1:T(8,128)(2,1)}, u32[]{:S(2)}) copy-start(bf16[512,10,2,64]{0,3,2,1:T(8,128)(2,1)} %get-tuple-element.37) | copy-start | bytes 3932164
  119.3 3.9 %collective-permute-start = (f32[28800]{0:T(1024)}, f32[28800]{0:T(1024)}, u32[]{:S(2)}, u32[]{:S(2)}) collective-permute-start(f32[28800]{0:T(1024)} %pad_maximum_fusion.5), channel_id=1, source_target_pairs={{0,1},{1,0},{2,3},{3,2},{4,5},{5,4},{6,7},{7,6},{8,9},{9,8},{10,11... | collective-permute-start | bytes 345608 | tf_op jit(solution)/shard_map/ppermute | solution.py:24
  119.4 33.8 %all-to-all-start.3 = ((bf16[32,8,1280]{2,1,0:T(8,128)(2,1)}), bf16[32,8,1280]{2,1,0:T(8,128)(2,1)S(1)}, u32[]{:S(2)}, u32[]{:S(2)}) async-start(bf16[32,8,1280]{2,1,0:T(8,128)(2,1)} %bitcast.33), calls=%async_computation.3 | async-start | bytes 1310720 | tf_op jit(solution)/shard_map/all_to_all | solution.py:141
  124.1 9.5 %collective-permute-start.1 = (f32[28800]{0:T(1024)S(1)}, f32[28800]{0:T(1024)S(1)}, u32[]{:S(2)}, u32[]{:S(2)}) collective-permute-start(f32[28800]{0:T(1024)S(1)} %fusion.100), channel_id=1, source_target_pairs={{0,2},{1,3},{2,0},{3,1},{4,6},{5,7},{6,4},{7,5},{8,10},{9,11},{10,... | collective-permute-start | bytes 345608 | tf_op jit(solution)/shard_map/ppermute | solution.py:24
  133.7 5.7 %collective-permute-start.2 = (f32[28800]{0:T(1024)S(1)}, f32[28800]{0:T(1024)S(1)}, u32[]{:S(2)}, u32[]{:S(2)}) collective-permute-start(f32[28800]{0:T(1024)S(1)} %add.144), channel_id=1, source_target_pairs={{0,4},{1,5},{2,6},{3,7},{4,0},{5,1},{6,2},{7,3},{8,12},{9,13},{10,... | collective-permute-start | bytes 345608 | tf_op jit(solution)/shard_map/ppermute | solution.py:24
  139.3 4.9 %collective-permute-start.3 = (f32[28800]{0:T(1024)S(1)}, f32[28800]{0:T(1024)S(1)}, u32[]{:S(2)}, u32[]{:S(2)}) collective-permute-start(f32[28800]{0:T(1024)S(1)} %add.145), channel_id=1, source_target_pairs={{0,8},{1,9},{2,10},{3,11},{4,12},{5,13},{6,14},{7,15},{8,0},{9,1},... | collective-permute-start | bytes 345608 | tf_op jit(solution)/shard_map/ppermute | solution.py:24
  144.3 7.1 %collective-permute-start.4 = (f32[28800]{0:T(1024)S(1)}, f32[28800]{0:T(1024)S(1)}, u32[]{:S(2)}, u32[]{:S(2)}) collective-permute-start(f32[28800]{0:T(1024)S(1)} %add.146), channel_id=1, source_target_pairs={{0,16},{1,17},{2,18},{3,19},{4,20},{5,21},{6,22},{7,23},{8,24},{9,... | collective-permute-start | bytes 345608 | tf_op jit(solution)/shard_map/ppermute | solution.py:24

commit v5 on v4

--- a/solution.py
+++ b/solution.py
@@ -155,8 +155,8 @@
     dz_slots = ret_grads.reshape(slot_total, TP, B, C)
     _, gb_conv, gb_bias, gb_theta = weight_grads(r_stack, r_gate, r_first, r_hidden, dz_slots)
     partial = (ga_conv + gb_conv, ga_bias + gb_bias, ga_theta + gb_theta)
+    partial, back_grads = lax.optimization_barrier((partial, back_grads))
     sum_conv, sum_bias, sum_theta = device_sum(partial, device_list)
-    _, back_grads = lax.optimization_barrier((partial, back_grads))
     dz = (
         (inner_sum + jnp.dot(members, back_grads, preferred_element_type=jnp.float32))
         .astype(jnp.bfloat16)

time: 166 us -> 152 us (0.916)
  waiting for transfers between devices: 68.6 us -> 53.9 us
  local copies, waits for them, and re-layouts: 23.4 us -> 26.6 us
  matrix products: 34.1 us -> 31.8 us
  other arithmetic: 13.6 us -> 11.7 us
    ppermute x5, waiting for transfers between devices: 20.9 us -> 6.19 us  [device_sum(): flat = flat + lax.ppermute(flat, ('region', 'sub'), perm)]
    unnamed x48 -> x58, local copies, waits for them, and re-layouts: 6.53 us -> 9.72 us
    reduce_sum x2, other arithmetic: 2.57 us -> 0.71 us  [weight_grads(): g_bias = jnp.sum(du.astype(jnp.float32), axis=(0, 1, 2))]
    dot_general x2, matrix products: 3.58 us -> 1.85 us  [weight_grads(): jnp.einsum('stbk,stbf->kf', st, du, preferred_element_type=jnp.float32)]
  transfers between devices with their start and end apart: 9 -> 9, of which waited for: 7 -> 6; matrix products, arithmetic and copies ran while one was open for 6% -> 23% of each run, Pallas kernels for 0% -> 0%
where the time goes in v5:
time: 152 us; the launch traced here: 151 us
  waiting for transfers between devices  53.9 us (35%)
  matrix products  31.8 us (21%)
  local copies, waits for them, and re-layouts  26.6 us (18%)
  starting transfers between devices  25.9 us (17%)
  other arithmetic  11.7 us (8%)
    all_to_all x1, waiting for transfers between devices, body(): lax.all_to_all(send_grads, ('region', 'sub'), split_axis=0, concat_axis=0...  17.4 us
    all_to_all x1, waiting for transfers between devices, body(): lax.all_to_all(ret_rows, ('region', 'sub'), split_axis=0, concat_axis=0,...  15.6 us
    all_to_all x1, waiting for transfers between devices, body(): lax.all_to_all(send, ('region', 'sub'), split_axis=0, concat_axis=0, tile...  14.7 us
    unnamed x58, local copies, waits for them, and re-layouts  9.72 us
    dot_general x2, matrix products, weight_grads(): jnp.einsum('stbd,cd->stbc', dzr, theta, preferred_element_type=jnp.float32)  7.95 us
    ppermute x5, starting transfers between devices, device_sum(): flat = flat + lax.ppermute(flat, ('region', 'sub'), perm)  7.66 us
    all_to_all x1, starting transfers between devices, body(): lax.all_to_all(send, ('region', 'sub'), split_axis=0, concat_axis=0, tile...  7.41 us
    ppermute x5, waiting for transfers between devices, device_sum(): flat = flat + lax.ppermute(flat, ('region', 'sub'), perm)  6.19 us
  transfers between devices with their start and end apart: 9, of which 6 were waited for; matrix products, arithmetic and copies ran while one was open for 23% of the time, Pallas kernels for 0%

profile of v5, /device:TPU:0, one launch (start us, length us, event | category | flops | bytes accessed | tf_op | source)
XLA Modules:
  0.0 151.1 jit_solution(11018919529809301206)
XLA Ops:
  0.6 0.7 fusion.82
  1.6 0.8 select_reduce_fusion
  2.4 0.7 fusion.94
  3.1 1.1 scatter_custom_fusion
  4.2 1.1 scatter_custom_fusion.1
  5.5 3.6 %gather_fusion = bf16[256,1536]{1,0:T(8,128)(2,1)S(1)} fusion(bf16[512,1536]{1,0:T(8,128)(2,1)} %param.10, s32[1024]{0:T(1024)S(1)} %pad_clamp_fusion), kind=kCustom, calls=%fused_computation | custom fusion | bytes 1573888 | tf_op jit(solution)/shard_map/jit(_take)/gather | solution.py:93
  9.4 1.0 pad_maximum_fusion.4
  10.4 7.4 %all-to-all-start = ((bf16[32,8,1664]{2,1,0:T(8,128)(2,1)}), bf16[32,8,1664]{2,1,0:T(8,128)(2,1)}, u32[]{:S(2)}, u32[]{:S(2)}) async-start(bf16[32,8,1664]{2,1,0:T(8,128)(2,1)} %pad_maximum_fusion.4), calls=%async_computation | async-start | bytes 1703936 | tf_op jit(solution)/shard_map/all_to_all | solution.py:104
  17.8 0.7 copy.66
  18.6 0.5 fusion.102
  19.4 1.0 broadcast_add_fusion
  20.8 0.4 copy-done.13
  21.2 0.7 multiply_convert_fusion.5
  21.9 1.6 %copy-done.2 = f32[512,10,2,128]{0,3,2,1:T(8,128)} copy-done((f32[512,10,2,128]{0,3,2,1:T(8,128)}, f32[512,10,2,128]{0,3,2,1:T(8,128)S(1)}, u32[]{:S(2)}) %copy-start.2) | copy-done | bytes 5242904
  23.5 0.5 convolution_convert_fusion.3
  24.1 0.5 copy-done.3
  24.6 0.6 fusion.67
  25.1 14.7 %all-to-all-done = bf16[32,8,1664]{2,1,0:T(8,128)(2,1)} async-done(((bf16[32,8,1664]{2,1,0:T(8,128)(2,1)}), bf16[32,8,1664]{2,1,0:T(8,128)(2,1)}, u32[]{:S(2)}, u32[]{:S(2)}) %all-to-all-start) | async-done | bytes 852000 | tf_op jit(solution)/shard_map/all_to_all | solution.py:104
  39.8 1.0 convert_reduce_fusion.4
  40.8 1.2 slice.104
  42.6 0.5 convolution_add_fusion.4
  45.5 1.2 fusion.14
  46.7 3.6 %all-to-all-start.1 = ((bf16[32,8,1280]{2,1,0:T(8,128)(2,1)}), bf16[32,8,1280]{2,1,0:T(8,128)(2,1)S(1)}, u32[]{:S(2)}, u32[]{:S(2)}) async-start(bf16[32,8,1280]{2,1,0:T(8,128)(2,1)} %fusion.14), calls=%async_computation.1 | async-start | bytes 1310720 | tf_op jit(solution)/shard_map/all_to_all | solution.py:128
  50.5 2.1 %fusion.65 = f32[512,1280]{1,0:T(8,128)} fusion(bf16[128,1280]{1,0:T(8,128)(2,1)S(1)} %fusion.16, s32[512]{0:T(512)S(1)} %bitcast.123, s32[512]{0:T(512)S(1)} %bitcast.118), kind=kOutput, calls=%fused_computation.86 | convolution fusion | flops 168165376 | bytes 2953216 | tf_op jit(solution)/shard_map/es,ef->sf/dot_general | solution.py:123
  52.6 15.6 %all-to-all-done.1 = bf16[32,8,1280]{2,1,0:T(8,128)(2,1)S(1)} async-done(((bf16[32,8,1280]{2,1,0:T(8,128)(2,1)}), bf16[32,8,1280]{2,1,0:T(8,128)(2,1)S(1)}, u32[]{:S(2)}, u32[]{:S(2)}) %all-to-all-start.1) | async-done | bytes 655392 | tf_op jit(solution)/shard_map/all_to_all | solution.py:128
  68.3 4.0 %divide_convert_fusion = (bf16[512,1280]{1,0:T(8,128)(2,1)S(1)}, bf16[512,1280]{1,0:T(8,128)(2,1)}) fusion(bf16[512,1280]{1,0:T(8,128)(2,1)} %param.19, f32[512]{0:T(512)S(1)} %broadcast_add_fusion.1, f32[512,1280]{1,0:T(8,128)} %fusion.65, bf16[32,8,1280]{2,1,0:T(8,128)(2,1)S(1)} %all-to-all-done.1, s32[256]{0:T(256)S(1)} %scatter_custom_fusion), kind=kOutput, calls=%fused_computation.27 | convolution fusion | flops 345767936 | bytes 7212032 | tf_op jit(solution)/shard_map/dot_general | solution.py:125
  72.3 1.4 fusion.15
  73.7 3.7 %all-to-all-start.2 = ((bf16[32,8,1280]{2,1,0:T(8,128)(2,1)}), bf16[32,8,1280]{2,1,0:T(8,128)(2,1)S(1)}, u32[]{:S(2)}, u32[]{:S(2)}) async-start(bf16[32,8,1280]{2,1,0:T(8,128)(2,1)} %fusion.15), calls=%async_computation.2 | async-start | bytes 1310720 | tf_op jit(solution)/shard_map/all_to_all | solution.py:135
  77.8 17.4 %all-to-all-done.2 = bf16[32,8,1280]{2,1,0:T(8,128)(2,1)S(1)} async-done(((bf16[32,8,1280]{2,1,0:T(8,128)(2,1)}), bf16[32,8,1280]{2,1,0:T(8,128)(2,1)S(1)}, u32[]{:S(2)}, u32[]{:S(2)}) %all-to-all-start.2) | async-done | bytes 655392 | tf_op jit(solution)/shard_map/all_to_all | solution.py:135
  95.4 1.3 convolution_convert_fusion
  96.7 0.5 fusion.61
  97.2 2.2 %copy.73 = bf16[256,1280]{0,1:T(8,128)(2,1)} copy(bf16[256,1280]{1,0:T(8,128)(2,1)} %convolution_convert_fusion) | data formatting | bytes 1310720 | tf_op jit(solution)/shard_map/optimization_barrier | solution.py:140
  99.5 3.5 %all-to-all-start.3 = ((bf16[32,8,1280]{2,1,0:T(8,128)(2,1)}), bf16[32,8,1280]{2,1,0:T(8,128)(2,1)S(1)}, u32[]{:S(2)}, u32[]{:S(2)}) async-start(bf16[32,8,1280]{2,1,0:T(8,128)(2,1)} %bitcast.33), calls=%async_computation.3 | async-start | bytes 1310720 | tf_op jit(solution)/shard_map/all_to_all | solution.py:141
  103.0 3.6 %multiply_convert_fusion.7 = (bf16[256,10,2,64]{0,3,2,1:T(8,128)(2,1)}, bf16[256,10,2,64]{0,3,2,1:T(8,128)(2,1)}) fusion(f32[256,10,2,128]{0,3,2,1:T(8,128)} %copy-done.5, bf16[256,10,2,64]{0,3,2,1:T(8,128)(2,1)} %bitcast.112, bf16[64,64]{1,0:T(8,128)(2,1)S(1)} %copy-done.24), kind=kOutput, calls=%fused_computation.59 | convolution fusion | flops 45219840 | bytes 4595712 | tf_op jit(solution)/shard_map/stbd,cd->stbc/dot_general | solution.py:147
  106.6 1.2 convert_element_type.120
  107.8 2.4 %copy.70 = bf16[512,1280]{0,1:T(8,128)(2,1)} copy(bf16[512,1280]{1,0:T(8,128)(2,1)} %convert_element_type.120) | data formatting | bytes 2621440 | tf_op jit(solution)/shard_map/convert_element_type | solution.py:153
  110.2 4.3 %multiply_convert_fusion.3 = (bf16[512,10,2,64]{0,3,2,1:T(8,128)(2,1)S(1)}, bf16[512,10,2,64]{0,3,2,1:T(8,128)(2,1)S(1)}) fusion(f32[512,10,2,128]{0,3,2,1:T(8,128)} %copy-done.2, bf16[512,10,2,64]{0,3,2,1:T(8,128)(2,1)} %bitcast.109, bf16[64,64]{1,0:T(8,128)(2,1)S(1)} %copy-done.24), kind=kOutput, calls=%fused_computation.26 | convolution fusion | flops 90439680 | bytes 9183232 | tf_op jit(solution)/shard_map/stbd,cd->stbc/dot_general | solution.py:147
  114.9 0.4 convert_reduce_fusion
  116.5 0.7 fusion.27
  117.1 0.6 copy-done.4
  117.8 0.4 copy-done.8
  118.2 0.5 fusion.47
  118.7 0.9 copy-done.10
  119.6 0.4 copy-done.12
  120.0 1.2 fusion.37
  121.2 0.7 pad_maximum_fusion.5
  122.1 1.6 %fusion.3 = bf16[512,1280]{1,0:T(8,128)(2,1)} fusion(f32[512,1280]{1,0:T(8,128)S(1)} %fusion.61, bf16[256,1280]{1,0:T(8,128)(2,1)S(1)} %bitcast.107, s32[256]{0:T(256)S(1)} %scatter_custom_fusion), kind=kOutput, calls=%fused_computation.11 | convolution fusion | flops 337248256 | bytes 4588544 | tf_op jit(solution)/shard_map/dot_general | solution.py:161
  123.7 1.6 %copy.80 = bf16[512,1280]{0,1:T(8,128)(2,1)S(1)} copy(bf16[512,1280]{1,0:T(8,128)(2,1)} %fusion.3) | data formatting | bytes 2621440 | tf_op jit(solution)/shard_map/convert_element_type | solution.py:162
  125.4 0.9 fusion.100
  126.3 1.8 %collective-permute-start.1 = (f32[28800]{0:T(1024)S(1)}, f32[28800]{0:T(1024)S(1)}, u32[]{:S(2)}, u32[]{:S(2)}) collective-permute-start(f32[28800]{0:T(1024)S(1)} %fusion.100), channel_id=1, source_target_pairs={{0,2},{1,3},{2,0},{3,1},{4,6},{5,7},{6,4},{7,5},{8,10},{9,11},{10,... | collective-permute-start | bytes 345608 | tf_op jit(solution)/shard_map/ppermute | solution.py:24
  128.0 3.8 %multiply_convert_fusion.1 = (bf16[512,10,2,64]{0,3,2,1:T(8,128)(2,1)S(1)}, bf16[512,10,2,64]{0,3,2,1:T(8,128)(2,1)S(1)}) fusion(f32[512,10,2,128]{0,3,2,1:T(8,128)} %copy-done.2, bf16[512,10,2,64]{0,3,2,1:T(8,128)(2,1)S(1)} %bitcast.111, bf16[64,64]{1,0:T(8,128)(2,1)S(1)} %copy-done.24), kind=kOutput, calls=%fused_computation.23 | convolution fusion | flops 90439680 | bytes 9183232 | tf_op jit(solution)/shard_map/stbd,cd->stbc/dot_general | solution.py:165
  131.9 1.7 %collective-permute-start.2 = (f32[28800]{0:T(1024)S(1)}, f32[28800]{0:T(1024)S(1)}, u32[]{:S(2)}, u32[]{:S(2)}) collective-permute-start(f32[28800]{0:T(1024)S(1)} %add.144), channel_id=1, source_target_pairs={{0,4},{1,5},{2,6},{3,7},{4,0},{5,1},{6,2},{7,3},{8,12},{9,13},{10,... | collective-permute-start | bytes 345608 | tf_op jit(solution)/shard_map/ppermute | solution.py:24
  133.6 1.2 fusion.7
  134.8 2.4 %collective-permute-done.2 = f32[28800]{0:T(1024)S(1)} collective-permute-done((f32[28800]{0:T(1024)S(1)}, f32[28800]{0:T(1024)S(1)}, u32[]{:S(2)}, u32[]{:S(2)}) %collective-permute-start.2) | collective-permute-done | bytes 115232 | tf_op jit(solution)/shard_map/ppermute | solution.py:24
  137.2 1.5 %collective-permute-start.3 = (f32[28800]{0:T(1024)S(1)}, f32[28800]{0:T(1024)S(1)}, u32[]{:S(2)}, u32[]{:S(2)}) collective-permute-start(f32[28800]{0:T(1024)S(1)} %add.145), channel_id=1, source_target_pairs={{0,8},{1,9},{2,10},{3,11},{4,12},{5,13},{6,14},{7,15},{8,0},{9,1},... | collective-permute-start | bytes 345608 | tf_op jit(solution)/shard_map/ppermute | solution.py:24
  138.7 1.6 %fusion.101 = (f32[512,10,2,64]{0,3,2,1:T(8,128)S(1)}, f32[512,10,2,64]{0,3,2,1:T(8,128)S(1)}, f32[512,10,2,64]{0,3,2,1:T(8,128)S(1)}) fusion(f32[512,10,2,192]{0,3,2,1:T(8,128)S(1)} %fusion.7), kind=kLoop, calls=%fused_computation.137 | loop fusion | bytes 15728640 | tf_op jit(solution)/shard_map/slice | solution.py:174
  140.4 1.7 %collective-permute-done.3 = f32[28800]{0:T(1024)S(1)} collective-permute-done((f32[28800]{0:T(1024)S(1)}, f32[28800]{0:T(1024)S(1)}, u32[]{:S(2)}, u32[]{:S(2)}) %collective-permute-start.3) | collective-permute-done | bytes 115232 | tf_op jit(solution)/shard_map/ppermute | solution.py:24
  142.1 2.4 %collective-permute-start.4 = (f32[28800]{0:T(1024)S(1)}, f32[28800]{0:T(1024)S(1)}, u32[]{:S(2)}, u32[]{:S(2)}) collective-permute-start(f32[28800]{0:T(1024)S(1)} %add.146), channel_id=1, source_target_pairs={{0,16},{1,17},{2,18},{3,19},{4,20},{5,21},{6,22},{7,23},{8,24},{9,... | collective-permute-start | bytes 345608 | tf_op jit(solution)/shard_map/ppermute | solution.py:24
  144.5 1.0 add_convert_fusion
  145.5 1.6 %copy.82 = bf16[512,1536]{1,0:T(8,128)(2,1)} copy(bf16[512,1536]{0,1:T(8,128)(2,1)S(1)} %bitcast.105) | data formatting | bytes 3145728
  147.1 2.1 %collective-permute-done.4 = f32[28800]{0:T(1024)S(1)} collective-permute-done((f32[28800]{0:T(1024)S(1)}, f32[28800]{0:T(1024)S(1)}, u32[]{:S(2)}, u32[]{:S(2)}) %collective-permute-start.4) | collective-permute-done | bytes 115232 | tf_op jit(solution)/shard_map/ppermute | solution.py:24
  149.2 0.5 slice_multiply_fusion.2
  149.7 0.6 fusion.77
  150.4 0.7 mul.133
  (84 shorter events, 6.8 us)
Async XLA Ops:
  0.6 18.8 %copy-start = (bf16[192,128]{1,0:T(8,128)(2,1)S(1)}, bf16[192,128]{1,0:T(8,128)(2,1)}, u32[]{:S(2)}) copy-start(bf16[192,128]{1,0:T(8,128)(2,1)} %param.11) | copy-start | bytes 147460
  9.2 8.6 %copy-start.1 = (bf16[512,1536]{1,0:T(8,128)(2,1)S(1)}, bf16[512,1536]{1,0:T(8,128)(2,1)}, u32[]{:S(2)}) copy-start(bf16[512,1536]{1,0:T(8,128)(2,1)} %param.10) | copy-start | bytes 4718596
  10.4 29.4 %all-to-all-start = ((bf16[32,8,1664]{2,1,0:T(8,128)(2,1)}), bf16[32,8,1664]{2,1,0:T(8,128)(2,1)}, u32[]{:S(2)}, u32[]{:S(2)}) async-start(bf16[32,8,1664]{2,1,0:T(8,128)(2,1)} %pad_maximum_fusion.4), calls=%async_computation | async-start | bytes 1703936 | tf_op jit(solution)/shard_map/all_to_all | solution.py:104
  18.5 0.7 copy-start.25
  18.6 0.8 copy-start.27
  19.2 1.2 copy-start.9
  19.2 1.6 %copy-start.11 = (bf16[512,10,2,64]{0,3,2,1:T(8,128)(2,1)}, bf16[512,10,2,64]{0,3,2,1:T(8,128)(2,1)S(1)}, u32[]{:S(2)}) copy-start(bf16[512,10,2,64]{0,3,2,1:T(8,128)(2,1)S(1)} %get-tuple-element.49) | copy-start | bytes 3932164
  19.2 2.0 %copy-start.13 = (bf16[512,10,2,64]{0,3,2,1:T(8,128)(2,1)}, bf16[512,10,2,64]{0,3,2,1:T(8,128)(2,1)S(1)}, u32[]{:S(2)}) copy-start(bf16[512,10,2,64]{0,3,2,1:T(8,128)(2,1)S(1)} %get-tuple-element.50) | copy-start | bytes 3932164
  21.2 2.3 %copy-start.2 = (f32[512,10,2,128]{0,3,2,1:T(8,128)}, f32[512,10,2,128]{0,3,2,1:T(8,128)S(1)}, u32[]{:S(2)}) copy-start(f32[512,10,2,128]{0,3,2,1:T(8,128)S(1)} %broadcast_add_fusion) | copy-start | bytes 15728644
  21.2 2.3 %copy-start.24 = (bf16[64,64]{1,0:T(8,128)(2,1)S(1)}, bf16[64,64]{1,0:T(8,128)(2,1)}, u32[]{:S(2)}) copy-start(bf16[64,64]{1,0:T(8,128)(2,1)} %param.13) | copy-start | bytes 24580
  23.5 1.1 copy-start.3
  42.6 0.8 copy-start.18
  42.6 1.1 copy-start.20
  42.6 1.2 copy-start.22
  43.8 1.5 copy-start.5
  43.8 0.8 copy-start.26
  44.2 1.4 copy-start.6
  46.7 21.5 %all-to-all-start.1 = ((bf16[32,8,1280]{2,1,0:T(8,128)(2,1)}), bf16[32,8,1280]{2,1,0:T(8,128)(2,1)S(1)}, u32[]{:S(2)}, u32[]{:S(2)}) async-start(bf16[32,8,1280]{2,1,0:T(8,128)(2,1)} %fusion.14), calls=%async_computation.1 | async-start | bytes 1310720 | tf_op jit(solution)/shard_map/all_to_all | solution.py:128
  73.7 21.4 %all-to-all-start.2 = ((bf16[32,8,1280]{2,1,0:T(8,128)(2,1)}), bf16[32,8,1280]{2,1,0:T(8,128)(2,1)S(1)}, u32[]{:S(2)}, u32[]{:S(2)}) async-start(bf16[32,8,1280]{2,1,0:T(8,128)(2,1)} %fusion.15), calls=%async_computation.2 | async-start | bytes 1310720 | tf_op jit(solution)/shard_map/all_to_all | solution.py:135
  99.5 21.7 %all-to-all-start.3 = ((bf16[32,8,1280]{2,1,0:T(8,128)(2,1)}), bf16[32,8,1280]{2,1,0:T(8,128)(2,1)S(1)}, u32[]{:S(2)}, u32[]{:S(2)}) async-start(bf16[32,8,1280]{2,1,0:T(8,128)(2,1)} %bitcast.33), calls=%async_computation.3 | async-start | bytes 1310720 | tf_op jit(solution)/shard_map/all_to_all | solution.py:141
  110.2 4.3 %copy-start.16 = (bf16[256,10,2,64]{0,3,2,1:T(8,128)(2,1)S(1)}, bf16[256,10,2,64]{0,3,2,1:T(8,128)(2,1)}, u32[]{:S(2)}) copy-start(bf16[256,10,2,64]{0,3,2,1:T(8,128)(2,1)} %get-tuple-element.44) | copy-start | bytes 1966084
  110.2 4.3 %copy-start.17 = (bf16[256,10,2,64]{0,3,2,1:T(8,128)(2,1)S(1)}, bf16[256,10,2,64]{0,3,2,1:T(8,128)(2,1)}, u32[]{:S(2)}) copy-start(bf16[256,10,2,64]{0,3,2,1:T(8,128)(2,1)} %get-tuple-element.45) | copy-start | bytes 1966084
  114.6 1.1 copy-start.7
  114.6 1.3 copy-start.15
  114.6 1.6 %copy-start.19 = (bf16[256,10,2,64]{0,3,2,1:T(8,128)(2,1)S(1)}, bf16[256,10,2,64]{0,3,2,1:T(8,128)(2,1)}, u32[]{:S(2)}) copy-start(bf16[256,10,2,64]{0,3,2,1:T(8,128)(2,1)} %copy-done.18) | copy-start | bytes 1966084
  114.6 1.6 %copy-start.21 = (bf16[256,10,2,64]{0,3,2,1:T(8,128)(2,1)S(1)}, bf16[256,10,2,64]{0,3,2,1:T(8,128)(2,1)}, u32[]{:S(2)}) copy-start(bf16[256,10,2,64]{0,3,2,1:T(8,128)(2,1)} %copy-done.20) | copy-start | bytes 1966084
  114.6 1.8 %copy-start.23 = (bf16[256,10,2,64]{0,3,2,1:T(8,128)(2,1)S(1)}, bf16[256,10,2,64]{0,3,2,1:T(8,128)(2,1)}, u32[]{:S(2)}) copy-start(bf16[256,10,2,64]{0,3,2,1:T(8,128)(2,1)} %copy-done.22) | copy-start | bytes 1966084
  116.5 1.3 copy-start.4
  116.5 1.7 %copy-start.8 = (bf16[512,1280]{0,1:T(8,128)(2,1)S(1)}, bf16[512,1280]{0,1:T(8,128)(2,1)}, u32[]{:S(2)}) copy-start(bf16[512,1280]{0,1:T(8,128)(2,1)} %copy.70) | copy-start | bytes 3932164
  116.5 2.2 %copy-start.14 = (bf16[512,10,2,64]{0,3,2,1:T(8,128)(2,1)S(1)}, bf16[512,10,2,64]{0,3,2,1:T(8,128)(2,1)}, u32[]{:S(2)}) copy-start(bf16[512,10,2,64]{0,3,2,1:T(8,128)(2,1)} %copy-done.13) | copy-start | bytes 3932164
  118.2 1.4 copy-start.10
  118.2 1.8 %copy-start.12 = (bf16[512,10,2,64]{0,3,2,1:T(8,128)(2,1)S(1)}, bf16[512,10,2,64]{0,3,2,1:T(8,128)(2,1)}, u32[]{:S(2)}) copy-start(bf16[512,10,2,64]{0,3,2,1:T(8,128)(2,1)} %copy-done.11) | copy-start | bytes 3932164
  121.9 3.4 %collective-permute-start = (f32[28800]{0:T(1024)}, f32[28800]{0:T(1024)}, u32[]{:S(2)}, u32[]{:S(2)}) collective-permute-start(f32[28800]{0:T(1024)} %pad_maximum_fusion.5), channel_id=1, source_target_pairs={{0,1},{1,0},{2,3},{3,2},{4,5},{5,4},{6,7},{7,6},{8,9},{9,8},{10,11... | collective-permute-start | bytes 345608 | tf_op jit(solution)/shard_map/ppermute | solution.py:24
  126.3 5.6 %collective-permute-start.1 = (f32[28800]{0:T(1024)S(1)}, f32[28800]{0:T(1024)S(1)}, u32[]{:S(2)}, u32[]{:S(2)}) collective-permute-start(f32[28800]{0:T(1024)S(1)} %fusion.100), channel_id=1, source_target_pairs={{0,2},{1,3},{2,0},{3,1},{4,6},{5,7},{6,4},{7,5},{8,10},{9,11},{10,... | collective-permute-start | bytes 345608 | tf_op jit(solution)/shard_map/ppermute | solution.py:24
  131.9 5.3 %collective-permute-start.2 = (f32[28800]{0:T(1024)S(1)}, f32[28800]{0:T(1024)S(1)}, u32[]{:S(2)}, u32[]{:S(2)}) collective-permute-start(f32[28800]{0:T(1024)S(1)} %add.144), channel_id=1, source_target_pairs={{0,4},{1,5},{2,6},{3,7},{4,0},{5,1},{6,2},{7,3},{8,12},{9,13},{10,... | collective-permute-start | bytes 345608 | tf_op jit(solution)/shard_map/ppermute | solution.py:24
  137.2 4.9 %collective-permute-start.3 = (f32[28800]{0:T(1024)S(1)}, f32[28800]{0:T(1024)S(1)}, u32[]{:S(2)}, u32[]{:S(2)}) collective-permute-start(f32[28800]{0:T(1024)S(1)} %add.145), channel_id=1, source_target_pairs={{0,8},{1,9},{2,10},{3,11},{4,12},{5,13},{6,14},{7,15},{8,0},{9,1},... | collective-permute-start | bytes 345608 | tf_op jit(solution)/shard_map/ppermute | solution.py:24
  142.1 7.1 %collective-permute-start.4 = (f32[28800]{0:T(1024)S(1)}, f32[28800]{0:T(1024)S(1)}, u32[]{:S(2)}, u32[]{:S(2)}) collective-permute-start(f32[28800]{0:T(1024)S(1)} %add.146), channel_id=1, source_target_pairs={{0,16},{1,17},{2,18},{3,19},{4,20},{5,21},{6,22},{7,23},{8,24},{9,... | collective-permute-start | bytes 345608 | tf_op jit(solution)/shard_map/ppermute | solution.py:24

commit v6 on v5

--- a/solution.py
+++ b/solution.py
@@ -90,13 +90,13 @@
     )
     degree = (MEM + jnp.sum(members, axis=1))[:, None]
     members = members.astype(jnp.bfloat16)
-    cut_rows = jnp.take(feats, jnp.clip(slotted_segment, 0, seg - 1), axis=0)
-    stack, gate, first, hidden, z = front(feats)
-
     def pick_slots(rows):
         return jnp.einsum("sn,sf->nf", members, rows, preferred_element_type=jnp.float32).astype(
             jnp.bfloat16
         )
+
+    cut_rows = pick_slots(feats)
+    stack, gate, first, hidden, z = front(feats)
 
     edge_cols = jnp.broadcast_to(slotted_hyperedge.astype(jnp.bfloat16)[:, None], (slot_total, 128))
     in_width = feats.shape[1]

time: 152 us -> 150 us (0.987)
  local copies, waits for them, and re-layouts: 26.6 us -> 22.8 us
  matrix products: 31.8 us -> 33.9 us
    gather x1 -> x0, local copies, waits for them, and re-layouts: 3.62 us -> none  [body(): cut_rows = jnp.take(feats, jnp.clip(slotted_segment, 0, seg - 1), axis=0)]
    dot_general x1 -> x2, matrix products: 1.38 us -> 3.5 us  [pick_slots(): jnp.einsum('sn,sf->nf', members, rows, preferred_element_type=jnp.float32)]
  transfers between devices with their start and end apart: 9 -> 9, of which waited for: 6 -> 7; matrix products, arithmetic and copies ran while one was open for 23% -> 23% of each run, Pallas kernels for 0% -> 0%
where the time goes in v6:
time: 150 us; the launch traced here: 149 us
  waiting for transfers between devices  54.1 us (36%)
  matrix products  33.9 us (23%)
  starting transfers between devices  25.7 us (17%)
  local copies, waits for them, and re-layouts  22.8 us (15%)
  other arithmetic  11.6 us (8%)
    all_to_all x1, waiting for transfers between devices, body(): lax.all_to_all(send_grads, ('region', 'sub'), split_axis=0, concat_axis=0...  17.6 us
    all_to_all x1, waiting for transfers between devices, body(): lax.all_to_all(ret_rows, ('region', 'sub'), split_axis=0, concat_axis=0,...  15.6 us
    all_to_all x1, waiting for transfers between devices, body(): lax.all_to_all(send, ('region', 'sub'), split_axis=0, concat_axis=0, tile...  14.7 us
    unnamed x58, local copies, waits for them, and re-layouts  9.71 us
    dot_general x2, matrix products, weight_grads(): jnp.einsum('stbd,cd->stbc', dzr, theta, preferred_element_type=jnp.float32)  7.93 us
    ppermute x5, starting transfers between devices, device_sum(): flat = flat + lax.ppermute(flat, ('region', 'sub'), perm)  7.48 us
    all_to_all x1, starting transfers between devices, body(): lax.all_to_all(send, ('region', 'sub'), split_axis=0, concat_axis=0, tile...  7.41 us
    ppermute x5, waiting for transfers between devices, device_sum(): flat = flat + lax.ppermute(flat, ('region', 'sub'), perm)  6.19 us
  transfers between devices with their start and end apart: 9, of which 7 were waited for; matrix products, arithmetic and copies ran while one was open for 23% of the time, Pallas kernels for 0%

profile of v6, /device:TPU:0, one launch (start us, length us, event | category | flops | bytes accessed | tf_op | source)
XLA Modules:
  0.0 149.2 jit_solution(399297800165976476)
XLA Ops:
  0.6 0.7 fusion.83
  1.6 0.8 select_reduce_fusion
  2.4 0.7 fusion.95
  3.1 1.1 scatter_custom_fusion
  4.2 1.1 scatter_custom_fusion.1
  5.3 2.1 %convolution_convert_fusion.3 = bf16[256,1536]{1,0:T(8,128)(2,1)S(1)} fusion(bf16[512,1536]{1,0:T(8,128)(2,1)} %param.10, s32[256]{0:T(256)S(1)} %scatter_custom_fusion), kind=kOutput, calls=%fused_computation.34 | convolution fusion | flops 403439616 | bytes 2360320 | tf_op jit(solution)/shard_map/sn,sf->nf/dot_general | solution.py:94
  7.6 1.0 maximum_bitcast_fusion
  8.5 7.4 %all-to-all-start = ((bf16[32,8,1664]{2,1,0:T(8,128)(2,1)}), bf16[32,8,1664]{2,1,0:T(8,128)(2,1)}, u32[]{:S(2)}, u32[]{:S(2)}) async-start(bf16[32,8,1664]{2,1,0:T(8,128)(2,1)} %maximum_bitcast_fusion), calls=%async_computation | async-start | bytes 1703936 | tf_op jit(solution)/shard_map/all_to_all | solution.py:104
  15.9 0.7 copy.66
  16.7 0.5 fusion.103
  17.5 1.0 broadcast_add_fusion
  18.9 0.4 copy-done.13
  19.3 0.7 multiply_convert_fusion.5
  20.1 1.6 %copy-done.2 = f32[512,10,2,128]{0,3,2,1:T(8,128)} copy-done((f32[512,10,2,128]{0,3,2,1:T(8,128)}, f32[512,10,2,128]{0,3,2,1:T(8,128)S(1)}, u32[]{:S(2)}) %copy-start.2) | copy-done | bytes 5242904
  21.6 0.6 convolution_convert_fusion.4
  22.2 0.5 copy-done.3
  22.7 0.6 fusion.68
  23.3 14.7 %all-to-all-done = bf16[32,8,1664]{2,1,0:T(8,128)(2,1)} async-done(((bf16[32,8,1664]{2,1,0:T(8,128)(2,1)}), bf16[32,8,1664]{2,1,0:T(8,128)(2,1)}, u32[]{:S(2)}, u32[]{:S(2)}) %all-to-all-start) | async-done | bytes 852000 | tf_op jit(solution)/shard_map/all_to_all | solution.py:104
  38.0 1.0 convert_reduce_fusion.4
  38.9 1.2 slice.102
  40.7 0.5 convolution_add_fusion.4
  43.7 1.2 fusion.14
  44.8 3.6 %all-to-all-start.1 = ((bf16[32,8,1280]{2,1,0:T(8,128)(2,1)}), bf16[32,8,1280]{2,1,0:T(8,128)(2,1)S(1)}, u32[]{:S(2)}, u32[]{:S(2)}) async-start(bf16[32,8,1280]{2,1,0:T(8,128)(2,1)} %fusion.14), calls=%async_computation.1 | async-start | bytes 1310720 | tf_op jit(solution)/shard_map/all_to_all | solution.py:128
  48.6 2.1 %fusion.66 = f32[512,1280]{1,0:T(8,128)} fusion(bf16[128,1280]{1,0:T(8,128)(2,1)S(1)} %fusion.16, s32[512]{0:T(512)S(1)} %bitcast.124, s32[512]{0:T(512)S(1)} %bitcast.119), kind=kOutput, calls=%fused_computation.86 | convolution fusion | flops 168165376 | bytes 2953216 | tf_op jit(solution)/shard_map/es,ef->sf/dot_general | solution.py:123
  50.8 15.6 %all-to-all-done.1 = bf16[32,8,1280]{2,1,0:T(8,128)(2,1)S(1)} async-done(((bf16[32,8,1280]{2,1,0:T(8,128)(2,1)}), bf16[32,8,1280]{2,1,0:T(8,128)(2,1)S(1)}, u32[]{:S(2)}, u32[]{:S(2)}) %all-to-all-start.1) | async-done | bytes 655392 | tf_op jit(solution)/shard_map/all_to_all | solution.py:128
  66.4 4.0 %divide_convert_fusion = (bf16[512,1280]{1,0:T(8,128)(2,1)S(1)}, bf16[512,1280]{1,0:T(8,128)(2,1)}) fusion(bf16[512,1280]{1,0:T(8,128)(2,1)} %param.19, f32[512]{0:T(512)S(1)} %broadcast_add_fusion.1, f32[512,1280]{1,0:T(8,128)} %fusion.66, bf16[32,8,1280]{2,1,0:T(8,128)(2,1)S(1)} %all-to-all-done.1, s32[256]{0:T(256)S(1)} %scatter_custom_fusion), kind=kOutput, calls=%fused_computation.26 | convolution fusion | flops 345767936 | bytes 7212032 | tf_op jit(solution)/shard_map/dot_general | solution.py:125
  70.4 1.4 fusion.15
  71.8 3.5 %all-to-all-start.2 = ((bf16[32,8,1280]{2,1,0:T(8,128)(2,1)}), bf16[32,8,1280]{2,1,0:T(8,128)(2,1)S(1)}, u32[]{:S(2)}, u32[]{:S(2)}) async-start(bf16[32,8,1280]{2,1,0:T(8,128)(2,1)} %fusion.15), calls=%async_computation.2 | async-start | bytes 1310720 | tf_op jit(solution)/shard_map/all_to_all | solution.py:135
  75.7 17.6 %all-to-all-done.2 = bf16[32,8,1280]{2,1,0:T(8,128)(2,1)S(1)} async-done(((bf16[32,8,1280]{2,1,0:T(8,128)(2,1)}), bf16[32,8,1280]{2,1,0:T(8,128)(2,1)S(1)}, u32[]{:S(2)}, u32[]{:S(2)}) %all-to-all-start.2) | async-done | bytes 655392 | tf_op jit(solution)/shard_map/all_to_all | solution.py:135
  93.5 1.3 convolution_convert_fusion
  94.8 0.5 fusion.62
  95.3 2.2 %copy.73 = bf16[256,1280]{0,1:T(8,128)(2,1)} copy(bf16[256,1280]{1,0:T(8,128)(2,1)} %convolution_convert_fusion) | data formatting | bytes 1310720 | tf_op jit(solution)/shard_map/optimization_barrier | solution.py:140
  97.6 3.7 %all-to-all-start.3 = ((bf16[32,8,1280]{2,1,0:T(8,128)(2,1)}), bf16[32,8,1280]{2,1,0:T(8,128)(2,1)S(1)}, u32[]{:S(2)}, u32[]{:S(2)}) async-start(bf16[32,8,1280]{2,1,0:T(8,128)(2,1)} %bitcast.33), calls=%async_computation.3 | async-start | bytes 1310720 | tf_op jit(solution)/shard_map/all_to_all | solution.py:141
  101.3 3.6 %multiply_convert_fusion.7 = (bf16[256,10,2,64]{0,3,2,1:T(8,128)(2,1)}, bf16[256,10,2,64]{0,3,2,1:T(8,128)(2,1)}) fusion(f32[256,10,2,128]{0,3,2,1:T(8,128)} %copy-done.5, bf16[256,10,2,64]{0,3,2,1:T(8,128)(2,1)} %bitcast.113, bf16[64,64]{1,0:T(8,128)(2,1)S(1)} %copy-done.24), kind=kOutput, calls=%fused_computation.59 | convolution fusion | flops 45219840 | bytes 4595712 | tf_op jit(solution)/shard_map/stbd,cd->stbc/dot_general | solution.py:147
  104.9 1.2 convert_element_type.124
  106.1 2.4 %copy.70 = bf16[512,1280]{0,1:T(8,128)(2,1)} copy(bf16[512,1280]{1,0:T(8,128)(2,1)} %convert_element_type.124) | data formatting | bytes 2621440 | tf_op jit(solution)/shard_map/convert_element_type | solution.py:153
  108.5 4.3 %multiply_convert_fusion.3 = (bf16[512,10,2,64]{0,3,2,1:T(8,128)(2,1)S(1)}, bf16[512,10,2,64]{0,3,2,1:T(8,128)(2,1)S(1)}) fusion(f32[512,10,2,128]{0,3,2,1:T(8,128)} %copy-done.2, bf16[512,10,2,64]{0,3,2,1:T(8,128)(2,1)} %bitcast.110, bf16[64,64]{1,0:T(8,128)(2,1)S(1)} %copy-done.24), kind=kOutput, calls=%fused_computation.25 | convolution fusion | flops 90439680 | bytes 9183232 | tf_op jit(solution)/shard_map/stbd,cd->stbc/dot_general | solution.py:147
  113.2 0.4 convert_reduce_fusion
  114.7 0.7 fusion.27
  115.4 0.6 copy-done.4
  116.1 0.4 copy-done.8
  116.4 0.5 fusion.47
  117.0 0.9 copy-done.10
  117.9 0.4 copy-done.12
  118.3 1.2 fusion.37
  119.5 0.7 pad_maximum_fusion.4
  120.3 1.6 %fusion.3 = bf16[512,1280]{1,0:T(8,128)(2,1)} fusion(f32[512,1280]{1,0:T(8,128)S(1)} %fusion.62, bf16[256,1280]{1,0:T(8,128)(2,1)S(1)} %bitcast.108, s32[256]{0:T(256)S(1)} %scatter_custom_fusion), kind=kOutput, calls=%fused_computation.10 | convolution fusion | flops 337248256 | bytes 4588544 | tf_op jit(solution)/shard_map/dot_general | solution.py:161
  121.9 1.6 %copy.80 = bf16[512,1280]{0,1:T(8,128)(2,1)S(1)} copy(bf16[512,1280]{1,0:T(8,128)(2,1)} %fusion.3) | data formatting | bytes 2621440 | tf_op jit(solution)/shard_map/convert_element_type | solution.py:162
  123.5 0.9 fusion.101
  124.4 1.7 %collective-permute-start.1 = (f32[28800]{0:T(1024)S(1)}, f32[28800]{0:T(1024)S(1)}, u32[]{:S(2)}, u32[]{:S(2)}) collective-permute-start(f32[28800]{0:T(1024)S(1)} %fusion.101), channel_id=1, source_target_pairs={{0,2},{1,3},{2,0},{3,1},{4,6},{5,7},{6,4},{7,5},{8,10},{9,11},{10,... | collective-permute-start | bytes 345608 | tf_op jit(solution)/shard_map/ppermute | solution.py:24
  126.2 3.8 %multiply_convert_fusion.1 = (bf16[512,10,2,64]{0,3,2,1:T(8,128)(2,1)S(1)}, bf16[512,10,2,64]{0,3,2,1:T(8,128)(2,1)S(1)}) fusion(f32[512,10,2,128]{0,3,2,1:T(8,128)} %copy-done.2, bf16[512,10,2,64]{0,3,2,1:T(8,128)(2,1)S(1)} %bitcast.112, bf16[64,64]{1,0:T(8,128)(2,1)S(1)} %copy-done.24), kind=kOutput, calls=%fused_computation.22 | convolution fusion | flops 90439680 | bytes 9183232 | tf_op jit(solution)/shard_map/stbd,cd->stbc/dot_general | solution.py:165
  130.1 1.7 %collective-permute-start.2 = (f32[28800]{0:T(1024)S(1)}, f32[28800]{0:T(1024)S(1)}, u32[]{:S(2)}, u32[]{:S(2)}) collective-permute-start(f32[28800]{0:T(1024)S(1)} %add.134), channel_id=1, source_target_pairs={{0,4},{1,5},{2,6},{3,7},{4,0},{5,1},{6,2},{7,3},{8,12},{9,13},{10,... | collective-permute-start | bytes 345608 | tf_op jit(solution)/shard_map/ppermute | solution.py:24
  131.8 1.2 fusion.7
  132.9 2.3 %collective-permute-done.2 = f32[28800]{0:T(1024)S(1)} collective-permute-done((f32[28800]{0:T(1024)S(1)}, f32[28800]{0:T(1024)S(1)}, u32[]{:S(2)}, u32[]{:S(2)}) %collective-permute-start.2) | collective-permute-done | bytes 115232 | tf_op jit(solution)/shard_map/ppermute | solution.py:24
  135.3 1.5 %collective-permute-start.3 = (f32[28800]{0:T(1024)S(1)}, f32[28800]{0:T(1024)S(1)}, u32[]{:S(2)}, u32[]{:S(2)}) collective-permute-start(f32[28800]{0:T(1024)S(1)} %add.135), channel_id=1, source_target_pairs={{0,8},{1,9},{2,10},{3,11},{4,12},{5,13},{6,14},{7,15},{8,0},{9,1},... | collective-permute-start | bytes 345608 | tf_op jit(solution)/shard_map/ppermute | solution.py:24
  136.8 1.6 %fusion.102 = (f32[512,10,2,64]{0,3,2,1:T(8,128)S(1)}, f32[512,10,2,64]{0,3,2,1:T(8,128)S(1)}, f32[512,10,2,64]{0,3,2,1:T(8,128)S(1)}) fusion(f32[512,10,2,192]{0,3,2,1:T(8,128)S(1)} %fusion.7), kind=kLoop, calls=%fused_computation.134 | loop fusion | bytes 15728640 | tf_op jit(solution)/shard_map/slice | solution.py:174
  138.5 1.7 %collective-permute-done.3 = f32[28800]{0:T(1024)S(1)} collective-permute-done((f32[28800]{0:T(1024)S(1)}, f32[28800]{0:T(1024)S(1)}, u32[]{:S(2)}, u32[]{:S(2)}) %collective-permute-start.3) | collective-permute-done | bytes 115232 | tf_op jit(solution)/shard_map/ppermute | solution.py:24
  140.2 2.5 %collective-permute-start.4 = (f32[28800]{0:T(1024)S(1)}, f32[28800]{0:T(1024)S(1)}, u32[]{:S(2)}, u32[]{:S(2)}) collective-permute-start(f32[28800]{0:T(1024)S(1)} %add.136), channel_id=1, source_target_pairs={{0,16},{1,17},{2,18},{3,19},{4,20},{5,21},{6,22},{7,23},{8,24},{9,... | collective-permute-start | bytes 345608 | tf_op jit(solution)/shard_map/ppermute | solution.py:24
  142.7 1.0 add_convert_fusion
  143.7 1.6 %copy.82 = bf16[512,1536]{1,0:T(8,128)(2,1)} copy(bf16[512,1536]{0,1:T(8,128)(2,1)S(1)} %bitcast.106) | data formatting | bytes 3145728
  145.3 2.0 %collective-permute-done.4 = f32[28800]{0:T(1024)S(1)} collective-permute-done((f32[28800]{0:T(1024)S(1)}, f32[28800]{0:T(1024)S(1)}, u32[]{:S(2)}, u32[]{:S(2)}) %collective-permute-start.4) | collective-permute-done | bytes 115232 | tf_op jit(solution)/shard_map/ppermute | solution.py:24
  147.3 0.5 slice_multiply_fusion.2
  147.8 0.6 fusion.78
  148.5 0.7 mul.133
  (78 shorter events, 6.4 us)
Async XLA Ops:
  0.6 16.9 %copy-start = (bf16[192,128]{1,0:T(8,128)(2,1)S(1)}, bf16[192,128]{1,0:T(8,128)(2,1)}, u32[]{:S(2)}) copy-start(bf16[192,128]{1,0:T(8,128)(2,1)} %param.11) | copy-start | bytes 147460
  5.3 10.6 %copy-start.1 = (bf16[512,1536]{1,0:T(8,128)(2,1)S(1)}, bf16[512,1536]{1,0:T(8,128)(2,1)}, u32[]{:S(2)}) copy-start(bf16[512,1536]{1,0:T(8,128)(2,1)} %param.10) | copy-start | bytes 4718596
  8.5 29.4 %all-to-all-start = ((bf16[32,8,1664]{2,1,0:T(8,128)(2,1)}), bf16[32,8,1664]{2,1,0:T(8,128)(2,1)}, u32[]{:S(2)}, u32[]{:S(2)}) async-start(bf16[32,8,1664]{2,1,0:T(8,128)(2,1)} %maximum_bitcast_fusion), calls=%async_computation | async-start | bytes 1703936 | tf_op jit(solution)/shard_map/all_to_all | solution.py:104
  16.7 0.7 copy-start.25
  16.7 0.8 copy-start.27
  17.4 1.2 copy-start.9
  17.4 1.6 %copy-start.11 = (bf16[512,10,2,64]{0,3,2,1:T(8,128)(2,1)}, bf16[512,10,2,64]{0,3,2,1:T(8,128)(2,1)S(1)}, u32[]{:S(2)}) copy-start(bf16[512,10,2,64]{0,3,2,1:T(8,128)(2,1)S(1)} %get-tuple-element.49) | copy-start | bytes 3932164
  17.4 2.0 %copy-start.13 = (bf16[512,10,2,64]{0,3,2,1:T(8,128)(2,1)}, bf16[512,10,2,64]{0,3,2,1:T(8,128)(2,1)S(1)}, u32[]{:S(2)}) copy-start(bf16[512,10,2,64]{0,3,2,1:T(8,128)(2,1)S(1)} %get-tuple-element.50) | copy-start | bytes 3932164
  19.3 2.3 %copy-start.2 = (f32[512,10,2,128]{0,3,2,1:T(8,128)}, f32[512,10,2,128]{0,3,2,1:T(8,128)S(1)}, u32[]{:S(2)}) copy-start(f32[512,10,2,128]{0,3,2,1:T(8,128)S(1)} %broadcast_add_fusion) | copy-start | bytes 15728644
  19.3 2.3 %copy-start.24 = (bf16[64,64]{1,0:T(8,128)(2,1)S(1)}, bf16[64,64]{1,0:T(8,128)(2,1)}, u32[]{:S(2)}) copy-start(bf16[64,64]{1,0:T(8,128)(2,1)} %param.13) | copy-start | bytes 24580
  21.6 1.1 copy-start.3
  40.7 0.8 copy-start.18
  40.7 1.1 copy-start.20
  40.7 1.2 copy-start.22
  41.9 1.5 copy-start.5
  41.9 0.8 copy-start.26
  42.3 1.4 copy-start.6
  44.8 21.5 %all-to-all-start.1 = ((bf16[32,8,1280]{2,1,0:T(8,128)(2,1)}), bf16[32,8,1280]{2,1,0:T(8,128)(2,1)S(1)}, u32[]{:S(2)}, u32[]{:S(2)}) async-start(bf16[32,8,1280]{2,1,0:T(8,128)(2,1)} %fusion.14), calls=%async_computation.1 | async-start | bytes 1310720 | tf_op jit(solution)/shard_map/all_to_all | solution.py:128
  71.8 21.4 %all-to-all-start.2 = ((bf16[32,8,1280]{2,1,0:T(8,128)(2,1)}), bf16[32,8,1280]{2,1,0:T(8,128)(2,1)S(1)}, u32[]{:S(2)}, u32[]{:S(2)}) async-start(bf16[32,8,1280]{2,1,0:T(8,128)(2,1)} %fusion.15), calls=%async_computation.2 | async-start | bytes 1310720 | tf_op jit(solution)/shard_map/all_to_all | solution.py:135
  97.6 21.9 %all-to-all-start.3 = ((bf16[32,8,1280]{2,1,0:T(8,128)(2,1)}), bf16[32,8,1280]{2,1,0:T(8,128)(2,1)S(1)}, u32[]{:S(2)}, u32[]{:S(2)}) async-start(bf16[32,8,1280]{2,1,0:T(8,128)(2,1)} %bitcast.33), calls=%async_computation.3 | async-start | bytes 1310720 | tf_op jit(solution)/shard_map/all_to_all | solution.py:141
  108.5 4.3 %copy-start.16 = (bf16[256,10,2,64]{0,3,2,1:T(8,128)(2,1)S(1)}, bf16[256,10,2,64]{0,3,2,1:T(8,128)(2,1)}, u32[]{:S(2)}) copy-start(bf16[256,10,2,64]{0,3,2,1:T(8,128)(2,1)} %get-tuple-element.44) | copy-start | bytes 1966084
  108.5 4.3 %copy-start.17 = (bf16[256,10,2,64]{0,3,2,1:T(8,128)(2,1)S(1)}, bf16[256,10,2,64]{0,3,2,1:T(8,128)(2,1)}, u32[]{:S(2)}) copy-start(bf16[256,10,2,64]{0,3,2,1:T(8,128)(2,1)} %get-tuple-element.45) | copy-start | bytes 1966084
  112.8 1.1 copy-start.7
  112.8 1.3 copy-start.15
  112.9 1.6 %copy-start.19 = (bf16[256,10,2,64]{0,3,2,1:T(8,128)(2,1)S(1)}, bf16[256,10,2,64]{0,3,2,1:T(8,128)(2,1)}, u32[]{:S(2)}) copy-start(bf16[256,10,2,64]{0,3,2,1:T(8,128)(2,1)} %copy-done.18) | copy-start | bytes 1966084
  112.9 1.6 %copy-start.21 = (bf16[256,10,2,64]{0,3,2,1:T(8,128)(2,1)S(1)}, bf16[256,10,2,64]{0,3,2,1:T(8,128)(2,1)}, u32[]{:S(2)}) copy-start(bf16[256,10,2,64]{0,3,2,1:T(8,128)(2,1)} %copy-done.20) | copy-start | bytes 1966084
  112.9 1.8 %copy-start.23 = (bf16[256,10,2,64]{0,3,2,1:T(8,128)(2,1)S(1)}, bf16[256,10,2,64]{0,3,2,1:T(8,128)(2,1)}, u32[]{:S(2)}) copy-start(bf16[256,10,2,64]{0,3,2,1:T(8,128)(2,1)} %copy-done.22) | copy-start | bytes 1966084
  114.7 1.3 copy-start.4
  114.7 1.7 %copy-start.8 = (bf16[512,1280]{0,1:T(8,128)(2,1)S(1)}, bf16[512,1280]{0,1:T(8,128)(2,1)}, u32[]{:S(2)}) copy-start(bf16[512,1280]{0,1:T(8,128)(2,1)} %copy.70) | copy-start | bytes 3932164
  114.7 2.2 %copy-start.14 = (bf16[512,10,2,64]{0,3,2,1:T(8,128)(2,1)S(1)}, bf16[512,10,2,64]{0,3,2,1:T(8,128)(2,1)}, u32[]{:S(2)}) copy-start(bf16[512,10,2,64]{0,3,2,1:T(8,128)(2,1)} %copy-done.13) | copy-start | bytes 3932164
  116.4 1.4 copy-start.10
  116.4 1.8 %copy-start.12 = (bf16[512,10,2,64]{0,3,2,1:T(8,128)(2,1)S(1)}, bf16[512,10,2,64]{0,3,2,1:T(8,128)(2,1)}, u32[]{:S(2)}) copy-start(bf16[512,10,2,64]{0,3,2,1:T(8,128)(2,1)} %copy-done.11) | copy-start | bytes 3932164
  120.2 3.3 %collective-permute-start = (f32[28800]{0:T(1024)}, f32[28800]{0:T(1024)}, u32[]{:S(2)}, u32[]{:S(2)}) collective-permute-start(f32[28800]{0:T(1024)} %pad_maximum_fusion.4), channel_id=1, source_target_pairs={{0,1},{1,0},{2,3},{3,2},{4,5},{5,4},{6,7},{7,6},{8,9},{9,8},{10,11... | collective-permute-start | bytes 345608 | tf_op jit(solution)/shard_map/ppermute | solution.py:24
  124.4 5.6 %collective-permute-start.1 = (f32[28800]{0:T(1024)S(1)}, f32[28800]{0:T(1024)S(1)}, u32[]{:S(2)}, u32[]{:S(2)}) collective-permute-start(f32[28800]{0:T(1024)S(1)} %fusion.101), channel_id=1, source_target_pairs={{0,2},{1,3},{2,0},{3,1},{4,6},{5,7},{6,4},{7,5},{8,10},{9,11},{10,... | collective-permute-start | bytes 345608 | tf_op jit(solution)/shard_map/ppermute | solution.py:24
  130.1 5.2 %collective-permute-start.2 = (f32[28800]{0:T(1024)S(1)}, f32[28800]{0:T(1024)S(1)}, u32[]{:S(2)}, u32[]{:S(2)}) collective-permute-start(f32[28800]{0:T(1024)S(1)} %add.134), channel_id=1, source_target_pairs={{0,4},{1,5},{2,6},{3,7},{4,0},{5,1},{6,2},{7,3},{8,12},{9,13},{10,... | collective-permute-start | bytes 345608 | tf_op jit(solution)/shard_map/ppermute | solution.py:24
  135.3 4.9 %collective-permute-start.3 = (f32[28800]{0:T(1024)S(1)}, f32[28800]{0:T(1024)S(1)}, u32[]{:S(2)}, u32[]{:S(2)}) collective-permute-start(f32[28800]{0:T(1024)S(1)} %add.135), channel_id=1, source_target_pairs={{0,8},{1,9},{2,10},{3,11},{4,12},{5,13},{6,14},{7,15},{8,0},{9,1},... | collective-permute-start | bytes 345608 | tf_op jit(solution)/shard_map/ppermute | solution.py:24
  140.2 7.1 %collective-permute-start.4 = (f32[28800]{0:T(1024)S(1)}, f32[28800]{0:T(1024)S(1)}, u32[]{:S(2)}, u32[]{:S(2)}) collective-permute-start(f32[28800]{0:T(1024)S(1)} %add.136), channel_id=1, source_target_pairs={{0,16},{1,17},{2,18},{3,19},{4,20},{5,21},{6,22},{7,23},{8,24},{9,... | collective-permute-start | bytes 345608 | tf_op jit(solution)/shard_map/ppermute | solution.py:24

commit v7 on v6

--- a/solution.py
+++ b/solution.py
@@ -15,14 +15,29 @@
 def device_sum(parts, n):
     sizes = [p.size for p in parts]
     flat = jnp.concatenate([p.reshape(-1) for p in parts])
+    n_sub = lax.axis_size("sub")
+    n_region = n // n_sub
     if n & (n - 1):
         flat = lax.psum(flat, ("region", "sub"))
     else:
+        last = n_sub if n_region <= 4 else n
         step = 1
-        while step < n:
+        while step < last:
             perm = [(i, i ^ step) for i in range(n)]
             flat = flat + lax.ppermute(flat, ("region", "sub"), perm)
             step *= 2
+    if not n & (n - 1) and n_region <= 4:
+        region = lax.axis_index("region")
+        got = [flat] + [
+            lax.ppermute(flat, ("region", "sub"), [(i, i ^ (m * n_sub)) for i in range(n)])
+            for m in range(1, n_region)
+        ]
+        got = jnp.stack(got)
+        total = None
+        for i in range(n_region):
+            v = lax.dynamic_index_in_dim(got, i ^ region, keepdims=False)
+            total = v if total is None else total + v
+        flat = total
     out, at = [], 0
     for p, size in zip(parts, sizes):
         out.append(flat[at : at + size].reshape(p.shape))
@@ -51,7 +66,7 @@
     width = TP * B * C
     def front(rows):
         n = rows.shape[0]
-        x4 = rows.reshape(n, T_SIZE, B, C)
+        x4 = rows.reshape(n, -1, B, C)
         stack = jnp.concatenate([x4[:, k : k + TP] for k in range(KT)], axis=-1)
         u = (
             jnp.einsum("stbk,kf->stbf", stack, conv_weight, preferred_element_type=jnp.float32)
@@ -98,11 +113,11 @@
     cut_rows = pick_slots(feats)
     stack, gate, first, hidden, z = front(feats)
 
-    edge_cols = jnp.broadcast_to(slotted_hyperedge.astype(jnp.bfloat16)[:, None], (slot_total, 128))
+    edge_cols = jnp.broadcast_to(slotted_hyperedge.astype(jnp.bfloat16)[:, None], (slot_total, B * C))
     in_width = feats.shape[1]
     send = jnp.concatenate([cut_rows, edge_cols], axis=1)
     recv_all = lax.all_to_all(send, ("region", "sub"), split_axis=0, concat_axis=0, tiled=True)
-    r_stack, r_gate, r_first, r_hidden, recv = front(recv_all[:, :in_width])
+    r_stack, r_gate, r_first, r_hidden, recv = front(recv_all)
     recv_edge = recv_all[:, in_width].astype(jnp.int32)
     owned = (recv_edge[None, :] == edge_index[:, None]).astype(jnp.float32)
     count = 1.0 + inner_count + jnp.sum(owned, axis=1)

time: 150 us -> 179 us (1.19)
  local copies, waits for them, and re-layouts: 22.8 us -> 35.2 us
  waiting for transfers between devices: 54.1 us -> 66.3 us
  matrix products: 33.9 us -> 37.1 us
    all_to_all x1, waiting for transfers between devices: 0.01 us -> 9.77 us  [body(): lax.all_to_all(ret_grads, ('region', 'sub'), split_axis=0, concat_axis=0,...]
    unnamed x58 -> x72, local copies, waits for them, and re-layouts: 9.71 us -> 17.2 us
    ppermute x0 -> x3, waiting for transfers between devices: none -> 5.04 us  [device_sum(): lax.ppermute(flat, ('region', 'sub'), [(i, i ^ m * n_sub) for i in range(...]
    ppermute x0 -> x3, starting transfers between devices: none -> 4.45 us  [device_sum(): lax.ppermute(flat, ('region', 'sub'), [(i, i ^ m * n_sub) for i in range(...]
    ppermute x5 -> x3, starting transfers between devices: 7.48 us -> 3.28 us  [device_sum(): flat = flat + lax.ppermute(flat, ('region', 'sub'), perm)]
    slice x2, local copies, waits for them, and re-layouts: 0.65 us -> 4.17 us  [front(): stack = jnp.concatenate([x4[:, k:k + TP] for k in range(KT)], axis=-1)]
    reshape x0 -> x1, local copies, waits for them, and re-layouts: none -> 3.42 us  [front(): x4 = rows.reshape(n, -1, B, C)]
    reduce_sum x2, other arithmetic: 0.71 us -> 2.58 us  [weight_grads(): g_bias = jnp.sum(du.astype(jnp.float32), axis=(0, 1, 2))]
  transfers between devices with their start and end apart: 9 -> 10, of which waited for: 7 -> 8; matrix products, arithmetic and copies ran while one was open for 23% -> 13% of each run, Pallas kernels for 0% -> 0%
where the time goes in v7:
time: 179 us; the launch traced here: 178 us
  waiting for transfers between devices  66.3 us (37%)
  matrix products  37.1 us (21%)
  local copies, waits for them, and re-layouts  35.2 us (20%)
  starting transfers between devices  25.8 us (14%)
  other arithmetic  12.7 us (7%)
    all_to_all x1, waiting for transfers between devices, body(): lax.all_to_all(send_grads, ('region', 'sub'), split_axis=0, concat_axis=0...  17.5 us
    unnamed x72, local copies, waits for them, and re-layouts  17.2 us
    all_to_all x1, waiting for transfers between devices, body(): lax.all_to_all(ret_rows, ('region', 'sub'), split_axis=0, concat_axis=0,...  15.6 us
    all_to_all x1, waiting for transfers between devices, body(): lax.all_to_all(send, ('region', 'sub'), split_axis=0, concat_axis=0, tile...  13.8 us
    all_to_all x1, waiting for transfers between devices, body(): lax.all_to_all(ret_grads, ('region', 'sub'), split_axis=0, concat_axis=0,...  9.77 us
    dot_general x2, matrix products, weight_grads(): jnp.einsum('stbd,cd->stbc', dzr, theta, preferred_element_type=jnp.float32)  9.43 us
    all_to_all x1, starting transfers between devices, body(): lax.all_to_all(send, ('region', 'sub'), split_axis=0, concat_axis=0, tile...  7.41 us
    ppermute x3, waiting for transfers between devices, device_sum(): lax.ppermute(flat, ('region', 'sub'), [(i, i ^ m * n_sub) for i in range(...  5.04 us
  transfers between devices with their start and end apart: 10, of which 8 were waited for; matrix products, arithmetic and copies ran while one was open for 13% of the time, Pallas kernels for 0%

profile of v7, /device:TPU:0, one launch (start us, length us, event | category | flops | bytes accessed | tf_op | source)
XLA Modules:
  0.0 178.4 jit_solution(3173110778813825352)
XLA Ops:
  0.6 0.7 fusion.82
  1.6 0.8 select_reduce_fusion
  2.4 0.7 fusion.95
  3.1 1.1 scatter_custom_fusion
  4.2 1.1 scatter_custom_fusion.1
  5.3 2.1 %convolution_convert_fusion.3 = bf16[256,1536]{1,0:T(8,128)(2,1)S(1)} fusion(bf16[512,1536]{1,0:T(8,128)(2,1)} %param.10, s32[256]{0:T(256)S(1)} %scatter_custom_fusion), kind=kOutput, calls=%fused_computation.34 | convolution fusion | flops 403439616 | bytes 2360320 | tf_op jit(solution)/shard_map/sn,sf->nf/dot_general | solution.py:109
  7.6 1.0 maximum_bitcast_fusion
  8.5 7.4 %all-to-all-start = ((bf16[32,8,1664]{2,1,0:T(8,128)(2,1)}), bf16[32,8,1664]{2,1,0:T(8,128)(2,1)}, u32[]{:S(2)}, u32[]{:S(2)}) async-start(bf16[32,8,1664]{2,1,0:T(8,128)(2,1)} %maximum_bitcast_fusion), calls=%async_computation | async-start | bytes 1703936 | tf_op jit(solution)/shard_map/all_to_all | solution.py:119
  15.9 0.7 copy.53
  17.5 1.0 broadcast_add_fusion
  19.3 0.7 multiply_convert_fusion.5
  20.1 1.6 copy-done.2
  21.7 0.6 convolution_convert_fusion.4
  22.8 1.4 fusion.68
  24.2 13.8 %all-to-all-done = bf16[32,8,1664]{2,1,0:T(8,128)(2,1)} async-done(((bf16[32,8,1664]{2,1,0:T(8,128)(2,1)}), bf16[32,8,1664]{2,1,0:T(8,128)(2,1)}, u32[]{:S(2)}, u32[]{:S(2)}) %all-to-all-start) | async-done | bytes 852000 | tf_op jit(solution)/shard_map/all_to_all | solution.py:119
  38.0 3.4 %reshape.98 = bf16[256,13,2,64]{3,2,1,0:T(2,128)(2,1)S(1)} reshape(bf16[32,8,1664]{2,1,0:T(8,128)(2,1)} %all-to-all-done) | data formatting | bytes 1703936 | tf_op jit(solution)/shard_map/reshape | solution.py:69
  41.4 3.7 %fusion.104 = (bf16[256,10,2,64]{3,2,1,0:T(2,128)(2,1)S(1)}, bf16[256,10,2,64]{3,2,1,0:T(2,128)(2,1)}, bf16[256,10,2,64]{3,2,1,0:T(2,128)(2,1)}) fusion(bf16[256,13,2,64]{3,2,1,0:T(2,128)(2,1)S(1)} %reshape.98), kind=kLoop, calls=%fused_computation.138 | loop fusion | bytes 3932160 | tf_op jit(solution)/shard_map/slice | solution.py:70
  45.1 2.7 %copy.90 = bf16[256,10,2,64]{0,3,2,1:T(8,128)(2,1)S(1)} copy(bf16[256,10,2,64]{3,2,1,0:T(2,128)(2,1)} %get-tuple-element.45) | data formatting | bytes 1310720
  47.8 2.1 %copy.89 = bf16[256,10,2,64]{0,3,2,1:T(8,128)(2,1)} copy(bf16[256,10,2,64]{3,2,1,0:T(2,128)(2,1)S(1)} %copy-done.5) | data formatting | bytes 1310720
  49.9 1.0 copy.88
  51.0 0.8 copy-done.26
  51.8 1.6 convolution_add_fusion.4
  53.4 1.5 copy-done.6
  55.3 0.9 copy-done.8
  56.6 0.9 slice_convert_fusion
  58.1 1.2 fusion.14
  59.3 3.6 %all-to-all-start.1 = ((bf16[32,8,1280]{2,1,0:T(8,128)(2,1)}), bf16[32,8,1280]{2,1,0:T(8,128)(2,1)S(1)}, u32[]{:S(2)}, u32[]{:S(2)}) async-start(bf16[32,8,1280]{2,1,0:T(8,128)(2,1)} %fusion.14), calls=%async_computation.1 | async-start | bytes 1310720 | tf_op jit(solution)/shard_map/all_to_all | solution.py:143
  63.0 2.1 %fusion.66 = f32[512,1280]{1,0:T(8,128)} fusion(bf16[128,1280]{1,0:T(8,128)(2,1)S(1)} %fusion.16, s32[512]{0:T(512)S(1)} %bitcast.123, s32[512]{0:T(512)S(1)} %bitcast.118), kind=kOutput, calls=%fused_computation.87 | convolution fusion | flops 168165376 | bytes 2953216 | tf_op jit(solution)/shard_map/es,ef->sf/dot_general | solution.py:138
  65.2 15.6 %all-to-all-done.1 = bf16[32,8,1280]{2,1,0:T(8,128)(2,1)S(1)} async-done(((bf16[32,8,1280]{2,1,0:T(8,128)(2,1)}), bf16[32,8,1280]{2,1,0:T(8,128)(2,1)S(1)}, u32[]{:S(2)}, u32[]{:S(2)}) %all-to-all-start.1) | async-done | bytes 655392 | tf_op jit(solution)/shard_map/all_to_all | solution.py:143
  80.8 3.8 %divide_convert_fusion = (bf16[512,1280]{1,0:T(8,128)(2,1)S(1)}, bf16[512,1280]{1,0:T(8,128)(2,1)}) fusion(bf16[512,1280]{1,0:T(8,128)(2,1)S(1)} %copy-done.31, f32[512]{0:T(512)S(1)} %broadcast_add_fusion.1, f32[512,1280]{1,0:T(8,128)} %fusion.66, bf16[32,8,1280]{2,1,0:T(8,128)(2,1)S(1)} %all-to-all-done.1, s32[256]{0:T(256)S(1)} %scatter_custom_fusion), kind=kOutput, calls=%fused_computation.26 | convolution fusion | flops 345767936 | bytes 7212032 | tf_op jit(solution)/shard_map/dot_general | solution.py:140
  84.6 1.4 fusion.15
  86.0 3.5 %all-to-all-start.2 = ((bf16[32,8,1280]{2,1,0:T(8,128)(2,1)}), bf16[32,8,1280]{2,1,0:T(8,128)(2,1)S(1)}, u32[]{:S(2)}, u32[]{:S(2)}) async-start(bf16[32,8,1280]{2,1,0:T(8,128)(2,1)} %fusion.15), calls=%async_computation.2 | async-start | bytes 1310720 | tf_op jit(solution)/shard_map/all_to_all | solution.py:150
  89.9 17.5 %all-to-all-done.2 = bf16[32,8,1280]{2,1,0:T(8,128)(2,1)S(1)} async-done(((bf16[32,8,1280]{2,1,0:T(8,128)(2,1)}), bf16[32,8,1280]{2,1,0:T(8,128)(2,1)S(1)}, u32[]{:S(2)}, u32[]{:S(2)}) %all-to-all-start.2) | async-done | bytes 655392 | tf_op jit(solution)/shard_map/all_to_all | solution.py:150
  108.3 1.2 convolution_convert_fusion
  109.5 1.3 copy.62
  110.8 3.7 %multiply_convert_fusion.7 = (bf16[256,10,2,64]{0,3,2,1:T(8,128)(2,1)}, bf16[256,10,2,64]{0,3,2,1:T(8,128)(2,1)}) fusion(f32[256,10,2,128]{0,3,2,1:T(8,128)} %copy-done.6, bf16[256,10,2,64]{0,3,2,1:T(8,128)(2,1)S(1)} %bitcast.111, bf16[64,64]{1,0:T(8,128)(2,1)S(1)} %copy-done.28), kind=kOutput, calls=%fused_computation.59 | convolution fusion | flops 45219840 | bytes 4595712 | tf_op jit(solution)/shard_map/stbd,cd->stbc/dot_general | solution.py:162
  114.5 1.2 convert_element_type.124
  115.7 2.4 %copy.59 = bf16[512,1280]{0,1:T(8,128)(2,1)} copy(bf16[512,1280]{1,0:T(8,128)(2,1)} %convert_element_type.124) | data formatting | bytes 2621440 | tf_op jit(solution)/shard_map/convert_element_type | solution.py:168
  118.1 5.8 %multiply_convert_fusion.3 = (bf16[512,10,2,64]{0,3,2,1:T(8,128)(2,1)}, bf16[512,10,2,64]{0,3,2,1:T(8,128)(2,1)}) fusion(f32[512,10,2,128]{0,3,2,1:T(8,128)} %copy-done.2, bf16[512,10,2,64]{0,3,2,1:T(8,128)(2,1)} %bitcast.108, bf16[64,64]{1,0:T(8,128)(2,1)S(1)} %copy-done.28), kind=kOutput, calls=%fused_computation.25 | convolution fusion | flops 90439680 | bytes 9183232 | tf_op jit(solution)/shard_map/stbd,cd->stbc/dot_general | solution.py:162
  123.9 3.5 %all-to-all-start.3 = ((bf16[32,8,1280]{2,1,0:T(8,128)(2,1)}), bf16[32,8,1280]{2,1,0:T(8,128)(2,1)S(1)}, u32[]{:S(2)}, u32[]{:S(2)}) async-start(bf16[32,8,1280]{2,1,0:T(8,128)(2,1)} %bitcast.33), calls=%async_computation.3 | async-start | bytes 1310720 | tf_op jit(solution)/shard_map/all_to_all | solution.py:156
  127.5 2.3 %convert_reduce_fusion = f32[128]{0:T(128)S(1)} fusion(bf16[512,10,2,64]{0,3,2,1:T(8,128)(2,1)} %get-tuple-element.38, bf16[512,10,2,64]{0,3,2,1:T(8,128)(2,1)} %get-tuple-element.37), kind=kLoop, calls=%fused_computation.2 | loop fusion | flops 6553472 | bytes 2621952 | tf_op jit(solution)/shard_map/reduce_sum | solution.py:165
  130.5 0.7 fusion.27
  131.2 0.6 copy-done.4
  133.4 0.6 copy-done.11
  134.4 1.2 fusion.37
  135.6 9.8 %all-to-all-done.3 = bf16[32,8,1280]{2,1,0:T(8,128)(2,1)S(1)} async-done(((bf16[32,8,1280]{2,1,0:T(8,128)(2,1)}), bf16[32,8,1280]{2,1,0:T(8,128)(2,1)S(1)}, u32[]{:S(2)}, u32[]{:S(2)}) %all-to-all-start.3) | async-done | bytes 655392 | tf_op jit(solution)/shard_map/all_to_all | solution.py:156
  145.3 1.6 fusion.3
  146.9 1.6 copy.69
  148.8 3.8 %multiply_convert_fusion.1 = (bf16[512,10,2,64]{0,3,2,1:T(8,128)(2,1)S(1)}, bf16[512,10,2,64]{0,3,2,1:T(8,128)(2,1)S(1)}) fusion(f32[512,10,2,128]{0,3,2,1:T(8,128)} %copy-done.2, bf16[512,10,2,64]{0,3,2,1:T(8,128)(2,1)S(1)} %bitcast.110, bf16[64,64]{1,0:T(8,128)(2,1)S(1)} %copy-done.28), kind=kOutput, calls=%fused_computation.22 | convolution fusion | flops 90439680 | bytes 9183232 | tf_op jit(solution)/shard_map/stbd,cd->stbc/dot_general | solution.py:180
  152.6 1.7 collective-permute-start.1
  154.3 1.2 fusion.7
  155.4 2.8 %collective-permute-done.1 = f32[28800]{0:T(1024)S(1)} collective-permute-done((f32[28800]{0:T(1024)S(1)}, f32[28800]{0:T(1024)S(1)}, u32[]{:S(2)}, u32[]{:S(2)}) %collective-permute-start.1) | collective-permute-done | bytes 115232 | tf_op jit(solution)/shard_map/ppermute | solution.py:27
  158.3 1.5 collective-permute-start.2
  159.8 1.6 fusion.103
  161.4 1.8 collective-permute-done.2
  163.2 1.2 collective-permute-start.5
  164.4 1.7 collective-permute-start.4
  166.1 1.5 collective-permute-start.3
  167.6 1.0 add_convert_fusion
  168.7 1.6 copy.71
  170.3 0.9 collective-permute-done.5
  171.3 4.1 %collective-permute-done.4 = f32[28800]{0:T(1024)S(1)} collective-permute-done((f32[28800]{0:T(1024)S(1)}, f32[28800]{0:T(1024)S(1)}, u32[]{:S(2)}, u32[]{:S(2)}) %collective-permute-start.4) | collective-permute-done | bytes 115232 | tf_op jit(solution)/shard_map/ppermute | solution.py:32
  176.4 0.7 slice_multiply_fusion
  177.7 0.7 mul.137
  (97 shorter events, 9.6 us)
Async XLA Ops:
  0.6 16.9 %copy-start = (bf16[192,128]{1,0:T(8,128)(2,1)S(1)}, bf16[192,128]{1,0:T(8,128)(2,1)}, u32[]{:S(2)}) copy-start(bf16[192,128]{1,0:T(8,128)(2,1)} %param.11) | copy-start | bytes 147460
  5.3 10.6 %copy-start.1 = (bf16[512,1536]{1,0:T(8,128)(2,1)S(1)}, bf16[512,1536]{1,0:T(8,128)(2,1)}, u32[]{:S(2)}) copy-start(bf16[512,1536]{1,0:T(8,128)(2,1)} %param.10) | copy-start | bytes 4718596
  8.5 29.4 %all-to-all-start = ((bf16[32,8,1664]{2,1,0:T(8,128)(2,1)}), bf16[32,8,1664]{2,1,0:T(8,128)(2,1)}, u32[]{:S(2)}, u32[]{:S(2)}) async-start(bf16[32,8,1664]{2,1,0:T(8,128)(2,1)} %maximum_bitcast_fusion), calls=%async_computation | async-start | bytes 1703936 | tf_op jit(solution)/shard_map/all_to_all | solution.py:119
  16.7 0.7 copy-start.29
  16.7 0.8 copy-start.32
  17.4 1.2 copy-start.13
  17.4 1.5 copy-start.15
  17.4 2.0 %copy-start.17 = (bf16[512,10,2,64]{0,3,2,1:T(8,128)(2,1)}, bf16[512,10,2,64]{0,3,2,1:T(8,128)(2,1)S(1)}, u32[]{:S(2)}) copy-start(bf16[512,10,2,64]{0,3,2,1:T(8,128)(2,1)S(1)} %get-tuple-element.48) | copy-start | bytes 3932164
  19.3 2.3 %copy-start.2 = (f32[512,10,2,128]{0,3,2,1:T(8,128)}, f32[512,10,2,128]{0,3,2,1:T(8,128)S(1)}, u32[]{:S(2)}) copy-start(f32[512,10,2,128]{0,3,2,1:T(8,128)S(1)} %broadcast_add_fusion) | copy-start | bytes 15728644
  19.3 2.3 %copy-start.28 = (bf16[64,64]{1,0:T(8,128)(2,1)S(1)}, bf16[64,64]{1,0:T(8,128)(2,1)}, u32[]{:S(2)}) copy-start(bf16[64,64]{1,0:T(8,128)(2,1)} %param.13) | copy-start | bytes 24580
  21.7 1.1 copy-start.3
  45.1 2.8 %copy-start.5 = (bf16[256,10,2,64]{3,2,1,0:T(2,128)(2,1)S(1)}, bf16[256,10,2,64]{3,2,1,0:T(2,128)(2,1)}, u32[]{:S(2)}) copy-start(bf16[256,10,2,64]{3,2,1,0:T(2,128)(2,1)} %get-tuple-element.44) | copy-start | bytes 1966084
  47.8 5.6 %copy-start.23 = (bf16[256,10,2,64]{0,3,2,1:T(8,128)(2,1)}, bf16[256,10,2,64]{0,3,2,1:T(8,128)(2,1)S(1)}, u32[]{:S(2)}) copy-start(bf16[256,10,2,64]{0,3,2,1:T(8,128)(2,1)S(1)} %copy.90) | copy-start | bytes 1966084
  50.9 0.8 copy-start.26
  53.4 1.5 copy-start.6
  54.9 2.7 %copy-start.30 = (f32[128]{0:T(128)S(1)}, f32[128]{0:T(128)}, u32[]{:S(2)}) copy-start(f32[128]{0:T(128)} %param.14) | copy-start | bytes 1540
  54.9 2.7 %copy-start.7 = (f32[128,1280]{1,0:T(8,128)S(1)}, f32[128,1280]{1,0:T(8,128)}, u32[]{:S(2)}) copy-start(f32[128,1280]{1,0:T(8,128)} %fusion.68) | copy-start | bytes 1966084
  55.3 0.9 copy-start.8
  58.0 22.7 %copy-start.31 = (bf16[512,1280]{1,0:T(8,128)(2,1)S(1)}, bf16[512,1280]{1,0:T(8,128)(2,1)}, u32[]{:S(2)}) copy-start(bf16[512,1280]{1,0:T(8,128)(2,1)} %param.19) | copy-start | bytes 3932164
  59.3 21.5 %all-to-all-start.1 = ((bf16[32,8,1280]{2,1,0:T(8,128)(2,1)}), bf16[32,8,1280]{2,1,0:T(8,128)(2,1)S(1)}, u32[]{:S(2)}, u32[]{:S(2)}) async-start(bf16[32,8,1280]{2,1,0:T(8,128)(2,1)} %fusion.14), calls=%async_computation.1 | async-start | bytes 1310720 | tf_op jit(solution)/shard_map/all_to_all | solution.py:143
  86.0 21.4 %all-to-all-start.2 = ((bf16[32,8,1280]{2,1,0:T(8,128)(2,1)}), bf16[32,8,1280]{2,1,0:T(8,128)(2,1)S(1)}, u32[]{:S(2)}, u32[]{:S(2)}) async-start(bf16[32,8,1280]{2,1,0:T(8,128)(2,1)} %fusion.15), calls=%async_computation.2 | async-start | bytes 1310720 | tf_op jit(solution)/shard_map/all_to_all | solution.py:150
  110.8 3.7 %copy-start.21 = (bf16[256,1280]{0,1:T(8,128)(2,1)}, bf16[256,1280]{0,1:T(8,128)(2,1)S(1)}, u32[]{:S(2)}) copy-start(bf16[256,1280]{0,1:T(8,128)(2,1)S(1)} %copy.62) | copy-start | bytes 1966084
  123.9 21.4 %all-to-all-start.3 = ((bf16[32,8,1280]{2,1,0:T(8,128)(2,1)}), bf16[32,8,1280]{2,1,0:T(8,128)(2,1)S(1)}, u32[]{:S(2)}, u32[]{:S(2)}) async-start(bf16[32,8,1280]{2,1,0:T(8,128)(2,1)} %bitcast.33), calls=%async_computation.3 | async-start | bytes 1310720 | tf_op jit(solution)/shard_map/all_to_all | solution.py:156
  127.4 2.4 %copy-start.19 = (bf16[256,10,2,64]{0,3,2,1:T(8,128)(2,1)S(1)}, bf16[256,10,2,64]{0,3,2,1:T(8,128)(2,1)}, u32[]{:S(2)}) copy-start(bf16[256,10,2,64]{0,3,2,1:T(8,128)(2,1)} %get-tuple-element.39) | copy-start | bytes 1966084
  127.4 2.4 %copy-start.20 = (bf16[256,10,2,64]{0,3,2,1:T(8,128)(2,1)S(1)}, bf16[256,10,2,64]{0,3,2,1:T(8,128)(2,1)}, u32[]{:S(2)}) copy-start(bf16[256,10,2,64]{0,3,2,1:T(8,128)(2,1)} %get-tuple-element.40) | copy-start | bytes 1966084
  127.4 2.7 %copy-start.9 = (bf16[256,10,2,64]{0,3,2,1:T(8,128)(2,1)S(1)}, bf16[256,10,2,64]{0,3,2,1:T(8,128)(2,1)}, u32[]{:S(2)}) copy-start(bf16[256,10,2,64]{0,3,2,1:T(8,128)(2,1)} %copy-done.8) | copy-start | bytes 1966084
  127.4 2.7 %copy-start.22 = (bf16[256,1280]{0,1:T(8,128)(2,1)S(1)}, bf16[256,1280]{0,1:T(8,128)(2,1)}, u32[]{:S(2)}) copy-start(bf16[256,1280]{0,1:T(8,128)(2,1)} %copy-done.21) | copy-start | bytes 1966084
  127.4 3.0 %copy-start.24 = (bf16[256,10,2,64]{0,3,2,1:T(8,128)(2,1)S(1)}, bf16[256,10,2,64]{0,3,2,1:T(8,128)(2,1)}, u32[]{:S(2)}) copy-start(bf16[256,10,2,64]{0,3,2,1:T(8,128)(2,1)} %copy-done.23) | copy-start | bytes 1966084
  127.5 3.0 %copy-start.25 = (bf16[256,10,2,64]{0,3,2,1:T(8,128)(2,1)S(1)}, bf16[256,10,2,64]{0,3,2,1:T(8,128)(2,1)}, u32[]{:S(2)}) copy-start(bf16[256,10,2,64]{0,3,2,1:T(8,128)(2,1)} %copy.89) | copy-start | bytes 1966084
  127.5 3.0 %copy-start.27 = (bf16[256,10,2,64]{0,3,2,1:T(8,128)(2,1)S(1)}, bf16[256,10,2,64]{0,3,2,1:T(8,128)(2,1)}, u32[]{:S(2)}) copy-start(bf16[256,10,2,64]{0,3,2,1:T(8,128)(2,1)} %copy-done.26) | copy-start | bytes 1966084
  130.5 1.3 copy-start.4
  130.5 1.7 copy-start.10
  130.5 2.2 %copy-start.14 = (bf16[512,10,2,64]{0,3,2,1:T(8,128)(2,1)S(1)}, bf16[512,10,2,64]{0,3,2,1:T(8,128)(2,1)}, u32[]{:S(2)}) copy-start(bf16[512,10,2,64]{0,3,2,1:T(8,128)(2,1)} %copy-done.13) | copy-start | bytes 3932164
  130.5 2.5 %copy-start.16 = (bf16[512,10,2,64]{0,3,2,1:T(8,128)(2,1)S(1)}, bf16[512,10,2,64]{0,3,2,1:T(8,128)(2,1)}, u32[]{:S(2)}) copy-start(bf16[512,10,2,64]{0,3,2,1:T(8,128)(2,1)} %copy-done.15) | copy-start | bytes 3932164
  130.5 2.9 %copy-start.18 = (bf16[512,10,2,64]{0,3,2,1:T(8,128)(2,1)S(1)}, bf16[512,10,2,64]{0,3,2,1:T(8,128)(2,1)}, u32[]{:S(2)}) copy-start(bf16[512,10,2,64]{0,3,2,1:T(8,128)(2,1)} %copy-done.17) | copy-start | bytes 3932164
  132.2 1.8 copy-start.11
  132.2 2.2 %copy-start.12 = (bf16[512,10,2,64]{0,3,2,1:T(8,128)(2,1)S(1)}, bf16[512,10,2,64]{0,3,2,1:T(8,128)(2,1)}, u32[]{:S(2)}) copy-start(bf16[512,10,2,64]{0,3,2,1:T(8,128)(2,1)} %get-tuple-element.38) | copy-start | bytes 3932164
  148.6 4.0 %collective-permute-start = (f32[28800]{0:T(1024)S(1)}, f32[28800]{0:T(1024)S(1)}, u32[]{:S(2)}, u32[]{:S(2)}) collective-permute-start(f32[28800]{0:T(1024)S(1)} %pad_maximum_fusion.5), channel_id=1, source_target_pairs={{0,1},{1,0},{2,3},{3,2},{4,5},{5,4},{6,7},{7,6},{8,9},{9,8},{10,11... | collective-permute-start | bytes 345608 | tf_op jit(solution)/shard_map/ppermute | solution.py:27
  152.6 5.6 %collective-permute-start.1 = (f32[28800]{0:T(1024)S(1)}, f32[28800]{0:T(1024)S(1)}, u32[]{:S(2)}, u32[]{:S(2)}) collective-permute-start(f32[28800]{0:T(1024)S(1)} %fusion.102), channel_id=1, source_target_pairs={{0,2},{1,3},{2,0},{3,1},{4,6},{5,7},{6,4},{7,5},{8,10},{9,11},{10,... | collective-permute-start | bytes 345608 | tf_op jit(solution)/shard_map/ppermute | solution.py:27
  158.3 4.9 %collective-permute-start.2 = (f32[28800]{0:T(1024)S(1)}, f32[28800]{0:T(1024)S(1)}, u32[]{:S(2)}, u32[]{:S(2)}) collective-permute-start(f32[28800]{0:T(1024)S(1)} %add.165), channel_id=1, source_target_pairs={{0,4},{1,5},{2,6},{3,7},{4,0},{5,1},{6,2},{7,3},{8,12},{9,13},{10,... | collective-permute-start | bytes 345608 | tf_op jit(solution)/shard_map/ppermute | solution.py:27
  163.2 8.0 %collective-permute-start.5 = (f32[28800]{0:T(1024)S(1)}, f32[28800]{0:T(1024)S(1)}, u32[]{:S(2)}, u32[]{:S(2)}) collective-permute-start(f32[28800]{0:T(1024)S(1)} %add.166), channel_id=1, source_target_pairs={{0,24},{1,25},{2,26},{3,27},{4,28},{5,29},{6,30},{7,31},{8,16},{9,... | collective-permute-start | bytes 345608 | tf_op jit(solution)/shard_map/ppermute | solution.py:32
  164.4 11.0 %collective-permute-start.4 = (f32[28800]{0:T(1024)S(1)}, f32[28800]{0:T(1024)S(1)}, u32[]{:S(2)}, u32[]{:S(2)}) collective-permute-start(f32[28800]{0:T(1024)S(1)} %add.166), channel_id=1, source_target_pairs={{0,16},{1,17},{2,18},{3,19},{4,20},{5,21},{6,22},{7,23},{8,24},{9,... | collective-permute-start | bytes 345608 | tf_op jit(solution)/shard_map/ppermute | solution.py:32
  166.1 9.4 %collective-permute-start.3 = (f32[28800]{0:T(1024)S(1)}, f32[28800]{0:T(1024)S(1)}, u32[]{:S(2)}, u32[]{:S(2)}) collective-permute-start(f32[28800]{0:T(1024)S(1)} %add.166), channel_id=1, source_target_pairs={{0,8},{1,9},{2,10},{3,11},{4,12},{5,13},{6,14},{7,15},{8,0},{9,1},... | collective-permute-start | bytes 345608 | tf_op jit(solution)/shard_map/ppermute | solution.py:32

commit v8 on v6

--- a/solution.py
+++ b/solution.py
@@ -110,9 +110,10 @@
     scale = (edge_weight / count)[:, None]
 
     def edge_side(local_rows, arrived):
-        total = jnp.dot(incidence, local_rows, preferred_element_type=jnp.float32) + jnp.dot(
-            owned, arrived, preferred_element_type=jnp.float32
+        local, arrived = lax.optimization_barrier(
+            (jnp.dot(incidence, local_rows, preferred_element_type=jnp.float32), arrived)
         )
+        total = local + jnp.dot(owned, arrived, preferred_element_type=jnp.float32)
         values = (scale * total).astype(jnp.bfloat16)
         returned = jnp.einsum(
             "en,ef->nf", owned, values, preferred_element_type=jnp.float32
@@ -120,9 +121,10 @@
         return (values, returned)
 
     def member_side(values, back):
-        return jnp.einsum(
-            "es,ef->sf", incidence, values, preferred_element_type=jnp.float32
-        ) + jnp.dot(members, back, preferred_element_type=jnp.float32)
+        local, back = lax.optimization_barrier(
+            (jnp.einsum("es,ef->sf", incidence, values, preferred_element_type=jnp.float32), back)
+        )
+        return local + jnp.dot(members, back, preferred_element_type=jnp.float32)
 
     edge_val, ret_rows = edge_side(z, recv)
     back = lax.all_to_all(ret_rows, ("region", "sub"), split_axis=0, concat_axis=0, tiled=True)

time: 150 us -> 150 us (level)
  no operation moved by 1% of the time
where the time goes in v8:
time: 150 us; the launch traced here: 149 us
  waiting for transfers between devices  54.1 us (36%)
  matrix products  33.9 us (23%)
  starting transfers between devices  25.7 us (17%)
  local copies, waits for them, and re-layouts  22.8 us (15%)
  other arithmetic  11.6 us (8%)
    all_to_all x1, waiting for transfers between devices, body(): lax.all_to_all(send_grads, ('region', 'sub'), split_axis=0, concat_axis=0...  17.6 us
    all_to_all x1, waiting for transfers between devices, body(): lax.all_to_all(ret_rows, ('region', 'sub'), split_axis=0, concat_axis=0,...  15.6 us
    all_to_all x1, waiting for transfers between devices, body(): lax.all_to_all(send, ('region', 'sub'), split_axis=0, concat_axis=0, tile...  14.7 us
    unnamed x58, local copies, waits for them, and re-layouts  9.71 us
    dot_general x2, matrix products, weight_grads(): jnp.einsum('stbd,cd->stbc', dzr, theta, preferred_element_type=jnp.float32)  7.93 us
    ppermute x5, starting transfers between devices, device_sum(): flat = flat + lax.ppermute(flat, ('region', 'sub'), perm)  7.48 us
    all_to_all x1, starting transfers between devices, body(): lax.all_to_all(send, ('region', 'sub'), split_axis=0, concat_axis=0, tile...  7.41 us
    ppermute x5, waiting for transfers between devices, device_sum(): flat = flat + lax.ppermute(flat, ('region', 'sub'), perm)  6.19 us
  transfers between devices with their start and end apart: 9, of which 7 were waited for; matrix products, arithmetic and copies ran while one was open for 23% of the time, Pallas kernels for 0%

profile of v8, /device:TPU:0, one launch (start us, length us, event | category | flops | bytes accessed | tf_op | source)
XLA Modules:
  0.0 149.2 jit_solution(4404673487697238301)
XLA Ops:
  0.6 0.7 fusion.81
  1.6 0.8 select_reduce_fusion
  2.4 0.7 fusion.93
  3.1 1.1 scatter_custom_fusion
  4.2 1.1 scatter_custom_fusion.1
  5.3 2.1 %convolution_convert_fusion.3 = bf16[256,1536]{1,0:T(8,128)(2,1)S(1)} fusion(bf16[512,1536]{1,0:T(8,128)(2,1)} %param.10, s32[256]{0:T(256)S(1)} %scatter_custom_fusion), kind=kOutput, calls=%fused_computation.34 | convolution fusion | flops 403439616 | bytes 2360320 | tf_op jit(solution)/shard_map/sn,sf->nf/dot_general | solution.py:94
  7.6 1.0 maximum_bitcast_fusion
  8.5 7.4 %all-to-all-start = ((bf16[32,8,1664]{2,1,0:T(8,128)(2,1)}), bf16[32,8,1664]{2,1,0:T(8,128)(2,1)}, u32[]{:S(2)}, u32[]{:S(2)}) async-start(bf16[32,8,1664]{2,1,0:T(8,128)(2,1)} %maximum_bitcast_fusion), calls=%async_computation | async-start | bytes 1703936 | tf_op jit(solution)/shard_map/all_to_all | solution.py:104
  15.9 0.7 copy.66
  16.7 0.5 fusion.101
  17.5 1.0 broadcast_add_fusion
  18.9 0.4 copy-done.13
  19.3 0.7 multiply_convert_fusion.5
  20.1 1.6 %copy-done.2 = f32[512,10,2,128]{0,3,2,1:T(8,128)} copy-done((f32[512,10,2,128]{0,3,2,1:T(8,128)}, f32[512,10,2,128]{0,3,2,1:T(8,128)S(1)}, u32[]{:S(2)}) %copy-start.2) | copy-done | bytes 5242904
  21.6 0.6 convolution_convert_fusion.4
  22.2 0.5 copy-done.3
  22.7 0.6 fusion.66
  23.3 14.7 %all-to-all-done = bf16[32,8,1664]{2,1,0:T(8,128)(2,1)} async-done(((bf16[32,8,1664]{2,1,0:T(8,128)(2,1)}), bf16[32,8,1664]{2,1,0:T(8,128)(2,1)}, u32[]{:S(2)}, u32[]{:S(2)}) %all-to-all-start) | async-done | bytes 852000 | tf_op jit(solution)/shard_map/all_to_all | solution.py:104
  38.0 1.0 convert_reduce_fusion.4
  38.9 1.2 slice.102
  40.7 0.5 convolution_add_fusion.4
  43.7 1.2 fusion.14
  44.8 3.6 %all-to-all-start.1 = ((bf16[32,8,1280]{2,1,0:T(8,128)(2,1)}), bf16[32,8,1280]{2,1,0:T(8,128)(2,1)S(1)}, u32[]{:S(2)}, u32[]{:S(2)}) async-start(bf16[32,8,1280]{2,1,0:T(8,128)(2,1)} %fusion.14), calls=%async_computation.1 | async-start | bytes 1310720 | tf_op jit(solution)/shard_map/all_to_all | solution.py:130
  48.6 2.1 %fusion.64 = f32[512,1280]{1,0:T(8,128)} fusion(bf16[128,1280]{1,0:T(8,128)(2,1)S(1)} %fusion.16, s32[512]{0:T(512)S(1)} %bitcast.122, s32[512]{0:T(512)S(1)} %bitcast.117), kind=kOutput, calls=%fused_computation.84 | convolution fusion | flops 168165376 | bytes 2953216 | tf_op jit(solution)/shard_map/es,ef->sf/dot_general | solution.py:125
  50.8 15.6 %all-to-all-done.1 = bf16[32,8,1280]{2,1,0:T(8,128)(2,1)S(1)} async-done(((bf16[32,8,1280]{2,1,0:T(8,128)(2,1)}), bf16[32,8,1280]{2,1,0:T(8,128)(2,1)S(1)}, u32[]{:S(2)}, u32[]{:S(2)}) %all-to-all-start.1) | async-done | bytes 655392 | tf_op jit(solution)/shard_map/all_to_all | solution.py:130
  66.4 4.0 %divide_convert_fusion = (bf16[512,1280]{1,0:T(8,128)(2,1)S(1)}, bf16[512,1280]{1,0:T(8,128)(2,1)}) fusion(bf16[512,1280]{1,0:T(8,128)(2,1)} %param.19, f32[512]{0:T(512)S(1)} %broadcast_add_fusion.1, f32[512,1280]{1,0:T(8,128)} %fusion.64, bf16[256,1280]{1,0:T(8,128)(2,1)S(1)} %bitcast.112, s32[256]{0:T(256)S(1)} %scatter_custom_fusion), kind=kOutput, calls=%fused_computation.26 | convolution fusion | flops 345767936 | bytes 7212032 | tf_op jit(solution)/shard_map/dot_general | solution.py:127
  70.4 1.4 fusion.15
  71.8 3.5 %all-to-all-start.2 = ((bf16[32,8,1280]{2,1,0:T(8,128)(2,1)}), bf16[32,8,1280]{2,1,0:T(8,128)(2,1)S(1)}, u32[]{:S(2)}, u32[]{:S(2)}) async-start(bf16[32,8,1280]{2,1,0:T(8,128)(2,1)} %fusion.15), calls=%async_computation.2 | async-start | bytes 1310720 | tf_op jit(solution)/shard_map/all_to_all | solution.py:137
  75.7 17.6 %all-to-all-done.2 = bf16[32,8,1280]{2,1,0:T(8,128)(2,1)S(1)} async-done(((bf16[32,8,1280]{2,1,0:T(8,128)(2,1)}), bf16[32,8,1280]{2,1,0:T(8,128)(2,1)S(1)}, u32[]{:S(2)}, u32[]{:S(2)}) %all-to-all-start.2) | async-done | bytes 655392 | tf_op jit(solution)/shard_map/all_to_all | solution.py:137
  93.5 1.3 convolution_convert_fusion
  94.8 0.5 fusion.60
  95.3 2.2 %copy.73 = bf16[256,1280]{0,1:T(8,128)(2,1)} copy(bf16[256,1280]{1,0:T(8,128)(2,1)} %convolution_convert_fusion) | data formatting | bytes 1310720 | tf_op jit(solution)/shard_map/optimization_barrier | solution.py:142
  97.6 3.7 %all-to-all-start.3 = ((bf16[32,8,1280]{2,1,0:T(8,128)(2,1)}), bf16[32,8,1280]{2,1,0:T(8,128)(2,1)S(1)}, u32[]{:S(2)}, u32[]{:S(2)}) async-start(bf16[32,8,1280]{2,1,0:T(8,128)(2,1)} %bitcast.33), calls=%async_computation.3 | async-start | bytes 1310720 | tf_op jit(solution)/shard_map/all_to_all | solution.py:143
  101.3 3.6 %multiply_convert_fusion.7 = (bf16[256,10,2,64]{0,3,2,1:T(8,128)(2,1)}, bf16[256,10,2,64]{0,3,2,1:T(8,128)(2,1)}) fusion(f32[256,10,2,128]{0,3,2,1:T(8,128)} %copy-done.5, bf16[256,10,2,64]{0,3,2,1:T(8,128)(2,1)} %bitcast.110, bf16[64,64]{1,0:T(8,128)(2,1)S(1)} %copy-done.24), kind=kOutput, calls=%fused_computation.59 | convolution fusion | flops 45219840 | bytes 4595712 | tf_op jit(solution)/shard_map/stbd,cd->stbc/dot_general | solution.py:149
  104.9 1.2 convert_element_type.124
  106.1 2.4 %copy.70 = bf16[512,1280]{0,1:T(8,128)(2,1)} copy(bf16[512,1280]{1,0:T(8,128)(2,1)} %convert_element_type.124) | data formatting | bytes 2621440 | tf_op jit(solution)/shard_map/convert_element_type | solution.py:155
  108.5 4.3 %multiply_convert_fusion.3 = (bf16[512,10,2,64]{0,3,2,1:T(8,128)(2,1)S(1)}, bf16[512,10,2,64]{0,3,2,1:T(8,128)(2,1)S(1)}) fusion(f32[512,10,2,128]{0,3,2,1:T(8,128)} %copy-done.2, bf16[512,10,2,64]{0,3,2,1:T(8,128)(2,1)} %bitcast.107, bf16[64,64]{1,0:T(8,128)(2,1)S(1)} %copy-done.24), kind=kOutput, calls=%fused_computation.25 | convolution fusion | flops 90439680 | bytes 9183232 | tf_op jit(solution)/shard_map/stbd,cd->stbc/dot_general | solution.py:149
  113.2 0.4 convert_reduce_fusion
  114.7 0.7 fusion.27
  115.4 0.6 copy-done.4
  116.1 0.4 copy-done.8
  116.4 0.5 fusion.47
  117.0 0.9 copy-done.10
  117.9 0.4 copy-done.12
  118.3 1.2 fusion.37
  119.5 0.7 pad_maximum_fusion.4
  120.3 1.6 %fusion.3 = bf16[512,1280]{1,0:T(8,128)(2,1)} fusion(f32[512,1280]{1,0:T(8,128)S(1)} %fusion.60, bf16[256,1280]{1,0:T(8,128)(2,1)S(1)} %bitcast.104, s32[256]{0:T(256)S(1)} %scatter_custom_fusion), kind=kOutput, calls=%fused_computation.10 | convolution fusion | flops 337248256 | bytes 4588544 | tf_op jit(solution)/shard_map/dot_general | solution.py:163
  121.9 1.6 %copy.80 = bf16[512,1280]{0,1:T(8,128)(2,1)S(1)} copy(bf16[512,1280]{1,0:T(8,128)(2,1)} %fusion.3) | data formatting | bytes 2621440 | tf_op jit(solution)/shard_map/convert_element_type | solution.py:164
  123.5 0.9 fusion.99
  124.4 1.7 %collective-permute-start.1 = (f32[28800]{0:T(1024)S(1)}, f32[28800]{0:T(1024)S(1)}, u32[]{:S(2)}, u32[]{:S(2)}) collective-permute-start(f32[28800]{0:T(1024)S(1)} %fusion.99), channel_id=1, source_target_pairs={{0,2},{1,3},{2,0},{3,1},{4,6},{5,7},{6,4},{7,5},{8,10},{9,11},{10,... | collective-permute-start | bytes 345608 | tf_op jit(solution)/shard_map/ppermute | solution.py:24
  126.2 3.8 %multiply_convert_fusion.1 = (bf16[512,10,2,64]{0,3,2,1:T(8,128)(2,1)S(1)}, bf16[512,10,2,64]{0,3,2,1:T(8,128)(2,1)S(1)}) fusion(f32[512,10,2,128]{0,3,2,1:T(8,128)} %copy-done.2, bf16[512,10,2,64]{0,3,2,1:T(8,128)(2,1)S(1)} %bitcast.109, bf16[64,64]{1,0:T(8,128)(2,1)S(1)} %copy-done.24), kind=kOutput, calls=%fused_computation.22 | convolution fusion | flops 90439680 | bytes 9183232 | tf_op jit(solution)/shard_map/stbd,cd->stbc/dot_general | solution.py:167
  130.1 1.7 %collective-permute-start.2 = (f32[28800]{0:T(1024)S(1)}, f32[28800]{0:T(1024)S(1)}, u32[]{:S(2)}, u32[]{:S(2)}) collective-permute-start(f32[28800]{0:T(1024)S(1)} %add.134), channel_id=1, source_target_pairs={{0,4},{1,5},{2,6},{3,7},{4,0},{5,1},{6,2},{7,3},{8,12},{9,13},{10,... | collective-permute-start | bytes 345608 | tf_op jit(solution)/shard_map/ppermute | solution.py:24
  131.8 1.2 fusion.7
  132.9 2.3 %collective-permute-done.2 = f32[28800]{0:T(1024)S(1)} collective-permute-done((f32[28800]{0:T(1024)S(1)}, f32[28800]{0:T(1024)S(1)}, u32[]{:S(2)}, u32[]{:S(2)}) %collective-permute-start.2) | collective-permute-done | bytes 115232 | tf_op jit(solution)/shard_map/ppermute | solution.py:24
  135.3 1.5 %collective-permute-start.3 = (f32[28800]{0:T(1024)S(1)}, f32[28800]{0:T(1024)S(1)}, u32[]{:S(2)}, u32[]{:S(2)}) collective-permute-start(f32[28800]{0:T(1024)S(1)} %add.135), channel_id=1, source_target_pairs={{0,8},{1,9},{2,10},{3,11},{4,12},{5,13},{6,14},{7,15},{8,0},{9,1},... | collective-permute-start | bytes 345608 | tf_op jit(solution)/shard_map/ppermute | solution.py:24
  136.8 1.6 %fusion.100 = (f32[512,10,2,64]{0,3,2,1:T(8,128)S(1)}, f32[512,10,2,64]{0,3,2,1:T(8,128)S(1)}, f32[512,10,2,64]{0,3,2,1:T(8,128)S(1)}) fusion(f32[512,10,2,192]{0,3,2,1:T(8,128)S(1)} %fusion.7), kind=kLoop, calls=%fused_computation.132 | loop fusion | bytes 15728640 | tf_op jit(solution)/shard_map/slice | solution.py:176
  138.5 1.7 %collective-permute-done.3 = f32[28800]{0:T(1024)S(1)} collective-permute-done((f32[28800]{0:T(1024)S(1)}, f32[28800]{0:T(1024)S(1)}, u32[]{:S(2)}, u32[]{:S(2)}) %collective-permute-start.3) | collective-permute-done | bytes 115232 | tf_op jit(solution)/shard_map/ppermute | solution.py:24
  140.2 2.5 %collective-permute-start.4 = (f32[28800]{0:T(1024)S(1)}, f32[28800]{0:T(1024)S(1)}, u32[]{:S(2)}, u32[]{:S(2)}) collective-permute-start(f32[28800]{0:T(1024)S(1)} %add.136), channel_id=1, source_target_pairs={{0,16},{1,17},{2,18},{3,19},{4,20},{5,21},{6,22},{7,23},{8,24},{9,... | collective-permute-start | bytes 345608 | tf_op jit(solution)/shard_map/ppermute | solution.py:24
  142.7 1.0 add_convert_fusion
  143.7 1.6 %copy.82 = bf16[512,1536]{1,0:T(8,128)(2,1)} copy(bf16[512,1536]{0,1:T(8,128)(2,1)S(1)} %bitcast.102) | data formatting | bytes 3145728
  145.3 2.0 %collective-permute-done.4 = f32[28800]{0:T(1024)S(1)} collective-permute-done((f32[28800]{0:T(1024)S(1)}, f32[28800]{0:T(1024)S(1)}, u32[]{:S(2)}, u32[]{:S(2)}) %collective-permute-start.4) | collective-permute-done | bytes 115232 | tf_op jit(solution)/shard_map/ppermute | solution.py:24
  147.3 0.5 slice_multiply_fusion.2
  147.8 0.6 fusion.76
  148.5 0.7 mul.133
  (78 shorter events, 6.4 us)
Async XLA Ops:
  0.6 16.9 %copy-start = (bf16[192,128]{1,0:T(8,128)(2,1)S(1)}, bf16[192,128]{1,0:T(8,128)(2,1)}, u32[]{:S(2)}) copy-start(bf16[192,128]{1,0:T(8,128)(2,1)} %param.11) | copy-start | bytes 147460
  5.3 10.6 %copy-start.1 = (bf16[512,1536]{1,0:T(8,128)(2,1)S(1)}, bf16[512,1536]{1,0:T(8,128)(2,1)}, u32[]{:S(2)}) copy-start(bf16[512,1536]{1,0:T(8,128)(2,1)} %param.10) | copy-start | bytes 4718596
  8.5 29.4 %all-to-all-start = ((bf16[32,8,1664]{2,1,0:T(8,128)(2,1)}), bf16[32,8,1664]{2,1,0:T(8,128)(2,1)}, u32[]{:S(2)}, u32[]{:S(2)}) async-start(bf16[32,8,1664]{2,1,0:T(8,128)(2,1)} %maximum_bitcast_fusion), calls=%async_computation | async-start | bytes 1703936 | tf_op jit(solution)/shard_map/all_to_all | solution.py:104
  16.7 0.7 copy-start.25
  16.7 0.8 copy-start.27
  17.4 1.2 copy-start.9
  17.4 1.6 %copy-start.11 = (bf16[512,10,2,64]{0,3,2,1:T(8,128)(2,1)}, bf16[512,10,2,64]{0,3,2,1:T(8,128)(2,1)S(1)}, u32[]{:S(2)}) copy-start(bf16[512,10,2,64]{0,3,2,1:T(8,128)(2,1)S(1)} %get-tuple-element.61) | copy-start | bytes 3932164
  17.4 2.0 %copy-start.13 = (bf16[512,10,2,64]{0,3,2,1:T(8,128)(2,1)}, bf16[512,10,2,64]{0,3,2,1:T(8,128)(2,1)S(1)}, u32[]{:S(2)}) copy-start(bf16[512,10,2,64]{0,3,2,1:T(8,128)(2,1)S(1)} %get-tuple-element.62) | copy-start | bytes 3932164
  19.3 2.3 %copy-start.2 = (f32[512,10,2,128]{0,3,2,1:T(8,128)}, f32[512,10,2,128]{0,3,2,1:T(8,128)S(1)}, u32[]{:S(2)}) copy-start(f32[512,10,2,128]{0,3,2,1:T(8,128)S(1)} %broadcast_add_fusion) | copy-start | bytes 15728644
  19.3 2.3 %copy-start.24 = (bf16[64,64]{1,0:T(8,128)(2,1)S(1)}, bf16[64,64]{1,0:T(8,128)(2,1)}, u32[]{:S(2)}) copy-start(bf16[64,64]{1,0:T(8,128)(2,1)} %param.13) | copy-start | bytes 24580
  21.6 1.1 copy-start.3
  40.7 0.8 copy-start.18
  40.7 1.1 copy-start.20
  40.7 1.2 copy-start.22
  41.9 1.5 copy-start.5
  41.9 0.8 copy-start.26
  42.3 1.4 copy-start.6
  44.8 21.5 %all-to-all-start.1 = ((bf16[32,8,1280]{2,1,0:T(8,128)(2,1)}), bf16[32,8,1280]{2,1,0:T(8,128)(2,1)S(1)}, u32[]{:S(2)}, u32[]{:S(2)}) async-start(bf16[32,8,1280]{2,1,0:T(8,128)(2,1)} %fusion.14), calls=%async_computation.1 | async-start | bytes 1310720 | tf_op jit(solution)/shard_map/all_to_all | solution.py:130
  71.8 21.4 %all-to-all-start.2 = ((bf16[32,8,1280]{2,1,0:T(8,128)(2,1)}), bf16[32,8,1280]{2,1,0:T(8,128)(2,1)S(1)}, u32[]{:S(2)}, u32[]{:S(2)}) async-start(bf16[32,8,1280]{2,1,0:T(8,128)(2,1)} %fusion.15), calls=%async_computation.2 | async-start | bytes 1310720 | tf_op jit(solution)/shard_map/all_to_all | solution.py:137
  97.6 21.9 %all-to-all-start.3 = ((bf16[32,8,1280]{2,1,0:T(8,128)(2,1)}), bf16[32,8,1280]{2,1,0:T(8,128)(2,1)S(1)}, u32[]{:S(2)}, u32[]{:S(2)}) async-start(bf16[32,8,1280]{2,1,0:T(8,128)(2,1)} %bitcast.33), calls=%async_computation.3 | async-start | bytes 1310720 | tf_op jit(solution)/shard_map/all_to_all | solution.py:143
  108.5 4.3 %copy-start.16 = (bf16[256,10,2,64]{0,3,2,1:T(8,128)(2,1)S(1)}, bf16[256,10,2,64]{0,3,2,1:T(8,128)(2,1)}, u32[]{:S(2)}) copy-start(bf16[256,10,2,64]{0,3,2,1:T(8,128)(2,1)} %get-tuple-element.56) | copy-start | bytes 1966084
  108.5 4.3 %copy-start.17 = (bf16[256,10,2,64]{0,3,2,1:T(8,128)(2,1)S(1)}, bf16[256,10,2,64]{0,3,2,1:T(8,128)(2,1)}, u32[]{:S(2)}) copy-start(bf16[256,10,2,64]{0,3,2,1:T(8,128)(2,1)} %get-tuple-element.57) | copy-start | bytes 1966084
  112.8 1.1 copy-start.7
  112.8 1.3 copy-start.15
  112.9 1.6 %copy-start.19 = (bf16[256,10,2,64]{0,3,2,1:T(8,128)(2,1)S(1)}, bf16[256,10,2,64]{0,3,2,1:T(8,128)(2,1)}, u32[]{:S(2)}) copy-start(bf16[256,10,2,64]{0,3,2,1:T(8,128)(2,1)} %copy-done.18) | copy-start | bytes 1966084
  112.9 1.6 %copy-start.21 = (bf16[256,10,2,64]{0,3,2,1:T(8,128)(2,1)S(1)}, bf16[256,10,2,64]{0,3,2,1:T(8,128)(2,1)}, u32[]{:S(2)}) copy-start(bf16[256,10,2,64]{0,3,2,1:T(8,128)(2,1)} %copy-done.20) | copy-start | bytes 1966084
  112.9 1.8 %copy-start.23 = (bf16[256,10,2,64]{0,3,2,1:T(8,128)(2,1)S(1)}, bf16[256,10,2,64]{0,3,2,1:T(8,128)(2,1)}, u32[]{:S(2)}) copy-start(bf16[256,10,2,64]{0,3,2,1:T(8,128)(2,1)} %copy-done.22) | copy-start | bytes 1966084
  114.7 1.3 copy-start.4
  114.7 1.7 %copy-start.8 = (bf16[512,1280]{0,1:T(8,128)(2,1)S(1)}, bf16[512,1280]{0,1:T(8,128)(2,1)}, u32[]{:S(2)}) copy-start(bf16[512,1280]{0,1:T(8,128)(2,1)} %copy.70) | copy-start | bytes 3932164
  114.7 2.2 %copy-start.14 = (bf16[512,10,2,64]{0,3,2,1:T(8,128)(2,1)S(1)}, bf16[512,10,2,64]{0,3,2,1:T(8,128)(2,1)}, u32[]{:S(2)}) copy-start(bf16[512,10,2,64]{0,3,2,1:T(8,128)(2,1)} %copy-done.13) | copy-start | bytes 3932164
  116.4 1.4 copy-start.10
  116.4 1.8 %copy-start.12 = (bf16[512,10,2,64]{0,3,2,1:T(8,128)(2,1)S(1)}, bf16[512,10,2,64]{0,3,2,1:T(8,128)(2,1)}, u32[]{:S(2)}) copy-start(bf16[512,10,2,64]{0,3,2,1:T(8,128)(2,1)} %copy-done.11) | copy-start | bytes 3932164
  120.2 3.3 %collective-permute-start = (f32[28800]{0:T(1024)}, f32[28800]{0:T(1024)}, u32[]{:S(2)}, u32[]{:S(2)}) collective-permute-start(f32[28800]{0:T(1024)} %pad_maximum_fusion.4), channel_id=1, source_target_pairs={{0,1},{1,0},{2,3},{3,2},{4,5},{5,4},{6,7},{7,6},{8,9},{9,8},{10,11... | collective-permute-start | bytes 345608 | tf_op jit(solution)/shard_map/ppermute | solution.py:24
  124.4 5.6 %collective-permute-start.1 = (f32[28800]{0:T(1024)S(1)}, f32[28800]{0:T(1024)S(1)}, u32[]{:S(2)}, u32[]{:S(2)}) collective-permute-start(f32[28800]{0:T(1024)S(1)} %fusion.99), channel_id=1, source_target_pairs={{0,2},{1,3},{2,0},{3,1},{4,6},{5,7},{6,4},{7,5},{8,10},{9,11},{10,... | collective-permute-start | bytes 345608 | tf_op jit(solution)/shard_map/ppermute | solution.py:24
  130.1 5.2 %collective-permute-start.2 = (f32[28800]{0:T(1024)S(1)}, f32[28800]{0:T(1024)S(1)}, u32[]{:S(2)}, u32[]{:S(2)}) collective-permute-start(f32[28800]{0:T(1024)S(1)} %add.134), channel_id=1, source_target_pairs={{0,4},{1,5},{2,6},{3,7},{4,0},{5,1},{6,2},{7,3},{8,12},{9,13},{10,... | collective-permute-start | bytes 345608 | tf_op jit(solution)/shard_map/ppermute | solution.py:24
  135.3 4.9 %collective-permute-start.3 = (f32[28800]{0:T(1024)S(1)}, f32[28800]{0:T(1024)S(1)}, u32[]{:S(2)}, u32[]{:S(2)}) collective-permute-start(f32[28800]{0:T(1024)S(1)} %add.135), channel_id=1, source_target_pairs={{0,8},{1,9},{2,10},{3,11},{4,12},{5,13},{6,14},{7,15},{8,0},{9,1},... | collective-permute-start | bytes 345608 | tf_op jit(solution)/shard_map/ppermute | solution.py:24
  140.2 7.1 %collective-permute-start.4 = (f32[28800]{0:T(1024)S(1)}, f32[28800]{0:T(1024)S(1)}, u32[]{:S(2)}, u32[]{:S(2)}) collective-permute-start(f32[28800]{0:T(1024)S(1)} %add.136), channel_id=1, source_target_pairs={{0,16},{1,17},{2,18},{3,19},{4,20},{5,21},{6,22},{7,23},{8,24},{9,... | collective-permute-start | bytes 345608 | tf_op jit(solution)/shard_map/ppermute | solution.py:24

commit v9 on v6

--- a/solution.py
+++ b/solution.py
@@ -136,8 +136,14 @@
         send_grads, ("region", "sub"), split_axis=0, concat_axis=0, tiled=True
     )
     dedge, ret_grads = edge_side(grad_rows, recv_grads)
-    inner_sum = jnp.einsum("es,ef->sf", incidence, dedge, preferred_element_type=jnp.float32)
-    inner_sum, ret_grads = lax.optimization_barrier((inner_sum, ret_grads))
+    dedge4 = dedge.reshape(EDGE_DEV, TP, B, C)
+    inner_sum = jnp.einsum(
+        "es,etbd->stbd", incidence, dedge4, preferred_element_type=jnp.float32
+    )
+    dz_slots = jnp.einsum(
+        "en,etbd->ntbd", owned, dedge4, preferred_element_type=jnp.float32
+    ).astype(jnp.bfloat16)
+    inner_sum, dz_slots, ret_grads = lax.optimization_barrier((inner_sum, dz_slots, ret_grads))
     back_grads = lax.all_to_all(
         ret_grads, ("region", "sub"), split_axis=0, concat_axis=0, tiled=True
     )
@@ -150,18 +156,19 @@
         g_bias = jnp.sum(du.astype(jnp.float32), axis=(0, 1, 2))
         return du, g_conv, g_bias, g_theta
 
-    dz_inner = inner_sum.astype(jnp.bfloat16).reshape(seg, TP, B, C)
+    dz_inner = inner_sum.astype(jnp.bfloat16)
     _, ga_conv, ga_bias, ga_theta = weight_grads(stack, gate, first, hidden, dz_inner)
-    dz_slots = ret_grads.reshape(slot_total, TP, B, C)
     _, gb_conv, gb_bias, gb_theta = weight_grads(r_stack, r_gate, r_first, r_hidden, dz_slots)
     partial = (ga_conv + gb_conv, ga_bias + gb_bias, ga_theta + gb_theta)
     partial, back_grads = lax.optimization_barrier((partial, back_grads))
     sum_conv, sum_bias, sum_theta = device_sum(partial, device_list)
-    dz = (
-        (inner_sum + jnp.dot(members, back_grads, preferred_element_type=jnp.float32))
-        .astype(jnp.bfloat16)
-        .reshape(seg, TP, B, C)
-    )
+    cut_sum = jnp.einsum(
+        "sn,ntbd->stbd",
+        members,
+        back_grads.reshape(slot_total, TP, B, C),
+        preferred_element_type=jnp.float32,
+    )
+    dz = (inner_sum + cut_sum).astype(jnp.bfloat16)
     dh = jnp.einsum("stbd,cd->stbc", dz, theta, preferred_element_type=jnp.float32)
     du = jnp.concatenate([dh * gate, dh * first * gate * (1.0 - gate)], axis=-1).astype(
         jnp.bfloat16

time: 150 us -> 152 us (1.013)
  waiting for transfers between devices: 54.1 us -> 63.6 us
  local copies, waits for them, and re-layouts: 22.8 us -> 18.5 us
  starting transfers between devices: 25.7 us -> 23.9 us
    all_to_all x1, waiting for transfers between devices: 0.01 us -> 8.57 us  [body(): lax.all_to_all(ret_grads, ('region', 'sub'), split_axis=0, concat_axis=0,...]
    convert_element_type x2 -> x0, local copies, waits for them, and re-layouts: 4.04 us -> none  [the longest x1 2.44 us: body(): dz_inner = inner_sum.astype(jnp.bfloat16).reshape(seg, TP, B, C)]
    dot_general x2, matrix products: 7.93 us -> 4.41 us  [weight_grads(): jnp.einsum('stbd,cd->stbc', dzr, theta, preferred_element_type=jnp.float32)]
    reduce_sum x2, other arithmetic: 0.71 us -> 3.66 us  [weight_grads(): g_bias = jnp.sum(du.astype(jnp.float32), axis=(0, 1, 2))]
    ppermute x5, waiting for transfers between devices: 6.19 us -> 8.44 us  [device_sum(): flat = flat + lax.ppermute(flat, ('region', 'sub'), perm)]
    optimization_barrier x1 -> x0, local copies, waits for them, and re-layouts: 2.23 us -> none  [body(): inner_sum, ret_grads = lax.optimization_barrier((inner_sum, ret_grads))]
    dot_general x2 -> x0, matrix products: 2.14 us -> none  [the longest x1 1.61 us: body(): jnp.dot(members, back_grads, preferred_element_type=jnp.float32)]
    unnamed x58 -> x70, local copies, waits for them, and re-layouts: 9.71 us -> 11.7 us
  transfers between devices with their start and end apart: 9 -> 9, of which waited for: 7 -> 9; matrix products, arithmetic and copies ran while one was open for 23% -> 16% of each run, Pallas kernels for 0% -> 0%
where the time goes in v9:
time: 152 us; the launch traced here: 151 us
  waiting for transfers between devices  63.6 us (42%)
  matrix products  32.4 us (21%)
  starting transfers between devices  23.9 us (16%)
  local copies, waits for them, and re-layouts  18.5 us (12%)
  other arithmetic  11.9 us (8%)
    all_to_all x1, waiting for transfers between devices, body(): lax.all_to_all(send_grads, ('region', 'sub'), split_axis=0, concat_axis=0...  16.6 us
    all_to_all x1, waiting for transfers between devices, body(): lax.all_to_all(ret_rows, ('region', 'sub'), split_axis=0, concat_axis=0,...  15.7 us
    all_to_all x1, waiting for transfers between devices, body(): lax.all_to_all(send, ('region', 'sub'), split_axis=0, concat_axis=0, tile...  14.4 us
    unnamed x70, local copies, waits for them, and re-layouts  11.7 us
    all_to_all x1, waiting for transfers between devices, body(): lax.all_to_all(ret_grads, ('region', 'sub'), split_axis=0, concat_axis=0,...  8.57 us
    ppermute x5, waiting for transfers between devices, device_sum(): flat = flat + lax.ppermute(flat, ('region', 'sub'), perm)  8.44 us
    all_to_all x1, starting transfers between devices, body(): lax.all_to_all(send, ('region', 'sub'), split_axis=0, concat_axis=0, tile...  7.41 us
    ppermute x5, starting transfers between devices, device_sum(): flat = flat + lax.ppermute(flat, ('region', 'sub'), perm)  5.65 us
  transfers between devices with their start and end apart: 9, of which 9 were waited for; matrix products, arithmetic and copies ran while one was open for 16% of the time, Pallas kernels for 0%

profile of v9, /device:TPU:0, one launch (start us, length us, event | category | flops | bytes accessed | tf_op | source)
XLA Modules:
  0.0 151.5 jit_solution(11925709381771343384)
XLA Ops:
  0.6 0.7 fusion.86
  1.6 0.8 select_reduce_fusion
  2.4 0.7 fusion.97
  3.1 1.1 scatter_custom_fusion
  4.2 1.1 scatter_custom_fusion.1
  5.3 2.1 %convolution_convert_fusion.3 = bf16[256,1536]{1,0:T(8,128)(2,1)S(1)} fusion(bf16[512,1536]{1,0:T(8,128)(2,1)} %param.10, s32[256]{0:T(256)S(1)} %scatter_custom_fusion), kind=kOutput, calls=%fused_computation.33 | convolution fusion | flops 403439616 | bytes 2360320 | tf_op jit(solution)/shard_map/sn,sf->nf/dot_general | solution.py:94
  7.6 1.0 maximum_bitcast_fusion
  8.5 7.4 %all-to-all-start = ((bf16[32,8,1664]{2,1,0:T(8,128)(2,1)}), bf16[32,8,1664]{2,1,0:T(8,128)(2,1)}, u32[]{:S(2)}, u32[]{:S(2)}) async-start(bf16[32,8,1664]{2,1,0:T(8,128)(2,1)} %maximum_bitcast_fusion), calls=%async_computation | async-start | bytes 1703936 | tf_op jit(solution)/shard_map/all_to_all | solution.py:104
  15.9 0.7 copy.47
  16.7 0.5 fusion.105
  17.5 1.0 broadcast_add_fusion
  19.3 0.7 multiply_convert_fusion.5
  20.1 1.6 %copy-done.5 = f32[512,10,2,128]{0,3,2,1:T(8,128)} copy-done((f32[512,10,2,128]{0,3,2,1:T(8,128)}, f32[512,10,2,128]{0,3,2,1:T(8,128)S(1)}, u32[]{:S(2)}) %copy-start.5) | copy-done | bytes 5242904
  21.6 0.5 convolution_convert_fusion.4
  22.2 1.4 fusion.69
  23.6 14.4 %all-to-all-done = bf16[32,8,1664]{2,1,0:T(8,128)(2,1)} async-done(((bf16[32,8,1664]{2,1,0:T(8,128)(2,1)}), bf16[32,8,1664]{2,1,0:T(8,128)(2,1)}, u32[]{:S(2)}, u32[]{:S(2)}) %all-to-all-start) | async-done | bytes 852000 | tf_op jit(solution)/shard_map/all_to_all | solution.py:104
  38.0 1.2 slice.102
  39.1 1.0 convert_reduce_fusion.4
  40.6 0.6 convolution_add_fusion.3
  42.8 0.7 copy-done.8
  43.9 1.2 fusion.13
  45.1 3.6 %all-to-all-start.1 = ((bf16[32,8,1280]{2,1,0:T(8,128)(2,1)}), bf16[32,8,1280]{2,1,0:T(8,128)(2,1)S(1)}, u32[]{:S(2)}, u32[]{:S(2)}) async-start(bf16[32,8,1280]{2,1,0:T(8,128)(2,1)} %fusion.13), calls=%async_computation.1 | async-start | bytes 1310720 | tf_op jit(solution)/shard_map/all_to_all | solution.py:128
  48.9 2.0 %fusion.67 = f32[512,1280]{1,0:T(8,128)} fusion(bf16[128,1280]{1,0:T(8,128)(2,1)S(1)} %fusion.15, s32[512]{0:T(512)S(1)} %bitcast.131, s32[512]{0:T(512)S(1)} %bitcast.126), kind=kOutput, calls=%fused_computation.87 | convolution fusion | flops 168165376 | bytes 2953216 | tf_op jit(solution)/shard_map/es,ef->sf/dot_general | solution.py:123
  50.9 15.7 %all-to-all-done.1 = bf16[32,8,1280]{2,1,0:T(8,128)(2,1)S(1)} async-done(((bf16[32,8,1280]{2,1,0:T(8,128)(2,1)}), bf16[32,8,1280]{2,1,0:T(8,128)(2,1)S(1)}, u32[]{:S(2)}, u32[]{:S(2)}) %all-to-all-start.1) | async-done | bytes 655392 | tf_op jit(solution)/shard_map/all_to_all | solution.py:128
  66.6 4.0 %divide_convert_fusion = (bf16[512,1280]{1,0:T(8,128)(2,1)S(1)}, bf16[512,1280]{1,0:T(8,128)(2,1)}) fusion(bf16[512,1280]{1,0:T(8,128)(2,1)} %param.19, f32[512]{0:T(512)S(1)} %broadcast_add_fusion.1, f32[512,1280]{1,0:T(8,128)} %fusion.67, bf16[32,8,1280]{2,1,0:T(8,128)(2,1)S(1)} %all-to-all-done.1, s32[256]{0:T(256)S(1)} %scatter_custom_fusion), kind=kOutput, calls=%fused_computation.25 | convolution fusion | flops 345767936 | bytes 7212032 | tf_op jit(solution)/shard_map/dot_general | solution.py:125
  70.7 1.4 fusion.14
  72.1 3.7 %all-to-all-start.2 = ((bf16[32,8,1280]{2,1,0:T(8,128)(2,1)}), bf16[32,8,1280]{2,1,0:T(8,128)(2,1)S(1)}, u32[]{:S(2)}, u32[]{:S(2)}) async-start(bf16[32,8,1280]{2,1,0:T(8,128)(2,1)} %fusion.14), calls=%async_computation.2 | async-start | bytes 1310720 | tf_op jit(solution)/shard_map/all_to_all | solution.py:135
  75.8 1.2 fusion.65
  77.0 16.6 %all-to-all-done.2 = bf16[32,8,1280]{2,1,0:T(8,128)(2,1)S(1)} async-done(((bf16[32,8,1280]{2,1,0:T(8,128)(2,1)}), bf16[32,8,1280]{2,1,0:T(8,128)(2,1)S(1)}, u32[]{:S(2)}, u32[]{:S(2)}) %all-to-all-start.2) | async-done | bytes 655392 | tf_op jit(solution)/shard_map/all_to_all | solution.py:135
  93.5 1.3 fusion.16
  95.2 1.2 convolution_convert_fusion
  96.4 0.5 fusion.63
  97.1 1.7 %copy-done.7 = f32[256,10,2,128]{0,3,2,1:T(8,128)S(1)} copy-done((f32[256,10,2,128]{0,3,2,1:T(8,128)S(1)}, f32[256,10,2,128]{0,3,2,1:T(8,128)}, u32[]{:S(2)}) %copy-start.7) | copy-done | bytes 2621464
  98.8 1.5 multiply_convert_fusion.7
  100.3 0.6 slice-done
  101.1 2.9 %multiply_convert_fusion.3 = (bf16[512,10,2,64]{0,3,2,1:T(8,128)(2,1)}, bf16[512,10,2,64]{0,3,2,1:T(8,128)(2,1)}) fusion(f32[512,10,2,128]{0,3,2,1:T(8,128)S(1)} %bitcast.116, bf16[64,64]{1,0:T(8,128)(2,1)S(1)} %copy-done.28, f32[512,10,2,64]{0,3,2,1:T(8,128)S(1)} %bitcast.110), kind=kOutput, calls=%fused_computation.24 | convolution fusion | flops 91095040 | bytes 10493952 | tf_op jit(solution)/shard_map/stbd,cd->stbc/dot_general | solution.py:153
  104.1 3.5 %all-to-all-start.3 = ((bf16[32,8,1280]{2,1,0:T(8,128)(2,1)}), bf16[32,8,1280]{2,1,0:T(8,128)(2,1)S(1)}, u32[]{:S(2)}, u32[]{:S(2)}) async-start(bf16[32,8,1280]{2,1,0:T(8,128)(2,1)} %bitcast.36), calls=%async_computation.3 | async-start | bytes 1310720 | tf_op jit(solution)/shard_map/all_to_all | solution.py:147
  107.7 1.5 convert_reduce_fusion.1
  109.2 2.1 %convert_reduce_fusion = f32[128]{0:T(128)S(1)} fusion(bf16[512,10,2,64]{0,3,2,1:T(8,128)(2,1)} %get-tuple-element.40, bf16[512,10,2,64]{0,3,2,1:T(8,128)(2,1)} %get-tuple-element.39), kind=kLoop, calls=%fused_computation.2 | loop fusion | flops 6553472 | bytes 2621952 | tf_op jit(solution)/shard_map/reduce_sum | solution.py:156
  111.7 0.7 fusion.27
  112.4 1.0 copy-done.2
  113.5 0.5 fusion.47
  114.2 0.7 copy-done.11
  115.0 0.4 copy-done.12
  115.4 0.4 copy-done.14
  115.7 1.2 fusion.37
  117.0 8.6 %all-to-all-done.3 = bf16[32,8,1280]{2,1,0:T(8,128)(2,1)S(1)} async-done(((bf16[32,8,1280]{2,1,0:T(8,128)(2,1)}), bf16[32,8,1280]{2,1,0:T(8,128)(2,1)S(1)}, u32[]{:S(2)}, u32[]{:S(2)}) %all-to-all-start.3) | async-done | bytes 655392 | tf_op jit(solution)/shard_map/all_to_all | solution.py:147
  125.8 0.6 fusion.56
  126.3 0.7 collective-permute-done
  127.0 1.4 collective-permute-start.1
  128.5 3.9 %multiply_convert_fusion.1 = (bf16[512,10,2,64]{0,3,2,1:T(8,128)(2,1)S(1)}, bf16[512,10,2,64]{0,3,2,1:T(8,128)(2,1)S(1)}) fusion(f32[512,10,2,128]{0,3,2,1:T(8,128)} %copy-done.5, f32[512,10,2,64]{0,3,2,1:T(8,128)S(1)} %bitcast.112, f32[512,10,2,64]{0,3,2,1:T(8,128)S(1)} %bitcast.119, bf16[64,64]{1,0:T(8,128)(2,1)S(1)} %copy-done.28), kind=kOutput, calls=%fused_computation.20 | convolution fusion | flops 91750400 | bytes 13115392 | tf_op jit(solution)/shard_map/stbd,cd->stbc/dot_general | solution.py:172
  132.4 1.5 %collective-permute-start.2 = (f32[28800]{0:T(1024)S(1)}, f32[28800]{0:T(1024)S(1)}, u32[]{:S(2)}, u32[]{:S(2)}) collective-permute-start(f32[28800]{0:T(1024)S(1)} %add.134), channel_id=1, source_target_pairs={{0,4},{1,5},{2,6},{3,7},{4,0},{5,1},{6,2},{7,3},{8,12},{9,13},{10,... | collective-permute-start | bytes 345608 | tf_op jit(solution)/shard_map/ppermute | solution.py:24
  133.9 1.2 fusion.6
  135.1 2.5 %collective-permute-done.2 = f32[28800]{0:T(1024)S(1)} collective-permute-done((f32[28800]{0:T(1024)S(1)}, f32[28800]{0:T(1024)S(1)}, u32[]{:S(2)}, u32[]{:S(2)}) %collective-permute-start.2) | collective-permute-done | bytes 115232 | tf_op jit(solution)/shard_map/ppermute | solution.py:24
  137.6 1.2 collective-permute-start.3
  138.8 1.6 %fusion.104 = (f32[512,10,2,64]{0,3,2,1:T(8,128)S(1)}, f32[512,10,2,64]{0,3,2,1:T(8,128)S(1)}, f32[512,10,2,64]{0,3,2,1:T(8,128)S(1)}) fusion(f32[512,10,2,192]{0,3,2,1:T(8,128)S(1)} %fusion.6), kind=kLoop, calls=%fused_computation.136 | loop fusion | bytes 15728640 | tf_op jit(solution)/shard_map/slice | solution.py:181
  140.5 2.0 %collective-permute-done.3 = f32[28800]{0:T(1024)S(1)} collective-permute-done((f32[28800]{0:T(1024)S(1)}, f32[28800]{0:T(1024)S(1)}, u32[]{:S(2)}, u32[]{:S(2)}) %collective-permute-start.3) | collective-permute-done | bytes 115232 | tf_op jit(solution)/shard_map/ppermute | solution.py:24
  142.5 1.4 collective-permute-start.4
  143.9 1.0 add_convert_fusion
  144.9 1.6 %copy.62 = bf16[512,1536]{1,0:T(8,128)(2,1)} copy(bf16[512,1536]{0,1:T(8,128)(2,1)S(1)} %bitcast.114) | data formatting | bytes 3145728
  146.5 3.1 %collective-permute-done.4 = f32[28800]{0:T(1024)S(1)} collective-permute-done((f32[28800]{0:T(1024)S(1)}, f32[28800]{0:T(1024)S(1)}, u32[]{:S(2)}, u32[]{:S(2)}) %collective-permute-start.4) | collective-permute-done | bytes 115232 | tf_op jit(solution)/shard_map/ppermute | solution.py:24
  149.6 0.7 fusion.80
  150.3 0.5 slice_multiply_fusion.2
  150.8 0.7 mul.133
  (89 shorter events, 5.8 us)
Async XLA Ops:
  0.6 16.9 %copy-start = (bf16[192,128]{1,0:T(8,128)(2,1)S(1)}, bf16[192,128]{1,0:T(8,128)(2,1)}, u32[]{:S(2)}) copy-start(bf16[192,128]{1,0:T(8,128)(2,1)} %param.11) | copy-start | bytes 147460
  5.3 10.6 %copy-start.4 = (bf16[512,1536]{1,0:T(8,128)(2,1)S(1)}, bf16[512,1536]{1,0:T(8,128)(2,1)}, u32[]{:S(2)}) copy-start(bf16[512,1536]{1,0:T(8,128)(2,1)} %param.10) | copy-start | bytes 4718596
  8.5 29.4 %all-to-all-start = ((bf16[32,8,1664]{2,1,0:T(8,128)(2,1)}), bf16[32,8,1664]{2,1,0:T(8,128)(2,1)}, u32[]{:S(2)}, u32[]{:S(2)}) async-start(bf16[32,8,1664]{2,1,0:T(8,128)(2,1)} %maximum_bitcast_fusion), calls=%async_computation | async-start | bytes 1703936 | tf_op jit(solution)/shard_map/all_to_all | solution.py:104
  16.7 0.7 copy-start.29
  16.7 0.8 copy-start.31
  17.4 1.2 copy-start.13
  17.4 1.6 %copy-start.15 = (bf16[512,10,2,64]{0,3,2,1:T(8,128)(2,1)}, bf16[512,10,2,64]{0,3,2,1:T(8,128)(2,1)S(1)}, u32[]{:S(2)}) copy-start(bf16[512,10,2,64]{0,3,2,1:T(8,128)(2,1)S(1)} %get-tuple-element.46) | copy-start | bytes 3932164
  17.4 2.0 %copy-start.17 = (bf16[512,10,2,64]{0,3,2,1:T(8,128)(2,1)}, bf16[512,10,2,64]{0,3,2,1:T(8,128)(2,1)S(1)}, u32[]{:S(2)}) copy-start(bf16[512,10,2,64]{0,3,2,1:T(8,128)(2,1)S(1)} %get-tuple-element.47) | copy-start | bytes 3932164
  19.3 2.3 %copy-start.5 = (f32[512,10,2,128]{0,3,2,1:T(8,128)}, f32[512,10,2,128]{0,3,2,1:T(8,128)S(1)}, u32[]{:S(2)}) copy-start(f32[512,10,2,128]{0,3,2,1:T(8,128)S(1)} %broadcast_add_fusion) | copy-start | bytes 15728644
  19.3 2.3 %copy-start.28 = (bf16[64,64]{1,0:T(8,128)(2,1)S(1)}, bf16[64,64]{1,0:T(8,128)(2,1)}, u32[]{:S(2)}) copy-start(bf16[64,64]{1,0:T(8,128)(2,1)} %param.13) | copy-start | bytes 24580
  40.6 0.8 copy-start.22
  40.6 1.1 copy-start.24
  40.6 1.3 copy-start.26
  41.9 2.0 %copy-start.6 = (f32[256,10,2,128]{0,3,2,1:T(8,128)}, f32[256,10,2,128]{0,3,2,1:T(8,128)S(1)}, u32[]{:S(2)}) copy-start(f32[256,10,2,128]{0,3,2,1:T(8,128)S(1)} %convolution_add_fusion.3) | copy-start | bytes 7864324
  41.9 0.9 copy-start.30
  41.9 1.6 %copy-start.8 = (f32[128,1280]{1,0:T(8,128)S(1)}, f32[128,1280]{1,0:T(8,128)}, u32[]{:S(2)}) copy-start(f32[128,1280]{1,0:T(8,128)} %fusion.69) | copy-start | bytes 1966084
  42.3 1.6 %copy-start.9 = (bf16[256,10,2,64]{0,3,2,1:T(8,128)(2,1)}, bf16[256,10,2,64]{0,3,2,1:T(8,128)(2,1)S(1)}, u32[]{:S(2)}) copy-start(bf16[256,10,2,64]{0,3,2,1:T(8,128)(2,1)S(1)} %multiply_convert_fusion.8) | copy-start | bytes 1966084
  45.1 21.6 %all-to-all-start.1 = ((bf16[32,8,1280]{2,1,0:T(8,128)(2,1)}), bf16[32,8,1280]{2,1,0:T(8,128)(2,1)S(1)}, u32[]{:S(2)}, u32[]{:S(2)}) async-start(bf16[32,8,1280]{2,1,0:T(8,128)(2,1)} %fusion.13), calls=%async_computation.1 | async-start | bytes 1310720 | tf_op jit(solution)/shard_map/all_to_all | solution.py:128
  72.1 21.4 %all-to-all-start.2 = ((bf16[32,8,1280]{2,1,0:T(8,128)(2,1)}), bf16[32,8,1280]{2,1,0:T(8,128)(2,1)S(1)}, u32[]{:S(2)}, u32[]{:S(2)}) async-start(bf16[32,8,1280]{2,1,0:T(8,128)(2,1)} %fusion.14), calls=%async_computation.2 | async-start | bytes 1310720 | tf_op jit(solution)/shard_map/all_to_all | solution.py:135
  96.4 2.3 %copy-start.7 = (f32[256,10,2,128]{0,3,2,1:T(8,128)S(1)}, f32[256,10,2,128]{0,3,2,1:T(8,128)}, u32[]{:S(2)}) copy-start(f32[256,10,2,128]{0,3,2,1:T(8,128)} %copy-done.6) | copy-start | bytes 7864324
  97.0 3.3 %copy-start.1 = (f32[512,1280]{0,1}, f32[512,1280]{0,1:S(1)}, u32[]{:S(2)}) copy-start(f32[512,1280]{0,1:S(1)} %fusion.63) | copy-start | bytes 7864324
  97.0 3.9 %slice-start = ((s8[5242880]{0:T(1024)(128)(4,1)}), s8[4194304]{0:T(1024)(128)(4,1)S(1)}, s32[]{:S(2)}) async-start(s8[5242880]{0:T(1024)(128)(4,1)} %bitcast.115), calls=%async_computation.4 | async-start | bytes 8388608
  97.1 3.2 %copy-start.20 = (bf16[256,10,2,64]{0,3,2,1:T(8,128)(2,1)}, bf16[256,10,2,64]{0,3,2,1:T(8,128)(2,1)S(1)}, u32[]{:S(2)}) copy-start(bf16[256,10,2,64]{0,3,2,1:T(8,128)(2,1)S(1)} %convert_element_type.126) | copy-start | bytes 1966084
  98.8 2.4 %slice-start.1 = ((s8[5242880]{0:T(1024)(128)(4,1)}), s8[1048576]{0:T(1024)(128)(4,1)S(1)}, s32[]{:S(2)}) async-start(s8[5242880]{0:T(1024)(128)(4,1)} %bitcast.115), calls=%async_computation.5 | async-start | bytes 2097152
  104.1 7.2 %copy-start.10 = (bf16[256,10,2,64]{0,3,2,1:T(8,128)(2,1)S(1)}, bf16[256,10,2,64]{0,3,2,1:T(8,128)(2,1)}, u32[]{:S(2)}) copy-start(bf16[256,10,2,64]{0,3,2,1:T(8,128)(2,1)} %copy-done.9) | copy-start | bytes 1966084
  104.1 21.4 %all-to-all-start.3 = ((bf16[32,8,1280]{2,1,0:T(8,128)(2,1)}), bf16[32,8,1280]{2,1,0:T(8,128)(2,1)S(1)}, u32[]{:S(2)}, u32[]{:S(2)}) async-start(bf16[32,8,1280]{2,1,0:T(8,128)(2,1)} %bitcast.36), calls=%async_computation.3 | async-start | bytes 1310720 | tf_op jit(solution)/shard_map/all_to_all | solution.py:147
  107.6 3.7 %copy-start.21 = (bf16[256,10,2,64]{0,3,2,1:T(8,128)(2,1)S(1)}, bf16[256,10,2,64]{0,3,2,1:T(8,128)(2,1)}, u32[]{:S(2)}) copy-start(bf16[256,10,2,64]{0,3,2,1:T(8,128)(2,1)} %copy-done.20) | copy-start | bytes 1966084
  107.6 4.1 %copy-start.19 = (bf16[256,10,2,64]{0,3,2,1:T(8,128)(2,1)S(1)}, bf16[256,10,2,64]{0,3,2,1:T(8,128)(2,1)}, u32[]{:S(2)}) copy-start(bf16[256,10,2,64]{0,3,2,1:T(8,128)(2,1)} %get-tuple-element.42) | copy-start | bytes 1966084
  107.6 4.1 %copy-start.23 = (bf16[256,10,2,64]{0,3,2,1:T(8,128)(2,1)S(1)}, bf16[256,10,2,64]{0,3,2,1:T(8,128)(2,1)}, u32[]{:S(2)}) copy-start(bf16[256,10,2,64]{0,3,2,1:T(8,128)(2,1)} %copy-done.22) | copy-start | bytes 1966084
  107.6 4.1 %copy-start.25 = (bf16[256,10,2,64]{0,3,2,1:T(8,128)(2,1)S(1)}, bf16[256,10,2,64]{0,3,2,1:T(8,128)(2,1)}, u32[]{:S(2)}) copy-start(bf16[256,10,2,64]{0,3,2,1:T(8,128)(2,1)} %copy-done.24) | copy-start | bytes 1966084
  107.7 4.1 %copy-start.27 = (bf16[256,10,2,64]{0,3,2,1:T(8,128)(2,1)S(1)}, bf16[256,10,2,64]{0,3,2,1:T(8,128)(2,1)}, u32[]{:S(2)}) copy-start(bf16[256,10,2,64]{0,3,2,1:T(8,128)(2,1)} %copy-done.26) | copy-start | bytes 1966084
  111.7 1.7 %copy-start.2 = (f32[512,1280]{0,1:S(1)}, f32[512,1280]{0,1}, u32[]{:S(2)}) copy-start(f32[512,1280]{0,1} %copy-done.1) | copy-start | bytes 7864324
  111.7 2.2 %copy-start.16 = (bf16[512,10,2,64]{0,3,2,1:T(8,128)(2,1)S(1)}, bf16[512,10,2,64]{0,3,2,1:T(8,128)(2,1)}, u32[]{:S(2)}) copy-start(bf16[512,10,2,64]{0,3,2,1:T(8,128)(2,1)} %copy-done.15) | copy-start | bytes 3932164
  111.7 2.5 %copy-start.18 = (bf16[512,10,2,64]{0,3,2,1:T(8,128)(2,1)S(1)}, bf16[512,10,2,64]{0,3,2,1:T(8,128)(2,1)}, u32[]{:S(2)}) copy-start(bf16[512,10,2,64]{0,3,2,1:T(8,128)(2,1)} %copy-done.17) | copy-start | bytes 3932164
  113.5 1.5 copy-start.11
  113.5 1.9 %copy-start.12 = (bf16[512,10,2,64]{0,3,2,1:T(8,128)(2,1)S(1)}, bf16[512,10,2,64]{0,3,2,1:T(8,128)(2,1)}, u32[]{:S(2)}) copy-start(bf16[512,10,2,64]{0,3,2,1:T(8,128)(2,1)} %get-tuple-element.40) | copy-start | bytes 3932164
  113.5 2.3 %copy-start.14 = (bf16[512,10,2,64]{0,3,2,1:T(8,128)(2,1)S(1)}, bf16[512,10,2,64]{0,3,2,1:T(8,128)(2,1)}, u32[]{:S(2)}) copy-start(bf16[512,10,2,64]{0,3,2,1:T(8,128)(2,1)} %copy-done.13) | copy-start | bytes 3932164
  117.0 11.5 %copy-start.3 = (f32[512,1280]{0,1:S(1)}, f32[512,1280]{0,1}, u32[]{:S(2)}) copy-start(f32[512,1280]{0,1} %copy-done.1) | copy-start | bytes 7864324
  125.6 1.4 collective-permute-start
  127.0 5.4 %collective-permute-start.1 = (f32[28800]{0:T(1024)S(1)}, f32[28800]{0:T(1024)S(1)}, u32[]{:S(2)}, u32[]{:S(2)}) collective-permute-start(f32[28800]{0:T(1024)S(1)} %fusion.103), channel_id=1, source_target_pairs={{0,2},{1,3},{2,0},{3,1},{4,6},{5,7},{6,4},{7,5},{8,10},{9,11},{10,... | collective-permute-start | bytes 345608 | tf_op jit(solution)/shard_map/ppermute | solution.py:24
  132.4 5.2 %collective-permute-start.2 = (f32[28800]{0:T(1024)S(1)}, f32[28800]{0:T(1024)S(1)}, u32[]{:S(2)}, u32[]{:S(2)}) collective-permute-start(f32[28800]{0:T(1024)S(1)} %add.134), channel_id=1, source_target_pairs={{0,4},{1,5},{2,6},{3,7},{4,0},{5,1},{6,2},{7,3},{8,12},{9,13},{10,... | collective-permute-start | bytes 345608 | tf_op jit(solution)/shard_map/ppermute | solution.py:24
  137.6 4.9 %collective-permute-start.3 = (f32[28800]{0:T(1024)S(1)}, f32[28800]{0:T(1024)S(1)}, u32[]{:S(2)}, u32[]{:S(2)}) collective-permute-start(f32[28800]{0:T(1024)S(1)} %add.135), channel_id=1, source_target_pairs={{0,8},{1,9},{2,10},{3,11},{4,12},{5,13},{6,14},{7,15},{8,0},{9,1},... | collective-permute-start | bytes 345608 | tf_op jit(solution)/shard_map/ppermute | solution.py:24
  142.5 7.1 %collective-permute-start.4 = (f32[28800]{0:T(1024)S(1)}, f32[28800]{0:T(1024)S(1)}, u32[]{:S(2)}, u32[]{:S(2)}) collective-permute-start(f32[28800]{0:T(1024)S(1)} %add.136), channel_id=1, source_target_pairs={{0,16},{1,17},{2,18},{3,19},{4,20},{5,21},{6,22},{7,23},{8,24},{9,... | collective-permute-start | bytes 345608 | tf_op jit(solution)/shard_map/ppermute | solution.py:24

commit v10 on v6

--- a/solution.py
+++ b/solution.py
@@ -137,7 +137,10 @@
     )
     dedge, ret_grads = edge_side(grad_rows, recv_grads)
     inner_sum = jnp.einsum("es,ef->sf", incidence, dedge, preferred_element_type=jnp.float32)
-    inner_sum, ret_grads = lax.optimization_barrier((inner_sum, ret_grads))
+    dz_slots = jnp.einsum(
+        "en,etbd->ntbd", owned, dedge.reshape(EDGE_DEV, TP, B, C), preferred_element_type=jnp.float32
+    ).astype(jnp.bfloat16)
+    inner_sum, dz_slots, ret_grads = lax.optimization_barrier((inner_sum, dz_slots, ret_grads))
     back_grads = lax.all_to_all(
         ret_grads, ("region", "sub"), split_axis=0, concat_axis=0, tiled=True
     )
@@ -152,7 +155,6 @@
 
     dz_inner = inner_sum.astype(jnp.bfloat16).reshape(seg, TP, B, C)
     _, ga_conv, ga_bias, ga_theta = weight_grads(stack, gate, first, hidden, dz_inner)
-    dz_slots = ret_grads.reshape(slot_total, TP, B, C)
     _, gb_conv, gb_bias, gb_theta = weight_grads(r_stack, r_gate, r_first, r_hidden, dz_slots)
     partial = (ga_conv + gb_conv, ga_bias + gb_bias, ga_theta + gb_theta)
     partial, back_grads = lax.optimization_barrier((partial, back_grads))

time: 150 us -> 149 us (level)
  waiting for transfers between devices: 54.1 us -> 57.5 us
  starting transfers between devices: 25.7 us -> 23.9 us
  matrix products: 33.9 us -> 32.3 us
    all_to_all x1, waiting for transfers between devices: 0.01 us -> 3.38 us  [body(): lax.all_to_all(ret_grads, ('region', 'sub'), split_axis=0, concat_axis=0,...]
    optimization_barrier x1 -> x0, local copies, waits for them, and re-layouts: 2.23 us -> none  [body(): inner_sum, ret_grads = lax.optimization_barrier((inner_sum, ret_grads))]
    dot_general x2, matrix products: 7.93 us -> 6.03 us  [weight_grads(): jnp.einsum('stbd,cd->stbc', dzr, theta, preferred_element_type=jnp.float32)]
    ppermute x5, starting transfers between devices: 7.48 us -> 5.88 us  [device_sum(): flat = flat + lax.ppermute(flat, ('region', 'sub'), perm)]
    unnamed x58 -> x62, local copies, waits for them, and re-layouts: 9.71 us -> 10.8 us
  transfers between devices with their start and end apart: 9 -> 9, of which waited for: 7 -> 8; matrix products, arithmetic and copies ran while one was open for 23% -> 21% of each run, Pallas kernels for 0% -> 0%
where the time goes in v10:
time: 149 us; the launch traced here: 148 us
  waiting for transfers between devices  57.5 us (39%)
  matrix products  32.3 us (22%)
  starting transfers between devices  23.9 us (16%)
  local copies, waits for them, and re-layouts  21.7 us (15%)
  other arithmetic  11.6 us (8%)
    all_to_all x1, waiting for transfers between devices, body(): lax.all_to_all(send_grads, ('region', 'sub'), split_axis=0, concat_axis=0...  17.6 us
    all_to_all x1, waiting for transfers between devices, body(): lax.all_to_all(ret_rows, ('region', 'sub'), split_axis=0, concat_axis=0,...  15.6 us
    all_to_all x1, waiting for transfers between devices, body(): lax.all_to_all(send, ('region', 'sub'), split_axis=0, concat_axis=0, tile...  14.7 us
    unnamed x62, local copies, waits for them, and re-layouts  10.8 us
    all_to_all x1, starting transfers between devices, body(): lax.all_to_all(send, ('region', 'sub'), split_axis=0, concat_axis=0, tile...  7.41 us
    ppermute x5, waiting for transfers between devices, device_sum(): flat = flat + lax.ppermute(flat, ('region', 'sub'), perm)  6.31 us
    dot_general x2, matrix products, weight_grads(): jnp.einsum('stbd,cd->stbc', dzr, theta, preferred_element_type=jnp.float32)  6.03 us
    ppermute x5, starting transfers between devices, device_sum(): flat = flat + lax.ppermute(flat, ('region', 'sub'), perm)  5.88 us
  transfers between devices with their start and end apart: 9, of which 8 were waited for; matrix products, arithmetic and copies ran while one was open for 21% of the time, Pallas kernels for 0%

profile of v10, /device:TPU:0, one launch (start us, length us, event | category | flops | bytes accessed | tf_op | source)
XLA Modules:
  0.0 148.3 jit_solution(6353866054196782910)
XLA Ops:
  0.6 0.7 fusion.85
  1.6 0.8 select_reduce_fusion
  2.4 0.7 fusion.97
  3.1 1.1 scatter_custom_fusion
  4.2 1.1 scatter_custom_fusion.1
  5.3 2.1 %convolution_convert_fusion.3 = bf16[256,1536]{1,0:T(8,128)(2,1)S(1)} fusion(bf16[512,1536]{1,0:T(8,128)(2,1)} %param.10, s32[256]{0:T(256)S(1)} %scatter_custom_fusion), kind=kOutput, calls=%fused_computation.34 | convolution fusion | flops 403439616 | bytes 2360320 | tf_op jit(solution)/shard_map/sn,sf->nf/dot_general | solution.py:94
  7.6 1.0 maximum_bitcast_fusion
  8.5 7.4 %all-to-all-start = ((bf16[32,8,1664]{2,1,0:T(8,128)(2,1)}), bf16[32,8,1664]{2,1,0:T(8,128)(2,1)}, u32[]{:S(2)}, u32[]{:S(2)}) async-start(bf16[32,8,1664]{2,1,0:T(8,128)(2,1)} %maximum_bitcast_fusion), calls=%async_computation | async-start | bytes 1703936 | tf_op jit(solution)/shard_map/all_to_all | solution.py:104
  15.9 0.7 copy.66
  16.7 0.5 fusion.105
  17.5 1.0 broadcast_add_fusion
  19.3 0.7 multiply_convert_fusion.5
  20.1 1.6 %copy-done.2 = f32[512,10,2,128]{0,3,2,1:T(8,128)} copy-done((f32[512,10,2,128]{0,3,2,1:T(8,128)}, f32[512,10,2,128]{0,3,2,1:T(8,128)S(1)}, u32[]{:S(2)}) %copy-start.2) | copy-done | bytes 5242904
  21.6 0.6 convolution_convert_fusion.4
  22.2 0.5 copy-done.3
  22.7 0.6 fusion.68
  23.3 14.7 %all-to-all-done = bf16[32,8,1664]{2,1,0:T(8,128)(2,1)} async-done(((bf16[32,8,1664]{2,1,0:T(8,128)(2,1)}), bf16[32,8,1664]{2,1,0:T(8,128)(2,1)}, u32[]{:S(2)}, u32[]{:S(2)}) %all-to-all-start) | async-done | bytes 852000 | tf_op jit(solution)/shard_map/all_to_all | solution.py:104
  38.0 1.0 convert_reduce_fusion.4
  38.9 1.2 slice.102
  40.7 0.5 convolution_add_fusion.4
  43.7 1.2 fusion.14
  44.9 3.6 %all-to-all-start.1 = ((bf16[32,8,1280]{2,1,0:T(8,128)(2,1)}), bf16[32,8,1280]{2,1,0:T(8,128)(2,1)S(1)}, u32[]{:S(2)}, u32[]{:S(2)}) async-start(bf16[32,8,1280]{2,1,0:T(8,128)(2,1)} %fusion.14), calls=%async_computation.1 | async-start | bytes 1310720 | tf_op jit(solution)/shard_map/all_to_all | solution.py:128
  48.7 2.1 %fusion.66 = f32[512,1280]{1,0:T(8,128)} fusion(bf16[128,1280]{1,0:T(8,128)(2,1)S(1)} %fusion.16, s32[512]{0:T(512)S(1)} %bitcast.128, s32[512]{0:T(512)S(1)} %bitcast.123), kind=kOutput, calls=%fused_computation.86 | convolution fusion | flops 168165376 | bytes 2953216 | tf_op jit(solution)/shard_map/es,ef->sf/dot_general | solution.py:123
  50.8 15.6 %all-to-all-done.1 = bf16[32,8,1280]{2,1,0:T(8,128)(2,1)S(1)} async-done(((bf16[32,8,1280]{2,1,0:T(8,128)(2,1)}), bf16[32,8,1280]{2,1,0:T(8,128)(2,1)S(1)}, u32[]{:S(2)}, u32[]{:S(2)}) %all-to-all-start.1) | async-done | bytes 655392 | tf_op jit(solution)/shard_map/all_to_all | solution.py:128
  66.4 4.0 %divide_convert_fusion = (bf16[512,1280]{1,0:T(8,128)(2,1)S(1)}, bf16[512,1280]{1,0:T(8,128)(2,1)}) fusion(bf16[512,1280]{1,0:T(8,128)(2,1)} %param.19, f32[512]{0:T(512)S(1)} %broadcast_add_fusion.1, f32[512,1280]{1,0:T(8,128)} %fusion.66, bf16[32,8,1280]{2,1,0:T(8,128)(2,1)S(1)} %all-to-all-done.1, s32[256]{0:T(256)S(1)} %scatter_custom_fusion), kind=kOutput, calls=%fused_computation.26 | convolution fusion | flops 345767936 | bytes 7212032 | tf_op jit(solution)/shard_map/dot_general | solution.py:125
  70.5 1.4 fusion.15
  71.8 3.5 %all-to-all-start.2 = ((bf16[32,8,1280]{2,1,0:T(8,128)(2,1)}), bf16[32,8,1280]{2,1,0:T(8,128)(2,1)S(1)}, u32[]{:S(2)}, u32[]{:S(2)}) async-start(bf16[32,8,1280]{2,1,0:T(8,128)(2,1)} %fusion.15), calls=%async_computation.2 | async-start | bytes 1310720 | tf_op jit(solution)/shard_map/all_to_all | solution.py:135
  75.7 17.6 %all-to-all-done.2 = bf16[32,8,1280]{2,1,0:T(8,128)(2,1)S(1)} async-done(((bf16[32,8,1280]{2,1,0:T(8,128)(2,1)}), bf16[32,8,1280]{2,1,0:T(8,128)(2,1)S(1)}, u32[]{:S(2)}, u32[]{:S(2)}) %all-to-all-start.2) | async-done | bytes 655392 | tf_op jit(solution)/shard_map/all_to_all | solution.py:135
  93.5 1.3 convolution_convert_fusion
  95.2 0.5 fusion.62
  95.8 1.1 copy-done.6
  96.9 1.7 %multiply_convert_fusion.7 = (bf16[256,10,2,64]{0,3,2,1:T(8,128)(2,1)}, bf16[256,10,2,64]{0,3,2,1:T(8,128)(2,1)}) fusion(f32[256,10,2,128]{0,3,2,1:T(8,128)S(1)} %copy-done.6, bf16[256,10,2,64]{0,3,2,1:T(8,128)(2,1)S(1)} %convert_element_type.126, bf16[64,64]{1,0:T(8,128)(2,1)S(1)} %copy-done.26), kind=kOutput, calls=%fused_computation.59 | convolution fusion | flops 45219840 | bytes 4595712 | tf_op jit(solution)/shard_map/stbd,cd->stbc/dot_general | solution.py:150
  98.7 3.5 %all-to-all-start.3 = ((bf16[32,8,1280]{2,1,0:T(8,128)(2,1)}), bf16[32,8,1280]{2,1,0:T(8,128)(2,1)S(1)}, u32[]{:S(2)}, u32[]{:S(2)}) async-start(bf16[32,8,1280]{2,1,0:T(8,128)(2,1)} %bitcast.114), calls=%async_computation.3 | async-start | bytes 1310720 | tf_op jit(solution)/shard_map/all_to_all | solution.py:144
  102.2 1.2 convert_element_type.128
  103.4 2.4 %copy.71 = bf16[512,1280]{0,1:T(8,128)(2,1)} copy(bf16[512,1280]{1,0:T(8,128)(2,1)} %convert_element_type.128) | data formatting | bytes 2621440 | tf_op jit(solution)/shard_map/convert_element_type | solution.py:156
  105.8 4.3 %multiply_convert_fusion.3 = (bf16[512,10,2,64]{0,3,2,1:T(8,128)(2,1)S(1)}, bf16[512,10,2,64]{0,3,2,1:T(8,128)(2,1)S(1)}) fusion(f32[512,10,2,128]{0,3,2,1:T(8,128)} %copy-done.2, bf16[512,10,2,64]{0,3,2,1:T(8,128)(2,1)} %bitcast.116, bf16[64,64]{1,0:T(8,128)(2,1)S(1)} %copy-done.26), kind=kOutput, calls=%fused_computation.25 | convolution fusion | flops 90439680 | bytes 9183232 | tf_op jit(solution)/shard_map/stbd,cd->stbc/dot_general | solution.py:150
  110.4 0.4 convert_reduce_fusion
  112.0 0.7 fusion.27
  112.7 0.6 copy-done.4
  113.3 0.4 copy-done.9
  113.7 0.5 fusion.47
  114.2 0.9 copy-done.11
  115.1 0.4 copy-done.13
  115.5 1.2 fusion.37
  116.7 3.4 %all-to-all-done.3 = bf16[32,8,1280]{2,1,0:T(8,128)(2,1)S(1)} async-done(((bf16[32,8,1280]{2,1,0:T(8,128)(2,1)}), bf16[32,8,1280]{2,1,0:T(8,128)(2,1)S(1)}, u32[]{:S(2)}, u32[]{:S(2)}) %all-to-all-start.3) | async-done | bytes 655392 | tf_op jit(solution)/shard_map/all_to_all | solution.py:144
  120.2 0.7 pad_maximum_fusion.4
  120.9 1.6 %fusion.3 = bf16[512,1280]{1,0:T(8,128)(2,1)} fusion(f32[512,1280]{1,0:T(8,128)S(1)} %fusion.62, bf16[256,1280]{1,0:T(8,128)(2,1)S(1)} %bitcast.113, s32[256]{0:T(256)S(1)} %scatter_custom_fusion), kind=kOutput, calls=%fused_computation.10 | convolution fusion | flops 337248256 | bytes 4588544 | tf_op jit(solution)/shard_map/dot_general | solution.py:163
  122.5 1.6 %copy.80 = bf16[512,1280]{0,1:T(8,128)(2,1)S(1)} copy(bf16[512,1280]{1,0:T(8,128)(2,1)} %fusion.3) | data formatting | bytes 2621440 | tf_op jit(solution)/shard_map/convert_element_type | solution.py:164
  124.1 0.9 fusion.103
  125.0 1.7 %collective-permute-start.1 = (f32[28800]{0:T(1024)S(1)}, f32[28800]{0:T(1024)S(1)}, u32[]{:S(2)}, u32[]{:S(2)}) collective-permute-start(f32[28800]{0:T(1024)S(1)} %fusion.103), channel_id=1, source_target_pairs={{0,2},{1,3},{2,0},{3,1},{4,6},{5,7},{6,4},{7,5},{8,10},{9,11},{10,... | collective-permute-start | bytes 345608 | tf_op jit(solution)/shard_map/ppermute | solution.py:24
  126.7 3.8 %multiply_convert_fusion.1 = (bf16[512,10,2,64]{0,3,2,1:T(8,128)(2,1)S(1)}, bf16[512,10,2,64]{0,3,2,1:T(8,128)(2,1)S(1)}) fusion(f32[512,10,2,128]{0,3,2,1:T(8,128)} %copy-done.2, bf16[512,10,2,64]{0,3,2,1:T(8,128)(2,1)S(1)} %bitcast.118, bf16[64,64]{1,0:T(8,128)(2,1)S(1)} %copy-done.26), kind=kOutput, calls=%fused_computation.22 | convolution fusion | flops 90439680 | bytes 9183232 | tf_op jit(solution)/shard_map/stbd,cd->stbc/dot_general | solution.py:167
  130.7 1.5 collective-permute-start.2
  132.2 1.2 fusion.7
  133.3 2.3 %collective-permute-done.2 = f32[28800]{0:T(1024)S(1)} collective-permute-done((f32[28800]{0:T(1024)S(1)}, f32[28800]{0:T(1024)S(1)}, u32[]{:S(2)}, u32[]{:S(2)}) %collective-permute-start.2) | collective-permute-done | bytes 115232 | tf_op jit(solution)/shard_map/ppermute | solution.py:24
  135.7 1.5 collective-permute-start.3
  137.2 1.6 %fusion.104 = (f32[512,10,2,64]{0,3,2,1:T(8,128)S(1)}, f32[512,10,2,64]{0,3,2,1:T(8,128)S(1)}, f32[512,10,2,64]{0,3,2,1:T(8,128)S(1)}) fusion(f32[512,10,2,192]{0,3,2,1:T(8,128)S(1)} %fusion.7), kind=kLoop, calls=%fused_computation.136 | loop fusion | bytes 15728640 | tf_op jit(solution)/shard_map/slice | solution.py:176
  138.8 1.8 %collective-permute-done.3 = f32[28800]{0:T(1024)S(1)} collective-permute-done((f32[28800]{0:T(1024)S(1)}, f32[28800]{0:T(1024)S(1)}, u32[]{:S(2)}, u32[]{:S(2)}) %collective-permute-start.3) | collective-permute-done | bytes 115232 | tf_op jit(solution)/shard_map/ppermute | solution.py:24
  140.6 1.2 collective-permute-start.4
  141.8 1.0 add_convert_fusion
  142.8 1.6 %copy.82 = bf16[512,1536]{1,0:T(8,128)(2,1)} copy(bf16[512,1536]{0,1:T(8,128)(2,1)S(1)} %bitcast.110) | data formatting | bytes 3145728
  144.4 2.0 %collective-permute-done.4 = f32[28800]{0:T(1024)S(1)} collective-permute-done((f32[28800]{0:T(1024)S(1)}, f32[28800]{0:T(1024)S(1)}, u32[]{:S(2)}, u32[]{:S(2)}) %collective-permute-start.4) | collective-permute-done | bytes 115232 | tf_op jit(solution)/shard_map/ppermute | solution.py:24
  146.4 0.5 slice_multiply_fusion.2
  147.0 0.6 fusion.79
  147.6 0.7 mul.133
  (83 shorter events, 7.3 us)
Async XLA Ops:
  0.6 16.9 %copy-start = (bf16[192,128]{1,0:T(8,128)(2,1)S(1)}, bf16[192,128]{1,0:T(8,128)(2,1)}, u32[]{:S(2)}) copy-start(bf16[192,128]{1,0:T(8,128)(2,1)} %param.11) | copy-start | bytes 147460
  5.3 10.6 %copy-start.1 = (bf16[512,1536]{1,0:T(8,128)(2,1)S(1)}, bf16[512,1536]{1,0:T(8,128)(2,1)}, u32[]{:S(2)}) copy-start(bf16[512,1536]{1,0:T(8,128)(2,1)} %param.10) | copy-start | bytes 4718596
  8.5 29.4 %all-to-all-start = ((bf16[32,8,1664]{2,1,0:T(8,128)(2,1)}), bf16[32,8,1664]{2,1,0:T(8,128)(2,1)}, u32[]{:S(2)}, u32[]{:S(2)}) async-start(bf16[32,8,1664]{2,1,0:T(8,128)(2,1)} %maximum_bitcast_fusion), calls=%async_computation | async-start | bytes 1703936 | tf_op jit(solution)/shard_map/all_to_all | solution.py:104
  16.7 0.7 copy-start.27
  16.7 0.8 copy-start.29
  17.4 1.2 copy-start.10
  17.4 1.6 %copy-start.12 = (bf16[512,10,2,64]{0,3,2,1:T(8,128)(2,1)}, bf16[512,10,2,64]{0,3,2,1:T(8,128)(2,1)S(1)}, u32[]{:S(2)}) copy-start(bf16[512,10,2,64]{0,3,2,1:T(8,128)(2,1)S(1)} %get-tuple-element.51) | copy-start | bytes 3932164
  17.4 2.0 %copy-start.14 = (bf16[512,10,2,64]{0,3,2,1:T(8,128)(2,1)}, bf16[512,10,2,64]{0,3,2,1:T(8,128)(2,1)S(1)}, u32[]{:S(2)}) copy-start(bf16[512,10,2,64]{0,3,2,1:T(8,128)(2,1)S(1)} %get-tuple-element.52) | copy-start | bytes 3932164
  19.3 2.3 %copy-start.2 = (f32[512,10,2,128]{0,3,2,1:T(8,128)}, f32[512,10,2,128]{0,3,2,1:T(8,128)S(1)}, u32[]{:S(2)}) copy-start(f32[512,10,2,128]{0,3,2,1:T(8,128)S(1)} %broadcast_add_fusion) | copy-start | bytes 15728644
  19.3 2.3 %copy-start.26 = (bf16[64,64]{1,0:T(8,128)(2,1)S(1)}, bf16[64,64]{1,0:T(8,128)(2,1)}, u32[]{:S(2)}) copy-start(bf16[64,64]{1,0:T(8,128)(2,1)} %param.13) | copy-start | bytes 24580
  21.6 1.1 copy-start.3
  40.7 0.9 copy-start.20
  40.7 1.1 copy-start.22
  40.7 1.3 copy-start.24
  41.9 1.5 %copy-start.5 = (f32[256,10,2,128]{0,3,2,1:T(8,128)}, f32[256,10,2,128]{0,3,2,1:T(8,128)S(1)}, u32[]{:S(2)}) copy-start(f32[256,10,2,128]{0,3,2,1:T(8,128)S(1)} %convolution_add_fusion.4) | copy-start | bytes 7864324
  42.0 0.8 copy-start.28
  42.3 1.3 copy-start.7
  44.9 21.5 %all-to-all-start.1 = ((bf16[32,8,1280]{2,1,0:T(8,128)(2,1)}), bf16[32,8,1280]{2,1,0:T(8,128)(2,1)S(1)}, u32[]{:S(2)}, u32[]{:S(2)}) async-start(bf16[32,8,1280]{2,1,0:T(8,128)(2,1)} %fusion.14), calls=%async_computation.1 | async-start | bytes 1310720 | tf_op jit(solution)/shard_map/all_to_all | solution.py:128
  71.8 21.4 %all-to-all-start.2 = ((bf16[32,8,1280]{2,1,0:T(8,128)(2,1)}), bf16[32,8,1280]{2,1,0:T(8,128)(2,1)S(1)}, u32[]{:S(2)}, u32[]{:S(2)}) async-start(bf16[32,8,1280]{2,1,0:T(8,128)(2,1)} %fusion.15), calls=%async_computation.2 | async-start | bytes 1310720 | tf_op jit(solution)/shard_map/all_to_all | solution.py:135
  95.2 1.7 %copy-start.6 = (f32[256,10,2,128]{0,3,2,1:T(8,128)S(1)}, f32[256,10,2,128]{0,3,2,1:T(8,128)}, u32[]{:S(2)}) copy-start(f32[256,10,2,128]{0,3,2,1:T(8,128)} %copy-done.5) | copy-start | bytes 7864324
  96.9 1.8 %copy-start.18 = (bf16[256,10,2,64]{0,3,2,1:T(8,128)(2,1)}, bf16[256,10,2,64]{0,3,2,1:T(8,128)(2,1)S(1)}, u32[]{:S(2)}) copy-start(bf16[256,10,2,64]{0,3,2,1:T(8,128)(2,1)S(1)} %convert_element_type.126) | copy-start | bytes 1966084
  98.7 21.4 %all-to-all-start.3 = ((bf16[32,8,1280]{2,1,0:T(8,128)(2,1)}), bf16[32,8,1280]{2,1,0:T(8,128)(2,1)S(1)}, u32[]{:S(2)}, u32[]{:S(2)}) async-start(bf16[32,8,1280]{2,1,0:T(8,128)(2,1)} %bitcast.114), calls=%async_computation.3 | async-start | bytes 1310720 | tf_op jit(solution)/shard_map/all_to_all | solution.py:144
  105.8 4.3 %copy-start.16 = (bf16[256,10,2,64]{0,3,2,1:T(8,128)(2,1)S(1)}, bf16[256,10,2,64]{0,3,2,1:T(8,128)(2,1)}, u32[]{:S(2)}) copy-start(bf16[256,10,2,64]{0,3,2,1:T(8,128)(2,1)} %get-tuple-element.46) | copy-start | bytes 1966084
  105.8 4.3 %copy-start.17 = (bf16[256,10,2,64]{0,3,2,1:T(8,128)(2,1)S(1)}, bf16[256,10,2,64]{0,3,2,1:T(8,128)(2,1)}, u32[]{:S(2)}) copy-start(bf16[256,10,2,64]{0,3,2,1:T(8,128)(2,1)} %get-tuple-element.47) | copy-start | bytes 1966084
  110.1 1.1 copy-start.8
  110.1 1.3 copy-start.19
  110.1 1.6 %copy-start.21 = (bf16[256,10,2,64]{0,3,2,1:T(8,128)(2,1)S(1)}, bf16[256,10,2,64]{0,3,2,1:T(8,128)(2,1)}, u32[]{:S(2)}) copy-start(bf16[256,10,2,64]{0,3,2,1:T(8,128)(2,1)} %copy-done.20) | copy-start | bytes 1966084
  110.1 1.6 %copy-start.23 = (bf16[256,10,2,64]{0,3,2,1:T(8,128)(2,1)S(1)}, bf16[256,10,2,64]{0,3,2,1:T(8,128)(2,1)}, u32[]{:S(2)}) copy-start(bf16[256,10,2,64]{0,3,2,1:T(8,128)(2,1)} %copy-done.22) | copy-start | bytes 1966084
  110.2 1.8 %copy-start.25 = (bf16[256,10,2,64]{0,3,2,1:T(8,128)(2,1)S(1)}, bf16[256,10,2,64]{0,3,2,1:T(8,128)(2,1)}, u32[]{:S(2)}) copy-start(bf16[256,10,2,64]{0,3,2,1:T(8,128)(2,1)} %copy-done.24) | copy-start | bytes 1966084
  112.0 1.3 copy-start.4
  112.0 1.7 %copy-start.9 = (bf16[512,1280]{0,1:T(8,128)(2,1)S(1)}, bf16[512,1280]{0,1:T(8,128)(2,1)}, u32[]{:S(2)}) copy-start(bf16[512,1280]{0,1:T(8,128)(2,1)} %copy.71) | copy-start | bytes 3932164
  112.0 2.2 %copy-start.15 = (bf16[512,10,2,64]{0,3,2,1:T(8,128)(2,1)S(1)}, bf16[512,10,2,64]{0,3,2,1:T(8,128)(2,1)}, u32[]{:S(2)}) copy-start(bf16[512,10,2,64]{0,3,2,1:T(8,128)(2,1)} %copy-done.14) | copy-start | bytes 3932164
  113.7 1.4 copy-start.11
  113.7 1.8 %copy-start.13 = (bf16[512,10,2,64]{0,3,2,1:T(8,128)(2,1)S(1)}, bf16[512,10,2,64]{0,3,2,1:T(8,128)(2,1)}, u32[]{:S(2)}) copy-start(bf16[512,10,2,64]{0,3,2,1:T(8,128)(2,1)} %copy-done.12) | copy-start | bytes 3932164
  120.8 3.3 %collective-permute-start = (f32[28800]{0:T(1024)}, f32[28800]{0:T(1024)}, u32[]{:S(2)}, u32[]{:S(2)}) collective-permute-start(f32[28800]{0:T(1024)} %pad_maximum_fusion.4), channel_id=1, source_target_pairs={{0,1},{1,0},{2,3},{3,2},{4,5},{5,4},{6,7},{7,6},{8,9},{9,8},{10,11... | collective-permute-start | bytes 345608 | tf_op jit(solution)/shard_map/ppermute | solution.py:24
  125.0 5.7 %collective-permute-start.1 = (f32[28800]{0:T(1024)S(1)}, f32[28800]{0:T(1024)S(1)}, u32[]{:S(2)}, u32[]{:S(2)}) collective-permute-start(f32[28800]{0:T(1024)S(1)} %fusion.103), channel_id=1, source_target_pairs={{0,2},{1,3},{2,0},{3,1},{4,6},{5,7},{6,4},{7,5},{8,10},{9,11},{10,... | collective-permute-start | bytes 345608 | tf_op jit(solution)/shard_map/ppermute | solution.py:24
  130.7 5.0 %collective-permute-start.2 = (f32[28800]{0:T(1024)S(1)}, f32[28800]{0:T(1024)S(1)}, u32[]{:S(2)}, u32[]{:S(2)}) collective-permute-start(f32[28800]{0:T(1024)S(1)} %add.134), channel_id=1, source_target_pairs={{0,4},{1,5},{2,6},{3,7},{4,0},{5,1},{6,2},{7,3},{8,12},{9,13},{10,... | collective-permute-start | bytes 345608 | tf_op jit(solution)/shard_map/ppermute | solution.py:24
  135.7 4.9 %collective-permute-start.3 = (f32[28800]{0:T(1024)S(1)}, f32[28800]{0:T(1024)S(1)}, u32[]{:S(2)}, u32[]{:S(2)}) collective-permute-start(f32[28800]{0:T(1024)S(1)} %add.135), channel_id=1, source_target_pairs={{0,8},{1,9},{2,10},{3,11},{4,12},{5,13},{6,14},{7,15},{8,0},{9,1},... | collective-permute-start | bytes 345608 | tf_op jit(solution)/shard_map/ppermute | solution.py:24
  140.6 5.8 %collective-permute-start.4 = (f32[28800]{0:T(1024)S(1)}, f32[28800]{0:T(1024)S(1)}, u32[]{:S(2)}, u32[]{:S(2)}) collective-permute-start(f32[28800]{0:T(1024)S(1)} %add.136), channel_id=1, source_target_pairs={{0,16},{1,17},{2,18},{3,19},{4,20},{5,21},{6,22},{7,23},{8,24},{9,... | collective-permute-start | bytes 345608 | tf_op jit(solution)/shard_map/ppermute | solution.py:24

commit v11 on v10

--- a/solution.py
+++ b/solution.py
@@ -76,15 +76,16 @@
     inner_count = jnp.sum(incidence, axis=1)
     incidence = incidence.astype(jnp.bfloat16)
     dest = cut_dest[:, 0]
-    dest_hot = (dest[:, None] == jnp.arange(device_list, dtype=jnp.int32)[None, :]).astype(
+    n_cut = dest.shape[0]
+    order = jnp.arange(n_cut, dtype=jnp.int32)
+    earlier = (dest[None, :] == dest[:, None]) & (order[None, :] < order[:, None])
+    rank = jnp.sum(earlier.astype(jnp.int32), axis=1)
+    slot_position = dest * slot_capacity + rank
+    slot_hot = (slot_position[:, None] == jnp.arange(slot_total, dtype=jnp.int32)[None, :]).astype(
         jnp.int32
     )
-    rank = jnp.sum((jnp.cumsum(dest_hot, axis=0) - 1) * dest_hot, axis=1)
-    slot_position = dest * slot_capacity + rank
-    slotted_segment = jnp.full((slot_total,), -1, jnp.int32).at[slot_position].set(crossing_segment)
-    slotted_hyperedge = (
-        jnp.full((slot_total,), -1, jnp.int32).at[slot_position].set(crossing_hyperedge)
-    )
+    slotted_segment = jnp.sum(slot_hot * (crossing_segment[:, None] + 1), axis=0) - 1
+    slotted_hyperedge = jnp.sum(slot_hot * (crossing_hyperedge[:, None] + 1), axis=0) - 1
     members = (slotted_segment[None, :] == jnp.arange(seg, dtype=jnp.int32)[:, None]).astype(
         jnp.float32
     )

time: 149 us -> 148 us (level)
  local copies, waits for them, and re-layouts: 21.7 us -> 19.6 us
    scatter x2 -> x0, local copies, waits for them, and re-layouts: 2.21 us -> none  [body(): jnp.full((slot_total,), -1, jnp.int32).at[slot_position]]
where the time goes in v11:
time: 148 us; the launch traced here: 147 us
  waiting for transfers between devices  57.3 us (39%)
  matrix products  32.3 us (22%)
  starting transfers between devices  24.1 us (16%)
  local copies, waits for them, and re-layouts  19.6 us (13%)
  other arithmetic  12.3 us (8%)
    all_to_all x1, waiting for transfers between devices, body(): lax.all_to_all(send_grads, ('region', 'sub'), split_axis=0, concat_axis=0...  17.6 us
    all_to_all x1, waiting for transfers between devices, body(): lax.all_to_all(ret_rows, ('region', 'sub'), split_axis=0, concat_axis=0,...  15.6 us
    all_to_all x1, waiting for transfers between devices, body(): lax.all_to_all(send, ('region', 'sub'), split_axis=0, concat_axis=0, tile...  14.6 us
    unnamed x62, local copies, waits for them, and re-layouts  10.9 us
    all_to_all x1, starting transfers between devices, body(): lax.all_to_all(send, ('region', 'sub'), split_axis=0, concat_axis=0, tile...  7.41 us
    ppermute x5, waiting for transfers between devices, device_sum(): flat = flat + lax.ppermute(flat, ('region', 'sub'), perm)  6.31 us
    dot_general x2, matrix products, weight_grads(): jnp.einsum('stbd,cd->stbc', dzr, theta, preferred_element_type=jnp.float32)  6.04 us
    ppermute x5, starting transfers between devices, device_sum(): flat = flat + lax.ppermute(flat, ('region', 'sub'), perm)  5.88 us
  transfers between devices with their start and end apart: 9, of which 8 were waited for; matrix products, arithmetic and copies ran while one was open for 21% of the time, Pallas kernels for 0%

profile of v11, /device:TPU:0, one launch (start us, length us, event | category | flops | bytes accessed | tf_op | source)
XLA Modules:
  0.0 146.7 jit_solution(3081591358260199178)
XLA Ops:
  0.6 0.7 broadcast_add_fusion.4
  1.3 0.7 broadcast_add_fusion.3
  2.0 0.9 convert_reduce_fusion.5
  2.9 0.7 fusion.97
  3.7 2.1 %convolution_convert_fusion.3 = bf16[256,1536]{1,0:T(8,128)(2,1)S(1)} fusion(bf16[512,1536]{1,0:T(8,128)(2,1)} %param.10, s32[256]{0:T(256)S(1)} %get-tuple-element.61), kind=kOutput, calls=%fused_computation.32 | convolution fusion | flops 403439616 | bytes 2360320 | tf_op jit(solution)/shard_map/sn,sf->nf/dot_general | solution.py:95
  5.9 1.0 maximum_bitcast_fusion
  6.9 7.4 %all-to-all-start = ((bf16[32,8,1664]{2,1,0:T(8,128)(2,1)}), bf16[32,8,1664]{2,1,0:T(8,128)(2,1)}, u32[]{:S(2)}, u32[]{:S(2)}) async-start(bf16[32,8,1664]{2,1,0:T(8,128)(2,1)} %maximum_bitcast_fusion), calls=%async_computation | async-start | bytes 1703936 | tf_op jit(solution)/shard_map/all_to_all | solution.py:105
  14.3 0.7 copy.66
  15.1 0.5 fusion.101
  15.9 1.0 broadcast_add_fusion
  17.3 0.4 copy-done.14
  17.7 0.7 multiply_convert_fusion.5
  18.4 1.6 %copy-done.2 = f32[512,10,2,128]{0,3,2,1:T(8,128)} copy-done((f32[512,10,2,128]{0,3,2,1:T(8,128)}, f32[512,10,2,128]{0,3,2,1:T(8,128)S(1)}, u32[]{:S(2)}) %copy-start.2) | copy-done | bytes 5242904
  20.0 0.6 convolution_convert_fusion.4
  20.6 0.5 copy-done.3
  21.1 0.6 fusion.68
  21.7 14.6 %all-to-all-done = bf16[32,8,1664]{2,1,0:T(8,128)(2,1)} async-done(((bf16[32,8,1664]{2,1,0:T(8,128)(2,1)}), bf16[32,8,1664]{2,1,0:T(8,128)(2,1)}, u32[]{:S(2)}, u32[]{:S(2)}) %all-to-all-start) | async-done | bytes 852000 | tf_op jit(solution)/shard_map/all_to_all | solution.py:105
  36.3 1.0 convert_reduce_fusion.4
  37.3 1.2 slice.102
  39.1 0.5 convolution_add_fusion.4
  42.1 1.2 fusion.14
  43.3 3.6 %all-to-all-start.1 = ((bf16[32,8,1280]{2,1,0:T(8,128)(2,1)}), bf16[32,8,1280]{2,1,0:T(8,128)(2,1)S(1)}, u32[]{:S(2)}, u32[]{:S(2)}) async-start(bf16[32,8,1280]{2,1,0:T(8,128)(2,1)} %fusion.14), calls=%async_computation.1 | async-start | bytes 1310720 | tf_op jit(solution)/shard_map/all_to_all | solution.py:129
  47.1 2.1 %fusion.66 = f32[512,1280]{1,0:T(8,128)} fusion(bf16[128,1280]{1,0:T(8,128)(2,1)S(1)} %fusion.16, s32[512]{0:T(512)S(1)} %bitcast.126, s32[512]{0:T(512)S(1)} %bitcast.121), kind=kOutput, calls=%fused_computation.84 | convolution fusion | flops 168165376 | bytes 2953216 | tf_op jit(solution)/shard_map/es,ef->sf/dot_general | solution.py:124
  49.2 15.6 %all-to-all-done.1 = bf16[32,8,1280]{2,1,0:T(8,128)(2,1)S(1)} async-done(((bf16[32,8,1280]{2,1,0:T(8,128)(2,1)}), bf16[32,8,1280]{2,1,0:T(8,128)(2,1)S(1)}, u32[]{:S(2)}, u32[]{:S(2)}) %all-to-all-start.1) | async-done | bytes 655392 | tf_op jit(solution)/shard_map/all_to_all | solution.py:129
  64.8 4.0 %divide_convert_fusion = (bf16[512,1280]{1,0:T(8,128)(2,1)S(1)}, bf16[512,1280]{1,0:T(8,128)(2,1)}) fusion(bf16[512,1280]{1,0:T(8,128)(2,1)} %param.19, f32[512]{0:T(512)S(1)} %broadcast_add_fusion.1, f32[512,1280]{1,0:T(8,128)} %fusion.66, bf16[32,8,1280]{2,1,0:T(8,128)(2,1)S(1)} %all-to-all-done.1, s32[256]{0:T(256)S(1)} %get-tuple-element.61), kind=kOutput, calls=%fused_computation.24 | convolution fusion | flops 345767936 | bytes 7212032 | tf_op jit(solution)/shard_map/dot_general | solution.py:126
  68.9 1.4 fusion.15
  70.3 3.5 %all-to-all-start.2 = ((bf16[32,8,1280]{2,1,0:T(8,128)(2,1)}), bf16[32,8,1280]{2,1,0:T(8,128)(2,1)S(1)}, u32[]{:S(2)}, u32[]{:S(2)}) async-start(bf16[32,8,1280]{2,1,0:T(8,128)(2,1)} %fusion.15), calls=%async_computation.2 | async-start | bytes 1310720 | tf_op jit(solution)/shard_map/all_to_all | solution.py:136
  74.1 17.6 %all-to-all-done.2 = bf16[32,8,1280]{2,1,0:T(8,128)(2,1)S(1)} async-done(((bf16[32,8,1280]{2,1,0:T(8,128)(2,1)}), bf16[32,8,1280]{2,1,0:T(8,128)(2,1)S(1)}, u32[]{:S(2)}, u32[]{:S(2)}) %all-to-all-start.2) | async-done | bytes 655392 | tf_op jit(solution)/shard_map/all_to_all | solution.py:136
  92.0 1.3 convolution_convert_fusion
  93.6 0.5 fusion.62
  94.2 1.1 copy-done.6
  95.3 1.7 %multiply_convert_fusion.7 = (bf16[256,10,2,64]{0,3,2,1:T(8,128)(2,1)}, bf16[256,10,2,64]{0,3,2,1:T(8,128)(2,1)}) fusion(f32[256,10,2,128]{0,3,2,1:T(8,128)S(1)} %copy-done.6, bf16[256,10,2,64]{0,3,2,1:T(8,128)(2,1)S(1)} %convert_element_type.131, bf16[64,64]{1,0:T(8,128)(2,1)S(1)} %copy-done.26), kind=kOutput, calls=%fused_computation.57 | convolution fusion | flops 45219840 | bytes 4595712 | tf_op jit(solution)/shard_map/stbd,cd->stbc/dot_general | solution.py:151
  97.1 3.7 %all-to-all-start.3 = ((bf16[32,8,1280]{2,1,0:T(8,128)(2,1)}), bf16[32,8,1280]{2,1,0:T(8,128)(2,1)S(1)}, u32[]{:S(2)}, u32[]{:S(2)}) async-start(bf16[32,8,1280]{2,1,0:T(8,128)(2,1)} %bitcast.112), calls=%async_computation.3 | async-start | bytes 1310720 | tf_op jit(solution)/shard_map/all_to_all | solution.py:145
  100.8 1.2 convert_element_type.133
  102.0 2.4 %copy.71 = bf16[512,1280]{0,1:T(8,128)(2,1)} copy(bf16[512,1280]{1,0:T(8,128)(2,1)} %convert_element_type.133) | data formatting | bytes 2621440 | tf_op jit(solution)/shard_map/convert_element_type | solution.py:157
  104.4 4.3 %multiply_convert_fusion.3 = (bf16[512,10,2,64]{0,3,2,1:T(8,128)(2,1)S(1)}, bf16[512,10,2,64]{0,3,2,1:T(8,128)(2,1)S(1)}) fusion(f32[512,10,2,128]{0,3,2,1:T(8,128)} %copy-done.2, bf16[512,10,2,64]{0,3,2,1:T(8,128)(2,1)} %bitcast.114, bf16[64,64]{1,0:T(8,128)(2,1)S(1)} %copy-done.26), kind=kOutput, calls=%fused_computation.23 | convolution fusion | flops 90439680 | bytes 9183232 | tf_op jit(solution)/shard_map/stbd,cd->stbc/dot_general | solution.py:151
  109.1 0.4 convert_reduce_fusion
  110.6 0.7 fusion.27
  111.3 0.6 copy-done.4
  111.9 0.4 copy-done.9
  112.3 0.5 fusion.47
  112.8 0.9 copy-done.11
  113.7 0.4 copy-done.13
  114.1 1.2 fusion.37
  115.3 3.2 %all-to-all-done.3 = bf16[32,8,1280]{2,1,0:T(8,128)(2,1)S(1)} async-done(((bf16[32,8,1280]{2,1,0:T(8,128)(2,1)}), bf16[32,8,1280]{2,1,0:T(8,128)(2,1)S(1)}, u32[]{:S(2)}, u32[]{:S(2)}) %all-to-all-start.3) | async-done | bytes 655392 | tf_op jit(solution)/shard_map/all_to_all | solution.py:145
  118.6 0.7 pad_maximum_fusion.4
  119.3 1.6 %fusion.3 = bf16[512,1280]{1,0:T(8,128)(2,1)} fusion(f32[512,1280]{1,0:T(8,128)S(1)} %fusion.62, bf16[256,1280]{1,0:T(8,128)(2,1)S(1)} %bitcast.111, s32[256]{0:T(256)S(1)} %get-tuple-element.61), kind=kOutput, calls=%fused_computation.8 | convolution fusion | flops 337248256 | bytes 4588544 | tf_op jit(solution)/shard_map/dot_general | solution.py:164
  120.9 1.6 %copy.80 = bf16[512,1280]{0,1:T(8,128)(2,1)S(1)} copy(bf16[512,1280]{1,0:T(8,128)(2,1)} %fusion.3) | data formatting | bytes 2621440 | tf_op jit(solution)/shard_map/convert_element_type | solution.py:165
  122.6 0.9 fusion.99
  123.5 1.7 %collective-permute-start.1 = (f32[28800]{0:T(1024)S(1)}, f32[28800]{0:T(1024)S(1)}, u32[]{:S(2)}, u32[]{:S(2)}) collective-permute-start(f32[28800]{0:T(1024)S(1)} %fusion.99), channel_id=1, source_target_pairs={{0,2},{1,3},{2,0},{3,1},{4,6},{5,7},{6,4},{7,5},{8,10},{9,11},{10,... | collective-permute-start | bytes 345608 | tf_op jit(solution)/shard_map/ppermute | solution.py:24
  125.1 3.8 %multiply_convert_fusion.1 = (bf16[512,10,2,64]{0,3,2,1:T(8,128)(2,1)S(1)}, bf16[512,10,2,64]{0,3,2,1:T(8,128)(2,1)S(1)}) fusion(f32[512,10,2,128]{0,3,2,1:T(8,128)} %copy-done.2, bf16[512,10,2,64]{0,3,2,1:T(8,128)(2,1)S(1)} %bitcast.116, bf16[64,64]{1,0:T(8,128)(2,1)S(1)} %copy-done.26), kind=kOutput, calls=%fused_computation.20 | convolution fusion | flops 90439680 | bytes 9183232 | tf_op jit(solution)/shard_map/stbd,cd->stbc/dot_general | solution.py:168
  129.2 1.5 collective-permute-start.2
  130.6 1.2 fusion.7
  131.8 2.3 %collective-permute-done.2 = f32[28800]{0:T(1024)S(1)} collective-permute-done((f32[28800]{0:T(1024)S(1)}, f32[28800]{0:T(1024)S(1)}, u32[]{:S(2)}, u32[]{:S(2)}) %collective-permute-start.2) | collective-permute-done | bytes 115232 | tf_op jit(solution)/shard_map/ppermute | solution.py:24
  134.1 1.5 collective-permute-start.3
  135.6 1.6 %fusion.100 = (f32[512,10,2,64]{0,3,2,1:T(8,128)S(1)}, f32[512,10,2,64]{0,3,2,1:T(8,128)S(1)}, f32[512,10,2,64]{0,3,2,1:T(8,128)S(1)}) fusion(f32[512,10,2,192]{0,3,2,1:T(8,128)S(1)} %fusion.7), kind=kLoop, calls=%fused_computation.136 | loop fusion | bytes 15728640 | tf_op jit(solution)/shard_map/slice | solution.py:177
  137.2 1.8 %collective-permute-done.3 = f32[28800]{0:T(1024)S(1)} collective-permute-done((f32[28800]{0:T(1024)S(1)}, f32[28800]{0:T(1024)S(1)}, u32[]{:S(2)}, u32[]{:S(2)}) %collective-permute-start.3) | collective-permute-done | bytes 115232 | tf_op jit(solution)/shard_map/ppermute | solution.py:24
  139.1 1.2 collective-permute-start.4
  140.3 1.0 add_convert_fusion
  141.3 1.6 %copy.82 = bf16[512,1536]{1,0:T(8,128)(2,1)} copy(bf16[512,1536]{0,1:T(8,128)(2,1)S(1)} %bitcast.108) | data formatting | bytes 3145728
  142.9 2.0 %collective-permute-done.4 = f32[28800]{0:T(1024)S(1)} collective-permute-done((f32[28800]{0:T(1024)S(1)}, f32[28800]{0:T(1024)S(1)}, u32[]{:S(2)}, u32[]{:S(2)}) %collective-permute-start.4) | collective-permute-done | bytes 115232 | tf_op jit(solution)/shard_map/ppermute | solution.py:24
  144.9 0.5 slice_multiply_fusion.2
  145.4 0.6 fusion.79
  146.1 0.7 mul.149
  (82 shorter events, 6.9 us)
Async XLA Ops:
  0.6 15.3 %copy-start = (bf16[192,128]{1,0:T(8,128)(2,1)S(1)}, bf16[192,128]{1,0:T(8,128)(2,1)}, u32[]{:S(2)}) copy-start(bf16[192,128]{1,0:T(8,128)(2,1)} %param.11) | copy-start | bytes 147460
  3.7 10.6 %copy-start.1 = (bf16[512,1536]{1,0:T(8,128)(2,1)S(1)}, bf16[512,1536]{1,0:T(8,128)(2,1)}, u32[]{:S(2)}) copy-start(bf16[512,1536]{1,0:T(8,128)(2,1)} %param.10) | copy-start | bytes 4718596
  6.9 29.4 %all-to-all-start = ((bf16[32,8,1664]{2,1,0:T(8,128)(2,1)}), bf16[32,8,1664]{2,1,0:T(8,128)(2,1)}, u32[]{:S(2)}, u32[]{:S(2)}) async-start(bf16[32,8,1664]{2,1,0:T(8,128)(2,1)} %maximum_bitcast_fusion), calls=%async_computation | async-start | bytes 1703936 | tf_op jit(solution)/shard_map/all_to_all | solution.py:105
  15.0 0.7 copy-start.27
  15.1 0.8 copy-start.29
  15.7 1.2 copy-start.10
  15.7 1.6 %copy-start.12 = (bf16[512,10,2,64]{0,3,2,1:T(8,128)(2,1)}, bf16[512,10,2,64]{0,3,2,1:T(8,128)(2,1)S(1)}, u32[]{:S(2)}) copy-start(bf16[512,10,2,64]{0,3,2,1:T(8,128)(2,1)S(1)} %get-tuple-element.53) | copy-start | bytes 3932164
  15.7 2.0 %copy-start.14 = (bf16[512,10,2,64]{0,3,2,1:T(8,128)(2,1)}, bf16[512,10,2,64]{0,3,2,1:T(8,128)(2,1)S(1)}, u32[]{:S(2)}) copy-start(bf16[512,10,2,64]{0,3,2,1:T(8,128)(2,1)S(1)} %get-tuple-element.54) | copy-start | bytes 3932164
  17.7 2.3 %copy-start.2 = (f32[512,10,2,128]{0,3,2,1:T(8,128)}, f32[512,10,2,128]{0,3,2,1:T(8,128)S(1)}, u32[]{:S(2)}) copy-start(f32[512,10,2,128]{0,3,2,1:T(8,128)S(1)} %broadcast_add_fusion) | copy-start | bytes 15728644
  17.7 2.3 %copy-start.26 = (bf16[64,64]{1,0:T(8,128)(2,1)S(1)}, bf16[64,64]{1,0:T(8,128)(2,1)}, u32[]{:S(2)}) copy-start(bf16[64,64]{1,0:T(8,128)(2,1)} %param.13) | copy-start | bytes 24580
  20.0 1.1 copy-start.3
  39.1 0.9 copy-start.20
  39.1 1.1 copy-start.22
  39.1 1.3 copy-start.24
  40.3 1.5 %copy-start.5 = (f32[256,10,2,128]{0,3,2,1:T(8,128)}, f32[256,10,2,128]{0,3,2,1:T(8,128)S(1)}, u32[]{:S(2)}) copy-start(f32[256,10,2,128]{0,3,2,1:T(8,128)S(1)} %convolution_add_fusion.4) | copy-start | bytes 7864324
  40.3 0.8 copy-start.28
  40.7 1.4 copy-start.7
  43.3 21.5 %all-to-all-start.1 = ((bf16[32,8,1280]{2,1,0:T(8,128)(2,1)}), bf16[32,8,1280]{2,1,0:T(8,128)(2,1)S(1)}, u32[]{:S(2)}, u32[]{:S(2)}) async-start(bf16[32,8,1280]{2,1,0:T(8,128)(2,1)} %fusion.14), calls=%async_computation.1 | async-start | bytes 1310720 | tf_op jit(solution)/shard_map/all_to_all | solution.py:129
  70.3 21.4 %all-to-all-start.2 = ((bf16[32,8,1280]{2,1,0:T(8,128)(2,1)}), bf16[32,8,1280]{2,1,0:T(8,128)(2,1)S(1)}, u32[]{:S(2)}, u32[]{:S(2)}) async-start(bf16[32,8,1280]{2,1,0:T(8,128)(2,1)} %fusion.15), calls=%async_computation.2 | async-start | bytes 1310720 | tf_op jit(solution)/shard_map/all_to_all | solution.py:136
  93.6 1.7 %copy-start.6 = (f32[256,10,2,128]{0,3,2,1:T(8,128)S(1)}, f32[256,10,2,128]{0,3,2,1:T(8,128)}, u32[]{:S(2)}) copy-start(f32[256,10,2,128]{0,3,2,1:T(8,128)} %copy-done.5) | copy-start | bytes 7864324
  95.3 1.7 %copy-start.18 = (bf16[256,10,2,64]{0,3,2,1:T(8,128)(2,1)}, bf16[256,10,2,64]{0,3,2,1:T(8,128)(2,1)S(1)}, u32[]{:S(2)}) copy-start(bf16[256,10,2,64]{0,3,2,1:T(8,128)(2,1)S(1)} %convert_element_type.131) | copy-start | bytes 1966084
  97.1 21.4 %all-to-all-start.3 = ((bf16[32,8,1280]{2,1,0:T(8,128)(2,1)}), bf16[32,8,1280]{2,1,0:T(8,128)(2,1)S(1)}, u32[]{:S(2)}, u32[]{:S(2)}) async-start(bf16[32,8,1280]{2,1,0:T(8,128)(2,1)} %bitcast.112), calls=%async_computation.3 | async-start | bytes 1310720 | tf_op jit(solution)/shard_map/all_to_all | solution.py:145
  104.4 4.3 %copy-start.16 = (bf16[256,10,2,64]{0,3,2,1:T(8,128)(2,1)S(1)}, bf16[256,10,2,64]{0,3,2,1:T(8,128)(2,1)}, u32[]{:S(2)}) copy-start(bf16[256,10,2,64]{0,3,2,1:T(8,128)(2,1)} %get-tuple-element.48) | copy-start | bytes 1966084
  104.4 4.3 %copy-start.17 = (bf16[256,10,2,64]{0,3,2,1:T(8,128)(2,1)S(1)}, bf16[256,10,2,64]{0,3,2,1:T(8,128)(2,1)}, u32[]{:S(2)}) copy-start(bf16[256,10,2,64]{0,3,2,1:T(8,128)(2,1)} %get-tuple-element.49) | copy-start | bytes 1966084
  108.7 1.1 copy-start.8
  108.7 1.3 copy-start.19
  108.8 1.6 %copy-start.21 = (bf16[256,10,2,64]{0,3,2,1:T(8,128)(2,1)S(1)}, bf16[256,10,2,64]{0,3,2,1:T(8,128)(2,1)}, u32[]{:S(2)}) copy-start(bf16[256,10,2,64]{0,3,2,1:T(8,128)(2,1)} %copy-done.20) | copy-start | bytes 1966084
  108.8 1.6 %copy-start.23 = (bf16[256,10,2,64]{0,3,2,1:T(8,128)(2,1)S(1)}, bf16[256,10,2,64]{0,3,2,1:T(8,128)(2,1)}, u32[]{:S(2)}) copy-start(bf16[256,10,2,64]{0,3,2,1:T(8,128)(2,1)} %copy-done.22) | copy-start | bytes 1966084
  108.8 1.8 %copy-start.25 = (bf16[256,10,2,64]{0,3,2,1:T(8,128)(2,1)S(1)}, bf16[256,10,2,64]{0,3,2,1:T(8,128)(2,1)}, u32[]{:S(2)}) copy-start(bf16[256,10,2,64]{0,3,2,1:T(8,128)(2,1)} %copy-done.24) | copy-start | bytes 1966084
  110.6 1.3 copy-start.4
  110.6 1.7 %copy-start.9 = (bf16[512,1280]{0,1:T(8,128)(2,1)S(1)}, bf16[512,1280]{0,1:T(8,128)(2,1)}, u32[]{:S(2)}) copy-start(bf16[512,1280]{0,1:T(8,128)(2,1)} %copy.71) | copy-start | bytes 3932164
  110.6 2.2 %copy-start.15 = (bf16[512,10,2,64]{0,3,2,1:T(8,128)(2,1)S(1)}, bf16[512,10,2,64]{0,3,2,1:T(8,128)(2,1)}, u32[]{:S(2)}) copy-start(bf16[512,10,2,64]{0,3,2,1:T(8,128)(2,1)} %copy-done.14) | copy-start | bytes 3932164
  112.3 1.4 copy-start.11
  112.3 1.8 %copy-start.13 = (bf16[512,10,2,64]{0,3,2,1:T(8,128)(2,1)S(1)}, bf16[512,10,2,64]{0,3,2,1:T(8,128)(2,1)}, u32[]{:S(2)}) copy-start(bf16[512,10,2,64]{0,3,2,1:T(8,128)(2,1)} %copy-done.12) | copy-start | bytes 3932164
  119.3 3.3 %collective-permute-start = (f32[28800]{0:T(1024)}, f32[28800]{0:T(1024)}, u32[]{:S(2)}, u32[]{:S(2)}) collective-permute-start(f32[28800]{0:T(1024)} %pad_maximum_fusion.4), channel_id=1, source_target_pairs={{0,1},{1,0},{2,3},{3,2},{4,5},{5,4},{6,7},{7,6},{8,9},{9,8},{10,11... | collective-permute-start | bytes 345608 | tf_op jit(solution)/shard_map/ppermute | solution.py:24
  123.5 5.7 %collective-permute-start.1 = (f32[28800]{0:T(1024)S(1)}, f32[28800]{0:T(1024)S(1)}, u32[]{:S(2)}, u32[]{:S(2)}) collective-permute-start(f32[28800]{0:T(1024)S(1)} %fusion.99), channel_id=1, source_target_pairs={{0,2},{1,3},{2,0},{3,1},{4,6},{5,7},{6,4},{7,5},{8,10},{9,11},{10,... | collective-permute-start | bytes 345608 | tf_op jit(solution)/shard_map/ppermute | solution.py:24
  129.2 5.0 %collective-permute-start.2 = (f32[28800]{0:T(1024)S(1)}, f32[28800]{0:T(1024)S(1)}, u32[]{:S(2)}, u32[]{:S(2)}) collective-permute-start(f32[28800]{0:T(1024)S(1)} %add.147), channel_id=1, source_target_pairs={{0,4},{1,5},{2,6},{3,7},{4,0},{5,1},{6,2},{7,3},{8,12},{9,13},{10,... | collective-permute-start | bytes 345608 | tf_op jit(solution)/shard_map/ppermute | solution.py:24
  134.1 4.9 %collective-permute-start.3 = (f32[28800]{0:T(1024)S(1)}, f32[28800]{0:T(1024)S(1)}, u32[]{:S(2)}, u32[]{:S(2)}) collective-permute-start(f32[28800]{0:T(1024)S(1)} %add.148), channel_id=1, source_target_pairs={{0,8},{1,9},{2,10},{3,11},{4,12},{5,13},{6,14},{7,15},{8,0},{9,1},... | collective-permute-start | bytes 345608 | tf_op jit(solution)/shard_map/ppermute | solution.py:24
  139.1 5.8 %collective-permute-start.4 = (f32[28800]{0:T(1024)S(1)}, f32[28800]{0:T(1024)S(1)}, u32[]{:S(2)}, u32[]{:S(2)}) collective-permute-start(f32[28800]{0:T(1024)S(1)} %add.149), channel_id=1, source_target_pairs={{0,16},{1,17},{2,18},{3,19},{4,20},{5,21},{6,22},{7,23},{8,24},{9,... | collective-permute-start | bytes 345608 | tf_op jit(solution)/shard_map/ppermute | solution.py:24

commit v12 on v11

--- a/solution.py
+++ b/solution.py
@@ -91,6 +91,16 @@
     )
     degree = (MEM + jnp.sum(members, axis=1))[:, None]
     members = members.astype(jnp.bfloat16)
+    valid = (slotted_segment >= 0)[:, None]
+    slot_deg = jnp.where(
+        valid, jnp.einsum("sn,sk->nk", members, degree.astype(jnp.bfloat16), preferred_element_type=jnp.float32), 1.0
+    )
+    slot_inner = jnp.einsum(
+        "es,sn->ne", incidence, members, preferred_element_type=jnp.float32
+    ).astype(jnp.bfloat16)
+    slot_same = jnp.einsum(
+        "sn,sm->nm", members, members, preferred_element_type=jnp.float32
+    ).astype(jnp.bfloat16)
     def pick_slots(rows):
         return jnp.einsum("sn,sf->nf", members, rows, preferred_element_type=jnp.float32).astype(
             jnp.bfloat16
@@ -132,7 +142,15 @@
     block_out = (y * sig_y).astype(jnp.bfloat16)
     dy = cotangent.astype(jnp.float32) * sig_y * (1.0 + y * (1.0 - sig_y))
     grad_rows = (dy / degree).astype(jnp.bfloat16)
-    send_grads = pick_slots(grad_rows)
+    slot_y = (
+        jnp.dot(slot_inner, edge_val, preferred_element_type=jnp.float32)
+        + jnp.dot(slot_same, back, preferred_element_type=jnp.float32)
+    ) / slot_deg
+    slot_sig = jax.nn.sigmoid(slot_y)
+    slot_dy = pick_slots(cotangent).astype(jnp.float32) * slot_sig * (
+        1.0 + slot_y * (1.0 - slot_sig)
+    )
+    send_grads = (slot_dy / slot_deg).astype(jnp.bfloat16)
     recv_grads = lax.all_to_all(
         send_grads, ("region", "sub"), split_axis=0, concat_axis=0, tiled=True
     )

time: 148 us -> 150 us (1.014)
  matrix products: 32.3 us -> 38.9 us
  waiting for transfers between devices: 57.3 us -> 52.7 us
    dot_general x0 -> x3, matrix products: none -> 5.04 us  [the longest x1 3.18 us: body(): jnp.dot(slot_same, back, preferred_element_type=jnp.float32)]
    all_to_all x1, waiting for transfers between devices: 17.6 us -> 13.1 us  [body(): lax.all_to_all(send_grads, ('region', 'sub'), split_axis=0, concat_axis=0...]
    dot_general x2, matrix products: 3.5 us -> 5.36 us  [pick_slots(): jnp.einsum('sn,sf->nf', members, rows, preferred_element_type=jnp.float32)]
    dot_general x1, matrix products: 2.13 us -> 0.54 us  [member_side(): jnp.einsum('es,ef->sf', incidence, values, preferred_element_type=jnp.flo...]
    unnamed x62 -> x64, local copies, waits for them, and re-layouts: 10.9 us -> 11.1 us
  transfers between devices with their start and end apart: 9 -> 9, of which waited for: 8 -> 8; matrix products, arithmetic and copies ran while one was open for 21% -> 23% of each run, Pallas kernels for 0% -> 0%
where the time goes in v12:
time: 150 us; the launch traced here: 149 us
  waiting for transfers between devices  52.7 us (35%)
  matrix products  38.9 us (26%)
  starting transfers between devices  24.3 us (16%)
  local copies, waits for them, and re-layouts  19.8 us (13%)
  other arithmetic  12.3 us (8%)
    all_to_all x1, waiting for transfers between devices, body(): lax.all_to_all(ret_rows, ('region', 'sub'), split_axis=0, concat_axis=0,...  15.3 us
    all_to_all x1, waiting for transfers between devices, body(): lax.all_to_all(send, ('region', 'sub'), split_axis=0, concat_axis=0, tile...  14.6 us
    all_to_all x1, waiting for transfers between devices, body(): lax.all_to_all(send_grads, ('region', 'sub'), split_axis=0, concat_axis=0...  13.1 us
    unnamed x64, local copies, waits for them, and re-layouts  11.1 us
    all_to_all x1, starting transfers between devices, body(): lax.all_to_all(send, ('region', 'sub'), split_axis=0, concat_axis=0, tile...  7.41 us
    ppermute x5, waiting for transfers between devices, device_sum(): flat = flat + lax.ppermute(flat, ('region', 'sub'), perm)  6.31 us
    dot_general x2, matrix products, weight_grads(): jnp.einsum('stbd,cd->stbc', dzr, theta, preferred_element_type=jnp.float32)  6.04 us
    ppermute x5, starting transfers between devices, device_sum(): flat = flat + lax.ppermute(flat, ('region', 'sub'), perm)  5.88 us
  transfers between devices with their start and end apart: 9, of which 8 were waited for; matrix products, arithmetic and copies ran while one was open for 23% of the time, Pallas kernels for 0%

profile of v12, /device:TPU:0, one launch (start us, length us, event | category | flops | bytes accessed | tf_op | source)
XLA Modules:
  0.0 149.1 jit_solution(11191589856635242809)
XLA Ops:
  0.6 0.7 broadcast_add_fusion.4
  1.3 0.7 broadcast_add_fusion.3
  2.0 0.9 convert_reduce_fusion.5
  2.9 0.7 fusion.117
  3.7 2.0 %convolution_convert_fusion.3 = bf16[256,1536]{1,0:T(8,128)(2,1)S(1)} fusion(bf16[512,1536]{1,0:T(8,128)(2,1)} %param.10, s32[256]{0:T(256)S(1)} %get-tuple-element.63), kind=kOutput, calls=%fused_computation.34 | convolution fusion | flops 403439616 | bytes 2360320 | tf_op jit(solution)/shard_map/sn,sf->nf/dot_general | solution.py:105
  5.8 1.0 maximum_bitcast_fusion
  6.8 7.4 %all-to-all-start = ((bf16[32,8,1664]{2,1,0:T(8,128)(2,1)}), bf16[32,8,1664]{2,1,0:T(8,128)(2,1)}, u32[]{:S(2)}, u32[]{:S(2)}) async-start(bf16[32,8,1664]{2,1,0:T(8,128)(2,1)} %maximum_bitcast_fusion), calls=%async_computation | async-start | bytes 1703936 | tf_op jit(solution)/shard_map/all_to_all | solution.py:115
  14.2 0.7 copy.66
  15.8 1.0 broadcast_add_fusion
  17.5 0.7 multiply_convert_fusion.5
  18.3 1.6 %copy-done.2 = f32[512,10,2,128]{0,3,2,1:T(8,128)} copy-done((f32[512,10,2,128]{0,3,2,1:T(8,128)}, f32[512,10,2,128]{0,3,2,1:T(8,128)S(1)}, u32[]{:S(2)}) %copy-start.2) | copy-done | bytes 5242904
  19.9 0.6 convolution_convert_fusion.4
  20.4 0.6 copy-done.3
  21.0 0.6 fusion.84
  21.6 14.6 %all-to-all-done = bf16[32,8,1664]{2,1,0:T(8,128)(2,1)} async-done(((bf16[32,8,1664]{2,1,0:T(8,128)(2,1)}), bf16[32,8,1664]{2,1,0:T(8,128)(2,1)}, u32[]{:S(2)}, u32[]{:S(2)}) %all-to-all-start) | async-done | bytes 852000 | tf_op jit(solution)/shard_map/all_to_all | solution.py:115
  36.2 1.0 convert_reduce_fusion.4
  37.2 1.2 slice.102
  39.0 0.6 convolution_add_fusion.5
  41.0 0.7 copy-done.5
  42.1 1.2 fusion.21
  43.3 3.7 %all-to-all-start.1 = ((bf16[32,8,1280]{2,1,0:T(8,128)(2,1)}), bf16[32,8,1280]{2,1,0:T(8,128)(2,1)}, u32[]{:S(2)}, u32[]{:S(2)}) async-start(bf16[32,8,1280]{2,1,0:T(8,128)(2,1)} %fusion.21), calls=%async_computation.1 | async-start | bytes 1310720 | tf_op jit(solution)/shard_map/all_to_all | solution.py:139
  47.4 1.7 %fusion.49 = f32[256,1280]{1,0:T(8,128)} fusion(bf16[128,1280]{1,0:T(8,128)(2,1)S(1)} %fusion.22, s32[256]{0:T(256)S(1)} %get-tuple-element.63, s32[512]{0:T(512)S(1)} %bitcast.131, s32[512]{0:T(512)S(1)} %bitcast.125), kind=kOutput, calls=%fused_computation.72 | convolution fusion | flops 118259712 | bytes 1643520 | tf_op jit(solution)/shard_map/dot_general | solution.py:146
  49.1 0.5 fusion.82
  49.6 15.3 %all-to-all-done.1 = bf16[32,8,1280]{2,1,0:T(8,128)(2,1)} async-done(((bf16[32,8,1280]{2,1,0:T(8,128)(2,1)}), bf16[32,8,1280]{2,1,0:T(8,128)(2,1)}, u32[]{:S(2)}, u32[]{:S(2)}) %all-to-all-start.1) | async-done | bytes 655392 | tf_op jit(solution)/shard_map/all_to_all | solution.py:139
  64.9 3.2 %fusion.4 = f32[256,1280]{1,0:T(8,128)} fusion(f32[256,1280]{1,0:T(8,128)} %fusion.49, bf16[32,8,1280]{2,1,0:T(8,128)(2,1)} %all-to-all-done.1, f32[256]{0:T(256)S(1)} %compare_select_fusion, s32[256]{0:T(256)S(1)} %get-tuple-element.63), kind=kOutput, calls=%fused_computation.10 | convolution fusion | flops 235995136 | bytes 3278848 | tf_op jit(solution)/shard_map/dot_general | solution.py:147
  68.1 3.4 %fusion.20 = bf16[32,8,1280]{2,1,0:T(8,128)(2,1)} fusion(bf16[512,1280]{1,0:T(8,128)(2,1)} %param.19, f32[256,1280]{1,0:T(8,128)} %fusion.4, f32[256]{0:T(256)S(1)} %compare_select_fusion, s32[256]{0:T(256)S(1)} %get-tuple-element.63), kind=kOutput, calls=%fused_computation.44 | convolution fusion | flops 339869696 | bytes 3278848 | tf_op jit(solution)/shard_map/sn,sf->nf/dot_general | solution.py:105
  71.5 3.8 %all-to-all-start.2 = ((bf16[32,8,1280]{2,1,0:T(8,128)(2,1)}), bf16[32,8,1280]{2,1,0:T(8,128)(2,1)}, u32[]{:S(2)}, u32[]{:S(2)}) async-start(bf16[32,8,1280]{2,1,0:T(8,128)(2,1)} %fusion.20), calls=%async_computation.2 | async-start | bytes 1310720 | tf_op jit(solution)/shard_map/all_to_all | solution.py:154
  75.3 3.2 %multiply_convert_fusion.4 = (bf16[512,1280]{1,0:T(8,128)(2,1)}, f32[512,1280]{1,0:T(8,128)S(1)}) fusion(f32[512]{0:T(512)S(1)} %get-tuple-element.59, f32[512,1280]{1,0:T(8,128)S(1)} %fusion.82, bf16[32,8,1280]{2,1,0:T(8,128)(2,1)} %all-to-all-done.1, s32[256]{0:T(256)S(1)} %get-tuple-element.63), kind=kOutput, calls=%fused_computation.27 | convolution fusion | flops 340525056 | bytes 7212032 | tf_op jit(solution)/shard_map/dot_general | solution.py:136
  78.5 1.4 fusion.33
  79.9 13.1 %all-to-all-done.2 = bf16[32,8,1280]{2,1,0:T(8,128)(2,1)} async-done(((bf16[32,8,1280]{2,1,0:T(8,128)(2,1)}), bf16[32,8,1280]{2,1,0:T(8,128)(2,1)}, u32[]{:S(2)}, u32[]{:S(2)}) %all-to-all-start.2) | async-done | bytes 655392 | tf_op jit(solution)/shard_map/all_to_all | solution.py:154
  93.0 1.3 fusion.23
  94.4 1.2 convolution_convert_fusion
  95.9 0.5 fusion.77
  96.6 1.1 copy-done.6
  97.7 1.7 %multiply_convert_fusion.7 = (bf16[256,10,2,64]{0,3,2,1:T(8,128)(2,1)}, bf16[256,10,2,64]{0,3,2,1:T(8,128)(2,1)}) fusion(f32[256,10,2,128]{0,3,2,1:T(8,128)S(1)} %copy-done.6, bf16[256,10,2,64]{0,3,2,1:T(8,128)(2,1)S(1)} %convert_element_type.154, bf16[64,64]{1,0:T(8,128)(2,1)S(1)} %copy-done.26), kind=kOutput, calls=%fused_computation.64 | convolution fusion | flops 45219840 | bytes 4595712 | tf_op jit(solution)/shard_map/stbd,cd->stbc/dot_general | solution.py:169
  99.4 3.5 %all-to-all-start.3 = ((bf16[32,8,1280]{2,1,0:T(8,128)(2,1)}), bf16[32,8,1280]{2,1,0:T(8,128)(2,1)S(1)}, u32[]{:S(2)}, u32[]{:S(2)}) async-start(bf16[32,8,1280]{2,1,0:T(8,128)(2,1)} %bitcast.116), calls=%async_computation.3 | async-start | bytes 1310720 | tf_op jit(solution)/shard_map/all_to_all | solution.py:163
  102.9 1.2 convert_element_type.156
  104.1 2.4 %copy.71 = bf16[512,1280]{0,1:T(8,128)(2,1)} copy(bf16[512,1280]{1,0:T(8,128)(2,1)} %convert_element_type.156) | data formatting | bytes 2621440 | tf_op jit(solution)/shard_map/convert_element_type | solution.py:175
  106.6 4.3 %multiply_convert_fusion.3 = (bf16[512,10,2,64]{0,3,2,1:T(8,128)(2,1)S(1)}, bf16[512,10,2,64]{0,3,2,1:T(8,128)(2,1)S(1)}) fusion(f32[512,10,2,128]{0,3,2,1:T(8,128)} %copy-done.2, bf16[512,10,2,64]{0,3,2,1:T(8,128)(2,1)} %bitcast.118, bf16[64,64]{1,0:T(8,128)(2,1)S(1)} %copy-done.26), kind=kOutput, calls=%fused_computation.25 | convolution fusion | flops 90439680 | bytes 9183232 | tf_op jit(solution)/shard_map/stbd,cd->stbc/dot_general | solution.py:169
  112.8 0.7 fusion.34
  113.5 0.6 copy-done.4
  114.6 0.5 fusion.55
  115.1 0.9 copy-done.11
  116.4 1.2 fusion.44
  117.6 3.3 %all-to-all-done.3 = bf16[32,8,1280]{2,1,0:T(8,128)(2,1)S(1)} async-done(((bf16[32,8,1280]{2,1,0:T(8,128)(2,1)}), bf16[32,8,1280]{2,1,0:T(8,128)(2,1)S(1)}, u32[]{:S(2)}, u32[]{:S(2)}) %all-to-all-start.3) | async-done | bytes 655392 | tf_op jit(solution)/shard_map/all_to_all | solution.py:163
  120.9 0.7 pad_maximum_fusion.4
  121.7 1.6 %fusion.3 = bf16[512,1280]{1,0:T(8,128)(2,1)} fusion(f32[512,1280]{1,0:T(8,128)S(1)} %fusion.77, bf16[256,1280]{1,0:T(8,128)(2,1)S(1)} %bitcast.115, s32[256]{0:T(256)S(1)} %get-tuple-element.63), kind=kOutput, calls=%fused_computation.8 | convolution fusion | flops 337248256 | bytes 4588544 | tf_op jit(solution)/shard_map/dot_general | solution.py:182
  123.3 1.6 %copy.80 = bf16[512,1280]{0,1:T(8,128)(2,1)S(1)} copy(bf16[512,1280]{1,0:T(8,128)(2,1)} %fusion.3) | data formatting | bytes 2621440 | tf_op jit(solution)/shard_map/convert_element_type | solution.py:183
  124.9 0.9 fusion.121
  125.8 1.7 %collective-permute-start.1 = (f32[28800]{0:T(1024)S(1)}, f32[28800]{0:T(1024)S(1)}, u32[]{:S(2)}, u32[]{:S(2)}) collective-permute-start(f32[28800]{0:T(1024)S(1)} %fusion.121), channel_id=1, source_target_pairs={{0,2},{1,3},{2,0},{3,1},{4,6},{5,7},{6,4},{7,5},{8,10},{9,11},{10,... | collective-permute-start | bytes 345608 | tf_op jit(solution)/shard_map/ppermute | solution.py:24
  127.5 3.8 %multiply_convert_fusion.1 = (bf16[512,10,2,64]{0,3,2,1:T(8,128)(2,1)S(1)}, bf16[512,10,2,64]{0,3,2,1:T(8,128)(2,1)S(1)}) fusion(f32[512,10,2,128]{0,3,2,1:T(8,128)} %copy-done.2, bf16[512,10,2,64]{0,3,2,1:T(8,128)(2,1)S(1)} %bitcast.120, bf16[64,64]{1,0:T(8,128)(2,1)S(1)} %copy-done.26), kind=kOutput, calls=%fused_computation.22 | convolution fusion | flops 90439680 | bytes 9183232 | tf_op jit(solution)/shard_map/stbd,cd->stbc/dot_general | solution.py:186
  131.5 1.5 collective-permute-start.2
  133.0 1.2 fusion.8
  134.1 2.3 %collective-permute-done.2 = f32[28800]{0:T(1024)S(1)} collective-permute-done((f32[28800]{0:T(1024)S(1)}, f32[28800]{0:T(1024)S(1)}, u32[]{:S(2)}, u32[]{:S(2)}) %collective-permute-start.2) | collective-permute-done | bytes 115232 | tf_op jit(solution)/shard_map/ppermute | solution.py:24
  136.5 1.5 collective-permute-start.3
  137.9 1.6 %fusion.122 = (f32[512,10,2,64]{0,3,2,1:T(8,128)S(1)}, f32[512,10,2,64]{0,3,2,1:T(8,128)S(1)}, f32[512,10,2,64]{0,3,2,1:T(8,128)S(1)}) fusion(f32[512,10,2,192]{0,3,2,1:T(8,128)S(1)} %fusion.8), kind=kLoop, calls=%fused_computation.156 | loop fusion | bytes 15728640 | tf_op jit(solution)/shard_map/slice | solution.py:195
  139.6 1.8 %collective-permute-done.3 = f32[28800]{0:T(1024)S(1)} collective-permute-done((f32[28800]{0:T(1024)S(1)}, f32[28800]{0:T(1024)S(1)}, u32[]{:S(2)}, u32[]{:S(2)}) %collective-permute-start.3) | collective-permute-done | bytes 115232 | tf_op jit(solution)/shard_map/ppermute | solution.py:24
  141.4 1.2 collective-permute-start.4
  142.6 1.0 add_convert_fusion
  143.6 1.6 %copy.82 = bf16[512,1536]{1,0:T(8,128)(2,1)} copy(bf16[512,1536]{0,1:T(8,128)(2,1)S(1)} %bitcast.112) | data formatting | bytes 3145728
  145.2 2.0 %collective-permute-done.4 = f32[28800]{0:T(1024)S(1)} collective-permute-done((f32[28800]{0:T(1024)S(1)}, f32[28800]{0:T(1024)S(1)}, u32[]{:S(2)}, u32[]{:S(2)}) %collective-permute-start.4) | collective-permute-done | bytes 115232 | tf_op jit(solution)/shard_map/ppermute | solution.py:24
  147.2 0.5 slice_multiply_fusion.2
  147.7 0.6 fusion.99
  148.4 0.7 mul.161
  (89 shorter events, 8.0 us)
Async XLA Ops:
  0.6 15.1 %copy-start = (bf16[192,128]{1,0:T(8,128)(2,1)S(1)}, bf16[192,128]{1,0:T(8,128)(2,1)}, u32[]{:S(2)}) copy-start(bf16[192,128]{1,0:T(8,128)(2,1)} %param.11) | copy-start | bytes 147460
  5.7 8.5 %copy-start.1 = (bf16[512,1536]{1,0:T(8,128)(2,1)S(1)}, bf16[512,1536]{1,0:T(8,128)(2,1)}, u32[]{:S(2)}) copy-start(bf16[512,1536]{1,0:T(8,128)(2,1)} %param.10) | copy-start | bytes 4718596
  6.8 29.4 %all-to-all-start = ((bf16[32,8,1664]{2,1,0:T(8,128)(2,1)}), bf16[32,8,1664]{2,1,0:T(8,128)(2,1)}, u32[]{:S(2)}, u32[]{:S(2)}) async-start(bf16[32,8,1664]{2,1,0:T(8,128)(2,1)} %maximum_bitcast_fusion), calls=%async_computation | async-start | bytes 1703936 | tf_op jit(solution)/shard_map/all_to_all | solution.py:115
  14.9 0.7 copy-start.27
  14.9 0.8 copy-start.30
  15.6 1.2 copy-start.10
  15.6 1.6 %copy-start.12 = (bf16[512,10,2,64]{0,3,2,1:T(8,128)(2,1)}, bf16[512,10,2,64]{0,3,2,1:T(8,128)(2,1)S(1)}, u32[]{:S(2)}) copy-start(bf16[512,10,2,64]{0,3,2,1:T(8,128)(2,1)S(1)} %get-tuple-element.51) | copy-start | bytes 3932164
  15.6 1.9 %copy-start.14 = (bf16[512,10,2,64]{0,3,2,1:T(8,128)(2,1)}, bf16[512,10,2,64]{0,3,2,1:T(8,128)(2,1)S(1)}, u32[]{:S(2)}) copy-start(bf16[512,10,2,64]{0,3,2,1:T(8,128)(2,1)S(1)} %get-tuple-element.52) | copy-start | bytes 3932164
  17.5 2.3 %copy-start.2 = (f32[512,10,2,128]{0,3,2,1:T(8,128)}, f32[512,10,2,128]{0,3,2,1:T(8,128)S(1)}, u32[]{:S(2)}) copy-start(f32[512,10,2,128]{0,3,2,1:T(8,128)S(1)} %broadcast_add_fusion) | copy-start | bytes 15728644
  17.5 2.3 %copy-start.26 = (bf16[64,64]{1,0:T(8,128)(2,1)S(1)}, bf16[64,64]{1,0:T(8,128)(2,1)}, u32[]{:S(2)}) copy-start(bf16[64,64]{1,0:T(8,128)(2,1)} %param.13) | copy-start | bytes 24580
  19.9 1.1 copy-start.3
  38.9 0.8 copy-start.20
  39.0 1.1 copy-start.22
  39.0 1.2 copy-start.24
  40.2 1.5 %copy-start.5 = (f32[256,10,2,128]{0,3,2,1:T(8,128)}, f32[256,10,2,128]{0,3,2,1:T(8,128)S(1)}, u32[]{:S(2)}) copy-start(f32[256,10,2,128]{0,3,2,1:T(8,128)S(1)} %convolution_add_fusion.5) | copy-start | bytes 7864324
  40.2 1.5 %copy-start.28 = (f32[128]{0:T(128)S(1)}, f32[128]{0:T(128)}, u32[]{:S(2)}) copy-start(f32[128]{0:T(128)} %param.14) | copy-start | bytes 1540
  40.6 1.5 %copy-start.7 = (bf16[256,10,2,64]{0,3,2,1:T(8,128)(2,1)}, bf16[256,10,2,64]{0,3,2,1:T(8,128)(2,1)S(1)}, u32[]{:S(2)}) copy-start(bf16[256,10,2,64]{0,3,2,1:T(8,128)(2,1)S(1)} %multiply_convert_fusion.8) | copy-start | bytes 1966084
  43.3 21.7 %all-to-all-start.1 = ((bf16[32,8,1280]{2,1,0:T(8,128)(2,1)}), bf16[32,8,1280]{2,1,0:T(8,128)(2,1)}, u32[]{:S(2)}, u32[]{:S(2)}) async-start(bf16[32,8,1280]{2,1,0:T(8,128)(2,1)} %fusion.21), calls=%async_computation.1 | async-start | bytes 1310720 | tf_op jit(solution)/shard_map/all_to_all | solution.py:139
  71.5 21.5 %all-to-all-start.2 = ((bf16[32,8,1280]{2,1,0:T(8,128)(2,1)}), bf16[32,8,1280]{2,1,0:T(8,128)(2,1)}, u32[]{:S(2)}, u32[]{:S(2)}) async-start(bf16[32,8,1280]{2,1,0:T(8,128)(2,1)} %fusion.20), calls=%async_computation.2 | async-start | bytes 1310720 | tf_op jit(solution)/shard_map/all_to_all | solution.py:154
  75.3 3.2 %copy-start.29 = (bf16[512,1280]{1,0:T(8,128)(2,1)S(1)}, bf16[512,1280]{1,0:T(8,128)(2,1)}, u32[]{:S(2)}) copy-start(bf16[512,1280]{1,0:T(8,128)(2,1)} %param.19) | copy-start | bytes 3932164
  95.9 1.7 %copy-start.6 = (f32[256,10,2,128]{0,3,2,1:T(8,128)S(1)}, f32[256,10,2,128]{0,3,2,1:T(8,128)}, u32[]{:S(2)}) copy-start(f32[256,10,2,128]{0,3,2,1:T(8,128)} %copy-done.5) | copy-start | bytes 7864324
  97.7 1.7 %copy-start.18 = (bf16[256,10,2,64]{0,3,2,1:T(8,128)(2,1)}, bf16[256,10,2,64]{0,3,2,1:T(8,128)(2,1)S(1)}, u32[]{:S(2)}) copy-start(bf16[256,10,2,64]{0,3,2,1:T(8,128)(2,1)S(1)} %convert_element_type.154) | copy-start | bytes 1966084
  99.4 21.4 %all-to-all-start.3 = ((bf16[32,8,1280]{2,1,0:T(8,128)(2,1)}), bf16[32,8,1280]{2,1,0:T(8,128)(2,1)S(1)}, u32[]{:S(2)}, u32[]{:S(2)}) async-start(bf16[32,8,1280]{2,1,0:T(8,128)(2,1)} %bitcast.116), calls=%async_computation.3 | async-start | bytes 1310720 | tf_op jit(solution)/shard_map/all_to_all | solution.py:163
  106.6 4.3 %copy-start.16 = (bf16[256,10,2,64]{0,3,2,1:T(8,128)(2,1)S(1)}, bf16[256,10,2,64]{0,3,2,1:T(8,128)(2,1)}, u32[]{:S(2)}) copy-start(bf16[256,10,2,64]{0,3,2,1:T(8,128)(2,1)} %get-tuple-element.48) | copy-start | bytes 1966084
  106.6 4.3 %copy-start.17 = (bf16[256,10,2,64]{0,3,2,1:T(8,128)(2,1)S(1)}, bf16[256,10,2,64]{0,3,2,1:T(8,128)(2,1)}, u32[]{:S(2)}) copy-start(bf16[256,10,2,64]{0,3,2,1:T(8,128)(2,1)} %get-tuple-element.49) | copy-start | bytes 1966084
  110.9 1.1 copy-start.8
  110.9 1.3 copy-start.19
  111.2 1.3 copy-start.21
  111.2 1.5 copy-start.23
  111.2 1.6 %copy-start.25 = (bf16[256,10,2,64]{0,3,2,1:T(8,128)(2,1)S(1)}, bf16[256,10,2,64]{0,3,2,1:T(8,128)(2,1)}, u32[]{:S(2)}) copy-start(bf16[256,10,2,64]{0,3,2,1:T(8,128)(2,1)} %copy-done.24) | copy-start | bytes 1966084
  112.8 1.3 copy-start.4
  112.8 1.7 %copy-start.9 = (bf16[512,1280]{0,1:T(8,128)(2,1)S(1)}, bf16[512,1280]{0,1:T(8,128)(2,1)}, u32[]{:S(2)}) copy-start(bf16[512,1280]{0,1:T(8,128)(2,1)} %copy.71) | copy-start | bytes 3932164
  112.8 2.2 %copy-start.15 = (bf16[512,10,2,64]{0,3,2,1:T(8,128)(2,1)S(1)}, bf16[512,10,2,64]{0,3,2,1:T(8,128)(2,1)}, u32[]{:S(2)}) copy-start(bf16[512,10,2,64]{0,3,2,1:T(8,128)(2,1)} %copy-done.14) | copy-start | bytes 3932164
  114.6 1.4 copy-start.11
  114.6 1.8 %copy-start.13 = (bf16[512,10,2,64]{0,3,2,1:T(8,128)(2,1)S(1)}, bf16[512,10,2,64]{0,3,2,1:T(8,128)(2,1)}, u32[]{:S(2)}) copy-start(bf16[512,10,2,64]{0,3,2,1:T(8,128)(2,1)} %copy-done.12) | copy-start | bytes 3932164
  121.6 3.3 %collective-permute-start = (f32[28800]{0:T(1024)}, f32[28800]{0:T(1024)}, u32[]{:S(2)}, u32[]{:S(2)}) collective-permute-start(f32[28800]{0:T(1024)} %pad_maximum_fusion.4), channel_id=1, source_target_pairs={{0,1},{1,0},{2,3},{3,2},{4,5},{5,4},{6,7},{7,6},{8,9},{9,8},{10,11... | collective-permute-start | bytes 345608 | tf_op jit(solution)/shard_map/ppermute | solution.py:24
  125.8 5.7 %collective-permute-start.1 = (f32[28800]{0:T(1024)S(1)}, f32[28800]{0:T(1024)S(1)}, u32[]{:S(2)}, u32[]{:S(2)}) collective-permute-start(f32[28800]{0:T(1024)S(1)} %fusion.121), channel_id=1, source_target_pairs={{0,2},{1,3},{2,0},{3,1},{4,6},{5,7},{6,4},{7,5},{8,10},{9,11},{10,... | collective-permute-start | bytes 345608 | tf_op jit(solution)/shard_map/ppermute | solution.py:24
  131.5 5.0 %collective-permute-start.2 = (f32[28800]{0:T(1024)S(1)}, f32[28800]{0:T(1024)S(1)}, u32[]{:S(2)}, u32[]{:S(2)}) collective-permute-start(f32[28800]{0:T(1024)S(1)} %add.161), channel_id=1, source_target_pairs={{0,4},{1,5},{2,6},{3,7},{4,0},{5,1},{6,2},{7,3},{8,12},{9,13},{10,... | collective-permute-start | bytes 345608 | tf_op jit(solution)/shard_map/ppermute | solution.py:24
  136.5 4.9 %collective-permute-start.3 = (f32[28800]{0:T(1024)S(1)}, f32[28800]{0:T(1024)S(1)}, u32[]{:S(2)}, u32[]{:S(2)}) collective-permute-start(f32[28800]{0:T(1024)S(1)} %add.162), channel_id=1, source_target_pairs={{0,8},{1,9},{2,10},{3,11},{4,12},{5,13},{6,14},{7,15},{8,0},{9,1},... | collective-permute-start | bytes 345608 | tf_op jit(solution)/shard_map/ppermute | solution.py:24
  141.4 5.8 %collective-permute-start.4 = (f32[28800]{0:T(1024)S(1)}, f32[28800]{0:T(1024)S(1)}, u32[]{:S(2)}, u32[]{:S(2)}) collective-permute-start(f32[28800]{0:T(1024)S(1)} %add.163), channel_id=1, source_target_pairs={{0,16},{1,17},{2,18},{3,19},{4,20},{5,21},{6,22},{7,23},{8,24},{9,... | collective-permute-start | bytes 345608 | tf_op jit(solution)/shard_map/ppermute | solution.py:24

commit v13 on v11

--- a/solution.py
+++ b/solution.py
@@ -18,11 +18,11 @@
     if n & (n - 1):
         flat = lax.psum(flat, ("region", "sub"))
     else:
-        step = 1
-        while step < n:
+        step = n // 2
+        while step >= 1:
             perm = [(i, i ^ step) for i in range(n)]
             flat = flat + lax.ppermute(flat, ("region", "sub"), perm)
-            step *= 2
+            step //= 2
     out, at = [], 0
     for p, size in zip(parts, sizes):
         out.append(flat[at : at + size].reshape(p.shape))

time: 148 us -> 149 us (level)
  waiting for transfers between devices: 57.3 us -> 60.8 us
  starting transfers between devices: 24.1 us -> 22.4 us
    ppermute x5, waiting for transfers between devices: 6.31 us -> 9.77 us  [device_sum(): flat = flat + lax.ppermute(flat, ('region', 'sub'), perm)]
    ppermute x5, starting transfers between devices: 5.88 us -> 4.12 us  [device_sum(): flat = flat + lax.ppermute(flat, ('region', 'sub'), perm)]
where the time goes in v13:
time: 149 us; the launch traced here: 148 us
  waiting for transfers between devices  60.8 us (41%)
  matrix products  32.3 us (22%)
  starting transfers between devices  22.4 us (15%)
  local copies, waits for them, and re-layouts  19.6 us (13%)
  other arithmetic  12.3 us (8%)
    all_to_all x1, waiting for transfers between devices, body(): lax.all_to_all(send_grads, ('region', 'sub'), split_axis=0, concat_axis=0...  17.6 us
    all_to_all x1, waiting for transfers between devices, body(): lax.all_to_all(ret_rows, ('region', 'sub'), split_axis=0, concat_axis=0,...  15.6 us
    all_to_all x1, waiting for transfers between devices, body(): lax.all_to_all(send, ('region', 'sub'), split_axis=0, concat_axis=0, tile...  14.6 us
    unnamed x62, local copies, waits for them, and re-layouts  10.9 us
    ppermute x5, waiting for transfers between devices, device_sum(): flat = flat + lax.ppermute(flat, ('region', 'sub'), perm)  9.77 us
    all_to_all x1, starting transfers between devices, body(): lax.all_to_all(send, ('region', 'sub'), split_axis=0, concat_axis=0, tile...  7.41 us
    dot_general x2, matrix products, weight_grads(): jnp.einsum('stbd,cd->stbc', dzr, theta, preferred_element_type=jnp.float32)  6.04 us
    ppermute x5, starting transfers between devices, device_sum(): flat = flat + lax.ppermute(flat, ('region', 'sub'), perm)  4.12 us
  transfers between devices with their start and end apart: 9, of which 8 were waited for; matrix products, arithmetic and copies ran while one was open for 21% of the time, Pallas kernels for 0%

profile of v13, /device:TPU:0, one launch (start us, length us, event | category | flops | bytes accessed | tf_op | source)
XLA Modules:
  0.0 148.5 jit_solution(10192637037285179807)
XLA Ops:
  0.6 0.7 broadcast_add_fusion.4
  1.3 0.7 broadcast_add_fusion.3
  2.0 0.9 convert_reduce_fusion.5
  2.9 0.7 fusion.97
  3.7 2.1 %convolution_convert_fusion.3 = bf16[256,1536]{1,0:T(8,128)(2,1)S(1)} fusion(bf16[512,1536]{1,0:T(8,128)(2,1)} %param.10, s32[256]{0:T(256)S(1)} %get-tuple-element.61), kind=kOutput, calls=%fused_computation.32 | convolution fusion | flops 403439616 | bytes 2360320 | tf_op jit(solution)/shard_map/sn,sf->nf/dot_general | solution.py:95
  5.9 1.0 maximum_bitcast_fusion
  6.9 7.4 %all-to-all-start = ((bf16[32,8,1664]{2,1,0:T(8,128)(2,1)}), bf16[32,8,1664]{2,1,0:T(8,128)(2,1)}, u32[]{:S(2)}, u32[]{:S(2)}) async-start(bf16[32,8,1664]{2,1,0:T(8,128)(2,1)} %maximum_bitcast_fusion), calls=%async_computation | async-start | bytes 1703936 | tf_op jit(solution)/shard_map/all_to_all | solution.py:105
  14.3 0.7 copy.66
  15.1 0.5 fusion.101
  15.9 1.0 broadcast_add_fusion
  17.3 0.4 copy-done.14
  17.7 0.7 multiply_convert_fusion.5
  18.4 1.6 %copy-done.2 = f32[512,10,2,128]{0,3,2,1:T(8,128)} copy-done((f32[512,10,2,128]{0,3,2,1:T(8,128)}, f32[512,10,2,128]{0,3,2,1:T(8,128)S(1)}, u32[]{:S(2)}) %copy-start.2) | copy-done | bytes 5242904
  20.0 0.6 convolution_convert_fusion.4
  20.6 0.5 copy-done.3
  21.1 0.6 fusion.68
  21.7 14.6 %all-to-all-done = bf16[32,8,1664]{2,1,0:T(8,128)(2,1)} async-done(((bf16[32,8,1664]{2,1,0:T(8,128)(2,1)}), bf16[32,8,1664]{2,1,0:T(8,128)(2,1)}, u32[]{:S(2)}, u32[]{:S(2)}) %all-to-all-start) | async-done | bytes 852000 | tf_op jit(solution)/shard_map/all_to_all | solution.py:105
  36.3 1.0 convert_reduce_fusion.4
  37.3 1.2 slice.102
  39.1 0.5 convolution_add_fusion.4
  42.1 1.2 fusion.14
  43.3 3.6 %all-to-all-start.1 = ((bf16[32,8,1280]{2,1,0:T(8,128)(2,1)}), bf16[32,8,1280]{2,1,0:T(8,128)(2,1)S(1)}, u32[]{:S(2)}, u32[]{:S(2)}) async-start(bf16[32,8,1280]{2,1,0:T(8,128)(2,1)} %fusion.14), calls=%async_computation.1 | async-start | bytes 1310720 | tf_op jit(solution)/shard_map/all_to_all | solution.py:129
  47.1 2.1 %fusion.66 = f32[512,1280]{1,0:T(8,128)} fusion(bf16[128,1280]{1,0:T(8,128)(2,1)S(1)} %fusion.16, s32[512]{0:T(512)S(1)} %bitcast.126, s32[512]{0:T(512)S(1)} %bitcast.121), kind=kOutput, calls=%fused_computation.84 | convolution fusion | flops 168165376 | bytes 2953216 | tf_op jit(solution)/shard_map/es,ef->sf/dot_general | solution.py:124
  49.2 15.6 %all-to-all-done.1 = bf16[32,8,1280]{2,1,0:T(8,128)(2,1)S(1)} async-done(((bf16[32,8,1280]{2,1,0:T(8,128)(2,1)}), bf16[32,8,1280]{2,1,0:T(8,128)(2,1)S(1)}, u32[]{:S(2)}, u32[]{:S(2)}) %all-to-all-start.1) | async-done | bytes 655392 | tf_op jit(solution)/shard_map/all_to_all | solution.py:129
  64.8 4.0 %divide_convert_fusion = (bf16[512,1280]{1,0:T(8,128)(2,1)S(1)}, bf16[512,1280]{1,0:T(8,128)(2,1)}) fusion(bf16[512,1280]{1,0:T(8,128)(2,1)} %param.19, f32[512]{0:T(512)S(1)} %broadcast_add_fusion.1, f32[512,1280]{1,0:T(8,128)} %fusion.66, bf16[32,8,1280]{2,1,0:T(8,128)(2,1)S(1)} %all-to-all-done.1, s32[256]{0:T(256)S(1)} %get-tuple-element.61), kind=kOutput, calls=%fused_computation.24 | convolution fusion | flops 345767936 | bytes 7212032 | tf_op jit(solution)/shard_map/dot_general | solution.py:126
  68.9 1.4 fusion.15
  70.3 3.5 %all-to-all-start.2 = ((bf16[32,8,1280]{2,1,0:T(8,128)(2,1)}), bf16[32,8,1280]{2,1,0:T(8,128)(2,1)S(1)}, u32[]{:S(2)}, u32[]{:S(2)}) async-start(bf16[32,8,1280]{2,1,0:T(8,128)(2,1)} %fusion.15), calls=%async_computation.2 | async-start | bytes 1310720 | tf_op jit(solution)/shard_map/all_to_all | solution.py:136
  74.1 17.6 %all-to-all-done.2 = bf16[32,8,1280]{2,1,0:T(8,128)(2,1)S(1)} async-done(((bf16[32,8,1280]{2,1,0:T(8,128)(2,1)}), bf16[32,8,1280]{2,1,0:T(8,128)(2,1)S(1)}, u32[]{:S(2)}, u32[]{:S(2)}) %all-to-all-start.2) | async-done | bytes 655392 | tf_op jit(solution)/shard_map/all_to_all | solution.py:136
  92.0 1.3 convolution_convert_fusion
  93.6 0.5 fusion.62
  94.2 1.1 copy-done.6
  95.3 1.7 %multiply_convert_fusion.7 = (bf16[256,10,2,64]{0,3,2,1:T(8,128)(2,1)}, bf16[256,10,2,64]{0,3,2,1:T(8,128)(2,1)}) fusion(f32[256,10,2,128]{0,3,2,1:T(8,128)S(1)} %copy-done.6, bf16[256,10,2,64]{0,3,2,1:T(8,128)(2,1)S(1)} %convert_element_type.131, bf16[64,64]{1,0:T(8,128)(2,1)S(1)} %copy-done.26), kind=kOutput, calls=%fused_computation.57 | convolution fusion | flops 45219840 | bytes 4595712 | tf_op jit(solution)/shard_map/stbd,cd->stbc/dot_general | solution.py:151
  97.1 3.7 %all-to-all-start.3 = ((bf16[32,8,1280]{2,1,0:T(8,128)(2,1)}), bf16[32,8,1280]{2,1,0:T(8,128)(2,1)S(1)}, u32[]{:S(2)}, u32[]{:S(2)}) async-start(bf16[32,8,1280]{2,1,0:T(8,128)(2,1)} %bitcast.112), calls=%async_computation.3 | async-start | bytes 1310720 | tf_op jit(solution)/shard_map/all_to_all | solution.py:145
  100.8 1.2 convert_element_type.133
  102.0 2.4 %copy.71 = bf16[512,1280]{0,1:T(8,128)(2,1)} copy(bf16[512,1280]{1,0:T(8,128)(2,1)} %convert_element_type.133) | data formatting | bytes 2621440 | tf_op jit(solution)/shard_map/convert_element_type | solution.py:157
  104.4 4.3 %multiply_convert_fusion.3 = (bf16[512,10,2,64]{0,3,2,1:T(8,128)(2,1)S(1)}, bf16[512,10,2,64]{0,3,2,1:T(8,128)(2,1)S(1)}) fusion(f32[512,10,2,128]{0,3,2,1:T(8,128)} %copy-done.2, bf16[512,10,2,64]{0,3,2,1:T(8,128)(2,1)} %bitcast.114, bf16[64,64]{1,0:T(8,128)(2,1)S(1)} %copy-done.26), kind=kOutput, calls=%fused_computation.23 | convolution fusion | flops 90439680 | bytes 9183232 | tf_op jit(solution)/shard_map/stbd,cd->stbc/dot_general | solution.py:151
  109.1 0.4 convert_reduce_fusion
  110.6 0.7 fusion.27
  111.3 0.6 copy-done.4
  111.9 0.4 copy-done.9
  112.3 0.5 fusion.47
  112.8 0.9 copy-done.11
  113.7 0.4 copy-done.13
  114.1 1.2 fusion.37
  115.3 3.2 %all-to-all-done.3 = bf16[32,8,1280]{2,1,0:T(8,128)(2,1)S(1)} async-done(((bf16[32,8,1280]{2,1,0:T(8,128)(2,1)}), bf16[32,8,1280]{2,1,0:T(8,128)(2,1)S(1)}, u32[]{:S(2)}, u32[]{:S(2)}) %all-to-all-start.3) | async-done | bytes 655392 | tf_op jit(solution)/shard_map/all_to_all | solution.py:145
  118.6 0.7 pad_maximum_fusion.4
  119.3 0.8 collective-permute-start
  120.1 1.6 %fusion.3 = bf16[512,1280]{1,0:T(8,128)(2,1)} fusion(f32[512,1280]{1,0:T(8,128)S(1)} %fusion.62, bf16[256,1280]{1,0:T(8,128)(2,1)S(1)} %bitcast.111, s32[256]{0:T(256)S(1)} %get-tuple-element.61), kind=kOutput, calls=%fused_computation.8 | convolution fusion | flops 337248256 | bytes 4588544 | tf_op jit(solution)/shard_map/dot_general | solution.py:164
  121.7 1.6 %copy.80 = bf16[512,1280]{0,1:T(8,128)(2,1)S(1)} copy(bf16[512,1280]{1,0:T(8,128)(2,1)} %fusion.3) | data formatting | bytes 2621440 | tf_op jit(solution)/shard_map/convert_element_type | solution.py:165
  123.3 5.0 %collective-permute-done = f32[28800]{0:T(1024)} collective-permute-done((f32[28800]{0:T(1024)}, f32[28800]{0:T(1024)}, u32[]{:S(2)}, u32[]{:S(2)}) %collective-permute-start) | collective-permute-done | bytes 115232 | tf_op jit(solution)/shard_map/ppermute | solution.py:24
  128.2 0.9 fusion.99
  129.2 3.8 %multiply_convert_fusion.1 = (bf16[512,10,2,64]{0,3,2,1:T(8,128)(2,1)S(1)}, bf16[512,10,2,64]{0,3,2,1:T(8,128)(2,1)S(1)}) fusion(f32[512,10,2,128]{0,3,2,1:T(8,128)} %copy-done.2, bf16[512,10,2,64]{0,3,2,1:T(8,128)(2,1)S(1)} %bitcast.116, bf16[64,64]{1,0:T(8,128)(2,1)S(1)} %copy-done.26), kind=kOutput, calls=%fused_computation.20 | convolution fusion | flops 90439680 | bytes 9183232 | tf_op jit(solution)/shard_map/stbd,cd->stbc/dot_general | solution.py:168
  133.1 1.0 collective-permute-done.1
  134.1 1.4 collective-permute-start.2
  135.5 1.2 fusion.7
  136.7 2.3 %collective-permute-done.2 = f32[28800]{0:T(1024)S(1)} collective-permute-done((f32[28800]{0:T(1024)S(1)}, f32[28800]{0:T(1024)S(1)}, u32[]{:S(2)}, u32[]{:S(2)}) %collective-permute-start.2) | collective-permute-done | bytes 115232 | tf_op jit(solution)/shard_map/ppermute | solution.py:24
  139.0 1.8 %collective-permute-start.3 = (f32[28800]{0:T(1024)S(1)}, f32[28800]{0:T(1024)S(1)}, u32[]{:S(2)}, u32[]{:S(2)}) collective-permute-start(f32[28800]{0:T(1024)S(1)} %add.148), channel_id=1, source_target_pairs={{0,2},{1,3},{2,0},{3,1},{4,6},{5,7},{6,4},{7,5},{8,10},{9,11},{10,... | collective-permute-start | bytes 345608 | tf_op jit(solution)/shard_map/ppermute | solution.py:24
  140.7 1.6 %fusion.100 = (f32[512,10,2,64]{0,3,2,1:T(8,128)S(1)}, f32[512,10,2,64]{0,3,2,1:T(8,128)S(1)}, f32[512,10,2,64]{0,3,2,1:T(8,128)S(1)}) fusion(f32[512,10,2,192]{0,3,2,1:T(8,128)S(1)} %fusion.7), kind=kLoop, calls=%fused_computation.136 | loop fusion | bytes 15728640 | tf_op jit(solution)/shard_map/slice | solution.py:177
  142.4 1.5 %collective-permute-done.3 = f32[28800]{0:T(1024)S(1)} collective-permute-done((f32[28800]{0:T(1024)S(1)}, f32[28800]{0:T(1024)S(1)}, u32[]{:S(2)}, u32[]{:S(2)}) %collective-permute-start.3) | collective-permute-done | bytes 115232 | tf_op jit(solution)/shard_map/ppermute | solution.py:24
  144.0 1.0 add_convert_fusion
  145.0 1.6 %copy.82 = bf16[512,1536]{1,0:T(8,128)(2,1)} copy(bf16[512,1536]{0,1:T(8,128)(2,1)S(1)} %bitcast.108) | data formatting | bytes 3145728
  146.6 0.5 slice_multiply_fusion.2
  147.1 0.6 fusion.79
  147.8 0.7 mul.149
  (82 shorter events, 6.8 us)
Async XLA Ops:
  0.6 15.3 %copy-start = (bf16[192,128]{1,0:T(8,128)(2,1)S(1)}, bf16[192,128]{1,0:T(8,128)(2,1)}, u32[]{:S(2)}) copy-start(bf16[192,128]{1,0:T(8,128)(2,1)} %param.11) | copy-start | bytes 147460
  3.7 10.6 %copy-start.1 = (bf16[512,1536]{1,0:T(8,128)(2,1)S(1)}, bf16[512,1536]{1,0:T(8,128)(2,1)}, u32[]{:S(2)}) copy-start(bf16[512,1536]{1,0:T(8,128)(2,1)} %param.10) | copy-start | bytes 4718596
  6.9 29.4 %all-to-all-start = ((bf16[32,8,1664]{2,1,0:T(8,128)(2,1)}), bf16[32,8,1664]{2,1,0:T(8,128)(2,1)}, u32[]{:S(2)}, u32[]{:S(2)}) async-start(bf16[32,8,1664]{2,1,0:T(8,128)(2,1)} %maximum_bitcast_fusion), calls=%async_computation | async-start | bytes 1703936 | tf_op jit(solution)/shard_map/all_to_all | solution.py:105
  15.0 0.7 copy-start.27
  15.1 0.8 copy-start.29
  15.7 1.2 copy-start.10
  15.7 1.6 %copy-start.12 = (bf16[512,10,2,64]{0,3,2,1:T(8,128)(2,1)}, bf16[512,10,2,64]{0,3,2,1:T(8,128)(2,1)S(1)}, u32[]{:S(2)}) copy-start(bf16[512,10,2,64]{0,3,2,1:T(8,128)(2,1)S(1)} %get-tuple-element.53) | copy-start | bytes 3932164
  15.7 2.0 %copy-start.14 = (bf16[512,10,2,64]{0,3,2,1:T(8,128)(2,1)}, bf16[512,10,2,64]{0,3,2,1:T(8,128)(2,1)S(1)}, u32[]{:S(2)}) copy-start(bf16[512,10,2,64]{0,3,2,1:T(8,128)(2,1)S(1)} %get-tuple-element.54) | copy-start | bytes 3932164
  17.7 2.3 %copy-start.2 = (f32[512,10,2,128]{0,3,2,1:T(8,128)}, f32[512,10,2,128]{0,3,2,1:T(8,128)S(1)}, u32[]{:S(2)}) copy-start(f32[512,10,2,128]{0,3,2,1:T(8,128)S(1)} %broadcast_add_fusion) | copy-start | bytes 15728644
  17.7 2.3 %copy-start.26 = (bf16[64,64]{1,0:T(8,128)(2,1)S(1)}, bf16[64,64]{1,0:T(8,128)(2,1)}, u32[]{:S(2)}) copy-start(bf16[64,64]{1,0:T(8,128)(2,1)} %param.13) | copy-start | bytes 24580
  20.0 1.1 copy-start.3
  39.1 0.9 copy-start.20
  39.1 1.1 copy-start.22
  39.1 1.3 copy-start.24
  40.3 1.5 %copy-start.5 = (f32[256,10,2,128]{0,3,2,1:T(8,128)}, f32[256,10,2,128]{0,3,2,1:T(8,128)S(1)}, u32[]{:S(2)}) copy-start(f32[256,10,2,128]{0,3,2,1:T(8,128)S(1)} %convolution_add_fusion.4) | copy-start | bytes 7864324
  40.3 0.8 copy-start.28
  40.7 1.4 copy-start.7
  43.3 21.5 %all-to-all-start.1 = ((bf16[32,8,1280]{2,1,0:T(8,128)(2,1)}), bf16[32,8,1280]{2,1,0:T(8,128)(2,1)S(1)}, u32[]{:S(2)}, u32[]{:S(2)}) async-start(bf16[32,8,1280]{2,1,0:T(8,128)(2,1)} %fusion.14), calls=%async_computation.1 | async-start | bytes 1310720 | tf_op jit(solution)/shard_map/all_to_all | solution.py:129
  70.3 21.4 %all-to-all-start.2 = ((bf16[32,8,1280]{2,1,0:T(8,128)(2,1)}), bf16[32,8,1280]{2,1,0:T(8,128)(2,1)S(1)}, u32[]{:S(2)}, u32[]{:S(2)}) async-start(bf16[32,8,1280]{2,1,0:T(8,128)(2,1)} %fusion.15), calls=%async_computation.2 | async-start | bytes 1310720 | tf_op jit(solution)/shard_map/all_to_all | solution.py:136
  93.6 1.7 %copy-start.6 = (f32[256,10,2,128]{0,3,2,1:T(8,128)S(1)}, f32[256,10,2,128]{0,3,2,1:T(8,128)}, u32[]{:S(2)}) copy-start(f32[256,10,2,128]{0,3,2,1:T(8,128)} %copy-done.5) | copy-start | bytes 7864324
  95.3 1.7 %copy-start.18 = (bf16[256,10,2,64]{0,3,2,1:T(8,128)(2,1)}, bf16[256,10,2,64]{0,3,2,1:T(8,128)(2,1)S(1)}, u32[]{:S(2)}) copy-start(bf16[256,10,2,64]{0,3,2,1:T(8,128)(2,1)S(1)} %convert_element_type.131) | copy-start | bytes 1966084
  97.1 21.4 %all-to-all-start.3 = ((bf16[32,8,1280]{2,1,0:T(8,128)(2,1)}), bf16[32,8,1280]{2,1,0:T(8,128)(2,1)S(1)}, u32[]{:S(2)}, u32[]{:S(2)}) async-start(bf16[32,8,1280]{2,1,0:T(8,128)(2,1)} %bitcast.112), calls=%async_computation.3 | async-start | bytes 1310720 | tf_op jit(solution)/shard_map/all_to_all | solution.py:145
  104.4 4.3 %copy-start.16 = (bf16[256,10,2,64]{0,3,2,1:T(8,128)(2,1)S(1)}, bf16[256,10,2,64]{0,3,2,1:T(8,128)(2,1)}, u32[]{:S(2)}) copy-start(bf16[256,10,2,64]{0,3,2,1:T(8,128)(2,1)} %get-tuple-element.48) | copy-start | bytes 1966084
  104.4 4.3 %copy-start.17 = (bf16[256,10,2,64]{0,3,2,1:T(8,128)(2,1)S(1)}, bf16[256,10,2,64]{0,3,2,1:T(8,128)(2,1)}, u32[]{:S(2)}) copy-start(bf16[256,10,2,64]{0,3,2,1:T(8,128)(2,1)} %get-tuple-element.49) | copy-start | bytes 1966084
  108.7 1.1 copy-start.8
  108.7 1.3 copy-start.19
  108.8 1.6 %copy-start.21 = (bf16[256,10,2,64]{0,3,2,1:T(8,128)(2,1)S(1)}, bf16[256,10,2,64]{0,3,2,1:T(8,128)(2,1)}, u32[]{:S(2)}) copy-start(bf16[256,10,2,64]{0,3,2,1:T(8,128)(2,1)} %copy-done.20) | copy-start | bytes 1966084
  108.8 1.6 %copy-start.23 = (bf16[256,10,2,64]{0,3,2,1:T(8,128)(2,1)S(1)}, bf16[256,10,2,64]{0,3,2,1:T(8,128)(2,1)}, u32[]{:S(2)}) copy-start(bf16[256,10,2,64]{0,3,2,1:T(8,128)(2,1)} %copy-done.22) | copy-start | bytes 1966084
  108.8 1.8 %copy-start.25 = (bf16[256,10,2,64]{0,3,2,1:T(8,128)(2,1)S(1)}, bf16[256,10,2,64]{0,3,2,1:T(8,128)(2,1)}, u32[]{:S(2)}) copy-start(bf16[256,10,2,64]{0,3,2,1:T(8,128)(2,1)} %copy-done.24) | copy-start | bytes 1966084
  110.6 1.3 copy-start.4
  110.6 1.7 %copy-start.9 = (bf16[512,1280]{0,1:T(8,128)(2,1)S(1)}, bf16[512,1280]{0,1:T(8,128)(2,1)}, u32[]{:S(2)}) copy-start(bf16[512,1280]{0,1:T(8,128)(2,1)} %copy.71) | copy-start | bytes 3932164
  110.6 2.2 %copy-start.15 = (bf16[512,10,2,64]{0,3,2,1:T(8,128)(2,1)S(1)}, bf16[512,10,2,64]{0,3,2,1:T(8,128)(2,1)}, u32[]{:S(2)}) copy-start(bf16[512,10,2,64]{0,3,2,1:T(8,128)(2,1)} %copy-done.14) | copy-start | bytes 3932164
  112.3 1.4 copy-start.11
  112.3 1.8 %copy-start.13 = (bf16[512,10,2,64]{0,3,2,1:T(8,128)(2,1)S(1)}, bf16[512,10,2,64]{0,3,2,1:T(8,128)(2,1)}, u32[]{:S(2)}) copy-start(bf16[512,10,2,64]{0,3,2,1:T(8,128)(2,1)} %copy-done.12) | copy-start | bytes 3932164
  119.3 9.0 %collective-permute-start = (f32[28800]{0:T(1024)}, f32[28800]{0:T(1024)}, u32[]{:S(2)}, u32[]{:S(2)}) collective-permute-start(f32[28800]{0:T(1024)} %pad_maximum_fusion.4), channel_id=1, source_target_pairs={{0,16},{1,17},{2,18},{3,19},{4,20},{5,21},{6,22},{7,23},{8,24},{9,... | collective-permute-start | bytes 345608 | tf_op jit(solution)/shard_map/ppermute | solution.py:24
  129.2 4.9 %collective-permute-start.1 = (f32[28800]{0:T(1024)S(1)}, f32[28800]{0:T(1024)S(1)}, u32[]{:S(2)}, u32[]{:S(2)}) collective-permute-start(f32[28800]{0:T(1024)S(1)} %fusion.99), channel_id=1, source_target_pairs={{0,8},{1,9},{2,10},{3,11},{4,12},{5,13},{6,14},{7,15},{8,0},{9,1},... | collective-permute-start | bytes 345608 | tf_op jit(solution)/shard_map/ppermute | solution.py:24
  134.1 4.9 %collective-permute-start.2 = (f32[28800]{0:T(1024)S(1)}, f32[28800]{0:T(1024)S(1)}, u32[]{:S(2)}, u32[]{:S(2)}) collective-permute-start(f32[28800]{0:T(1024)S(1)} %add.147), channel_id=1, source_target_pairs={{0,4},{1,5},{2,6},{3,7},{4,0},{5,1},{6,2},{7,3},{8,12},{9,13},{10,... | collective-permute-start | bytes 345608 | tf_op jit(solution)/shard_map/ppermute | solution.py:24
  139.0 4.9 %collective-permute-start.3 = (f32[28800]{0:T(1024)S(1)}, f32[28800]{0:T(1024)S(1)}, u32[]{:S(2)}, u32[]{:S(2)}) collective-permute-start(f32[28800]{0:T(1024)S(1)} %add.148), channel_id=1, source_target_pairs={{0,2},{1,3},{2,0},{3,1},{4,6},{5,7},{6,4},{7,5},{8,10},{9,11},{10,... | collective-permute-start | bytes 345608 | tf_op jit(solution)/shard_map/ppermute | solution.py:24
  143.9 2.7 %collective-permute-start.4 = (f32[28800]{0:T(1024)S(1)}, f32[28800]{0:T(1024)S(1)}, u32[]{:S(2)}, u32[]{:S(2)}) collective-permute-start(f32[28800]{0:T(1024)S(1)} %add.149), channel_id=1, source_target_pairs={{0,1},{1,0},{2,3},{3,2},{4,5},{5,4},{6,7},{7,6},{8,9},{9,8},{10,11... | collective-permute-start | bytes 345608 | tf_op jit(solution)/shard_map/ppermute | solution.py:24

commit v14 on v11

--- a/solution.py
+++ b/solution.py
@@ -99,11 +99,19 @@
     cut_rows = pick_slots(feats)
     stack, gate, first, hidden, z = front(feats)
 
+    def gate_factors(gt, fi):
+        return lax.optimization_barrier(
+            ((gt).astype(jnp.bfloat16), (fi * gt * (1.0 - gt)).astype(jnp.bfloat16))
+        )
+
+    fa, fb = gate_factors(gate, first)
+
     edge_cols = jnp.broadcast_to(slotted_hyperedge.astype(jnp.bfloat16)[:, None], (slot_total, 128))
     in_width = feats.shape[1]
     send = jnp.concatenate([cut_rows, edge_cols], axis=1)
     recv_all = lax.all_to_all(send, ("region", "sub"), split_axis=0, concat_axis=0, tiled=True)
     r_stack, r_gate, r_first, r_hidden, recv = front(recv_all[:, :in_width])
+    r_fa, r_fb = gate_factors(r_gate, r_first)
     recv_edge = recv_all[:, in_width].astype(jnp.int32)
     owned = (recv_edge[None, :] == edge_index[:, None]).astype(jnp.float32)
     count = 1.0 + inner_count + jnp.sum(owned, axis=1)
@@ -149,14 +157,14 @@
     def weight_grads(st, gt, fi, hi, dzr):
         g_theta = jnp.einsum("stbc,stbd->cd", hi, dzr, preferred_element_type=jnp.float32)
         dh = jnp.einsum("stbd,cd->stbc", dzr, theta, preferred_element_type=jnp.float32)
-        du = jnp.concatenate([dh * gt, dh * fi * gt * (1.0 - gt)], axis=-1).astype(jnp.bfloat16)
+        du = jnp.concatenate([dh * gt, dh * fi], axis=-1).astype(jnp.bfloat16)
         g_conv = jnp.einsum("stbk,stbf->kf", st, du, preferred_element_type=jnp.float32)
         g_bias = jnp.sum(du.astype(jnp.float32), axis=(0, 1, 2))
         return du, g_conv, g_bias, g_theta
 
     dz_inner = inner_sum.astype(jnp.bfloat16).reshape(seg, TP, B, C)
-    _, ga_conv, ga_bias, ga_theta = weight_grads(stack, gate, first, hidden, dz_inner)
-    _, gb_conv, gb_bias, gb_theta = weight_grads(r_stack, r_gate, r_first, r_hidden, dz_slots)
+    _, ga_conv, ga_bias, ga_theta = weight_grads(stack, fa, fb, hidden, dz_inner)
+    _, gb_conv, gb_bias, gb_theta = weight_grads(r_stack, r_fa, r_fb, r_hidden, dz_slots)
     partial = (ga_conv + gb_conv, ga_bias + gb_bias, ga_theta + gb_theta)
     partial, back_grads = lax.optimization_barrier((partial, back_grads))
     sum_conv, sum_bias, sum_theta = device_sum(partial, device_list)
@@ -166,7 +174,7 @@
         .reshape(seg, TP, B, C)
     )
     dh = jnp.einsum("stbd,cd->stbc", dz, theta, preferred_element_type=jnp.float32)
-    du = jnp.concatenate([dh * gate, dh * first * gate * (1.0 - gate)], axis=-1).astype(
+    du = jnp.concatenate([dh * fa, dh * fb], axis=-1).astype(
         jnp.bfloat16
     )
     norm = 1.0 / jnp.sqrt(jnp.float32(seg * device_list * TP * B))

time: 148 us -> 148 us (level)
  matrix products: 32.3 us -> 26.7 us
  other arithmetic: 12.3 us -> 16 us
  waiting for transfers between devices: 57.3 us -> 58.9 us
    dot_general x2, matrix products: 6.04 us -> 2.62 us  [weight_grads(): jnp.einsum('stbd,cd->stbc', dzr, theta, preferred_element_type=jnp.float32)]
    convert_element_type x2, other arithmetic: 1.1 us -> 4.05 us  [gate_factors(): (fi * gt * (1.0 - gt)).astype(jnp.bfloat16)]
    dot_general x1, matrix products: 3.81 us -> 1.92 us  [body(): jnp.einsum('stbd,cd->stbc', dz, theta, preferred_element_type=jnp.float32)]
    ppermute x5, waiting for transfers between devices: 6.31 us -> 8.02 us  [device_sum(): flat = flat + lax.ppermute(flat, ('region', 'sub'), perm)]
    all_to_all x1, waiting for transfers between devices: 14.6 us -> 13.1 us  [body(): lax.all_to_all(send, ('region', 'sub'), split_axis=0, concat_axis=0, tile...]
    unnamed x62 -> x58, local copies, waits for them, and re-layouts: 10.9 us -> 10.1 us
  transfers between devices with their start and end apart: 9 -> 9, of which waited for: 8 -> 8; matrix products, arithmetic and copies ran while one was open for 21% -> 20% of each run, Pallas kernels for 0% -> 0%
where the time goes in v14:
time: 148 us; the launch traced here: 147 us
  waiting for transfers between devices  58.9 us (40%)
  matrix products  26.7 us (18%)
  starting transfers between devices  24.2 us (16%)
  local copies, waits for them, and re-layouts  19.8 us (13%)
  other arithmetic  16 us (11%)
    all_to_all x1, waiting for transfers between devices, body(): lax.all_to_all(send_grads, ('region', 'sub'), split_axis=0, concat_axis=0...  17.6 us
    all_to_all x1, waiting for transfers between devices, body(): lax.all_to_all(ret_rows, ('region', 'sub'), split_axis=0, concat_axis=0,...  15.7 us
    all_to_all x1, waiting for transfers between devices, body(): lax.all_to_all(send, ('region', 'sub'), split_axis=0, concat_axis=0, tile...  13.1 us
    unnamed x58, local copies, waits for them, and re-layouts  10.1 us
    ppermute x5, waiting for transfers between devices, device_sum(): flat = flat + lax.ppermute(flat, ('region', 'sub'), perm)  8.02 us
    all_to_all x1, starting transfers between devices, body(): lax.all_to_all(send, ('region', 'sub'), split_axis=0, concat_axis=0, tile...  7.41 us
    ppermute x5, starting transfers between devices, device_sum(): flat = flat + lax.ppermute(flat, ('region', 'sub'), perm)  5.99 us
    all_to_all x1, waiting for transfers between devices, body(): lax.all_to_all(ret_grads, ('region', 'sub'), split_axis=0, concat_axis=0,...  4.56 us
  transfers between devices with their start and end apart: 9, of which 8 were waited for; matrix products, arithmetic and copies ran while one was open for 20% of the time, Pallas kernels for 0%

profile of v14, /device:TPU:0, one launch (start us, length us, event | category | flops | bytes accessed | tf_op | source)
XLA Modules:
  0.0 146.9 jit_solution(13674882568854624323)
XLA Ops:
  0.6 0.7 broadcast_add_fusion.4
  1.3 0.7 broadcast_add_fusion.3
  2.0 0.9 convert_reduce_fusion.5
  2.9 0.7 fusion.103
  3.7 2.0 %convolution_convert_fusion.3 = bf16[256,1536]{1,0:T(8,128)(2,1)S(1)} fusion(bf16[512,1536]{1,0:T(8,128)(2,1)} %param.10, s32[256]{0:T(256)S(1)} %get-tuple-element.75), kind=kOutput, calls=%fused_computation.37 | convolution fusion | flops 403439616 | bytes 2360320 | tf_op jit(solution)/shard_map/sn,sf->nf/dot_general | solution.py:95
  5.8 1.0 maximum_bitcast_fusion
  6.8 7.4 %all-to-all-start = ((bf16[32,8,1664]{2,1,0:T(8,128)(2,1)}), bf16[32,8,1664]{2,1,0:T(8,128)(2,1)}, u32[]{:S(2)}, u32[]{:S(2)}) async-start(bf16[32,8,1664]{2,1,0:T(8,128)(2,1)} %maximum_bitcast_fusion), calls=%async_computation | async-start | bytes 1703936 | tf_op jit(solution)/shard_map/all_to_all | solution.py:112
  14.2 0.7 copy.66
  15.0 0.5 fusion.109
  15.6 0.9 copy-done.12
  17.4 1.0 broadcast_add_fusion
  18.4 2.5 %multiply_convert_fusion = (bf16[512,10,2,64]{0,3,2,1:T(8,128)(2,1)}, bf16[512,10,2,64]{0,3,2,1:T(8,128)(2,1)}, bf16[512,10,2,64]{0,3,2,1:T(8,128)(2,1)S(1)}) fusion(f32[512,10,2,128]{0,3,2,1:T(8,128)S(1)} %broadcast_add_fusion), kind=kLoop, calls=%fused_computation.29 | loop fusion | flops 5898240 | bytes 9175040 | tf_op jit(solution)/shard_map/convert_element_type | solution.py:104
  20.9 1.2 copy-done.6
  22.0 0.6 convolution_convert_fusion.4
  22.6 0.6 fusion.74
  23.2 13.1 %all-to-all-done = bf16[32,8,1664]{2,1,0:T(8,128)(2,1)} async-done(((bf16[32,8,1664]{2,1,0:T(8,128)(2,1)}), bf16[32,8,1664]{2,1,0:T(8,128)(2,1)}, u32[]{:S(2)}, u32[]{:S(2)}) %all-to-all-start) | async-done | bytes 852000 | tf_op jit(solution)/shard_map/all_to_all | solution.py:112
  36.2 1.0 convert_reduce_fusion.4
  37.2 1.2 slice.102
  39.0 0.8 copy-done.20
  40.0 0.5 convolution_add_fusion.4
  40.6 1.6 %multiply_convert_fusion.4 = (bf16[256,10,2,64]{0,3,2,1:T(8,128)(2,1)}, bf16[256,10,2,64]{0,3,2,1:T(8,128)(2,1)}, bf16[256,10,2,64]{0,3,2,1:T(8,128)(2,1)S(1)}) fusion(f32[256,10,2,128]{0,3,2,1:T(8,128)S(1)} %convolution_add_fusion.4), kind=kLoop, calls=%fused_computation.64 | loop fusion | flops 2949120 | bytes 4587520 | tf_op jit(solution)/shard_map/convert_element_type | solution.py:104
  43.4 1.2 fusion.18
  44.6 3.6 %all-to-all-start.1 = ((bf16[32,8,1280]{2,1,0:T(8,128)(2,1)}), bf16[32,8,1280]{2,1,0:T(8,128)(2,1)S(1)}, u32[]{:S(2)}, u32[]{:S(2)}) async-start(bf16[32,8,1280]{2,1,0:T(8,128)(2,1)} %fusion.18), calls=%async_computation.1 | async-start | bytes 1310720 | tf_op jit(solution)/shard_map/all_to_all | solution.py:137
  48.4 2.0 %fusion.72 = f32[512,1280]{1,0:T(8,128)} fusion(bf16[128,1280]{1,0:T(8,128)(2,1)S(1)} %fusion.20, s32[512]{0:T(512)S(1)} %bitcast.126, s32[512]{0:T(512)S(1)} %bitcast.121), kind=kOutput, calls=%fused_computation.92 | convolution fusion | flops 168165376 | bytes 2953216 | tf_op jit(solution)/shard_map/es,ef->sf/dot_general | solution.py:132
  50.4 15.7 %all-to-all-done.1 = bf16[32,8,1280]{2,1,0:T(8,128)(2,1)S(1)} async-done(((bf16[32,8,1280]{2,1,0:T(8,128)(2,1)}), bf16[32,8,1280]{2,1,0:T(8,128)(2,1)S(1)}, u32[]{:S(2)}, u32[]{:S(2)}) %all-to-all-start.1) | async-done | bytes 655392 | tf_op jit(solution)/shard_map/all_to_all | solution.py:137
  66.2 4.0 %divide_convert_fusion = (bf16[512,1280]{1,0:T(8,128)(2,1)S(1)}, bf16[512,1280]{1,0:T(8,128)(2,1)}) fusion(bf16[512,1280]{1,0:T(8,128)(2,1)} %param.19, f32[512]{0:T(512)S(1)} %broadcast_add_fusion.1, f32[512,1280]{1,0:T(8,128)} %fusion.72, bf16[32,8,1280]{2,1,0:T(8,128)(2,1)S(1)} %all-to-all-done.1, s32[256]{0:T(256)S(1)} %get-tuple-element.75), kind=kOutput, calls=%fused_computation.30 | convolution fusion | flops 345767936 | bytes 7212032 | tf_op jit(solution)/shard_map/dot_general | solution.py:134
  70.2 1.4 fusion.19
  71.6 3.5 %all-to-all-start.2 = ((bf16[32,8,1280]{2,1,0:T(8,128)(2,1)}), bf16[32,8,1280]{2,1,0:T(8,128)(2,1)S(1)}, u32[]{:S(2)}, u32[]{:S(2)}) async-start(bf16[32,8,1280]{2,1,0:T(8,128)(2,1)} %fusion.19), calls=%async_computation.2 | async-start | bytes 1310720 | tf_op jit(solution)/shard_map/all_to_all | solution.py:144
  75.5 17.6 %all-to-all-done.2 = bf16[32,8,1280]{2,1,0:T(8,128)(2,1)S(1)} async-done(((bf16[32,8,1280]{2,1,0:T(8,128)(2,1)}), bf16[32,8,1280]{2,1,0:T(8,128)(2,1)S(1)}, u32[]{:S(2)}, u32[]{:S(2)}) %all-to-all-start.2) | async-done | bytes 655392 | tf_op jit(solution)/shard_map/all_to_all | solution.py:144
  93.3 1.2 convolution_convert_fusion
  94.8 0.5 fusion.68
  95.4 0.9 convert_element_type.157
  96.3 3.7 %all-to-all-start.3 = ((bf16[32,8,1280]{2,1,0:T(8,128)(2,1)}), bf16[32,8,1280]{2,1,0:T(8,128)(2,1)S(1)}, u32[]{:S(2)}, u32[]{:S(2)}) async-start(bf16[32,8,1280]{2,1,0:T(8,128)(2,1)} %bitcast.115), calls=%async_computation.3 | async-start | bytes 1310720 | tf_op jit(solution)/shard_map/all_to_all | solution.py:153
  100.0 1.2 convert_element_type.159
  101.2 2.5 %copy.71 = bf16[512,1280]{0,1:T(8,128)(2,1)} copy(bf16[512,1280]{1,0:T(8,128)(2,1)} %convert_element_type.159) | data formatting | bytes 2621440 | tf_op jit(solution)/shard_map/convert_element_type | solution.py:165
  103.7 2.0 %multiply_convert_fusion.3 = (bf16[256,10,2,64]{0,3,2,1:T(8,128)(2,1)S(1)}, bf16[256,10,2,64]{0,3,2,1:T(8,128)(2,1)S(1)}) fusion(bf16[256,10,2,64]{0,3,2,1:T(8,128)(2,1)} %get-tuple-element.20, bf16[256,10,2,64]{0,3,2,1:T(8,128)(2,1)} %get-tuple-element.21, bf16[256,10,2,64]{0,3,2,1:T(8,128)(2,1)} %convert_element_type.157, bf16[64,64]{1,0:T(8,128)(2,1)S(1)} %copy-done.24), kind=kOutput, calls=%fused_computation.63 | convolution fusion | flops 43909120 | bytes 3284992 | tf_op jit(solution)/shard_map/stbd,cd->stbc/dot_general | solution.py:159
  106.3 0.6 fusion.4
  107.5 0.6 copy-done.10
  108.9 0.7 fusion.31
  109.5 0.6 copy-done.7
  110.2 0.5 fusion.51
  110.7 0.9 copy-done.13
  112.0 1.2 fusion.41
  113.2 4.6 %all-to-all-done.3 = bf16[32,8,1280]{2,1,0:T(8,128)(2,1)S(1)} async-done(((bf16[32,8,1280]{2,1,0:T(8,128)(2,1)}), bf16[32,8,1280]{2,1,0:T(8,128)(2,1)S(1)}, u32[]{:S(2)}, u32[]{:S(2)}) %all-to-all-start.3) | async-done | bytes 655392 | tf_op jit(solution)/shard_map/all_to_all | solution.py:153
  117.8 0.6 pad_maximum_fusion.4
  118.5 1.6 %fusion.3 = bf16[512,1280]{1,0:T(8,128)(2,1)} fusion(f32[512,1280]{1,0:T(8,128)S(1)} %fusion.68, bf16[256,1280]{1,0:T(8,128)(2,1)S(1)} %bitcast.114, s32[256]{0:T(256)S(1)} %get-tuple-element.75), kind=kOutput, calls=%fused_computation.12 | convolution fusion | flops 337248256 | bytes 4588544 | tf_op jit(solution)/shard_map/dot_general | solution.py:172
  120.1 2.6 %copy.80 = bf16[512,1280]{0,1:T(8,128)(2,1)} copy(bf16[512,1280]{1,0:T(8,128)(2,1)} %fusion.3) | data formatting | bytes 2621440 | tf_op jit(solution)/shard_map/convert_element_type | solution.py:173
  122.8 0.9 fusion.105
  123.7 1.7 %collective-permute-start.1 = (f32[28800]{0:T(1024)S(1)}, f32[28800]{0:T(1024)S(1)}, u32[]{:S(2)}, u32[]{:S(2)}) collective-permute-start(f32[28800]{0:T(1024)S(1)} %fusion.105), channel_id=1, source_target_pairs={{0,2},{1,3},{2,0},{3,1},{4,6},{5,7},{6,4},{7,5},{8,10},{9,11},{10,... | collective-permute-start | bytes 345608 | tf_op jit(solution)/shard_map/ppermute | solution.py:24
  125.3 1.9 %fusion.5 = (bf16[512,10,2,64]{0,3,2,1:T(8,128)(2,1)S(1)}, bf16[512,10,2,64]{0,3,2,1:T(8,128)(2,1)S(1)}) fusion(bf16[512,10,2,64]{0,3,2,1:T(8,128)(2,1)S(1)} %copy-done.4, bf16[512,10,2,64]{0,3,2,1:T(8,128)(2,1)S(1)} %copy-done.2, bf16[512,10,2,64]{0,3,2,1:T(8,128)(2,1)} %bitcast.113, bf16[64,64]{1,0:T(8,128)(2,1)S(1)} %copy-done.24), kind=kOutput, calls=%fused_computation.14 | convolution fusion | flops 87818240 | bytes 6561792 | tf_op jit(solution)/shard_map/stbd,cd->stbc/dot_general | solution.py:176
  127.3 2.1 %collective-permute-done.1 = f32[28800]{0:T(1024)S(1)} collective-permute-done((f32[28800]{0:T(1024)S(1)}, f32[28800]{0:T(1024)S(1)}, u32[]{:S(2)}, u32[]{:S(2)}) %collective-permute-start.1) | collective-permute-done | bytes 115232 | tf_op jit(solution)/shard_map/ppermute | solution.py:24
  129.3 1.5 collective-permute-start.2
  130.8 1.2 fusion.11
  132.0 2.3 %collective-permute-done.2 = f32[28800]{0:T(1024)S(1)} collective-permute-done((f32[28800]{0:T(1024)S(1)}, f32[28800]{0:T(1024)S(1)}, u32[]{:S(2)}, u32[]{:S(2)}) %collective-permute-start.2) | collective-permute-done | bytes 115232 | tf_op jit(solution)/shard_map/ppermute | solution.py:24
  134.3 1.5 %collective-permute-start.3 = (f32[28800]{0:T(1024)S(1)}, f32[28800]{0:T(1024)S(1)}, u32[]{:S(2)}, u32[]{:S(2)}) collective-permute-start(f32[28800]{0:T(1024)S(1)} %add.148), channel_id=1, source_target_pairs={{0,8},{1,9},{2,10},{3,11},{4,12},{5,13},{6,14},{7,15},{8,0},{9,1},... | collective-permute-start | bytes 345608 | tf_op jit(solution)/shard_map/ppermute | solution.py:24
  135.8 1.6 %fusion.108 = (f32[512,10,2,64]{0,3,2,1:T(8,128)S(1)}, f32[512,10,2,64]{0,3,2,1:T(8,128)S(1)}, f32[512,10,2,64]{0,3,2,1:T(8,128)S(1)}) fusion(f32[512,10,2,192]{0,3,2,1:T(8,128)S(1)} %fusion.11), kind=kLoop, calls=%fused_computation.146 | loop fusion | bytes 15728640 | tf_op jit(solution)/shard_map/slice | solution.py:185
  137.4 1.7 %collective-permute-done.3 = f32[28800]{0:T(1024)S(1)} collective-permute-done((f32[28800]{0:T(1024)S(1)}, f32[28800]{0:T(1024)S(1)}, u32[]{:S(2)}, u32[]{:S(2)}) %collective-permute-start.3) | collective-permute-done | bytes 115232 | tf_op jit(solution)/shard_map/ppermute | solution.py:24
  139.2 1.3 collective-permute-start.4
  140.5 1.0 add_convert_fusion
  141.5 1.6 %copy.82 = bf16[512,1536]{1,0:T(8,128)(2,1)} copy(bf16[512,1536]{0,1:T(8,128)(2,1)S(1)} %bitcast.108) | data formatting | bytes 3145728
  143.1 1.9 %collective-permute-done.4 = f32[28800]{0:T(1024)S(1)} collective-permute-done((f32[28800]{0:T(1024)S(1)}, f32[28800]{0:T(1024)S(1)}, u32[]{:S(2)}, u32[]{:S(2)}) %collective-permute-start.4) | collective-permute-done | bytes 115232 | tf_op jit(solution)/shard_map/ppermute | solution.py:24
  145.0 0.5 slice_multiply_fusion.4
  145.5 0.6 fusion.85
  146.2 0.7 mul.135
  (78 shorter events, 6.9 us)
Async XLA Ops:
  0.6 16.7 %copy-start = (bf16[192,128]{1,0:T(8,128)(2,1)S(1)}, bf16[192,128]{1,0:T(8,128)(2,1)}, u32[]{:S(2)}) copy-start(bf16[192,128]{1,0:T(8,128)(2,1)} %param.11) | copy-start | bytes 147460
  5.7 8.5 %copy-start.5 = (bf16[512,1536]{1,0:T(8,128)(2,1)S(1)}, bf16[512,1536]{1,0:T(8,128)(2,1)}, u32[]{:S(2)}) copy-start(bf16[512,1536]{1,0:T(8,128)(2,1)} %param.10) | copy-start | bytes 4718596
  6.8 29.4 %all-to-all-start = ((bf16[32,8,1664]{2,1,0:T(8,128)(2,1)}), bf16[32,8,1664]{2,1,0:T(8,128)(2,1)}, u32[]{:S(2)}, u32[]{:S(2)}) async-start(bf16[32,8,1664]{2,1,0:T(8,128)(2,1)} %maximum_bitcast_fusion), calls=%async_computation | async-start | bytes 1703936 | tf_op jit(solution)/shard_map/all_to_all | solution.py:112
  14.2 0.7 copy-start.25
  15.0 2.4 %copy-start.27 = (f32[128]{0:T(128)S(1)}, f32[128]{0:T(128)}, u32[]{:S(2)}) copy-start(f32[128]{0:T(128)} %param.12) | copy-start | bytes 1540
  15.5 1.1 copy-start.12
  15.5 1.5 %copy-start.14 = (bf16[512,10,2,64]{0,3,2,1:T(8,128)(2,1)}, bf16[512,10,2,64]{0,3,2,1:T(8,128)(2,1)S(1)}, u32[]{:S(2)}) copy-start(bf16[512,10,2,64]{0,3,2,1:T(8,128)(2,1)S(1)} %get-tuple-element.65) | copy-start | bytes 3932164
  15.5 1.9 %copy-start.16 = (bf16[512,10,2,64]{0,3,2,1:T(8,128)(2,1)}, bf16[512,10,2,64]{0,3,2,1:T(8,128)(2,1)S(1)}, u32[]{:S(2)}) copy-start(bf16[512,10,2,64]{0,3,2,1:T(8,128)(2,1)S(1)} %get-tuple-element.66) | copy-start | bytes 3932164
  18.4 3.6 %copy-start.24 = (bf16[64,64]{1,0:T(8,128)(2,1)S(1)}, bf16[64,64]{1,0:T(8,128)(2,1)}, u32[]{:S(2)}) copy-start(bf16[64,64]{1,0:T(8,128)(2,1)} %param.13) | copy-start | bytes 24580
  20.9 1.2 copy-start.6
  38.9 0.8 copy-start.20
  39.0 1.1 copy-start.22
  39.0 1.6 %copy-start.18 = (bf16[256,10,2,64]{0,3,2,1:T(8,128)(2,1)}, bf16[256,10,2,64]{0,3,2,1:T(8,128)(2,1)S(1)}, u32[]{:S(2)}) copy-start(bf16[256,10,2,64]{0,3,2,1:T(8,128)(2,1)S(1)} %get-tuple-element.69) | copy-start | bytes 1966084
  40.6 2.0 %copy-start.26 = (f32[128]{0:T(128)S(1)}, f32[128]{0:T(128)}, u32[]{:S(2)}) copy-start(f32[128]{0:T(128)} %param.14) | copy-start | bytes 1540
  42.2 0.8 copy-start.9
  44.6 21.5 %all-to-all-start.1 = ((bf16[32,8,1280]{2,1,0:T(8,128)(2,1)}), bf16[32,8,1280]{2,1,0:T(8,128)(2,1)S(1)}, u32[]{:S(2)}, u32[]{:S(2)}) async-start(bf16[32,8,1280]{2,1,0:T(8,128)(2,1)} %fusion.18), calls=%async_computation.1 | async-start | bytes 1310720 | tf_op jit(solution)/shard_map/all_to_all | solution.py:137
  71.6 21.4 %all-to-all-start.2 = ((bf16[32,8,1280]{2,1,0:T(8,128)(2,1)}), bf16[32,8,1280]{2,1,0:T(8,128)(2,1)S(1)}, u32[]{:S(2)}, u32[]{:S(2)}) async-start(bf16[32,8,1280]{2,1,0:T(8,128)(2,1)} %fusion.19), calls=%async_computation.2 | async-start | bytes 1310720 | tf_op jit(solution)/shard_map/all_to_all | solution.py:144
  96.3 21.4 %all-to-all-start.3 = ((bf16[32,8,1280]{2,1,0:T(8,128)(2,1)}), bf16[32,8,1280]{2,1,0:T(8,128)(2,1)S(1)}, u32[]{:S(2)}, u32[]{:S(2)}) async-start(bf16[32,8,1280]{2,1,0:T(8,128)(2,1)} %bitcast.115), calls=%async_computation.3 | async-start | bytes 1310720 | tf_op jit(solution)/shard_map/all_to_all | solution.py:153
  103.6 2.3 %copy-start.1 = (bf16[512,10,2,64]{0,3,2,1:T(8,128)(2,1)S(1)}, bf16[512,10,2,64]{0,3,2,1:T(8,128)(2,1)}, u32[]{:S(2)}) copy-start(bf16[512,10,2,64]{0,3,2,1:T(8,128)(2,1)} %get-tuple-element.18) | copy-start | bytes 3932164
  103.6 2.3 %copy-start.3 = (bf16[512,10,2,64]{0,3,2,1:T(8,128)(2,1)S(1)}, bf16[512,10,2,64]{0,3,2,1:T(8,128)(2,1)}, u32[]{:S(2)}) copy-start(bf16[512,10,2,64]{0,3,2,1:T(8,128)(2,1)} %get-tuple-element.17) | copy-start | bytes 3932164
  103.7 2.7 %copy-start.8 = (bf16[512,1280]{0,1:T(8,128)(2,1)S(1)}, bf16[512,1280]{0,1:T(8,128)(2,1)}, u32[]{:S(2)}) copy-start(bf16[512,1280]{0,1:T(8,128)(2,1)} %copy.71) | copy-start | bytes 3932164
  107.0 1.1 copy-start.10
  107.0 1.3 copy-start.11
  107.0 1.6 %copy-start.19 = (bf16[256,10,2,64]{0,3,2,1:T(8,128)(2,1)S(1)}, bf16[256,10,2,64]{0,3,2,1:T(8,128)(2,1)}, u32[]{:S(2)}) copy-start(bf16[256,10,2,64]{0,3,2,1:T(8,128)(2,1)} %copy-done.18) | copy-start | bytes 1966084
  107.0 1.7 %copy-start.21 = (bf16[256,10,2,64]{0,3,2,1:T(8,128)(2,1)S(1)}, bf16[256,10,2,64]{0,3,2,1:T(8,128)(2,1)}, u32[]{:S(2)}) copy-start(bf16[256,10,2,64]{0,3,2,1:T(8,128)(2,1)} %copy-done.20) | copy-start | bytes 1966084
  107.0 1.8 %copy-start.23 = (bf16[256,10,2,64]{0,3,2,1:T(8,128)(2,1)S(1)}, bf16[256,10,2,64]{0,3,2,1:T(8,128)(2,1)}, u32[]{:S(2)}) copy-start(bf16[256,10,2,64]{0,3,2,1:T(8,128)(2,1)} %copy-done.22) | copy-start | bytes 1966084
  108.9 1.3 copy-start.7
  108.9 1.8 %copy-start.17 = (bf16[512,10,2,64]{0,3,2,1:T(8,128)(2,1)S(1)}, bf16[512,10,2,64]{0,3,2,1:T(8,128)(2,1)}, u32[]{:S(2)}) copy-start(bf16[512,10,2,64]{0,3,2,1:T(8,128)(2,1)} %copy-done.16) | copy-start | bytes 3932164
  110.2 1.4 copy-start.13
  110.2 1.8 %copy-start.15 = (bf16[512,10,2,64]{0,3,2,1:T(8,128)(2,1)S(1)}, bf16[512,10,2,64]{0,3,2,1:T(8,128)(2,1)}, u32[]{:S(2)}) copy-start(bf16[512,10,2,64]{0,3,2,1:T(8,128)(2,1)} %copy-done.14) | copy-start | bytes 3932164
  118.5 4.3 %collective-permute-start = (f32[28800]{0:T(1024)}, f32[28800]{0:T(1024)}, u32[]{:S(2)}, u32[]{:S(2)}) collective-permute-start(f32[28800]{0:T(1024)} %pad_maximum_fusion.4), channel_id=1, source_target_pairs={{0,1},{1,0},{2,3},{3,2},{4,5},{5,4},{6,7},{7,6},{8,9},{9,8},{10,11... | collective-permute-start | bytes 345608 | tf_op jit(solution)/shard_map/ppermute | solution.py:24
  120.1 5.2 %copy-start.2 = (bf16[512,10,2,64]{0,3,2,1:T(8,128)(2,1)S(1)}, bf16[512,10,2,64]{0,3,2,1:T(8,128)(2,1)}, u32[]{:S(2)}) copy-start(bf16[512,10,2,64]{0,3,2,1:T(8,128)(2,1)} %get-tuple-element.18) | copy-start | bytes 3932164
  120.1 5.2 %copy-start.4 = (bf16[512,10,2,64]{0,3,2,1:T(8,128)(2,1)S(1)}, bf16[512,10,2,64]{0,3,2,1:T(8,128)(2,1)}, u32[]{:S(2)}) copy-start(bf16[512,10,2,64]{0,3,2,1:T(8,128)(2,1)} %get-tuple-element.17) | copy-start | bytes 3932164
  123.7 5.7 %collective-permute-start.1 = (f32[28800]{0:T(1024)S(1)}, f32[28800]{0:T(1024)S(1)}, u32[]{:S(2)}, u32[]{:S(2)}) collective-permute-start(f32[28800]{0:T(1024)S(1)} %fusion.105), channel_id=1, source_target_pairs={{0,2},{1,3},{2,0},{3,1},{4,6},{5,7},{6,4},{7,5},{8,10},{9,11},{10,... | collective-permute-start | bytes 345608 | tf_op jit(solution)/shard_map/ppermute | solution.py:24
  129.3 4.9 %collective-permute-start.2 = (f32[28800]{0:T(1024)S(1)}, f32[28800]{0:T(1024)S(1)}, u32[]{:S(2)}, u32[]{:S(2)}) collective-permute-start(f32[28800]{0:T(1024)S(1)} %add.147), channel_id=1, source_target_pairs={{0,4},{1,5},{2,6},{3,7},{4,0},{5,1},{6,2},{7,3},{8,12},{9,13},{10,... | collective-permute-start | bytes 345608 | tf_op jit(solution)/shard_map/ppermute | solution.py:24
  134.3 4.9 %collective-permute-start.3 = (f32[28800]{0:T(1024)S(1)}, f32[28800]{0:T(1024)S(1)}, u32[]{:S(2)}, u32[]{:S(2)}) collective-permute-start(f32[28800]{0:T(1024)S(1)} %add.148), channel_id=1, source_target_pairs={{0,8},{1,9},{2,10},{3,11},{4,12},{5,13},{6,14},{7,15},{8,0},{9,1},... | collective-permute-start | bytes 345608 | tf_op jit(solution)/shard_map/ppermute | solution.py:24
  139.2 5.8 %collective-permute-start.4 = (f32[28800]{0:T(1024)S(1)}, f32[28800]{0:T(1024)S(1)}, u32[]{:S(2)}, u32[]{:S(2)}) collective-permute-start(f32[28800]{0:T(1024)S(1)} %add.149), channel_id=1, source_target_pairs={{0,16},{1,17},{2,18},{3,19},{4,20},{5,21},{6,22},{7,23},{8,24},{9,... | collective-permute-start | bytes 345608 | tf_op jit(solution)/shard_map/ppermute | solution.py:24

commit v15 on v11

--- a/solution.py
+++ b/solution.py
@@ -12,22 +12,27 @@
 EDGE_DEV = 128
 
 
-def device_sum(parts, n):
+def device_sum(parts, n, tie):
     sizes = [p.size for p in parts]
     flat = jnp.concatenate([p.reshape(-1) for p in parts])
     if n & (n - 1):
+        flat, tie = lax.optimization_barrier((flat, tie))
         flat = lax.psum(flat, ("region", "sub"))
     else:
         step = 1
         while step < n:
             perm = [(i, i ^ step) for i in range(n)]
             flat = flat + lax.ppermute(flat, ("region", "sub"), perm)
+            if step == 1:
+                flat, tie = lax.optimization_barrier((flat, tie))
             step *= 2
+        if n == 1:
+            flat, tie = lax.optimization_barrier((flat, tie))
     out, at = [], 0
     for p, size in zip(parts, sizes):
         out.append(flat[at : at + size].reshape(p.shape))
         at += size
-    return out
+    return out, tie
 
 
 def body(
@@ -158,8 +163,7 @@
     _, ga_conv, ga_bias, ga_theta = weight_grads(stack, gate, first, hidden, dz_inner)
     _, gb_conv, gb_bias, gb_theta = weight_grads(r_stack, r_gate, r_first, r_hidden, dz_slots)
     partial = (ga_conv + gb_conv, ga_bias + gb_bias, ga_theta + gb_theta)
-    partial, back_grads = lax.optimization_barrier((partial, back_grads))
-    sum_conv, sum_bias, sum_theta = device_sum(partial, device_list)
+    (sum_conv, sum_bias, sum_theta), back_grads = device_sum(partial, device_list, back_grads)
     dz = (
         (inner_sum + jnp.dot(members, back_grads, preferred_element_type=jnp.float32))
         .astype(jnp.bfloat16)

time: 148 us -> 148 us (level)
  matrix products: 32.3 us -> 35.2 us
  local copies, waits for them, and re-layouts: 19.6 us -> 16.8 us
    unnamed x62 -> x48, local copies, waits for them, and re-layouts: 10.9 us -> 8.14 us
    ppermute x5, waiting for transfers between devices: 6.31 us -> 8.82 us  [device_sum(): flat = flat + lax.ppermute(flat, ('region', 'sub'), perm)]
    all_to_all x1, waiting for transfers between devices: 3.18 us -> 0.77 us  [body(): lax.all_to_all(ret_grads, ('region', 'sub'), split_axis=0, concat_axis=0,...]
    dot_general x2, matrix products: 1.86 us -> 4.24 us  [weight_grads(): jnp.einsum('stbk,stbf->kf', st, du, preferred_element_type=jnp.float32)]
    reduce_sum x2, other arithmetic: 0.71 us -> 2.56 us  [weight_grads(): g_bias = jnp.sum(du.astype(jnp.float32), axis=(0, 1, 2))]
where the time goes in v15:
time: 148 us; the launch traced here: 147 us
  waiting for transfers between devices  57.5 us (39%)
  matrix products  35.2 us (24%)
  starting transfers between devices  24 us (16%)
  local copies, waits for them, and re-layouts  16.8 us (11%)
  other arithmetic  12.6 us (9%)
    all_to_all x1, waiting for transfers between devices, body(): lax.all_to_all(send_grads, ('region', 'sub'), split_axis=0, concat_axis=0...  17.6 us
    all_to_all x1, waiting for transfers between devices, body(): lax.all_to_all(ret_rows, ('region', 'sub'), split_axis=0, concat_axis=0,...  15.6 us
    all_to_all x1, waiting for transfers between devices, body(): lax.all_to_all(send, ('region', 'sub'), split_axis=0, concat_axis=0, tile...  14.7 us
    ppermute x5, waiting for transfers between devices, device_sum(): flat = flat + lax.ppermute(flat, ('region', 'sub'), perm)  8.82 us
    unnamed x48, local copies, waits for them, and re-layouts  8.14 us
    all_to_all x1, starting transfers between devices, body(): lax.all_to_all(send, ('region', 'sub'), split_axis=0, concat_axis=0, tile...  7.41 us
    dot_general x2, matrix products, weight_grads(): jnp.einsum('stbd,cd->stbc', dzr, theta, preferred_element_type=jnp.float32)  6.51 us
    ppermute x5, starting transfers between devices, device_sum(): flat = flat + lax.ppermute(flat, ('region', 'sub'), perm)  5.81 us
  transfers between devices with their start and end apart: 9, of which 8 were waited for; matrix products, arithmetic and copies ran while one was open for 21% of the time, Pallas kernels for 0%

profile of v15, /device:TPU:0, one launch (start us, length us, event | category | flops | bytes accessed | tf_op | source)
XLA Modules:
  0.0 147.1 jit_solution(16019479340422243543)
XLA Ops:
  0.6 0.7 broadcast_add_fusion.4
  1.3 0.7 broadcast_add_fusion.3
  2.0 0.9 convert_reduce_fusion.5
  2.9 0.7 fusion.102
  3.7 2.1 %convolution_convert_fusion.3 = bf16[256,1536]{1,0:T(8,128)(2,1)S(1)} fusion(bf16[512,1536]{1,0:T(8,128)(2,1)} %param.10, s32[256]{0:T(256)S(1)} %get-tuple-element.57), kind=kOutput, calls=%fused_computation.32 | convolution fusion | flops 403439616 | bytes 2360320 | tf_op jit(solution)/shard_map/sn,sf->nf/dot_general | solution.py:100
  5.9 1.0 maximum_bitcast_fusion
  6.9 7.4 %all-to-all-start = ((bf16[32,8,1664]{2,1,0:T(8,128)(2,1)}), bf16[32,8,1664]{2,1,0:T(8,128)(2,1)}, u32[]{:S(2)}, u32[]{:S(2)}) async-start(bf16[32,8,1664]{2,1,0:T(8,128)(2,1)} %maximum_bitcast_fusion), calls=%async_computation | async-start | bytes 1703936 | tf_op jit(solution)/shard_map/all_to_all | solution.py:110
  14.3 0.7 copy.66
  15.1 0.5 fusion.106
  15.9 1.0 broadcast_add_fusion
  17.2 0.5 copy-done.12
  17.7 0.7 multiply_convert_fusion.5
  18.4 1.6 %copy-done.2 = f32[512,10,2,128]{0,3,2,1:T(8,128)} copy-done((f32[512,10,2,128]{0,3,2,1:T(8,128)}, f32[512,10,2,128]{0,3,2,1:T(8,128)S(1)}, u32[]{:S(2)}) %copy-start.2) | copy-done | bytes 5242904
  20.0 0.6 convolution_convert_fusion.4
  20.6 0.5 copy-done.3
  21.1 0.6 fusion.73
  21.6 14.7 %all-to-all-done = bf16[32,8,1664]{2,1,0:T(8,128)(2,1)} async-done(((bf16[32,8,1664]{2,1,0:T(8,128)(2,1)}), bf16[32,8,1664]{2,1,0:T(8,128)(2,1)}, u32[]{:S(2)}, u32[]{:S(2)}) %all-to-all-start) | async-done | bytes 852000 | tf_op jit(solution)/shard_map/all_to_all | solution.py:110
  36.3 1.0 convert_reduce_fusion.4
  37.3 1.2 slice.102
  39.1 0.5 convolution_add_fusion.4
  40.3 0.4 multiply_convert_fusion.8
  40.7 0.4 convolution_convert_fusion.5
  41.1 0.4 fusion.16
  41.8 1.2 fusion.14
  43.0 3.6 %all-to-all-start.1 = ((bf16[32,8,1280]{2,1,0:T(8,128)(2,1)}), bf16[32,8,1280]{2,1,0:T(8,128)(2,1)S(1)}, u32[]{:S(2)}, u32[]{:S(2)}) async-start(bf16[32,8,1280]{2,1,0:T(8,128)(2,1)} %fusion.14), calls=%async_computation.1 | async-start | bytes 1310720 | tf_op jit(solution)/shard_map/all_to_all | solution.py:134
  46.8 2.1 %fusion.71 = f32[512,1280]{1,0:T(8,128)} fusion(bf16[128,1280]{1,0:T(8,128)(2,1)S(1)} %fusion.16, s32[512]{0:T(512)S(1)} %bitcast.127, s32[512]{0:T(512)S(1)} %bitcast.122), kind=kOutput, calls=%fused_computation.85 | convolution fusion | flops 168165376 | bytes 2953216 | tf_op jit(solution)/shard_map/es,ef->sf/dot_general | solution.py:129
  48.9 15.6 %all-to-all-done.1 = bf16[32,8,1280]{2,1,0:T(8,128)(2,1)S(1)} async-done(((bf16[32,8,1280]{2,1,0:T(8,128)(2,1)}), bf16[32,8,1280]{2,1,0:T(8,128)(2,1)S(1)}, u32[]{:S(2)}, u32[]{:S(2)}) %all-to-all-start.1) | async-done | bytes 655392 | tf_op jit(solution)/shard_map/all_to_all | solution.py:134
  64.5 4.0 %divide_convert_fusion = (bf16[512,1280]{1,0:T(8,128)(2,1)S(1)}, bf16[512,1280]{1,0:T(8,128)(2,1)}) fusion(bf16[512,1280]{1,0:T(8,128)(2,1)} %param.19, f32[512]{0:T(512)S(1)} %broadcast_add_fusion.1, f32[512,1280]{1,0:T(8,128)} %fusion.71, bf16[32,8,1280]{2,1,0:T(8,128)(2,1)S(1)} %all-to-all-done.1, s32[256]{0:T(256)S(1)} %get-tuple-element.57), kind=kOutput, calls=%fused_computation.24 | convolution fusion | flops 345767936 | bytes 7212032 | tf_op jit(solution)/shard_map/dot_general | solution.py:131
  68.6 1.4 fusion.15
  69.9 3.5 %all-to-all-start.2 = ((bf16[32,8,1280]{2,1,0:T(8,128)(2,1)}), bf16[32,8,1280]{2,1,0:T(8,128)(2,1)S(1)}, u32[]{:S(2)}, u32[]{:S(2)}) async-start(bf16[32,8,1280]{2,1,0:T(8,128)(2,1)} %fusion.15), calls=%async_computation.2 | async-start | bytes 1310720 | tf_op jit(solution)/shard_map/all_to_all | solution.py:141
  73.5 0.3 fusion.69
  73.8 17.6 %all-to-all-done.2 = bf16[32,8,1280]{2,1,0:T(8,128)(2,1)S(1)} async-done(((bf16[32,8,1280]{2,1,0:T(8,128)(2,1)}), bf16[32,8,1280]{2,1,0:T(8,128)(2,1)S(1)}, u32[]{:S(2)}, u32[]{:S(2)}) %all-to-all-start.2) | async-done | bytes 655392 | tf_op jit(solution)/shard_map/all_to_all | solution.py:141
  91.6 1.3 convolution_convert_fusion
  92.9 0.3 fusion.75
  93.3 0.5 fusion.67
  93.9 1.1 copy-done.6
  95.0 0.6 multiply_convert_fusion.7
  96.5 1.3 fusion.27
  98.1 3.7 %all-to-all-start.3 = ((bf16[32,8,1280]{2,1,0:T(8,128)(2,1)}), bf16[32,8,1280]{2,1,0:T(8,128)(2,1)S(1)}, u32[]{:S(2)}, u32[]{:S(2)}) async-start(bf16[32,8,1280]{2,1,0:T(8,128)(2,1)} %bitcast.115), calls=%async_computation.3 | async-start | bytes 1310720 | tf_op jit(solution)/shard_map/all_to_all | solution.py:150
  101.8 1.2 convert_element_type.133
  103.0 2.4 %copy.71 = bf16[512,1280]{0,1:T(8,128)(2,1)} copy(bf16[512,1280]{1,0:T(8,128)(2,1)} %convert_element_type.133) | data formatting | bytes 2621440 | tf_op jit(solution)/shard_map/convert_element_type | solution.py:162
  105.4 5.9 %multiply_convert_fusion.3 = (bf16[512,10,2,64]{0,3,2,1:T(8,128)(2,1)}, bf16[512,10,2,64]{0,3,2,1:T(8,128)(2,1)}) fusion(f32[512,10,2,128]{0,3,2,1:T(8,128)} %copy-done.2, bf16[512,10,2,64]{0,3,2,1:T(8,128)(2,1)} %bitcast.118, bf16[64,64]{1,0:T(8,128)(2,1)S(1)} %copy-done.19), kind=kOutput, calls=%fused_computation.23 | convolution fusion | flops 90439680 | bytes 9183232 | tf_op jit(solution)/shard_map/stbd,cd->stbc/dot_general | solution.py:156
  111.3 0.5 fusion.52
  111.8 2.3 %convert_reduce_fusion = f32[128]{0:T(128)S(1)} fusion(bf16[512,10,2,64]{0,3,2,1:T(8,128)(2,1)} %get-tuple-element.43, bf16[512,10,2,64]{0,3,2,1:T(8,128)(2,1)} %get-tuple-element.42), kind=kLoop, calls=%fused_computation | loop fusion | flops 6553472 | bytes 2621952 | tf_op jit(solution)/shard_map/reduce_sum | solution.py:159
  114.3 2.9 %fusion.42 = f32[24576]{0:T(1024)S(1)} fusion(f32[192,128]{1,0:T(8,128)} %fusion.27, bf16[512,10,2,64]{0,3,2,1:T(8,128)(2,1)} %copy-done.11, bf16[512,10,2,64]{0,3,2,1:T(8,128)(2,1)} %copy-done.12, bf16[512,10,2,64]{0,3,2,1:T(8,128)(2,1)} %copy-done.10, bf16[512,10,2,64]{0,3,2,1:T(8,128)(2,1)S(1)} %copy-done.9, bf16[512,10,2,64]{0,3,2,1:T(8,128)(2,1)S(1)} %copy-done.8), kind=kOutput, calls=%fused_computation.62 | convolution fusion | flops 520380416 | bytes 6750208 | tf_op jit(solution)/shard_map/stbk,stbf->kf/dot_general | solution.py:158
  117.5 1.2 collective-permute-done
  118.7 0.8 all-to-all-done.3
  119.5 1.6 %fusion.3 = bf16[512,1280]{1,0:T(8,128)(2,1)} fusion(f32[512,1280]{1,0:T(8,128)S(1)} %fusion.67, bf16[256,1280]{1,0:T(8,128)(2,1)S(1)} %bitcast.114, s32[256]{0:T(256)S(1)} %get-tuple-element.57), kind=kOutput, calls=%fused_computation.8 | convolution fusion | flops 337248256 | bytes 4588544 | tf_op jit(solution)/shard_map/dot_general | solution.py:168
  121.1 1.6 %copy.80 = bf16[512,1280]{0,1:T(8,128)(2,1)S(1)} copy(bf16[512,1280]{1,0:T(8,128)(2,1)} %fusion.3) | data formatting | bytes 2621440 | tf_op jit(solution)/shard_map/convert_element_type | solution.py:169
  122.7 1.4 collective-permute-start.1
  124.2 3.8 %multiply_convert_fusion.1 = (bf16[512,10,2,64]{0,3,2,1:T(8,128)(2,1)S(1)}, bf16[512,10,2,64]{0,3,2,1:T(8,128)(2,1)S(1)}) fusion(f32[512,10,2,128]{0,3,2,1:T(8,128)} %copy-done.2, bf16[512,10,2,64]{0,3,2,1:T(8,128)(2,1)S(1)} %bitcast.117, bf16[64,64]{1,0:T(8,128)(2,1)S(1)} %copy-done.19), kind=kOutput, calls=%fused_computation.20 | convolution fusion | flops 90439680 | bytes 9183232 | tf_op jit(solution)/shard_map/stbd,cd->stbc/dot_general | solution.py:172
  128.0 1.5 %collective-permute-start.2 = (f32[28800]{0:T(1024)S(1)}, f32[28800]{0:T(1024)S(1)}, u32[]{:S(2)}, u32[]{:S(2)}) collective-permute-start(f32[28800]{0:T(1024)S(1)} %add.147), channel_id=1, source_target_pairs={{0,4},{1,5},{2,6},{3,7},{4,0},{5,1},{6,2},{7,3},{8,12},{9,13},{10,... | collective-permute-start | bytes 345608 | tf_op jit(solution)/shard_map/ppermute | solution.py:25
  129.6 1.2 fusion.7
  130.7 2.5 %collective-permute-done.2 = f32[28800]{0:T(1024)S(1)} collective-permute-done((f32[28800]{0:T(1024)S(1)}, f32[28800]{0:T(1024)S(1)}, u32[]{:S(2)}, u32[]{:S(2)}) %collective-permute-start.2) | collective-permute-done | bytes 115232 | tf_op jit(solution)/shard_map/ppermute | solution.py:25
  133.2 1.0 collective-permute-start.3
  134.2 1.6 %fusion.105 = (f32[512,10,2,64]{0,3,2,1:T(8,128)S(1)}, f32[512,10,2,64]{0,3,2,1:T(8,128)S(1)}, f32[512,10,2,64]{0,3,2,1:T(8,128)S(1)}) fusion(f32[512,10,2,192]{0,3,2,1:T(8,128)S(1)} %fusion.7), kind=kLoop, calls=%fused_computation.137 | loop fusion | bytes 15728640 | tf_op jit(solution)/shard_map/slice | solution.py:181
  135.8 2.3 %collective-permute-done.3 = f32[28800]{0:T(1024)S(1)} collective-permute-done((f32[28800]{0:T(1024)S(1)}, f32[28800]{0:T(1024)S(1)}, u32[]{:S(2)}, u32[]{:S(2)}) %collective-permute-start.3) | collective-permute-done | bytes 115232 | tf_op jit(solution)/shard_map/ppermute | solution.py:25
  138.2 1.8 %collective-permute-start.4 = (f32[28800]{0:T(1024)S(1)}, f32[28800]{0:T(1024)S(1)}, u32[]{:S(2)}, u32[]{:S(2)}) collective-permute-start(f32[28800]{0:T(1024)S(1)} %add.149), channel_id=1, source_target_pairs={{0,16},{1,17},{2,18},{3,19},{4,20},{5,21},{6,22},{7,23},{8,24},{9,... | collective-permute-start | bytes 345608 | tf_op jit(solution)/shard_map/ppermute | solution.py:25
  139.9 1.0 add_convert_fusion
  140.9 1.6 %copy.82 = bf16[512,1536]{1,0:T(8,128)(2,1)} copy(bf16[512,1536]{0,1:T(8,128)(2,1)S(1)} %bitcast.111) | data formatting | bytes 3145728
  142.5 2.7 %collective-permute-done.4 = f32[28800]{0:T(1024)S(1)} collective-permute-done((f32[28800]{0:T(1024)S(1)}, f32[28800]{0:T(1024)S(1)}, u32[]{:S(2)}, u32[]{:S(2)}) %collective-permute-start.4) | collective-permute-done | bytes 115232 | tf_op jit(solution)/shard_map/ppermute | solution.py:25
  145.3 0.5 slice_multiply_fusion.2
  145.8 0.6 fusion.84
  146.4 0.7 mul.149
  (68 shorter events, 4.6 us)
Async XLA Ops:
  0.6 15.3 %copy-start = (bf16[192,128]{1,0:T(8,128)(2,1)S(1)}, bf16[192,128]{1,0:T(8,128)(2,1)}, u32[]{:S(2)}) copy-start(bf16[192,128]{1,0:T(8,128)(2,1)} %param.11) | copy-start | bytes 147460
  3.7 10.6 %copy-start.1 = (bf16[512,1536]{1,0:T(8,128)(2,1)S(1)}, bf16[512,1536]{1,0:T(8,128)(2,1)}, u32[]{:S(2)}) copy-start(bf16[512,1536]{1,0:T(8,128)(2,1)} %param.10) | copy-start | bytes 4718596
  6.9 29.4 %all-to-all-start = ((bf16[32,8,1664]{2,1,0:T(8,128)(2,1)}), bf16[32,8,1664]{2,1,0:T(8,128)(2,1)}, u32[]{:S(2)}, u32[]{:S(2)}) async-start(bf16[32,8,1664]{2,1,0:T(8,128)(2,1)} %maximum_bitcast_fusion), calls=%async_computation | async-start | bytes 1703936 | tf_op jit(solution)/shard_map/all_to_all | solution.py:110
  15.0 0.7 copy-start.20
  15.1 0.8 copy-start.22
  15.7 1.2 copy-start.10
  15.7 1.5 %copy-start.11 = (bf16[512,10,2,64]{0,3,2,1:T(8,128)(2,1)}, bf16[512,10,2,64]{0,3,2,1:T(8,128)(2,1)S(1)}, u32[]{:S(2)}) copy-start(bf16[512,10,2,64]{0,3,2,1:T(8,128)(2,1)S(1)} %get-tuple-element.49) | copy-start | bytes 3932164
  15.7 2.0 %copy-start.12 = (bf16[512,10,2,64]{0,3,2,1:T(8,128)(2,1)}, bf16[512,10,2,64]{0,3,2,1:T(8,128)(2,1)S(1)}, u32[]{:S(2)}) copy-start(bf16[512,10,2,64]{0,3,2,1:T(8,128)(2,1)S(1)} %get-tuple-element.50) | copy-start | bytes 3932164
  17.7 2.3 %copy-start.2 = (f32[512,10,2,128]{0,3,2,1:T(8,128)}, f32[512,10,2,128]{0,3,2,1:T(8,128)S(1)}, u32[]{:S(2)}) copy-start(f32[512,10,2,128]{0,3,2,1:T(8,128)S(1)} %broadcast_add_fusion) | copy-start | bytes 15728644
  17.7 2.3 %copy-start.19 = (bf16[64,64]{1,0:T(8,128)(2,1)S(1)}, bf16[64,64]{1,0:T(8,128)(2,1)}, u32[]{:S(2)}) copy-start(bf16[64,64]{1,0:T(8,128)(2,1)} %param.13) | copy-start | bytes 24580
  20.0 1.1 copy-start.3
  39.1 0.8 copy-start.13
  39.1 1.1 copy-start.15
  39.1 1.2 copy-start.17
  40.3 1.5 copy-start.5
  40.3 0.8 copy-start.21
  43.0 21.5 %all-to-all-start.1 = ((bf16[32,8,1280]{2,1,0:T(8,128)(2,1)}), bf16[32,8,1280]{2,1,0:T(8,128)(2,1)S(1)}, u32[]{:S(2)}, u32[]{:S(2)}) async-start(bf16[32,8,1280]{2,1,0:T(8,128)(2,1)} %fusion.14), calls=%async_computation.1 | async-start | bytes 1310720 | tf_op jit(solution)/shard_map/all_to_all | solution.py:134
  69.9 21.4 %all-to-all-start.2 = ((bf16[32,8,1280]{2,1,0:T(8,128)(2,1)}), bf16[32,8,1280]{2,1,0:T(8,128)(2,1)S(1)}, u32[]{:S(2)}, u32[]{:S(2)}) async-start(bf16[32,8,1280]{2,1,0:T(8,128)(2,1)} %fusion.15), calls=%async_computation.2 | async-start | bytes 1310720 | tf_op jit(solution)/shard_map/all_to_all | solution.py:141
  93.3 1.7 %copy-start.6 = (f32[256,10,2,128]{0,3,2,1:T(8,128)S(1)}, f32[256,10,2,128]{0,3,2,1:T(8,128)}, u32[]{:S(2)}) copy-start(f32[256,10,2,128]{0,3,2,1:T(8,128)} %copy-done.5) | copy-start | bytes 7864324
  95.0 1.1 copy-start.14
  95.0 1.3 copy-start.16
  95.0 1.5 %copy-start.18 = (bf16[256,10,2,64]{0,3,2,1:T(8,128)(2,1)S(1)}, bf16[256,10,2,64]{0,3,2,1:T(8,128)(2,1)}, u32[]{:S(2)}) copy-start(bf16[256,10,2,64]{0,3,2,1:T(8,128)(2,1)} %copy-done.17) | copy-start | bytes 1966084
  98.1 21.4 %all-to-all-start.3 = ((bf16[32,8,1280]{2,1,0:T(8,128)(2,1)}), bf16[32,8,1280]{2,1,0:T(8,128)(2,1)S(1)}, u32[]{:S(2)}, u32[]{:S(2)}) async-start(bf16[32,8,1280]{2,1,0:T(8,128)(2,1)} %bitcast.115), calls=%async_computation.3 | async-start | bytes 1310720 | tf_op jit(solution)/shard_map/all_to_all | solution.py:150
  105.4 5.9 %copy-start.4 = (bf16[512,10,2,64]{0,3,2,1:T(8,128)(2,1)S(1)}, bf16[512,10,2,64]{0,3,2,1:T(8,128)(2,1)}, u32[]{:S(2)}) copy-start(bf16[512,10,2,64]{0,3,2,1:T(8,128)(2,1)} %copy-done.3) | copy-start | bytes 3932164
  105.4 5.9 %copy-start.7 = (bf16[512,1280]{0,1:T(8,128)(2,1)S(1)}, bf16[512,1280]{0,1:T(8,128)(2,1)}, u32[]{:S(2)}) copy-start(bf16[512,1280]{0,1:T(8,128)(2,1)} %copy.71) | copy-start | bytes 3932164
  111.8 2.3 %copy-start.8 = (bf16[512,10,2,64]{0,3,2,1:T(8,128)(2,1)S(1)}, bf16[512,10,2,64]{0,3,2,1:T(8,128)(2,1)}, u32[]{:S(2)}) copy-start(bf16[512,10,2,64]{0,3,2,1:T(8,128)(2,1)} %get-tuple-element.42) | copy-start | bytes 3932164
  111.8 2.5 %copy-start.9 = (bf16[512,10,2,64]{0,3,2,1:T(8,128)(2,1)S(1)}, bf16[512,10,2,64]{0,3,2,1:T(8,128)(2,1)}, u32[]{:S(2)}) copy-start(bf16[512,10,2,64]{0,3,2,1:T(8,128)(2,1)} %get-tuple-element.43) | copy-start | bytes 3932164
  117.3 1.4 collective-permute-start
  122.7 5.3 %collective-permute-start.1 = (f32[28800]{0:T(1024)S(1)}, f32[28800]{0:T(1024)S(1)}, u32[]{:S(2)}, u32[]{:S(2)}) collective-permute-start(f32[28800]{0:T(1024)S(1)} %fusion.104), channel_id=1, source_target_pairs={{0,2},{1,3},{2,0},{3,1},{4,6},{5,7},{6,4},{7,5},{8,10},{9,11},{10,... | collective-permute-start | bytes 345608 | tf_op jit(solution)/shard_map/ppermute | solution.py:25
  128.0 5.2 %collective-permute-start.2 = (f32[28800]{0:T(1024)S(1)}, f32[28800]{0:T(1024)S(1)}, u32[]{:S(2)}, u32[]{:S(2)}) collective-permute-start(f32[28800]{0:T(1024)S(1)} %add.147), channel_id=1, source_target_pairs={{0,4},{1,5},{2,6},{3,7},{4,0},{5,1},{6,2},{7,3},{8,12},{9,13},{10,... | collective-permute-start | bytes 345608 | tf_op jit(solution)/shard_map/ppermute | solution.py:25
  133.2 4.9 %collective-permute-start.3 = (f32[28800]{0:T(1024)S(1)}, f32[28800]{0:T(1024)S(1)}, u32[]{:S(2)}, u32[]{:S(2)}) collective-permute-start(f32[28800]{0:T(1024)S(1)} %add.148), channel_id=1, source_target_pairs={{0,8},{1,9},{2,10},{3,11},{4,12},{5,13},{6,14},{7,15},{8,0},{9,1},... | collective-permute-start | bytes 345608 | tf_op jit(solution)/shard_map/ppermute | solution.py:25
  138.2 7.1 %collective-permute-start.4 = (f32[28800]{0:T(1024)S(1)}, f32[28800]{0:T(1024)S(1)}, u32[]{:S(2)}, u32[]{:S(2)}) collective-permute-start(f32[28800]{0:T(1024)S(1)} %add.149), channel_id=1, source_target_pairs={{0,16},{1,17},{2,18},{3,19},{4,20},{5,21},{6,22},{7,23},{8,24},{9,... | collective-permute-start | bytes 345608 | tf_op jit(solution)/shard_map/ppermute | solution.py:25

commit v16 on v15

--- a/solution.py
+++ b/solution.py
@@ -19,15 +19,28 @@
         flat, tie = lax.optimization_barrier((flat, tie))
         flat = lax.psum(flat, ("region", "sub"))
     else:
-        step = 1
-        while step < n:
-            perm = [(i, i ^ step) for i in range(n)]
-            flat = flat + lax.ppermute(flat, ("region", "sub"), perm)
-            if step == 1:
-                flat, tie = lax.optimization_barrier((flat, tie))
-            step *= 2
-        if n == 1:
+        axes = ("region", "sub")
+        if n == 1 or flat.shape[0] % 2:
             flat, tie = lax.optimization_barrier((flat, tie))
+            step = 1
+            while step < n:
+                flat = flat + lax.ppermute(flat, axes, [(i, i ^ step) for i in range(n)])
+                step *= 2
+        else:
+            half = flat.shape[0] // 2
+            low = lax.axis_index(axes) % 2 == 0
+            lo, hi = flat[:half], flat[half:]
+            pair = [(i, i ^ 1) for i in range(n)]
+            kept = jnp.where(low, lo, hi) + lax.ppermute(jnp.where(low, hi, lo), axes, pair)
+            kept, tie = lax.optimization_barrier((kept, tie))
+            step = 2
+            while step < n:
+                kept = kept + lax.ppermute(kept, axes, [(i, i ^ step) for i in range(n)])
+                step *= 2
+            other = lax.ppermute(kept, axes, pair)
+            flat = jnp.where(
+                low, jnp.concatenate([kept, other]), jnp.concatenate([other, kept])
+            )
     out, at = [], 0
     for p, size in zip(parts, sizes):
         out.append(flat[at : at + size].reshape(p.shape))

time: 148 us -> 154 us (1.041)
  waiting for transfers between devices: 57.5 us -> 66.3 us
  starting transfers between devices: 24 us -> 22.2 us
  local copies, waits for them, and re-layouts: 16.8 us -> 15.2 us
    all_to_all x1, waiting for transfers between devices: 0.77 us -> 10.8 us  [body(): lax.all_to_all(ret_grads, ('region', 'sub'), split_axis=0, concat_axis=0,...]
    ppermute x5 -> x6, starting transfers between devices: 5.81 us -> 3.73 us  [the longest x4 3.56 us: device_sum(): kept = kept + lax.ppermute(kept, axes, [(i, i ^ step) for i in range(n)])]
    ppermute x5 -> x6, waiting for transfers between devices: 8.82 us -> 7.83 us  [the longest x4 6.62 us: device_sum(): kept = kept + lax.ppermute(kept, axes, [(i, i ^ step) for i in range(n)])]
  transfers between devices with their start and end apart: 9 -> 10, of which waited for: 8 -> 7; matrix products, arithmetic and copies ran while one was open for 21% -> 16% of each run, Pallas kernels for 0% -> 0%
where the time goes in v16:
time: 154 us
  waiting for transfers between devices  66.3 us (43%)
  matrix products  35.2 us (23%)
  starting transfers between devices  22.2 us (14%)
  local copies, waits for them, and re-layouts  15.2 us (10%)
  other arithmetic  13.4 us (9%)
    all_to_all x1, waiting for transfers between devices, body(): lax.all_to_all(send_grads, ('region', 'sub'), split_axis=0, concat_axis=0...  17.4 us
    all_to_all x1, waiting for transfers between devices, body(): lax.all_to_all(ret_rows, ('region', 'sub'), split_axis=0, concat_axis=0,...  15.6 us
    all_to_all x1, waiting for transfers between devices, body(): lax.all_to_all(send, ('region', 'sub'), split_axis=0, concat_axis=0, tile...  14.7 us
    all_to_all x1, waiting for transfers between devices, body(): lax.all_to_all(ret_grads, ('region', 'sub'), split_axis=0, concat_axis=0,...  10.8 us
    all_to_all x1, starting transfers between devices, body(): lax.all_to_all(send, ('region', 'sub'), split_axis=0, concat_axis=0, tile...  7.41 us
    unnamed x48, local copies, waits for them, and re-layouts  7.09 us
    ppermute x4, waiting for transfers between devices, device_sum(): kept = kept + lax.ppermute(kept, axes, [(i, i ^ step) for i in range(n)])  6.62 us
    dot_general x2, matrix products, weight_grads(): jnp.einsum('stbd,cd->stbc', dzr, theta, preferred_element_type=jnp.float32)  6.52 us
  transfers between devices with their start and end apart: 10, of which 7 were waited for; matrix products, arithmetic and copies ran while one was open for 16% of the time, Pallas kernels for 0%

profile of v16, /device:TPU:0, one launch (start us, length us, event | category | flops | bytes accessed | tf_op | source)
XLA Modules:
  0.0 153.5 jit_solution(17101126218287612883)
XLA Ops:
  0.6 0.7 broadcast_add_fusion.4
  1.3 0.9 convert_reduce_fusion.5
  2.2 0.7 fusion.104
  2.9 0.7 broadcast_add_fusion.3
  3.7 2.1 %convolution_convert_fusion.3 = bf16[256,1536]{1,0:T(8,128)(2,1)S(1)} fusion(bf16[512,1536]{1,0:T(8,128)(2,1)} %param.10, s32[256]{0:T(256)S(1)} %get-tuple-element.57), kind=kOutput, calls=%fused_computation.32 | convolution fusion | flops 403439616 | bytes 2360320 | tf_op jit(solution)/shard_map/sn,sf->nf/dot_general | solution.py:113
  5.9 1.0 maximum_bitcast_fusion
  6.9 7.4 %all-to-all-start = ((bf16[32,8,1664]{2,1,0:T(8,128)(2,1)}), bf16[32,8,1664]{2,1,0:T(8,128)(2,1)}, u32[]{:S(2)}, u32[]{:S(2)}) async-start(bf16[32,8,1664]{2,1,0:T(8,128)(2,1)} %maximum_bitcast_fusion), calls=%async_computation | async-start | bytes 1703936 | tf_op jit(solution)/shard_map/all_to_all | solution.py:123
  14.3 0.7 copy.66
  15.1 0.5 fusion.107
  15.9 1.0 broadcast_add_fusion
  16.9 0.3 copy-done.11
  17.2 0.4 copy-done.12
  17.7 0.7 multiply_convert_fusion.5
  18.4 1.6 %copy-done.2 = f32[512,10,2,128]{0,3,2,1:T(8,128)} copy-done((f32[512,10,2,128]{0,3,2,1:T(8,128)}, f32[512,10,2,128]{0,3,2,1:T(8,128)S(1)}, u32[]{:S(2)}) %copy-start.2) | copy-done | bytes 5242904
  20.0 0.6 convolution_convert_fusion.4
  20.6 0.5 copy-done.3
  21.0 0.6 fusion.73
  21.6 14.7 %all-to-all-done = bf16[32,8,1664]{2,1,0:T(8,128)(2,1)} async-done(((bf16[32,8,1664]{2,1,0:T(8,128)(2,1)}), bf16[32,8,1664]{2,1,0:T(8,128)(2,1)}, u32[]{:S(2)}, u32[]{:S(2)}) %all-to-all-start) | async-done | bytes 852000 | tf_op jit(solution)/shard_map/all_to_all | solution.py:123
  36.3 1.2 slice.97
  37.5 1.0 convert_reduce_fusion.4
  39.0 0.5 convolution_add_fusion.4
  39.5 0.3 copy-done.13
  40.2 0.4 multiply_convert_fusion.8
  40.6 0.4 convolution_convert_fusion.5
  41.1 0.4 fusion.16
  41.7 1.2 fusion.14
  42.9 3.6 %all-to-all-start.1 = ((bf16[32,8,1280]{2,1,0:T(8,128)(2,1)}), bf16[32,8,1280]{2,1,0:T(8,128)(2,1)S(1)}, u32[]{:S(2)}, u32[]{:S(2)}) async-start(bf16[32,8,1280]{2,1,0:T(8,128)(2,1)} %fusion.14), calls=%async_computation.1 | async-start | bytes 1310720 | tf_op jit(solution)/shard_map/all_to_all | solution.py:147
  46.7 2.1 %fusion.71 = f32[512,1280]{1,0:T(8,128)} fusion(bf16[128,1280]{1,0:T(8,128)(2,1)S(1)} %fusion.16, s32[512]{0:T(512)S(1)} %bitcast.127, s32[512]{0:T(512)S(1)} %bitcast.122), kind=kOutput, calls=%fused_computation.85 | convolution fusion | flops 168165376 | bytes 2953216 | tf_op jit(solution)/shard_map/es,ef->sf/dot_general | solution.py:142
  48.8 15.6 %all-to-all-done.1 = bf16[32,8,1280]{2,1,0:T(8,128)(2,1)S(1)} async-done(((bf16[32,8,1280]{2,1,0:T(8,128)(2,1)}), bf16[32,8,1280]{2,1,0:T(8,128)(2,1)S(1)}, u32[]{:S(2)}, u32[]{:S(2)}) %all-to-all-start.1) | async-done | bytes 655392 | tf_op jit(solution)/shard_map/all_to_all | solution.py:147
  64.4 4.0 %divide_convert_fusion = (bf16[512,1280]{1,0:T(8,128)(2,1)S(1)}, bf16[512,1280]{1,0:T(8,128)(2,1)}) fusion(bf16[512,1280]{1,0:T(8,128)(2,1)} %param.19, f32[512]{0:T(512)S(1)} %broadcast_add_fusion.1, f32[512,1280]{1,0:T(8,128)} %fusion.71, bf16[32,8,1280]{2,1,0:T(8,128)(2,1)S(1)} %all-to-all-done.1, s32[256]{0:T(256)S(1)} %get-tuple-element.57), kind=kOutput, calls=%fused_computation.24 | convolution fusion | flops 345767936 | bytes 7212032 | tf_op jit(solution)/shard_map/dot_general | solution.py:144
  68.5 1.5 fusion.15
  69.9 3.7 %all-to-all-start.2 = ((bf16[32,8,1280]{2,1,0:T(8,128)(2,1)}), bf16[32,8,1280]{2,1,0:T(8,128)(2,1)S(1)}, u32[]{:S(2)}, u32[]{:S(2)}) async-start(bf16[32,8,1280]{2,1,0:T(8,128)(2,1)} %fusion.15), calls=%async_computation.2 | async-start | bytes 1310720 | tf_op jit(solution)/shard_map/all_to_all | solution.py:154
  73.6 0.3 fusion.69
  74.0 17.4 %all-to-all-done.2 = bf16[32,8,1280]{2,1,0:T(8,128)(2,1)S(1)} async-done(((bf16[32,8,1280]{2,1,0:T(8,128)(2,1)}), bf16[32,8,1280]{2,1,0:T(8,128)(2,1)S(1)}, u32[]{:S(2)}, u32[]{:S(2)}) %all-to-all-start.2) | async-done | bytes 655392 | tf_op jit(solution)/shard_map/all_to_all | solution.py:154
  91.6 0.5 fusion.67
  92.2 0.4 fusion.75
  92.5 1.2 convolution_convert_fusion
  94.0 0.6 multiply_convert_fusion.7
  94.7 0.3 convolution_bitcast_fusion
  95.5 1.3 fusion.27
  97.1 1.2 convert_element_type.133
  98.3 2.4 %copy.71 = bf16[512,1280]{0,1:T(8,128)(2,1)} copy(bf16[512,1280]{1,0:T(8,128)(2,1)} %convert_element_type.133) | data formatting | bytes 2621440 | tf_op jit(solution)/shard_map/convert_element_type | solution.py:175
  100.7 5.9 %multiply_convert_fusion.3 = (bf16[512,10,2,64]{0,3,2,1:T(8,128)(2,1)}, bf16[512,10,2,64]{0,3,2,1:T(8,128)(2,1)}) fusion(f32[512,10,2,128]{0,3,2,1:T(8,128)} %copy-done.2, bf16[512,10,2,64]{0,3,2,1:T(8,128)(2,1)} %bitcast.118, bf16[64,64]{1,0:T(8,128)(2,1)S(1)} %copy-done.19), kind=kOutput, calls=%fused_computation.23 | convolution fusion | flops 90439680 | bytes 9183232 | tf_op jit(solution)/shard_map/stbd,cd->stbc/dot_general | solution.py:169
  106.6 0.5 fusion.52
  107.2 3.7 %all-to-all-start.3 = ((bf16[32,8,1280]{2,1,0:T(8,128)(2,1)}), bf16[32,8,1280]{2,1,0:T(8,128)(2,1)S(1)}, u32[]{:S(2)}, u32[]{:S(2)}) async-start(bf16[32,8,1280]{2,1,0:T(8,128)(2,1)} %bitcast.115), calls=%async_computation.3 | async-start | bytes 1310720 | tf_op jit(solution)/shard_map/all_to_all | solution.py:163
  111.0 2.3 %convert_reduce_fusion = f32[128]{0:T(128)S(1)} fusion(bf16[512,10,2,64]{0,3,2,1:T(8,128)(2,1)} %get-tuple-element.43, bf16[512,10,2,64]{0,3,2,1:T(8,128)(2,1)} %get-tuple-element.42), kind=kLoop, calls=%fused_computation | loop fusion | flops 6553472 | bytes 2621952 | tf_op jit(solution)/shard_map/reduce_sum | solution.py:172
  113.5 2.9 %fusion.42 = f32[24576]{0:T(1024)S(1)} fusion(f32[192,128]{1,0:T(8,128)} %fusion.27, bf16[512,10,2,64]{0,3,2,1:T(8,128)(2,1)} %copy-done.11, bf16[512,10,2,64]{0,3,2,1:T(8,128)(2,1)} %copy-done.12, bf16[512,10,2,64]{0,3,2,1:T(8,128)(2,1)} %copy-done.10, bf16[512,10,2,64]{0,3,2,1:T(8,128)(2,1)S(1)} %copy-done.9, bf16[512,10,2,64]{0,3,2,1:T(8,128)(2,1)S(1)} %copy-done.8), kind=kOutput, calls=%fused_computation.62 | convolution fusion | flops 520380416 | bytes 6750208 | tf_op jit(solution)/shard_map/stbk,stbf->kf/dot_general | solution.py:171
  116.6 1.2 collective-permute-done
  117.9 10.8 %all-to-all-done.3 = bf16[32,8,1280]{2,1,0:T(8,128)(2,1)S(1)} async-done(((bf16[32,8,1280]{2,1,0:T(8,128)(2,1)}), bf16[32,8,1280]{2,1,0:T(8,128)(2,1)S(1)}, u32[]{:S(2)}, u32[]{:S(2)}) %all-to-all-start.3) | async-done | bytes 655392 | tf_op jit(solution)/shard_map/all_to_all | solution.py:163
  128.7 1.4 collective-permute-start.1
  130.0 1.6 %fusion.3 = bf16[512,1280]{1,0:T(8,128)(2,1)} fusion(f32[512,1280]{1,0:T(8,128)S(1)} %fusion.67, bf16[256,1280]{1,0:T(8,128)(2,1)S(1)} %bitcast.114, s32[256]{0:T(256)S(1)} %get-tuple-element.57), kind=kOutput, calls=%fused_computation.8 | convolution fusion | flops 337248256 | bytes 4588544 | tf_op jit(solution)/shard_map/dot_general | solution.py:181
  131.6 1.6 %copy.80 = bf16[512,1280]{0,1:T(8,128)(2,1)S(1)} copy(bf16[512,1280]{1,0:T(8,128)(2,1)} %fusion.3) | data formatting | bytes 2621440 | tf_op jit(solution)/shard_map/convert_element_type | solution.py:182
  133.3 1.6 %collective-permute-start.2 = (f32[14400]{0:T(1024)S(1)}, f32[14400]{0:T(1024)S(1)}, u32[]{:S(2)}, u32[]{:S(2)}) collective-permute-start(f32[14400]{0:T(1024)S(1)} %add.156), channel_id=1, source_target_pairs={{0,4},{1,5},{2,6},{3,7},{4,0},{5,1},{6,2},{7,3},{8,12},{9,13},{10,... | collective-permute-start | bytes 172808 | tf_op jit(solution)/shard_map/ppermute | solution.py:38
  134.8 3.8 %multiply_convert_fusion.1 = (bf16[512,10,2,64]{0,3,2,1:T(8,128)(2,1)S(1)}, bf16[512,10,2,64]{0,3,2,1:T(8,128)(2,1)S(1)}) fusion(f32[512,10,2,128]{0,3,2,1:T(8,128)} %copy-done.2, bf16[512,10,2,64]{0,3,2,1:T(8,128)(2,1)S(1)} %bitcast.117, bf16[64,64]{1,0:T(8,128)(2,1)S(1)} %copy-done.19), kind=kOutput, calls=%fused_computation.20 | convolution fusion | flops 90439680 | bytes 9183232 | tf_op jit(solution)/shard_map/stbd,cd->stbc/dot_general | solution.py:185
  138.7 0.6 collective-permute-start.3
  139.2 1.2 fusion.7
  140.4 2.5 %collective-permute-done.3 = f32[14400]{0:T(1024)S(1)} collective-permute-done((f32[14400]{0:T(1024)S(1)}, f32[14400]{0:T(1024)S(1)}, u32[]{:S(2)}, u32[]{:S(2)}) %collective-permute-start.3) | collective-permute-done | bytes 57632 | tf_op jit(solution)/shard_map/ppermute | solution.py:38
  143.0 1.6 %fusion.106 = (f32[512,10,2,64]{0,3,2,1:T(8,128)S(1)}, f32[512,10,2,64]{0,3,2,1:T(8,128)S(1)}, f32[512,10,2,64]{0,3,2,1:T(8,128)S(1)}) fusion(f32[512,10,2,192]{0,3,2,1:T(8,128)S(1)} %fusion.7), kind=kLoop, calls=%fused_computation.143 | loop fusion | bytes 15728640 | tf_op jit(solution)/shard_map/slice | solution.py:194
  144.7 4.1 %collective-permute-done.4 = f32[14400]{0:T(1024)S(1)} collective-permute-done((f32[14400]{0:T(1024)S(1)}, f32[14400]{0:T(1024)S(1)}, u32[]{:S(2)}, u32[]{:S(2)}) %collective-permute-start.4) | collective-permute-done | bytes 57632 | tf_op jit(solution)/shard_map/ppermute | solution.py:38
  148.8 1.0 add_convert_fusion
  149.9 1.6 %copy.82 = bf16[512,1536]{1,0:T(8,128)(2,1)} copy(bf16[512,1536]{0,1:T(8,128)(2,1)S(1)} %bitcast.111) | data formatting | bytes 3145728
  151.6 0.7 fusion.84
  152.3 0.5 slice_multiply_fusion.1
  152.9 0.6 fusion.95
  (72 shorter events, 4.2 us)
Async XLA Ops:
  0.6 15.3 %copy-start = (bf16[192,128]{1,0:T(8,128)(2,1)S(1)}, bf16[192,128]{1,0:T(8,128)(2,1)}, u32[]{:S(2)}) copy-start(bf16[192,128]{1,0:T(8,128)(2,1)} %param.11) | copy-start | bytes 147460
  3.7 10.6 %copy-start.1 = (bf16[512,1536]{1,0:T(8,128)(2,1)S(1)}, bf16[512,1536]{1,0:T(8,128)(2,1)}, u32[]{:S(2)}) copy-start(bf16[512,1536]{1,0:T(8,128)(2,1)} %param.10) | copy-start | bytes 4718596
  6.9 29.4 %all-to-all-start = ((bf16[32,8,1664]{2,1,0:T(8,128)(2,1)}), bf16[32,8,1664]{2,1,0:T(8,128)(2,1)}, u32[]{:S(2)}, u32[]{:S(2)}) async-start(bf16[32,8,1664]{2,1,0:T(8,128)(2,1)} %maximum_bitcast_fusion), calls=%async_computation | async-start | bytes 1703936 | tf_op jit(solution)/shard_map/all_to_all | solution.py:123
  15.0 0.7 copy-start.20
  15.1 0.8 copy-start.22
  15.7 1.2 copy-start.10
  15.7 1.5 copy-start.11
  15.7 1.9 %copy-start.12 = (bf16[512,10,2,64]{0,3,2,1:T(8,128)(2,1)}, bf16[512,10,2,64]{0,3,2,1:T(8,128)(2,1)S(1)}, u32[]{:S(2)}) copy-start(bf16[512,10,2,64]{0,3,2,1:T(8,128)(2,1)S(1)} %get-tuple-element.50) | copy-start | bytes 3932164
  17.7 2.3 %copy-start.2 = (f32[512,10,2,128]{0,3,2,1:T(8,128)}, f32[512,10,2,128]{0,3,2,1:T(8,128)S(1)}, u32[]{:S(2)}) copy-start(f32[512,10,2,128]{0,3,2,1:T(8,128)S(1)} %broadcast_add_fusion) | copy-start | bytes 15728644
  17.7 2.3 %copy-start.19 = (bf16[64,64]{1,0:T(8,128)(2,1)S(1)}, bf16[64,64]{1,0:T(8,128)(2,1)}, u32[]{:S(2)}) copy-start(bf16[64,64]{1,0:T(8,128)(2,1)} %param.13) | copy-start | bytes 24580
  20.0 1.1 copy-start.3
  38.9 0.9 copy-start.13
  38.9 1.1 copy-start.15
  39.0 1.3 copy-start.17
  40.2 1.5 copy-start.5
  40.2 0.9 copy-start.21
  42.9 21.5 %all-to-all-start.1 = ((bf16[32,8,1280]{2,1,0:T(8,128)(2,1)}), bf16[32,8,1280]{2,1,0:T(8,128)(2,1)S(1)}, u32[]{:S(2)}, u32[]{:S(2)}) async-start(bf16[32,8,1280]{2,1,0:T(8,128)(2,1)} %fusion.14), calls=%async_computation.1 | async-start | bytes 1310720 | tf_op jit(solution)/shard_map/all_to_all | solution.py:147
  69.9 21.4 %all-to-all-start.2 = ((bf16[32,8,1280]{2,1,0:T(8,128)(2,1)}), bf16[32,8,1280]{2,1,0:T(8,128)(2,1)S(1)}, u32[]{:S(2)}, u32[]{:S(2)}) async-start(bf16[32,8,1280]{2,1,0:T(8,128)(2,1)} %fusion.15), calls=%async_computation.2 | async-start | bytes 1310720 | tf_op jit(solution)/shard_map/all_to_all | solution.py:154
  92.2 1.9 %copy-start.6 = (f32[256,10,2,128]{0,3,2,1:T(8,128)S(1)}, f32[256,10,2,128]{0,3,2,1:T(8,128)}, u32[]{:S(2)}) copy-start(f32[256,10,2,128]{0,3,2,1:T(8,128)} %copy-done.5) | copy-start | bytes 7864324
  94.0 1.1 copy-start.14
  94.0 1.3 copy-start.16
  94.0 1.5 copy-start.18
  100.7 5.9 %copy-start.4 = (bf16[512,10,2,64]{0,3,2,1:T(8,128)(2,1)S(1)}, bf16[512,10,2,64]{0,3,2,1:T(8,128)(2,1)}, u32[]{:S(2)}) copy-start(bf16[512,10,2,64]{0,3,2,1:T(8,128)(2,1)} %copy-done.3) | copy-start | bytes 3932164
  100.7 5.9 %copy-start.7 = (bf16[512,1280]{0,1:T(8,128)(2,1)S(1)}, bf16[512,1280]{0,1:T(8,128)(2,1)}, u32[]{:S(2)}) copy-start(bf16[512,1280]{0,1:T(8,128)(2,1)} %copy.71) | copy-start | bytes 3932164
  107.2 21.4 %all-to-all-start.3 = ((bf16[32,8,1280]{2,1,0:T(8,128)(2,1)}), bf16[32,8,1280]{2,1,0:T(8,128)(2,1)S(1)}, u32[]{:S(2)}, u32[]{:S(2)}) async-start(bf16[32,8,1280]{2,1,0:T(8,128)(2,1)} %bitcast.115), calls=%async_computation.3 | async-start | bytes 1310720 | tf_op jit(solution)/shard_map/all_to_all | solution.py:163
  111.0 2.3 %copy-start.8 = (bf16[512,10,2,64]{0,3,2,1:T(8,128)(2,1)S(1)}, bf16[512,10,2,64]{0,3,2,1:T(8,128)(2,1)}, u32[]{:S(2)}) copy-start(bf16[512,10,2,64]{0,3,2,1:T(8,128)(2,1)} %get-tuple-element.42) | copy-start | bytes 3932164
  111.0 2.5 %copy-start.9 = (bf16[512,10,2,64]{0,3,2,1:T(8,128)(2,1)S(1)}, bf16[512,10,2,64]{0,3,2,1:T(8,128)(2,1)}, u32[]{:S(2)}) copy-start(bf16[512,10,2,64]{0,3,2,1:T(8,128)(2,1)} %get-tuple-element.43) | copy-start | bytes 3932164
  116.5 1.3 collective-permute-start
  128.7 4.6 %collective-permute-start.1 = (f32[14400]{0:T(1024)S(1)}, f32[14400]{0:T(1024)S(1)}, u32[]{:S(2)}, u32[]{:S(2)}) collective-permute-start(f32[14400]{0:T(1024)S(1)} %select_add_fusion), channel_id=1, source_target_pairs={{0,2},{1,3},{2,0},{3,1},{4,6},{5,7},{6,4},{7,5},{8,10},{9,11},{10,... | collective-permute-start | bytes 172808 | tf_op jit(solution)/shard_map/ppermute | solution.py:38
  133.3 5.4 %collective-permute-start.2 = (f32[14400]{0:T(1024)S(1)}, f32[14400]{0:T(1024)S(1)}, u32[]{:S(2)}, u32[]{:S(2)}) collective-permute-start(f32[14400]{0:T(1024)S(1)} %add.156), channel_id=1, source_target_pairs={{0,4},{1,5},{2,6},{3,7},{4,0},{5,1},{6,2},{7,3},{8,12},{9,13},{10,... | collective-permute-start | bytes 172808 | tf_op jit(solution)/shard_map/ppermute | solution.py:38
  138.7 4.3 %collective-permute-start.3 = (f32[14400]{0:T(1024)S(1)}, f32[14400]{0:T(1024)S(1)}, u32[]{:S(2)}, u32[]{:S(2)}) collective-permute-start(f32[14400]{0:T(1024)S(1)} %add.157), channel_id=1, source_target_pairs={{0,8},{1,9},{2,10},{3,11},{4,12},{5,13},{6,14},{7,15},{8,0},{9,1},... | collective-permute-start | bytes 172808 | tf_op jit(solution)/shard_map/ppermute | solution.py:38
  143.0 5.8 %collective-permute-start.4 = (f32[14400]{0:T(1024)S(1)}, f32[14400]{0:T(1024)S(1)}, u32[]{:S(2)}, u32[]{:S(2)}) collective-permute-start(f32[14400]{0:T(1024)S(1)} %add.158), channel_id=1, source_target_pairs={{0,16},{1,17},{2,18},{3,19},{4,20},{5,21},{6,22},{7,23},{8,24},{9,... | collective-permute-start | bytes 172808 | tf_op jit(solution)/shard_map/ppermute | solution.py:38
  148.8 2.8 %collective-permute-start.5 = (f32[14400]{0:T(1024)S(1)}, f32[14400]{0:T(1024)S(1)}, u32[]{:S(2)}, u32[]{:S(2)}) collective-permute-start(f32[14400]{0:T(1024)S(1)} %add.159), channel_id=1, source_target_pairs={{0,1},{1,0},{2,3},{3,2},{4,5},{5,4},{6,7},{7,6},{8,9},{9,8},{10,11... | collective-permute-start | bytes 172808 | tf_op jit(solution)/shard_map/ppermute | solution.py:40

commit v17 on v11

--- a/solution.py
+++ b/solution.py
@@ -129,7 +129,6 @@
     back = lax.all_to_all(ret_rows, ("region", "sub"), split_axis=0, concat_axis=0, tiled=True)
     y = member_side(edge_val, back) / degree
     sig_y = jax.nn.sigmoid(y)
-    block_out = (y * sig_y).astype(jnp.bfloat16)
     dy = cotangent.astype(jnp.float32) * sig_y * (1.0 + y * (1.0 - sig_y))
     grad_rows = (dy / degree).astype(jnp.bfloat16)
     send_grads = pick_slots(grad_rows)
@@ -158,7 +157,11 @@
     _, ga_conv, ga_bias, ga_theta = weight_grads(stack, gate, first, hidden, dz_inner)
     _, gb_conv, gb_bias, gb_theta = weight_grads(r_stack, r_gate, r_first, r_hidden, dz_slots)
     partial = (ga_conv + gb_conv, ga_bias + gb_bias, ga_theta + gb_theta)
-    partial, back_grads = lax.optimization_barrier((partial, back_grads))
+    partial, back_grads, late_val, late_back = lax.optimization_barrier(
+        (partial, back_grads, edge_val, back)
+    )
+    y_late = member_side(late_val, late_back) / degree
+    block_out = (y_late * jax.nn.sigmoid(y_late)).astype(jnp.bfloat16)
     sum_conv, sum_bias, sum_theta = device_sum(partial, device_list)
     dz = (
         (inner_sum + jnp.dot(members, back_grads, preferred_element_type=jnp.float32))

time: 148 us -> 151 us (1.020)
  matrix products: 32.3 us -> 35.6 us
  other arithmetic: 12.3 us -> 10.7 us
    dot_general x1 -> x2, matrix products: 4.05 us -> 5.79 us  [member_side(): jnp.dot(members, back, preferred_element_type=jnp.float32)]
    unnamed x62 -> x66, local copies, waits for them, and re-layouts: 10.9 us -> 11.2 us
  transfers between devices with their start and end apart: 9 -> 9, of which waited for: 8 -> 8; matrix products, arithmetic and copies ran while one was open for 21% -> 23% of each run, Pallas kernels for 0% -> 0%
where the time goes in v17:
time: 151 us; the launch traced here: 150 us
  waiting for transfers between devices  58.7 us (39%)
  matrix products  35.6 us (24%)
  starting transfers between devices  24 us (16%)
  local copies, waits for them, and re-layouts  19.8 us (13%)
  other arithmetic  10.7 us (7%)
    all_to_all x1, waiting for transfers between devices, body(): lax.all_to_all(send_grads, ('region', 'sub'), split_axis=0, concat_axis=0...  17.6 us
    all_to_all x1, waiting for transfers between devices, body(): lax.all_to_all(ret_rows, ('region', 'sub'), split_axis=0, concat_axis=0,...  15.6 us
    all_to_all x1, waiting for transfers between devices, body(): lax.all_to_all(send, ('region', 'sub'), split_axis=0, concat_axis=0, tile...  14.6 us
    unnamed x66, local copies, waits for them, and re-layouts  11.2 us
    ppermute x5, waiting for transfers between devices, device_sum(): flat = flat + lax.ppermute(flat, ('region', 'sub'), perm)  7.72 us
    all_to_all x1, starting transfers between devices, body(): lax.all_to_all(send, ('region', 'sub'), split_axis=0, concat_axis=0, tile...  7.41 us
    dot_general x2, matrix products, weight_grads(): jnp.einsum('stbd,cd->stbc', dzr, theta, preferred_element_type=jnp.float32)  6.01 us
    dot_general x2, matrix products, member_side(): jnp.dot(members, back, preferred_element_type=jnp.float32)  5.79 us
  transfers between devices with their start and end apart: 9, of which 8 were waited for; matrix products, arithmetic and copies ran while one was open for 23% of the time, Pallas kernels for 0%

profile of v17, /device:TPU:0, one launch (start us, length us, event | category | flops | bytes accessed | tf_op | source)
XLA Modules:
  0.0 150.1 jit_solution(39848235040380768)
XLA Ops:
  0.6 0.7 broadcast_add_fusion.4
  1.3 0.7 broadcast_add_fusion.3
  2.0 0.9 convert_reduce_fusion.5
  2.9 0.7 fusion.102
  3.7 2.1 %convolution_convert_fusion.3 = bf16[256,1536]{1,0:T(8,128)(2,1)S(1)} fusion(bf16[512,1536]{1,0:T(8,128)(2,1)} %param.10, s32[256]{0:T(256)S(1)} %get-tuple-element.63), kind=kOutput, calls=%fused_computation.33 | convolution fusion | flops 403439616 | bytes 2360320 | tf_op jit(solution)/shard_map/sn,sf->nf/dot_general | solution.py:95
  5.9 1.0 maximum_bitcast_fusion
  6.9 7.4 %all-to-all-start = ((bf16[32,8,1664]{2,1,0:T(8,128)(2,1)}), bf16[32,8,1664]{2,1,0:T(8,128)(2,1)}, u32[]{:S(2)}, u32[]{:S(2)}) async-start(bf16[32,8,1664]{2,1,0:T(8,128)(2,1)} %maximum_bitcast_fusion), calls=%async_computation | async-start | bytes 1703936 | tf_op jit(solution)/shard_map/all_to_all | solution.py:105
  14.3 0.7 copy.66
  15.1 0.5 fusion.107
  15.9 1.0 broadcast_add_fusion
  17.3 0.4 copy-done.14
  17.7 0.7 multiply_convert_fusion.5
  18.4 1.6 %copy-done.2 = f32[512,10,2,128]{0,3,2,1:T(8,128)} copy-done((f32[512,10,2,128]{0,3,2,1:T(8,128)}, f32[512,10,2,128]{0,3,2,1:T(8,128)S(1)}, u32[]{:S(2)}) %copy-start.2) | copy-done | bytes 5242904
  20.0 0.5 convolution_convert_fusion.4
  20.6 0.5 copy-done.3
  21.1 0.6 fusion.71
  21.7 14.6 %all-to-all-done = bf16[32,8,1664]{2,1,0:T(8,128)(2,1)} async-done(((bf16[32,8,1664]{2,1,0:T(8,128)(2,1)}), bf16[32,8,1664]{2,1,0:T(8,128)(2,1)}, u32[]{:S(2)}, u32[]{:S(2)}) %all-to-all-start) | async-done | bytes 852000 | tf_op jit(solution)/shard_map/all_to_all | solution.py:105
  36.3 1.0 convert_reduce_fusion.4
  37.3 1.2 slice.102
  39.1 0.5 convolution_add_fusion.5
  42.0 1.2 fusion.15
  43.2 3.6 %all-to-all-start.1 = ((bf16[32,8,1280]{2,1,0:T(8,128)(2,1)}), bf16[32,8,1280]{2,1,0:T(8,128)(2,1)S(1)}, u32[]{:S(2)}, u32[]{:S(2)}) async-start(bf16[32,8,1280]{2,1,0:T(8,128)(2,1)} %fusion.15), calls=%async_computation.1 | async-start | bytes 1310720 | tf_op jit(solution)/shard_map/all_to_all | solution.py:129
  47.0 2.1 %fusion.69 = f32[512,1280]{1,0:T(8,128)} fusion(bf16[128,1280]{1,0:T(8,128)(2,1)S(1)} %fusion.17, s32[512]{0:T(512)S(1)} %bitcast.127, s32[512]{0:T(512)S(1)} %bitcast.121), kind=kOutput, calls=%fused_computation.86 | convolution fusion | flops 168165376 | bytes 2953216 | tf_op jit(solution)/shard_map/es,ef->sf/dot_general | solution.py:124
  49.1 15.6 %all-to-all-done.1 = bf16[32,8,1280]{2,1,0:T(8,128)(2,1)S(1)} async-done(((bf16[32,8,1280]{2,1,0:T(8,128)(2,1)}), bf16[32,8,1280]{2,1,0:T(8,128)(2,1)S(1)}, u32[]{:S(2)}, u32[]{:S(2)}) %all-to-all-start.1) | async-done | bytes 655392 | tf_op jit(solution)/shard_map/all_to_all | solution.py:129
  64.7 3.7 %divide_convert_fusion = bf16[512,1280]{1,0:T(8,128)(2,1)S(1)} fusion(f32[512,1280]{1,0:T(8,128)} %fusion.69, bf16[512,1280]{1,0:T(8,128)(2,1)} %param.19, f32[512]{0:T(512)S(1)} %broadcast_add_fusion.1, s32[256]{0:T(256)S(1)} %get-tuple-element.63, bf16[32,8,1280]{2,1,0:T(8,128)(2,1)S(1)} %all-to-all-done.1), kind=kOutput, calls=%fused_computation.27 | convolution fusion | flops 344457216 | bytes 5901312 | tf_op jit(solution)/shard_map/dot_general | solution.py:126
  68.5 1.4 fusion.16
  69.9 3.5 %all-to-all-start.2 = ((bf16[32,8,1280]{2,1,0:T(8,128)(2,1)}), bf16[32,8,1280]{2,1,0:T(8,128)(2,1)S(1)}, u32[]{:S(2)}, u32[]{:S(2)}) async-start(bf16[32,8,1280]{2,1,0:T(8,128)(2,1)} %fusion.16), calls=%async_computation.2 | async-start | bytes 1310720 | tf_op jit(solution)/shard_map/all_to_all | solution.py:135
  73.7 17.6 %all-to-all-done.2 = bf16[32,8,1280]{2,1,0:T(8,128)(2,1)S(1)} async-done(((bf16[32,8,1280]{2,1,0:T(8,128)(2,1)}), bf16[32,8,1280]{2,1,0:T(8,128)(2,1)S(1)}, u32[]{:S(2)}, u32[]{:S(2)}) %all-to-all-start.2) | async-done | bytes 655392 | tf_op jit(solution)/shard_map/all_to_all | solution.py:135
  91.6 1.2 convolution_convert_fusion
  93.2 0.5 fusion.65
  93.8 1.1 copy-done.6
  94.9 1.7 %multiply_convert_fusion.7 = (bf16[256,10,2,64]{0,3,2,1:T(8,128)(2,1)}, bf16[256,10,2,64]{0,3,2,1:T(8,128)(2,1)}) fusion(f32[256,10,2,128]{0,3,2,1:T(8,128)S(1)} %copy-done.6, bf16[256,10,2,64]{0,3,2,1:T(8,128)(2,1)S(1)} %convert_element_type.130, bf16[64,64]{1,0:T(8,128)(2,1)S(1)} %copy-done.28), kind=kOutput, calls=%fused_computation.58 | convolution fusion | flops 45219840 | bytes 4595712 | tf_op jit(solution)/shard_map/stbd,cd->stbc/dot_general | solution.py:150
  96.6 3.8 %all-to-all-start.3 = ((bf16[32,8,1280]{2,1,0:T(8,128)(2,1)}), bf16[32,8,1280]{2,1,0:T(8,128)(2,1)}, u32[]{:S(2)}, u32[]{:S(2)}) async-start(bf16[32,8,1280]{2,1,0:T(8,128)(2,1)} %bitcast.111), calls=%async_computation.3 | async-start | bytes 1310720 | tf_op jit(solution)/shard_map/all_to_all | solution.py:144
  100.4 1.2 convert_element_type.132
  101.6 2.4 %copy.71 = bf16[512,1280]{0,1:T(8,128)(2,1)} copy(bf16[512,1280]{1,0:T(8,128)(2,1)} %convert_element_type.132) | data formatting | bytes 2621440 | tf_op jit(solution)/shard_map/convert_element_type | solution.py:156
  104.1 4.3 %multiply_convert_fusion.4 = (bf16[512,10,2,64]{0,3,2,1:T(8,128)(2,1)S(1)}, bf16[512,10,2,64]{0,3,2,1:T(8,128)(2,1)S(1)}) fusion(f32[512,10,2,128]{0,3,2,1:T(8,128)} %copy-done.2, bf16[512,10,2,64]{0,3,2,1:T(8,128)(2,1)} %bitcast.113, bf16[64,64]{1,0:T(8,128)(2,1)S(1)} %copy-done.28), kind=kOutput, calls=%fused_computation.26 | convolution fusion | flops 90439680 | bytes 9183232 | tf_op jit(solution)/shard_map/stbd,cd->stbc/dot_general | solution.py:150
  108.7 0.4 convert_reduce_fusion
  110.3 0.7 fusion.28
  110.9 0.6 copy-done.4
  111.6 0.4 copy-done.9
  112.0 0.5 fusion.48
  112.5 0.9 copy-done.11
  113.4 0.4 copy-done.13
  113.8 1.2 fusion.38
  115.0 3.2 %all-to-all-done.3 = bf16[32,8,1280]{2,1,0:T(8,128)(2,1)} async-done(((bf16[32,8,1280]{2,1,0:T(8,128)(2,1)}), bf16[32,8,1280]{2,1,0:T(8,128)(2,1)}, u32[]{:S(2)}, u32[]{:S(2)}) %all-to-all-start.3) | async-done | bytes 655392 | tf_op jit(solution)/shard_map/all_to_all | solution.py:144
  118.4 0.5 fusion.63
  119.3 2.0 %multiply_convert_fusion.2 = bf16[512,1280]{1,0:T(8,128)(2,1)} fusion(f32[512,1280]{1,0:T(8,128)S(1)} %fusion.63, bf16[256,1280]{1,0:T(8,128)(2,1)S(1)} %bitcast.116, f32[512]{0:T(512)S(1)} %broadcast_add_fusion.1, s32[256]{0:T(256)S(1)} %get-tuple-element.63), kind=kOutput, calls=%fused_computation.23 | convolution fusion | flops 340525056 | bytes 4590592 | tf_op jit(solution)/shard_map/dot_general | solution.py:126
  121.4 2.7 %fusion.4 = bf16[512,1280]{1,0:T(8,128)(2,1)} fusion(f32[512,1280]{1,0:T(8,128)S(1)} %fusion.65, bf16[256,1280]{1,0:T(8,128)(2,1)} %bitcast.36, s32[256]{0:T(256)S(1)} %get-tuple-element.63), kind=kOutput, calls=%fused_computation.10 | convolution fusion | flops 337248256 | bytes 4588544 | tf_op jit(solution)/shard_map/dot_general | solution.py:167
  124.0 1.6 %copy.80 = bf16[512,1280]{0,1:T(8,128)(2,1)S(1)} copy(bf16[512,1280]{1,0:T(8,128)(2,1)} %fusion.4) | data formatting | bytes 2621440 | tf_op jit(solution)/shard_map/convert_element_type | solution.py:168
  125.7 1.4 collective-permute-start.1
  127.1 3.8 %multiply_convert_fusion.1 = (bf16[512,10,2,64]{0,3,2,1:T(8,128)(2,1)S(1)}, bf16[512,10,2,64]{0,3,2,1:T(8,128)(2,1)S(1)}) fusion(f32[512,10,2,128]{0,3,2,1:T(8,128)} %copy-done.2, bf16[512,10,2,64]{0,3,2,1:T(8,128)(2,1)S(1)} %bitcast.115, bf16[64,64]{1,0:T(8,128)(2,1)S(1)} %copy-done.28), kind=kOutput, calls=%fused_computation.22 | convolution fusion | flops 90439680 | bytes 9183232 | tf_op jit(solution)/shard_map/stbd,cd->stbc/dot_general | solution.py:171
  131.0 1.5 %collective-permute-start.2 = (f32[28800]{0:T(1024)S(1)}, f32[28800]{0:T(1024)S(1)}, u32[]{:S(2)}, u32[]{:S(2)}) collective-permute-start(f32[28800]{0:T(1024)S(1)} %add.155), channel_id=1, source_target_pairs={{0,4},{1,5},{2,6},{3,7},{4,0},{5,1},{6,2},{7,3},{8,12},{9,13},{10,... | collective-permute-start | bytes 345608 | tf_op jit(solution)/shard_map/ppermute | solution.py:24
  132.5 1.2 fusion.8
  133.7 2.5 %collective-permute-done.2 = f32[28800]{0:T(1024)S(1)} collective-permute-done((f32[28800]{0:T(1024)S(1)}, f32[28800]{0:T(1024)S(1)}, u32[]{:S(2)}, u32[]{:S(2)}) %collective-permute-start.2) | collective-permute-done | bytes 115232 | tf_op jit(solution)/shard_map/ppermute | solution.py:24
  136.2 1.2 collective-permute-start.3
  137.4 1.6 %fusion.106 = (f32[512,10,2,64]{0,3,2,1:T(8,128)S(1)}, f32[512,10,2,64]{0,3,2,1:T(8,128)S(1)}, f32[512,10,2,64]{0,3,2,1:T(8,128)S(1)}) fusion(f32[512,10,2,192]{0,3,2,1:T(8,128)S(1)} %fusion.8), kind=kLoop, calls=%fused_computation.141 | loop fusion | bytes 15728640 | tf_op jit(solution)/shard_map/slice | solution.py:180
  139.0 2.1 %collective-permute-done.3 = f32[28800]{0:T(1024)S(1)} collective-permute-done((f32[28800]{0:T(1024)S(1)}, f32[28800]{0:T(1024)S(1)}, u32[]{:S(2)}, u32[]{:S(2)}) %collective-permute-start.3) | collective-permute-done | bytes 115232 | tf_op jit(solution)/shard_map/ppermute | solution.py:24
  141.1 1.4 collective-permute-start.4
  142.5 1.0 add_convert_fusion
  143.6 1.6 %copy.82 = bf16[512,1536]{1,0:T(8,128)(2,1)} copy(bf16[512,1536]{0,1:T(8,128)(2,1)S(1)} %bitcast.108) | data formatting | bytes 3145728
  145.1 3.1 %collective-permute-done.4 = f32[28800]{0:T(1024)S(1)} collective-permute-done((f32[28800]{0:T(1024)S(1)}, f32[28800]{0:T(1024)S(1)}, u32[]{:S(2)}, u32[]{:S(2)}) %collective-permute-start.4) | collective-permute-done | bytes 115232 | tf_op jit(solution)/shard_map/ppermute | solution.py:24
  148.2 0.5 slice_multiply_fusion.2
  148.7 0.6 fusion.84
  149.4 0.7 mul.149
  (88 shorter events, 7.2 us)
Async XLA Ops:
  0.6 15.3 %copy-start = (bf16[192,128]{1,0:T(8,128)(2,1)S(1)}, bf16[192,128]{1,0:T(8,128)(2,1)}, u32[]{:S(2)}) copy-start(bf16[192,128]{1,0:T(8,128)(2,1)} %param.11) | copy-start | bytes 147460
  3.7 10.6 %copy-start.1 = (bf16[512,1536]{1,0:T(8,128)(2,1)S(1)}, bf16[512,1536]{1,0:T(8,128)(2,1)}, u32[]{:S(2)}) copy-start(bf16[512,1536]{1,0:T(8,128)(2,1)} %param.10) | copy-start | bytes 4718596
  6.9 29.4 %all-to-all-start = ((bf16[32,8,1664]{2,1,0:T(8,128)(2,1)}), bf16[32,8,1664]{2,1,0:T(8,128)(2,1)}, u32[]{:S(2)}, u32[]{:S(2)}) async-start(bf16[32,8,1664]{2,1,0:T(8,128)(2,1)} %maximum_bitcast_fusion), calls=%async_computation | async-start | bytes 1703936 | tf_op jit(solution)/shard_map/all_to_all | solution.py:105
  15.0 0.7 copy-start.29
  15.1 0.8 copy-start.31
  15.7 1.2 copy-start.10
  15.7 1.5 %copy-start.12 = (bf16[512,10,2,64]{0,3,2,1:T(8,128)(2,1)}, bf16[512,10,2,64]{0,3,2,1:T(8,128)(2,1)S(1)}, u32[]{:S(2)}) copy-start(bf16[512,10,2,64]{0,3,2,1:T(8,128)(2,1)S(1)} %get-tuple-element.55) | copy-start | bytes 3932164
  15.7 1.9 %copy-start.14 = (bf16[512,10,2,64]{0,3,2,1:T(8,128)(2,1)}, bf16[512,10,2,64]{0,3,2,1:T(8,128)(2,1)S(1)}, u32[]{:S(2)}) copy-start(bf16[512,10,2,64]{0,3,2,1:T(8,128)(2,1)S(1)} %get-tuple-element.56) | copy-start | bytes 3932164
  17.7 2.3 %copy-start.2 = (f32[512,10,2,128]{0,3,2,1:T(8,128)}, f32[512,10,2,128]{0,3,2,1:T(8,128)S(1)}, u32[]{:S(2)}) copy-start(f32[512,10,2,128]{0,3,2,1:T(8,128)S(1)} %broadcast_add_fusion) | copy-start | bytes 15728644
  17.7 2.3 %copy-start.28 = (bf16[64,64]{1,0:T(8,128)(2,1)S(1)}, bf16[64,64]{1,0:T(8,128)(2,1)}, u32[]{:S(2)}) copy-start(bf16[64,64]{1,0:T(8,128)(2,1)} %param.13) | copy-start | bytes 24580
  20.0 1.1 copy-start.3
  39.1 0.9 copy-start.22
  39.1 1.0 copy-start.24
  39.1 1.3 copy-start.26
  40.3 1.5 %copy-start.5 = (f32[256,10,2,128]{0,3,2,1:T(8,128)}, f32[256,10,2,128]{0,3,2,1:T(8,128)S(1)}, u32[]{:S(2)}) copy-start(f32[256,10,2,128]{0,3,2,1:T(8,128)S(1)} %convolution_add_fusion.5) | copy-start | bytes 7864324
  40.3 0.8 copy-start.30
  40.7 1.3 copy-start.7
  43.2 21.5 %all-to-all-start.1 = ((bf16[32,8,1280]{2,1,0:T(8,128)(2,1)}), bf16[32,8,1280]{2,1,0:T(8,128)(2,1)S(1)}, u32[]{:S(2)}, u32[]{:S(2)}) async-start(bf16[32,8,1280]{2,1,0:T(8,128)(2,1)} %fusion.15), calls=%async_computation.1 | async-start | bytes 1310720 | tf_op jit(solution)/shard_map/all_to_all | solution.py:129
  64.7 3.8 %copy-start.16 = (bf16[32,8,1280]{2,1,0:T(8,128)(2,1)}, bf16[32,8,1280]{2,1,0:T(8,128)(2,1)S(1)}, u32[]{:S(2)}) copy-start(bf16[32,8,1280]{2,1,0:T(8,128)(2,1)S(1)} %all-to-all-done.1) | copy-start | bytes 1966084
  69.9 21.4 %all-to-all-start.2 = ((bf16[32,8,1280]{2,1,0:T(8,128)(2,1)}), bf16[32,8,1280]{2,1,0:T(8,128)(2,1)S(1)}, u32[]{:S(2)}, u32[]{:S(2)}) async-start(bf16[32,8,1280]{2,1,0:T(8,128)(2,1)} %fusion.16), calls=%async_computation.2 | async-start | bytes 1310720 | tf_op jit(solution)/shard_map/all_to_all | solution.py:135
  93.2 1.7 %copy-start.6 = (f32[256,10,2,128]{0,3,2,1:T(8,128)S(1)}, f32[256,10,2,128]{0,3,2,1:T(8,128)}, u32[]{:S(2)}) copy-start(f32[256,10,2,128]{0,3,2,1:T(8,128)} %copy-done.5) | copy-start | bytes 7864324
  94.9 1.7 %copy-start.20 = (bf16[256,10,2,64]{0,3,2,1:T(8,128)(2,1)}, bf16[256,10,2,64]{0,3,2,1:T(8,128)(2,1)S(1)}, u32[]{:S(2)}) copy-start(bf16[256,10,2,64]{0,3,2,1:T(8,128)(2,1)S(1)} %convert_element_type.130) | copy-start | bytes 1966084
  96.6 21.5 %all-to-all-start.3 = ((bf16[32,8,1280]{2,1,0:T(8,128)(2,1)}), bf16[32,8,1280]{2,1,0:T(8,128)(2,1)}, u32[]{:S(2)}, u32[]{:S(2)}) async-start(bf16[32,8,1280]{2,1,0:T(8,128)(2,1)} %bitcast.111), calls=%async_computation.3 | async-start | bytes 1310720 | tf_op jit(solution)/shard_map/all_to_all | solution.py:144
  104.1 4.3 %copy-start.18 = (bf16[256,10,2,64]{0,3,2,1:T(8,128)(2,1)S(1)}, bf16[256,10,2,64]{0,3,2,1:T(8,128)(2,1)}, u32[]{:S(2)}) copy-start(bf16[256,10,2,64]{0,3,2,1:T(8,128)(2,1)} %get-tuple-element.52) | copy-start | bytes 1966084
  104.1 4.3 %copy-start.19 = (bf16[256,10,2,64]{0,3,2,1:T(8,128)(2,1)S(1)}, bf16[256,10,2,64]{0,3,2,1:T(8,128)(2,1)}, u32[]{:S(2)}) copy-start(bf16[256,10,2,64]{0,3,2,1:T(8,128)(2,1)} %get-tuple-element.53) | copy-start | bytes 1966084
  108.4 1.1 copy-start.8
  108.4 1.3 copy-start.21
  108.4 1.6 %copy-start.23 = (bf16[256,10,2,64]{0,3,2,1:T(8,128)(2,1)S(1)}, bf16[256,10,2,64]{0,3,2,1:T(8,128)(2,1)}, u32[]{:S(2)}) copy-start(bf16[256,10,2,64]{0,3,2,1:T(8,128)(2,1)} %copy-done.22) | copy-start | bytes 1966084
  108.4 1.6 %copy-start.25 = (bf16[256,10,2,64]{0,3,2,1:T(8,128)(2,1)S(1)}, bf16[256,10,2,64]{0,3,2,1:T(8,128)(2,1)}, u32[]{:S(2)}) copy-start(bf16[256,10,2,64]{0,3,2,1:T(8,128)(2,1)} %copy-done.24) | copy-start | bytes 1966084
  108.4 1.8 %copy-start.27 = (bf16[256,10,2,64]{0,3,2,1:T(8,128)(2,1)S(1)}, bf16[256,10,2,64]{0,3,2,1:T(8,128)(2,1)}, u32[]{:S(2)}) copy-start(bf16[256,10,2,64]{0,3,2,1:T(8,128)(2,1)} %copy-done.26) | copy-start | bytes 1966084
  110.3 1.3 copy-start.4
  110.3 1.7 %copy-start.9 = (bf16[512,1280]{0,1:T(8,128)(2,1)S(1)}, bf16[512,1280]{0,1:T(8,128)(2,1)}, u32[]{:S(2)}) copy-start(bf16[512,1280]{0,1:T(8,128)(2,1)} %copy.71) | copy-start | bytes 3932164
  110.3 2.2 %copy-start.15 = (bf16[512,10,2,64]{0,3,2,1:T(8,128)(2,1)S(1)}, bf16[512,10,2,64]{0,3,2,1:T(8,128)(2,1)}, u32[]{:S(2)}) copy-start(bf16[512,10,2,64]{0,3,2,1:T(8,128)(2,1)} %copy-done.14) | copy-start | bytes 3932164
  112.0 1.4 copy-start.11
  112.0 1.8 %copy-start.13 = (bf16[512,10,2,64]{0,3,2,1:T(8,128)(2,1)S(1)}, bf16[512,10,2,64]{0,3,2,1:T(8,128)(2,1)}, u32[]{:S(2)}) copy-start(bf16[512,10,2,64]{0,3,2,1:T(8,128)(2,1)} %copy-done.12) | copy-start | bytes 3932164
  118.2 1.1 copy-start.17
  118.3 7.4 %collective-permute-start = (f32[28800]{0:T(1024)S(1)}, f32[28800]{0:T(1024)S(1)}, u32[]{:S(2)}, u32[]{:S(2)}) collective-permute-start(f32[28800]{0:T(1024)S(1)} %pad_maximum_fusion.4), channel_id=1, source_target_pairs={{0,1},{1,0},{2,3},{3,2},{4,5},{5,4},{6,7},{7,6},{8,9},{9,8},{10,11... | collective-permute-start | bytes 345608 | tf_op jit(solution)/shard_map/ppermute | solution.py:24
  125.7 5.3 %collective-permute-start.1 = (f32[28800]{0:T(1024)S(1)}, f32[28800]{0:T(1024)S(1)}, u32[]{:S(2)}, u32[]{:S(2)}) collective-permute-start(f32[28800]{0:T(1024)S(1)} %fusion.105), channel_id=1, source_target_pairs={{0,2},{1,3},{2,0},{3,1},{4,6},{5,7},{6,4},{7,5},{8,10},{9,11},{10,... | collective-permute-start | bytes 345608 | tf_op jit(solution)/shard_map/ppermute | solution.py:24
  131.0 5.2 %collective-permute-start.2 = (f32[28800]{0:T(1024)S(1)}, f32[28800]{0:T(1024)S(1)}, u32[]{:S(2)}, u32[]{:S(2)}) collective-permute-start(f32[28800]{0:T(1024)S(1)} %add.155), channel_id=1, source_target_pairs={{0,4},{1,5},{2,6},{3,7},{4,0},{5,1},{6,2},{7,3},{8,12},{9,13},{10,... | collective-permute-start | bytes 345608 | tf_op jit(solution)/shard_map/ppermute | solution.py:24
  136.2 4.9 %collective-permute-start.3 = (f32[28800]{0:T(1024)S(1)}, f32[28800]{0:T(1024)S(1)}, u32[]{:S(2)}, u32[]{:S(2)}) collective-permute-start(f32[28800]{0:T(1024)S(1)} %add.156), channel_id=1, source_target_pairs={{0,8},{1,9},{2,10},{3,11},{4,12},{5,13},{6,14},{7,15},{8,0},{9,1},... | collective-permute-start | bytes 345608 | tf_op jit(solution)/shard_map/ppermute | solution.py:24
  141.1 7.1 %collective-permute-start.4 = (f32[28800]{0:T(1024)S(1)}, f32[28800]{0:T(1024)S(1)}, u32[]{:S(2)}, u32[]{:S(2)}) collective-permute-start(f32[28800]{0:T(1024)S(1)} %add.157), channel_id=1, source_target_pairs={{0,16},{1,17},{2,18},{3,19},{4,20},{5,21},{6,22},{7,23},{8,24},{9,... | collective-permute-start | bytes 345608 | tf_op jit(solution)/shard_map/ppermute | solution.py:24

commit v18 on v11

--- a/solution.py
+++ b/solution.py
@@ -157,7 +157,8 @@
     dz_inner = inner_sum.astype(jnp.bfloat16).reshape(seg, TP, B, C)
     _, ga_conv, ga_bias, ga_theta = weight_grads(stack, gate, first, hidden, dz_inner)
     _, gb_conv, gb_bias, gb_theta = weight_grads(r_stack, r_gate, r_first, r_hidden, dz_slots)
-    partial = (ga_conv + gb_conv, ga_bias + gb_bias, ga_theta + gb_theta)
+    norm = 1.0 / jnp.sqrt(jnp.float32(seg * device_list * TP * B))
+    partial = ((ga_conv + gb_conv) * norm, (ga_bias + gb_bias) * norm, (ga_theta + gb_theta) * norm)
     partial, back_grads = lax.optimization_barrier((partial, back_grads))
     sum_conv, sum_bias, sum_theta = device_sum(partial, device_list)
     dz = (
@@ -169,7 +170,6 @@
     du = jnp.concatenate([dh * gate, dh * first * gate * (1.0 - gate)], axis=-1).astype(
         jnp.bfloat16
     )
-    norm = 1.0 / jnp.sqrt(jnp.float32(seg * device_list * TP * B))
     dstack = jnp.einsum("stbf,kf->stbk", du, conv_weight, preferred_element_type=jnp.float32)
     grad_sum = jnp.zeros((seg, T_SIZE, B, C), jnp.float32)
     for k in range(KT):
@@ -177,7 +177,7 @@
             dstack[..., k * C : (k + 1) * C], ((0, 0), (k, KT - 1 - k), (0, 0), (0, 0))
         )
     grad_feats = grad_sum.astype(jnp.bfloat16).reshape(seg, T_SIZE * B * C)
-    return (block_out, grad_feats, sum_conv * norm, sum_bias * norm, sum_theta * norm)
+    return (block_out, grad_feats, sum_conv, sum_bias, sum_theta)
 
 
 def solution(mesh):

time: 148 us -> 148 us (level)
    slice x0 -> x4, local copies, waits for them, and re-layouts: none -> 1.85 us  [device_sum(): out.append(flat[at:at + size].reshape(p.shape))]
where the time goes in v18:
time: 148 us; the launch traced here: 147 us
  waiting for transfers between devices  57.3 us (39%)
  matrix products  32.3 us (22%)
  starting transfers between devices  24.1 us (16%)
  local copies, waits for them, and re-layouts  20.8 us (14%)
  other arithmetic  11.1 us (8%)
    all_to_all x1, waiting for transfers between devices, body(): lax.all_to_all(send_grads, ('region', 'sub'), split_axis=0, concat_axis=0...  17.6 us
    all_to_all x1, waiting for transfers between devices, body(): lax.all_to_all(ret_rows, ('region', 'sub'), split_axis=0, concat_axis=0,...  15.6 us
    all_to_all x1, waiting for transfers between devices, body(): lax.all_to_all(send, ('region', 'sub'), split_axis=0, concat_axis=0, tile...  14.6 us
    unnamed x62, local copies, waits for them, and re-layouts  10.9 us
    all_to_all x1, starting transfers between devices, body(): lax.all_to_all(send, ('region', 'sub'), split_axis=0, concat_axis=0, tile...  7.41 us
    ppermute x5, waiting for transfers between devices, device_sum(): flat = flat + lax.ppermute(flat, ('region', 'sub'), perm)  6.31 us
    dot_general x2, matrix products, weight_grads(): jnp.einsum('stbd,cd->stbc', dzr, theta, preferred_element_type=jnp.float32)  6.04 us
    ppermute x5, starting transfers between devices, device_sum(): flat = flat + lax.ppermute(flat, ('region', 'sub'), perm)  5.88 us
  transfers between devices with their start and end apart: 9, of which 8 were waited for; matrix products, arithmetic and copies ran while one was open for 21% of the time, Pallas kernels for 0%

profile of v18, /device:TPU:0, one launch (start us, length us, event | category | flops | bytes accessed | tf_op | source)
XLA Modules:
  0.0 146.7 jit_solution(6287377858130725333)
XLA Ops:
  0.6 0.7 broadcast_add_fusion.4
  1.3 0.7 broadcast_add_fusion.3
  2.0 0.9 convert_reduce_fusion.5
  2.9 0.7 fusion.106
  3.7 2.1 %convolution_convert_fusion.3 = bf16[256,1536]{1,0:T(8,128)(2,1)S(1)} fusion(bf16[512,1536]{1,0:T(8,128)(2,1)} %param.10, s32[256]{0:T(256)S(1)} %get-tuple-element.61), kind=kOutput, calls=%fused_computation.32 | convolution fusion | flops 403439616 | bytes 2360320 | tf_op jit(solution)/shard_map/sn,sf->nf/dot_general | solution.py:95
  5.9 1.0 maximum_bitcast_fusion
  6.9 7.4 %all-to-all-start = ((bf16[32,8,1664]{2,1,0:T(8,128)(2,1)}), bf16[32,8,1664]{2,1,0:T(8,128)(2,1)}, u32[]{:S(2)}, u32[]{:S(2)}) async-start(bf16[32,8,1664]{2,1,0:T(8,128)(2,1)} %maximum_bitcast_fusion), calls=%async_computation | async-start | bytes 1703936 | tf_op jit(solution)/shard_map/all_to_all | solution.py:105
  14.3 0.7 copy.66
  15.1 0.5 fusion.110
  15.9 1.0 broadcast_add_fusion
  17.3 0.4 copy-done.14
  17.7 0.7 multiply_convert_fusion.5
  18.4 1.6 %copy-done.2 = f32[512,10,2,128]{0,3,2,1:T(8,128)} copy-done((f32[512,10,2,128]{0,3,2,1:T(8,128)}, f32[512,10,2,128]{0,3,2,1:T(8,128)S(1)}, u32[]{:S(2)}) %copy-start.2) | copy-done | bytes 5242904
  20.0 0.6 convolution_convert_fusion.4
  20.6 0.5 copy-done.3
  21.1 0.6 fusion.78
  21.7 14.6 %all-to-all-done = bf16[32,8,1664]{2,1,0:T(8,128)(2,1)} async-done(((bf16[32,8,1664]{2,1,0:T(8,128)(2,1)}), bf16[32,8,1664]{2,1,0:T(8,128)(2,1)}, u32[]{:S(2)}, u32[]{:S(2)}) %all-to-all-start) | async-done | bytes 852000 | tf_op jit(solution)/shard_map/all_to_all | solution.py:105
  36.3 1.0 convert_reduce_fusion.4
  37.3 1.2 slice.108
  39.1 0.5 convolution_add_fusion.4
  42.1 1.2 fusion.14
  43.3 3.6 %all-to-all-start.1 = ((bf16[32,8,1280]{2,1,0:T(8,128)(2,1)}), bf16[32,8,1280]{2,1,0:T(8,128)(2,1)S(1)}, u32[]{:S(2)}, u32[]{:S(2)}) async-start(bf16[32,8,1280]{2,1,0:T(8,128)(2,1)} %fusion.14), calls=%async_computation.1 | async-start | bytes 1310720 | tf_op jit(solution)/shard_map/all_to_all | solution.py:129
  47.1 2.1 %fusion.76 = f32[512,1280]{1,0:T(8,128)} fusion(bf16[128,1280]{1,0:T(8,128)(2,1)S(1)} %fusion.16, s32[512]{0:T(512)S(1)} %bitcast.130, s32[512]{0:T(512)S(1)} %bitcast.125), kind=kOutput, calls=%fused_computation.86 | convolution fusion | flops 168165376 | bytes 2953216 | tf_op jit(solution)/shard_map/es,ef->sf/dot_general | solution.py:124
  49.2 15.6 %all-to-all-done.1 = bf16[32,8,1280]{2,1,0:T(8,128)(2,1)S(1)} async-done(((bf16[32,8,1280]{2,1,0:T(8,128)(2,1)}), bf16[32,8,1280]{2,1,0:T(8,128)(2,1)S(1)}, u32[]{:S(2)}, u32[]{:S(2)}) %all-to-all-start.1) | async-done | bytes 655392 | tf_op jit(solution)/shard_map/all_to_all | solution.py:129
  64.8 4.0 %divide_convert_fusion = (bf16[512,1280]{1,0:T(8,128)(2,1)S(1)}, bf16[512,1280]{1,0:T(8,128)(2,1)}) fusion(bf16[512,1280]{1,0:T(8,128)(2,1)} %param.19, f32[512]{0:T(512)S(1)} %broadcast_add_fusion.1, f32[512,1280]{1,0:T(8,128)} %fusion.76, bf16[32,8,1280]{2,1,0:T(8,128)(2,1)S(1)} %all-to-all-done.1, s32[256]{0:T(256)S(1)} %get-tuple-element.61), kind=kOutput, calls=%fused_computation.24 | convolution fusion | flops 345767936 | bytes 7212032 | tf_op jit(solution)/shard_map/dot_general | solution.py:126
  68.9 1.4 fusion.15
  70.3 3.5 %all-to-all-start.2 = ((bf16[32,8,1280]{2,1,0:T(8,128)(2,1)}), bf16[32,8,1280]{2,1,0:T(8,128)(2,1)S(1)}, u32[]{:S(2)}, u32[]{:S(2)}) async-start(bf16[32,8,1280]{2,1,0:T(8,128)(2,1)} %fusion.15), calls=%async_computation.2 | async-start | bytes 1310720 | tf_op jit(solution)/shard_map/all_to_all | solution.py:136
  74.1 17.6 %all-to-all-done.2 = bf16[32,8,1280]{2,1,0:T(8,128)(2,1)S(1)} async-done(((bf16[32,8,1280]{2,1,0:T(8,128)(2,1)}), bf16[32,8,1280]{2,1,0:T(8,128)(2,1)S(1)}, u32[]{:S(2)}, u32[]{:S(2)}) %all-to-all-start.2) | async-done | bytes 655392 | tf_op jit(solution)/shard_map/all_to_all | solution.py:136
  92.0 1.3 convolution_convert_fusion
  93.6 0.5 fusion.72
  94.2 1.1 copy-done.6
  95.3 1.7 %multiply_convert_fusion.7 = (bf16[256,10,2,64]{0,3,2,1:T(8,128)(2,1)}, bf16[256,10,2,64]{0,3,2,1:T(8,128)(2,1)}) fusion(f32[256,10,2,128]{0,3,2,1:T(8,128)S(1)} %copy-done.6, bf16[256,10,2,64]{0,3,2,1:T(8,128)(2,1)S(1)} %convert_element_type.131, bf16[64,64]{1,0:T(8,128)(2,1)S(1)} %copy-done.26), kind=kOutput, calls=%fused_computation.57 | convolution fusion | flops 45219840 | bytes 4595712 | tf_op jit(solution)/shard_map/stbd,cd->stbc/dot_general | solution.py:151
  97.1 3.7 %all-to-all-start.3 = ((bf16[32,8,1280]{2,1,0:T(8,128)(2,1)}), bf16[32,8,1280]{2,1,0:T(8,128)(2,1)S(1)}, u32[]{:S(2)}, u32[]{:S(2)}) async-start(bf16[32,8,1280]{2,1,0:T(8,128)(2,1)} %bitcast.116), calls=%async_computation.3 | async-start | bytes 1310720 | tf_op jit(solution)/shard_map/all_to_all | solution.py:145
  100.8 1.2 convert_element_type.133
  102.0 2.4 %copy.71 = bf16[512,1280]{0,1:T(8,128)(2,1)} copy(bf16[512,1280]{1,0:T(8,128)(2,1)} %convert_element_type.133) | data formatting | bytes 2621440 | tf_op jit(solution)/shard_map/convert_element_type | solution.py:157
  104.4 4.3 %multiply_convert_fusion.3 = (bf16[512,10,2,64]{0,3,2,1:T(8,128)(2,1)S(1)}, bf16[512,10,2,64]{0,3,2,1:T(8,128)(2,1)S(1)}) fusion(f32[512,10,2,128]{0,3,2,1:T(8,128)} %copy-done.2, bf16[512,10,2,64]{0,3,2,1:T(8,128)(2,1)} %bitcast.118, bf16[64,64]{1,0:T(8,128)(2,1)S(1)} %copy-done.26), kind=kOutput, calls=%fused_computation.23 | convolution fusion | flops 90439680 | bytes 9183232 | tf_op jit(solution)/shard_map/stbd,cd->stbc/dot_general | solution.py:151
  109.1 0.4 convert_reduce_fusion
  110.6 0.7 fusion.27
  111.3 0.6 copy-done.4
  111.9 0.4 copy-done.9
  112.3 0.5 fusion.57
  112.8 0.9 copy-done.11
  113.7 0.4 copy-done.13
  114.1 1.2 fusion.42
  115.3 3.2 %all-to-all-done.3 = bf16[32,8,1280]{2,1,0:T(8,128)(2,1)S(1)} async-done(((bf16[32,8,1280]{2,1,0:T(8,128)(2,1)}), bf16[32,8,1280]{2,1,0:T(8,128)(2,1)S(1)}, u32[]{:S(2)}, u32[]{:S(2)}) %all-to-all-start.3) | async-done | bytes 655392 | tf_op jit(solution)/shard_map/all_to_all | solution.py:145
  118.6 0.7 pad_maximum_fusion.4
  119.3 1.6 %fusion.3 = bf16[512,1280]{1,0:T(8,128)(2,1)} fusion(f32[512,1280]{1,0:T(8,128)S(1)} %fusion.72, bf16[256,1280]{1,0:T(8,128)(2,1)S(1)} %bitcast.115, s32[256]{0:T(256)S(1)} %get-tuple-element.61), kind=kOutput, calls=%fused_computation.8 | convolution fusion | flops 337248256 | bytes 4588544 | tf_op jit(solution)/shard_map/dot_general | solution.py:165
  120.9 1.6 %copy.80 = bf16[512,1280]{0,1:T(8,128)(2,1)S(1)} copy(bf16[512,1280]{1,0:T(8,128)(2,1)} %fusion.3) | data formatting | bytes 2621440 | tf_op jit(solution)/shard_map/convert_element_type | solution.py:166
  122.6 0.9 fusion.108
  123.5 1.7 %collective-permute-start.1 = (f32[28800]{0:T(1024)S(1)}, f32[28800]{0:T(1024)S(1)}, u32[]{:S(2)}, u32[]{:S(2)}) collective-permute-start(f32[28800]{0:T(1024)S(1)} %fusion.108), channel_id=1, source_target_pairs={{0,2},{1,3},{2,0},{3,1},{4,6},{5,7},{6,4},{7,5},{8,10},{9,11},{10,... | collective-permute-start | bytes 345608 | tf_op jit(solution)/shard_map/ppermute | solution.py:24
  125.1 3.8 %multiply_convert_fusion.1 = (bf16[512,10,2,64]{0,3,2,1:T(8,128)(2,1)S(1)}, bf16[512,10,2,64]{0,3,2,1:T(8,128)(2,1)S(1)}) fusion(f32[512,10,2,128]{0,3,2,1:T(8,128)} %copy-done.2, bf16[512,10,2,64]{0,3,2,1:T(8,128)(2,1)S(1)} %bitcast.120, bf16[64,64]{1,0:T(8,128)(2,1)S(1)} %copy-done.26), kind=kOutput, calls=%fused_computation.20 | convolution fusion | flops 90439680 | bytes 9183232 | tf_op jit(solution)/shard_map/stbd,cd->stbc/dot_general | solution.py:169
  129.2 1.5 collective-permute-start.2
  130.6 1.2 fusion.7
  131.8 2.3 %collective-permute-done.2 = f32[28800]{0:T(1024)S(1)} collective-permute-done((f32[28800]{0:T(1024)S(1)}, f32[28800]{0:T(1024)S(1)}, u32[]{:S(2)}, u32[]{:S(2)}) %collective-permute-start.2) | collective-permute-done | bytes 115232 | tf_op jit(solution)/shard_map/ppermute | solution.py:24
  134.1 1.5 collective-permute-start.3
  135.6 1.6 %fusion.109 = (f32[512,10,2,64]{0,3,2,1:T(8,128)S(1)}, f32[512,10,2,64]{0,3,2,1:T(8,128)S(1)}, f32[512,10,2,64]{0,3,2,1:T(8,128)S(1)}) fusion(f32[512,10,2,192]{0,3,2,1:T(8,128)S(1)} %fusion.7), kind=kLoop, calls=%fused_computation.136 | loop fusion | bytes 15728640 | tf_op jit(solution)/shard_map/slice | solution.py:177
  137.2 1.8 %collective-permute-done.3 = f32[28800]{0:T(1024)S(1)} collective-permute-done((f32[28800]{0:T(1024)S(1)}, f32[28800]{0:T(1024)S(1)}, u32[]{:S(2)}, u32[]{:S(2)}) %collective-permute-start.3) | collective-permute-done | bytes 115232 | tf_op jit(solution)/shard_map/ppermute | solution.py:24
  139.1 1.2 collective-permute-start.4
  140.3 1.0 add_convert_fusion
  141.3 1.6 %copy.82 = bf16[512,1536]{1,0:T(8,128)(2,1)} copy(bf16[512,1536]{0,1:T(8,128)(2,1)S(1)} %bitcast.112) | data formatting | bytes 3145728
  142.9 2.0 %collective-permute-done.4 = f32[28800]{0:T(1024)S(1)} collective-permute-done((f32[28800]{0:T(1024)S(1)}, f32[28800]{0:T(1024)S(1)}, u32[]{:S(2)}, u32[]{:S(2)}) %collective-permute-start.4) | collective-permute-done | bytes 115232 | tf_op jit(solution)/shard_map/ppermute | solution.py:24
  144.9 0.5 slice.118
  145.4 0.6 slice_bitcast_fusion
  146.0 0.7 slice.101
  (82 shorter events, 6.9 us)
Async XLA Ops:
  0.6 15.3 %copy-start = (bf16[192,128]{1,0:T(8,128)(2,1)S(1)}, bf16[192,128]{1,0:T(8,128)(2,1)}, u32[]{:S(2)}) copy-start(bf16[192,128]{1,0:T(8,128)(2,1)} %param.11) | copy-start | bytes 147460
  3.7 10.6 %copy-start.1 = (bf16[512,1536]{1,0:T(8,128)(2,1)S(1)}, bf16[512,1536]{1,0:T(8,128)(2,1)}, u32[]{:S(2)}) copy-start(bf16[512,1536]{1,0:T(8,128)(2,1)} %param.10) | copy-start | bytes 4718596
  6.9 29.4 %all-to-all-start = ((bf16[32,8,1664]{2,1,0:T(8,128)(2,1)}), bf16[32,8,1664]{2,1,0:T(8,128)(2,1)}, u32[]{:S(2)}, u32[]{:S(2)}) async-start(bf16[32,8,1664]{2,1,0:T(8,128)(2,1)} %maximum_bitcast_fusion), calls=%async_computation | async-start | bytes 1703936 | tf_op jit(solution)/shard_map/all_to_all | solution.py:105
  15.0 0.7 copy-start.27
  15.1 0.8 copy-start.29
  15.7 1.2 copy-start.10
  15.7 1.6 %copy-start.12 = (bf16[512,10,2,64]{0,3,2,1:T(8,128)(2,1)}, bf16[512,10,2,64]{0,3,2,1:T(8,128)(2,1)S(1)}, u32[]{:S(2)}) copy-start(bf16[512,10,2,64]{0,3,2,1:T(8,128)(2,1)S(1)} %get-tuple-element.53) | copy-start | bytes 3932164
  15.7 2.0 %copy-start.14 = (bf16[512,10,2,64]{0,3,2,1:T(8,128)(2,1)}, bf16[512,10,2,64]{0,3,2,1:T(8,128)(2,1)S(1)}, u32[]{:S(2)}) copy-start(bf16[512,10,2,64]{0,3,2,1:T(8,128)(2,1)S(1)} %get-tuple-element.54) | copy-start | bytes 3932164
  17.7 2.3 %copy-start.2 = (f32[512,10,2,128]{0,3,2,1:T(8,128)}, f32[512,10,2,128]{0,3,2,1:T(8,128)S(1)}, u32[]{:S(2)}) copy-start(f32[512,10,2,128]{0,3,2,1:T(8,128)S(1)} %broadcast_add_fusion) | copy-start | bytes 15728644
  17.7 2.3 %copy-start.26 = (bf16[64,64]{1,0:T(8,128)(2,1)S(1)}, bf16[64,64]{1,0:T(8,128)(2,1)}, u32[]{:S(2)}) copy-start(bf16[64,64]{1,0:T(8,128)(2,1)} %param.13) | copy-start | bytes 24580
  20.0 1.1 copy-start.3
  39.1 0.9 copy-start.20
  39.1 1.1 copy-start.22
  39.1 1.3 copy-start.24
  40.3 1.5 %copy-start.5 = (f32[256,10,2,128]{0,3,2,1:T(8,128)}, f32[256,10,2,128]{0,3,2,1:T(8,128)S(1)}, u32[]{:S(2)}) copy-start(f32[256,10,2,128]{0,3,2,1:T(8,128)S(1)} %convolution_add_fusion.4) | copy-start | bytes 7864324
  40.3 0.8 copy-start.28
  40.7 1.4 copy-start.7
  43.3 21.5 %all-to-all-start.1 = ((bf16[32,8,1280]{2,1,0:T(8,128)(2,1)}), bf16[32,8,1280]{2,1,0:T(8,128)(2,1)S(1)}, u32[]{:S(2)}, u32[]{:S(2)}) async-start(bf16[32,8,1280]{2,1,0:T(8,128)(2,1)} %fusion.14), calls=%async_computation.1 | async-start | bytes 1310720 | tf_op jit(solution)/shard_map/all_to_all | solution.py:129
  70.3 21.4 %all-to-all-start.2 = ((bf16[32,8,1280]{2,1,0:T(8,128)(2,1)}), bf16[32,8,1280]{2,1,0:T(8,128)(2,1)S(1)}, u32[]{:S(2)}, u32[]{:S(2)}) async-start(bf16[32,8,1280]{2,1,0:T(8,128)(2,1)} %fusion.15), calls=%async_computation.2 | async-start | bytes 1310720 | tf_op jit(solution)/shard_map/all_to_all | solution.py:136
  93.6 1.7 %copy-start.6 = (f32[256,10,2,128]{0,3,2,1:T(8,128)S(1)}, f32[256,10,2,128]{0,3,2,1:T(8,128)}, u32[]{:S(2)}) copy-start(f32[256,10,2,128]{0,3,2,1:T(8,128)} %copy-done.5) | copy-start | bytes 7864324
  95.3 1.7 %copy-start.18 = (bf16[256,10,2,64]{0,3,2,1:T(8,128)(2,1)}, bf16[256,10,2,64]{0,3,2,1:T(8,128)(2,1)S(1)}, u32[]{:S(2)}) copy-start(bf16[256,10,2,64]{0,3,2,1:T(8,128)(2,1)S(1)} %convert_element_type.131) | copy-start | bytes 1966084
  97.1 21.4 %all-to-all-start.3 = ((bf16[32,8,1280]{2,1,0:T(8,128)(2,1)}), bf16[32,8,1280]{2,1,0:T(8,128)(2,1)S(1)}, u32[]{:S(2)}, u32[]{:S(2)}) async-start(bf16[32,8,1280]{2,1,0:T(8,128)(2,1)} %bitcast.116), calls=%async_computation.3 | async-start | bytes 1310720 | tf_op jit(solution)/shard_map/all_to_all | solution.py:145
  104.4 4.3 %copy-start.16 = (bf16[256,10,2,64]{0,3,2,1:T(8,128)(2,1)S(1)}, bf16[256,10,2,64]{0,3,2,1:T(8,128)(2,1)}, u32[]{:S(2)}) copy-start(bf16[256,10,2,64]{0,3,2,1:T(8,128)(2,1)} %get-tuple-element.48) | copy-start | bytes 1966084
  104.4 4.3 %copy-start.17 = (bf16[256,10,2,64]{0,3,2,1:T(8,128)(2,1)S(1)}, bf16[256,10,2,64]{0,3,2,1:T(8,128)(2,1)}, u32[]{:S(2)}) copy-start(bf16[256,10,2,64]{0,3,2,1:T(8,128)(2,1)} %get-tuple-element.49) | copy-start | bytes 1966084
  108.7 1.1 copy-start.8
  108.7 1.3 copy-start.19
  108.8 1.6 %copy-start.21 = (bf16[256,10,2,64]{0,3,2,1:T(8,128)(2,1)S(1)}, bf16[256,10,2,64]{0,3,2,1:T(8,128)(2,1)}, u32[]{:S(2)}) copy-start(bf16[256,10,2,64]{0,3,2,1:T(8,128)(2,1)} %copy-done.20) | copy-start | bytes 1966084
  108.8 1.6 %copy-start.23 = (bf16[256,10,2,64]{0,3,2,1:T(8,128)(2,1)S(1)}, bf16[256,10,2,64]{0,3,2,1:T(8,128)(2,1)}, u32[]{:S(2)}) copy-start(bf16[256,10,2,64]{0,3,2,1:T(8,128)(2,1)} %copy-done.22) | copy-start | bytes 1966084
  108.8 1.8 %copy-start.25 = (bf16[256,10,2,64]{0,3,2,1:T(8,128)(2,1)S(1)}, bf16[256,10,2,64]{0,3,2,1:T(8,128)(2,1)}, u32[]{:S(2)}) copy-start(bf16[256,10,2,64]{0,3,2,1:T(8,128)(2,1)} %copy-done.24) | copy-start | bytes 1966084
  110.6 1.3 copy-start.4
  110.6 1.7 %copy-start.9 = (bf16[512,1280]{0,1:T(8,128)(2,1)S(1)}, bf16[512,1280]{0,1:T(8,128)(2,1)}, u32[]{:S(2)}) copy-start(bf16[512,1280]{0,1:T(8,128)(2,1)} %copy.71) | copy-start | bytes 3932164
  110.6 2.2 %copy-start.15 = (bf16[512,10,2,64]{0,3,2,1:T(8,128)(2,1)S(1)}, bf16[512,10,2,64]{0,3,2,1:T(8,128)(2,1)}, u32[]{:S(2)}) copy-start(bf16[512,10,2,64]{0,3,2,1:T(8,128)(2,1)} %copy-done.14) | copy-start | bytes 3932164
  112.3 1.4 copy-start.11
  112.3 1.8 %copy-start.13 = (bf16[512,10,2,64]{0,3,2,1:T(8,128)(2,1)S(1)}, bf16[512,10,2,64]{0,3,2,1:T(8,128)(2,1)}, u32[]{:S(2)}) copy-start(bf16[512,10,2,64]{0,3,2,1:T(8,128)(2,1)} %copy-done.12) | copy-start | bytes 3932164
  119.3 3.3 %collective-permute-start = (f32[28800]{0:T(1024)}, f32[28800]{0:T(1024)}, u32[]{:S(2)}, u32[]{:S(2)}) collective-permute-start(f32[28800]{0:T(1024)} %pad_maximum_fusion.4), channel_id=1, source_target_pairs={{0,1},{1,0},{2,3},{3,2},{4,5},{5,4},{6,7},{7,6},{8,9},{9,8},{10,11... | collective-permute-start | bytes 345608 | tf_op jit(solution)/shard_map/ppermute | solution.py:24
  123.5 5.7 %collective-permute-start.1 = (f32[28800]{0:T(1024)S(1)}, f32[28800]{0:T(1024)S(1)}, u32[]{:S(2)}, u32[]{:S(2)}) collective-permute-start(f32[28800]{0:T(1024)S(1)} %fusion.108), channel_id=1, source_target_pairs={{0,2},{1,3},{2,0},{3,1},{4,6},{5,7},{6,4},{7,5},{8,10},{9,11},{10,... | collective-permute-start | bytes 345608 | tf_op jit(solution)/shard_map/ppermute | solution.py:24
  129.2 5.0 %collective-permute-start.2 = (f32[28800]{0:T(1024)S(1)}, f32[28800]{0:T(1024)S(1)}, u32[]{:S(2)}, u32[]{:S(2)}) collective-permute-start(f32[28800]{0:T(1024)S(1)} %add.147), channel_id=1, source_target_pairs={{0,4},{1,5},{2,6},{3,7},{4,0},{5,1},{6,2},{7,3},{8,12},{9,13},{10,... | collective-permute-start | bytes 345608 | tf_op jit(solution)/shard_map/ppermute | solution.py:24
  134.1 4.9 %collective-permute-start.3 = (f32[28800]{0:T(1024)S(1)}, f32[28800]{0:T(1024)S(1)}, u32[]{:S(2)}, u32[]{:S(2)}) collective-permute-start(f32[28800]{0:T(1024)S(1)} %add.148), channel_id=1, source_target_pairs={{0,8},{1,9},{2,10},{3,11},{4,12},{5,13},{6,14},{7,15},{8,0},{9,1},... | collective-permute-start | bytes 345608 | tf_op jit(solution)/shard_map/ppermute | solution.py:24
  139.1 5.8 %collective-permute-start.4 = (f32[28800]{0:T(1024)S(1)}, f32[28800]{0:T(1024)S(1)}, u32[]{:S(2)}, u32[]{:S(2)}) collective-permute-start(f32[28800]{0:T(1024)S(1)} %add.149), channel_id=1, source_target_pairs={{0,16},{1,17},{2,18},{3,19},{4,20},{5,21},{6,22},{7,23},{8,24},{9,... | collective-permute-start | bytes 345608 | tf_op jit(solution)/shard_map/ppermute | solution.py:24

commit v19 on v15

--- a/solution.py
+++ b/solution.py
@@ -162,7 +162,8 @@
     dz_inner = inner_sum.astype(jnp.bfloat16).reshape(seg, TP, B, C)
     _, ga_conv, ga_bias, ga_theta = weight_grads(stack, gate, first, hidden, dz_inner)
     _, gb_conv, gb_bias, gb_theta = weight_grads(r_stack, r_gate, r_first, r_hidden, dz_slots)
-    partial = (ga_conv + gb_conv, ga_bias + gb_bias, ga_theta + gb_theta)
+    norm = 1.0 / jnp.sqrt(jnp.float32(seg * device_list * TP * B))
+    partial = ((ga_conv + gb_conv) * norm, (ga_bias + gb_bias) * norm, (ga_theta + gb_theta) * norm)
     (sum_conv, sum_bias, sum_theta), back_grads = device_sum(partial, device_list, back_grads)
     dz = (
         (inner_sum + jnp.dot(members, back_grads, preferred_element_type=jnp.float32))
@@ -173,7 +174,6 @@
     du = jnp.concatenate([dh * gate, dh * first * gate * (1.0 - gate)], axis=-1).astype(
         jnp.bfloat16
     )
-    norm = 1.0 / jnp.sqrt(jnp.float32(seg * device_list * TP * B))
     dstack = jnp.einsum("stbf,kf->stbk", du, conv_weight, preferred_element_type=jnp.float32)
     grad_sum = jnp.zeros((seg, T_SIZE, B, C), jnp.float32)
     for k in range(KT):
@@ -181,7 +181,7 @@
             dstack[..., k * C : (k + 1) * C], ((0, 0), (k, KT - 1 - k), (0, 0), (0, 0))
         )
     grad_feats = grad_sum.astype(jnp.bfloat16).reshape(seg, T_SIZE * B * C)
-    return (block_out, grad_feats, sum_conv * norm, sum_bias * norm, sum_theta * norm)
+    return (block_out, grad_feats, sum_conv, sum_bias, sum_theta)
 
 
 def solution(mesh):

time: 148 us -> 148 us (level)
    slice x0 -> x4, local copies, waits for them, and re-layouts: none -> 1.85 us  [device_sum(): out.append(flat[at:at + size].reshape(p.shape))]
where the time goes in v19:
time: 148 us; the launch traced here: 147 us
  waiting for transfers between devices  57.5 us (39%)
  matrix products  35.2 us (24%)
  starting transfers between devices  24 us (16%)
  local copies, waits for them, and re-layouts  17.9 us (12%)
  other arithmetic  11.4 us (8%)
    all_to_all x1, waiting for transfers between devices, body(): lax.all_to_all(send_grads, ('region', 'sub'), split_axis=0, concat_axis=0...  17.6 us
    all_to_all x1, waiting for transfers between devices, body(): lax.all_to_all(ret_rows, ('region', 'sub'), split_axis=0, concat_axis=0,...  15.6 us
    all_to_all x1, waiting for transfers between devices, body(): lax.all_to_all(send, ('region', 'sub'), split_axis=0, concat_axis=0, tile...  14.7 us
    ppermute x5, waiting for transfers between devices, device_sum(): flat = flat + lax.ppermute(flat, ('region', 'sub'), perm)  8.84 us
    unnamed x48, local copies, waits for them, and re-layouts  8.14 us
    all_to_all x1, starting transfers between devices, body(): lax.all_to_all(send, ('region', 'sub'), split_axis=0, concat_axis=0, tile...  7.41 us
    dot_general x2, matrix products, weight_grads(): jnp.einsum('stbd,cd->stbc', dzr, theta, preferred_element_type=jnp.float32)  6.51 us
    ppermute x5, starting transfers between devices, device_sum(): flat = flat + lax.ppermute(flat, ('region', 'sub'), perm)  5.8 us
  transfers between devices with their start and end apart: 9, of which 8 were waited for; matrix products, arithmetic and copies ran while one was open for 21% of the time, Pallas kernels for 0%

profile of v19, /device:TPU:0, one launch (start us, length us, event | category | flops | bytes accessed | tf_op | source)
XLA Modules:
  0.0 147.1 jit_solution(4422539227553676526)
XLA Ops:
  0.6 0.7 broadcast_add_fusion.4
  1.3 0.7 broadcast_add_fusion.3
  2.0 0.9 convert_reduce_fusion.5
  2.9 0.7 fusion.111
  3.7 2.1 %convolution_convert_fusion.3 = bf16[256,1536]{1,0:T(8,128)(2,1)S(1)} fusion(bf16[512,1536]{1,0:T(8,128)(2,1)} %param.10, s32[256]{0:T(256)S(1)} %get-tuple-element.57), kind=kOutput, calls=%fused_computation.32 | convolution fusion | flops 403439616 | bytes 2360320 | tf_op jit(solution)/shard_map/sn,sf->nf/dot_general | solution.py:100
  5.9 1.0 maximum_bitcast_fusion
  6.9 7.4 %all-to-all-start = ((bf16[32,8,1664]{2,1,0:T(8,128)(2,1)}), bf16[32,8,1664]{2,1,0:T(8,128)(2,1)}, u32[]{:S(2)}, u32[]{:S(2)}) async-start(bf16[32,8,1664]{2,1,0:T(8,128)(2,1)} %maximum_bitcast_fusion), calls=%async_computation | async-start | bytes 1703936 | tf_op jit(solution)/shard_map/all_to_all | solution.py:110
  14.3 0.7 copy.66
  15.1 0.5 fusion.115
  15.9 1.0 broadcast_add_fusion
  17.2 0.5 copy-done.12
  17.7 0.7 multiply_convert_fusion.5
  18.4 1.6 %copy-done.2 = f32[512,10,2,128]{0,3,2,1:T(8,128)} copy-done((f32[512,10,2,128]{0,3,2,1:T(8,128)}, f32[512,10,2,128]{0,3,2,1:T(8,128)S(1)}, u32[]{:S(2)}) %copy-start.2) | copy-done | bytes 5242904
  20.0 0.6 convolution_convert_fusion.4
  20.6 0.5 copy-done.3
  21.1 0.6 fusion.83
  21.6 14.7 %all-to-all-done = bf16[32,8,1664]{2,1,0:T(8,128)(2,1)} async-done(((bf16[32,8,1664]{2,1,0:T(8,128)(2,1)}), bf16[32,8,1664]{2,1,0:T(8,128)(2,1)}, u32[]{:S(2)}, u32[]{:S(2)}) %all-to-all-start) | async-done | bytes 852000 | tf_op jit(solution)/shard_map/all_to_all | solution.py:110
  36.3 1.0 convert_reduce_fusion.4
  37.3 1.2 slice.108
  39.1 0.5 convolution_add_fusion.4
  40.3 0.4 multiply_convert_fusion.8
  40.7 0.4 convolution_convert_fusion.5
  41.1 0.4 fusion.16
  41.8 1.2 fusion.14
  43.0 3.6 %all-to-all-start.1 = ((bf16[32,8,1280]{2,1,0:T(8,128)(2,1)}), bf16[32,8,1280]{2,1,0:T(8,128)(2,1)S(1)}, u32[]{:S(2)}, u32[]{:S(2)}) async-start(bf16[32,8,1280]{2,1,0:T(8,128)(2,1)} %fusion.14), calls=%async_computation.1 | async-start | bytes 1310720 | tf_op jit(solution)/shard_map/all_to_all | solution.py:134
  46.8 2.1 %fusion.81 = f32[512,1280]{1,0:T(8,128)} fusion(bf16[128,1280]{1,0:T(8,128)(2,1)S(1)} %fusion.16, s32[512]{0:T(512)S(1)} %bitcast.131, s32[512]{0:T(512)S(1)} %bitcast.126), kind=kOutput, calls=%fused_computation.87 | convolution fusion | flops 168165376 | bytes 2953216 | tf_op jit(solution)/shard_map/es,ef->sf/dot_general | solution.py:129
  48.9 15.6 %all-to-all-done.1 = bf16[32,8,1280]{2,1,0:T(8,128)(2,1)S(1)} async-done(((bf16[32,8,1280]{2,1,0:T(8,128)(2,1)}), bf16[32,8,1280]{2,1,0:T(8,128)(2,1)S(1)}, u32[]{:S(2)}, u32[]{:S(2)}) %all-to-all-start.1) | async-done | bytes 655392 | tf_op jit(solution)/shard_map/all_to_all | solution.py:134
  64.5 4.0 %divide_convert_fusion = (bf16[512,1280]{1,0:T(8,128)(2,1)S(1)}, bf16[512,1280]{1,0:T(8,128)(2,1)}) fusion(bf16[512,1280]{1,0:T(8,128)(2,1)} %param.19, f32[512]{0:T(512)S(1)} %broadcast_add_fusion.1, f32[512,1280]{1,0:T(8,128)} %fusion.81, bf16[32,8,1280]{2,1,0:T(8,128)(2,1)S(1)} %all-to-all-done.1, s32[256]{0:T(256)S(1)} %get-tuple-element.57), kind=kOutput, calls=%fused_computation.24 | convolution fusion | flops 345767936 | bytes 7212032 | tf_op jit(solution)/shard_map/dot_general | solution.py:131
  68.6 1.4 fusion.15
  69.9 3.5 %all-to-all-start.2 = ((bf16[32,8,1280]{2,1,0:T(8,128)(2,1)}), bf16[32,8,1280]{2,1,0:T(8,128)(2,1)S(1)}, u32[]{:S(2)}, u32[]{:S(2)}) async-start(bf16[32,8,1280]{2,1,0:T(8,128)(2,1)} %fusion.15), calls=%async_computation.2 | async-start | bytes 1310720 | tf_op jit(solution)/shard_map/all_to_all | solution.py:141
  73.5 0.3 fusion.79
  73.8 17.6 %all-to-all-done.2 = bf16[32,8,1280]{2,1,0:T(8,128)(2,1)S(1)} async-done(((bf16[32,8,1280]{2,1,0:T(8,128)(2,1)}), bf16[32,8,1280]{2,1,0:T(8,128)(2,1)S(1)}, u32[]{:S(2)}, u32[]{:S(2)}) %all-to-all-start.2) | async-done | bytes 655392 | tf_op jit(solution)/shard_map/all_to_all | solution.py:141
  91.6 1.3 convolution_convert_fusion
  92.9 0.3 fusion.85
  93.3 0.5 fusion.77
  93.9 1.1 copy-done.6
  95.0 0.6 multiply_convert_fusion.7
  96.5 1.3 fusion.27
  98.1 3.7 %all-to-all-start.3 = ((bf16[32,8,1280]{2,1,0:T(8,128)(2,1)}), bf16[32,8,1280]{2,1,0:T(8,128)(2,1)S(1)}, u32[]{:S(2)}, u32[]{:S(2)}) async-start(bf16[32,8,1280]{2,1,0:T(8,128)(2,1)} %bitcast.119), calls=%async_computation.3 | async-start | bytes 1310720 | tf_op jit(solution)/shard_map/all_to_all | solution.py:150
  101.8 1.2 convert_element_type.133
  103.0 2.4 %copy.71 = bf16[512,1280]{0,1:T(8,128)(2,1)} copy(bf16[512,1280]{1,0:T(8,128)(2,1)} %convert_element_type.133) | data formatting | bytes 2621440 | tf_op jit(solution)/shard_map/convert_element_type | solution.py:162
  105.4 5.9 %multiply_convert_fusion.3 = (bf16[512,10,2,64]{0,3,2,1:T(8,128)(2,1)}, bf16[512,10,2,64]{0,3,2,1:T(8,128)(2,1)}) fusion(f32[512,10,2,128]{0,3,2,1:T(8,128)} %copy-done.2, bf16[512,10,2,64]{0,3,2,1:T(8,128)(2,1)} %bitcast.122, bf16[64,64]{1,0:T(8,128)(2,1)S(1)} %copy-done.19), kind=kOutput, calls=%fused_computation.23 | convolution fusion | flops 90439680 | bytes 9183232 | tf_op jit(solution)/shard_map/stbd,cd->stbc/dot_general | solution.py:156
  111.3 0.5 fusion.62
  111.9 2.3 %convert_reduce_fusion = f32[128]{0:T(128)S(1)} fusion(bf16[512,10,2,64]{0,3,2,1:T(8,128)(2,1)} %get-tuple-element.43, bf16[512,10,2,64]{0,3,2,1:T(8,128)(2,1)} %get-tuple-element.42), kind=kLoop, calls=%fused_computation | loop fusion | flops 6553472 | bytes 2621952 | tf_op jit(solution)/shard_map/reduce_sum | solution.py:159
  114.3 2.9 %fusion.47 = f32[24576]{0:T(1024)S(1)} fusion(f32[192,128]{1,0:T(8,128)} %fusion.27, bf16[512,10,2,64]{0,3,2,1:T(8,128)(2,1)} %copy-done.11, bf16[512,10,2,64]{0,3,2,1:T(8,128)(2,1)} %copy-done.12, bf16[512,10,2,64]{0,3,2,1:T(8,128)(2,1)} %copy-done.10, bf16[512,10,2,64]{0,3,2,1:T(8,128)(2,1)S(1)} %copy-done.9, bf16[512,10,2,64]{0,3,2,1:T(8,128)(2,1)S(1)} %copy-done.8), kind=kOutput, calls=%fused_computation.63 | convolution fusion | flops 520404992 | bytes 6750208 | tf_op jit(solution)/shard_map/stbk,stbf->kf/dot_general | solution.py:158
  117.5 1.3 collective-permute-done
  118.7 0.8 all-to-all-done.3
  119.5 1.6 %fusion.3 = bf16[512,1280]{1,0:T(8,128)(2,1)} fusion(f32[512,1280]{1,0:T(8,128)S(1)} %fusion.77, bf16[256,1280]{1,0:T(8,128)(2,1)S(1)} %bitcast.118, s32[256]{0:T(256)S(1)} %get-tuple-element.57), kind=kOutput, calls=%fused_computation.8 | convolution fusion | flops 337248256 | bytes 4588544 | tf_op jit(solution)/shard_map/dot_general | solution.py:169
  121.1 1.6 %copy.80 = bf16[512,1280]{0,1:T(8,128)(2,1)S(1)} copy(bf16[512,1280]{1,0:T(8,128)(2,1)} %fusion.3) | data formatting | bytes 2621440 | tf_op jit(solution)/shard_map/convert_element_type | solution.py:170
  122.7 1.4 collective-permute-start.1
  124.2 3.8 %multiply_convert_fusion.1 = (bf16[512,10,2,64]{0,3,2,1:T(8,128)(2,1)S(1)}, bf16[512,10,2,64]{0,3,2,1:T(8,128)(2,1)S(1)}) fusion(f32[512,10,2,128]{0,3,2,1:T(8,128)} %copy-done.2, bf16[512,10,2,64]{0,3,2,1:T(8,128)(2,1)S(1)} %bitcast.121, bf16[64,64]{1,0:T(8,128)(2,1)S(1)} %copy-done.19), kind=kOutput, calls=%fused_computation.20 | convolution fusion | flops 90439680 | bytes 9183232 | tf_op jit(solution)/shard_map/stbd,cd->stbc/dot_general | solution.py:173
  128.0 1.5 %collective-permute-start.2 = (f32[28800]{0:T(1024)S(1)}, f32[28800]{0:T(1024)S(1)}, u32[]{:S(2)}, u32[]{:S(2)}) collective-permute-start(f32[28800]{0:T(1024)S(1)} %add.147), channel_id=1, source_target_pairs={{0,4},{1,5},{2,6},{3,7},{4,0},{5,1},{6,2},{7,3},{8,12},{9,13},{10,... | collective-permute-start | bytes 345608 | tf_op jit(solution)/shard_map/ppermute | solution.py:25
  129.6 1.2 fusion.7
  130.7 2.5 %collective-permute-done.2 = f32[28800]{0:T(1024)S(1)} collective-permute-done((f32[28800]{0:T(1024)S(1)}, f32[28800]{0:T(1024)S(1)}, u32[]{:S(2)}, u32[]{:S(2)}) %collective-permute-start.2) | collective-permute-done | bytes 115232 | tf_op jit(solution)/shard_map/ppermute | solution.py:25
  133.2 1.0 collective-permute-start.3
  134.2 1.6 %fusion.114 = (f32[512,10,2,64]{0,3,2,1:T(8,128)S(1)}, f32[512,10,2,64]{0,3,2,1:T(8,128)S(1)}, f32[512,10,2,64]{0,3,2,1:T(8,128)S(1)}) fusion(f32[512,10,2,192]{0,3,2,1:T(8,128)S(1)} %fusion.7), kind=kLoop, calls=%fused_computation.137 | loop fusion | bytes 15728640 | tf_op jit(solution)/shard_map/slice | solution.py:181
  135.8 2.3 %collective-permute-done.3 = f32[28800]{0:T(1024)S(1)} collective-permute-done((f32[28800]{0:T(1024)S(1)}, f32[28800]{0:T(1024)S(1)}, u32[]{:S(2)}, u32[]{:S(2)}) %collective-permute-start.3) | collective-permute-done | bytes 115232 | tf_op jit(solution)/shard_map/ppermute | solution.py:25
  138.2 1.7 %collective-permute-start.4 = (f32[28800]{0:T(1024)S(1)}, f32[28800]{0:T(1024)S(1)}, u32[]{:S(2)}, u32[]{:S(2)}) collective-permute-start(f32[28800]{0:T(1024)S(1)} %add.149), channel_id=1, source_target_pairs={{0,16},{1,17},{2,18},{3,19},{4,20},{5,21},{6,22},{7,23},{8,24},{9,... | collective-permute-start | bytes 345608 | tf_op jit(solution)/shard_map/ppermute | solution.py:25
  139.9 1.0 add_convert_fusion
  140.9 1.6 %copy.82 = bf16[512,1536]{1,0:T(8,128)(2,1)} copy(bf16[512,1536]{0,1:T(8,128)(2,1)S(1)} %bitcast.115) | data formatting | bytes 3145728
  142.5 2.8 %collective-permute-done.4 = f32[28800]{0:T(1024)S(1)} collective-permute-done((f32[28800]{0:T(1024)S(1)}, f32[28800]{0:T(1024)S(1)}, u32[]{:S(2)}, u32[]{:S(2)}) %collective-permute-start.4) | collective-permute-done | bytes 115232 | tf_op jit(solution)/shard_map/ppermute | solution.py:25
  145.3 0.5 slice.118
  145.8 0.6 slice_bitcast_fusion
  146.4 0.7 slice.101
  (68 shorter events, 4.6 us)
Async XLA Ops:
  0.6 15.3 %copy-start = (bf16[192,128]{1,0:T(8,128)(2,1)S(1)}, bf16[192,128]{1,0:T(8,128)(2,1)}, u32[]{:S(2)}) copy-start(bf16[192,128]{1,0:T(8,128)(2,1)} %param.11) | copy-start | bytes 147460
  3.7 10.6 %copy-start.1 = (bf16[512,1536]{1,0:T(8,128)(2,1)S(1)}, bf16[512,1536]{1,0:T(8,128)(2,1)}, u32[]{:S(2)}) copy-start(bf16[512,1536]{1,0:T(8,128)(2,1)} %param.10) | copy-start | bytes 4718596
  6.9 29.4 %all-to-all-start = ((bf16[32,8,1664]{2,1,0:T(8,128)(2,1)}), bf16[32,8,1664]{2,1,0:T(8,128)(2,1)}, u32[]{:S(2)}, u32[]{:S(2)}) async-start(bf16[32,8,1664]{2,1,0:T(8,128)(2,1)} %maximum_bitcast_fusion), calls=%async_computation | async-start | bytes 1703936 | tf_op jit(solution)/shard_map/all_to_all | solution.py:110
  15.0 0.7 copy-start.20
  15.1 0.8 copy-start.22
  15.7 1.2 copy-start.10
  15.7 1.5 %copy-start.11 = (bf16[512,10,2,64]{0,3,2,1:T(8,128)(2,1)}, bf16[512,10,2,64]{0,3,2,1:T(8,128)(2,1)S(1)}, u32[]{:S(2)}) copy-start(bf16[512,10,2,64]{0,3,2,1:T(8,128)(2,1)S(1)} %get-tuple-element.49) | copy-start | bytes 3932164
  15.7 2.0 %copy-start.12 = (bf16[512,10,2,64]{0,3,2,1:T(8,128)(2,1)}, bf16[512,10,2,64]{0,3,2,1:T(8,128)(2,1)S(1)}, u32[]{:S(2)}) copy-start(bf16[512,10,2,64]{0,3,2,1:T(8,128)(2,1)S(1)} %get-tuple-element.50) | copy-start | bytes 3932164
  17.7 2.3 %copy-start.2 = (f32[512,10,2,128]{0,3,2,1:T(8,128)}, f32[512,10,2,128]{0,3,2,1:T(8,128)S(1)}, u32[]{:S(2)}) copy-start(f32[512,10,2,128]{0,3,2,1:T(8,128)S(1)} %broadcast_add_fusion) | copy-start | bytes 15728644
  17.7 2.3 %copy-start.19 = (bf16[64,64]{1,0:T(8,128)(2,1)S(1)}, bf16[64,64]{1,0:T(8,128)(2,1)}, u32[]{:S(2)}) copy-start(bf16[64,64]{1,0:T(8,128)(2,1)} %param.13) | copy-start | bytes 24580
  20.0 1.1 copy-start.3
  39.1 0.8 copy-start.13
  39.1 1.1 copy-start.15
  39.1 1.2 copy-start.17
  40.3 1.5 copy-start.5
  40.3 0.8 copy-start.21
  43.0 21.5 %all-to-all-start.1 = ((bf16[32,8,1280]{2,1,0:T(8,128)(2,1)}), bf16[32,8,1280]{2,1,0:T(8,128)(2,1)S(1)}, u32[]{:S(2)}, u32[]{:S(2)}) async-start(bf16[32,8,1280]{2,1,0:T(8,128)(2,1)} %fusion.14), calls=%async_computation.1 | async-start | bytes 1310720 | tf_op jit(solution)/shard_map/all_to_all | solution.py:134
  69.9 21.4 %all-to-all-start.2 = ((bf16[32,8,1280]{2,1,0:T(8,128)(2,1)}), bf16[32,8,1280]{2,1,0:T(8,128)(2,1)S(1)}, u32[]{:S(2)}, u32[]{:S(2)}) async-start(bf16[32,8,1280]{2,1,0:T(8,128)(2,1)} %fusion.15), calls=%async_computation.2 | async-start | bytes 1310720 | tf_op jit(solution)/shard_map/all_to_all | solution.py:141
  93.3 1.7 %copy-start.6 = (f32[256,10,2,128]{0,3,2,1:T(8,128)S(1)}, f32[256,10,2,128]{0,3,2,1:T(8,128)}, u32[]{:S(2)}) copy-start(f32[256,10,2,128]{0,3,2,1:T(8,128)} %copy-done.5) | copy-start | bytes 7864324
  95.0 1.1 copy-start.14
  95.0 1.3 copy-start.16
  95.0 1.5 %copy-start.18 = (bf16[256,10,2,64]{0,3,2,1:T(8,128)(2,1)S(1)}, bf16[256,10,2,64]{0,3,2,1:T(8,128)(2,1)}, u32[]{:S(2)}) copy-start(bf16[256,10,2,64]{0,3,2,1:T(8,128)(2,1)} %copy-done.17) | copy-start | bytes 1966084
  98.1 21.4 %all-to-all-start.3 = ((bf16[32,8,1280]{2,1,0:T(8,128)(2,1)}), bf16[32,8,1280]{2,1,0:T(8,128)(2,1)S(1)}, u32[]{:S(2)}, u32[]{:S(2)}) async-start(bf16[32,8,1280]{2,1,0:T(8,128)(2,1)} %bitcast.119), calls=%async_computation.3 | async-start | bytes 1310720 | tf_op jit(solution)/shard_map/all_to_all | solution.py:150
  105.4 5.9 %copy-start.4 = (bf16[512,10,2,64]{0,3,2,1:T(8,128)(2,1)S(1)}, bf16[512,10,2,64]{0,3,2,1:T(8,128)(2,1)}, u32[]{:S(2)}) copy-start(bf16[512,10,2,64]{0,3,2,1:T(8,128)(2,1)} %copy-done.3) | copy-start | bytes 3932164
  105.4 5.9 %copy-start.7 = (bf16[512,1280]{0,1:T(8,128)(2,1)S(1)}, bf16[512,1280]{0,1:T(8,128)(2,1)}, u32[]{:S(2)}) copy-start(bf16[512,1280]{0,1:T(8,128)(2,1)} %copy.71) | copy-start | bytes 3932164
  111.8 2.3 %copy-start.8 = (bf16[512,10,2,64]{0,3,2,1:T(8,128)(2,1)S(1)}, bf16[512,10,2,64]{0,3,2,1:T(8,128)(2,1)}, u32[]{:S(2)}) copy-start(bf16[512,10,2,64]{0,3,2,1:T(8,128)(2,1)} %get-tuple-element.42) | copy-start | bytes 3932164
  111.8 2.5 %copy-start.9 = (bf16[512,10,2,64]{0,3,2,1:T(8,128)(2,1)S(1)}, bf16[512,10,2,64]{0,3,2,1:T(8,128)(2,1)}, u32[]{:S(2)}) copy-start(bf16[512,10,2,64]{0,3,2,1:T(8,128)(2,1)} %get-tuple-element.43) | copy-start | bytes 3932164
  117.3 1.4 collective-permute-start
  122.7 5.3 %collective-permute-start.1 = (f32[28800]{0:T(1024)S(1)}, f32[28800]{0:T(1024)S(1)}, u32[]{:S(2)}, u32[]{:S(2)}) collective-permute-start(f32[28800]{0:T(1024)S(1)} %fusion.113), channel_id=1, source_target_pairs={{0,2},{1,3},{2,0},{3,1},{4,6},{5,7},{6,4},{7,5},{8,10},{9,11},{10,... | collective-permute-start | bytes 345608 | tf_op jit(solution)/shard_map/ppermute | solution.py:25
  128.0 5.2 %collective-permute-start.2 = (f32[28800]{0:T(1024)S(1)}, f32[28800]{0:T(1024)S(1)}, u32[]{:S(2)}, u32[]{:S(2)}) collective-permute-start(f32[28800]{0:T(1024)S(1)} %add.147), channel_id=1, source_target_pairs={{0,4},{1,5},{2,6},{3,7},{4,0},{5,1},{6,2},{7,3},{8,12},{9,13},{10,... | collective-permute-start | bytes 345608 | tf_op jit(solution)/shard_map/ppermute | solution.py:25
  133.2 4.9 %collective-permute-start.3 = (f32[28800]{0:T(1024)S(1)}, f32[28800]{0:T(1024)S(1)}, u32[]{:S(2)}, u32[]{:S(2)}) collective-permute-start(f32[28800]{0:T(1024)S(1)} %add.148), channel_id=1, source_target_pairs={{0,8},{1,9},{2,10},{3,11},{4,12},{5,13},{6,14},{7,15},{8,0},{9,1},... | collective-permute-start | bytes 345608 | tf_op jit(solution)/shard_map/ppermute | solution.py:25
  138.2 7.1 %collective-permute-start.4 = (f32[28800]{0:T(1024)S(1)}, f32[28800]{0:T(1024)S(1)}, u32[]{:S(2)}, u32[]{:S(2)}) collective-permute-start(f32[28800]{0:T(1024)S(1)} %add.149), channel_id=1, source_target_pairs={{0,16},{1,17},{2,18},{3,19},{4,20},{5,21},{6,22},{7,23},{8,24},{9,... | collective-permute-start | bytes 345608 | tf_op jit(solution)/shard_map/ppermute | solution.py:25
